TPU v7x, 128 devices: a whole 4x4x4 slice. The times are simulated.
128 devices in a mesh: shaft: 32 (over z, y, core), ply: 4 (over x).
Axes of the slice: x: 4, y: 4, z: 4, core: 2. Of those that a mesh axis runs over, the one named last changes fastest.
Arguments:
- displacement: float32 [64, 4, 8192], P(None, 'ply', 'shaft'), may hold values from -6 to 6
- velocity: float32 [64, 4, 8192], P(None, 'ply', 'shaft'), may hold values from -6 to 6
- external: float32 [64, 4, 8192], P(None, 'ply', 'shaft'), may hold values from -6 to 6
- mass_inverse: float32 [64, 4, 8192], P(None, 'ply', 'shaft'), may hold values from 0.5 to 2
- pattern: int32 [5, 4, 8192], P(None, 'ply', 'shaft'), may hold values from 0 to 8, as said below
- coupled: int32 [4, 8192], P('ply', 'shaft'), may hold values from 1 to 5
- stiffness_old: bfloat16 [5, 64, 64, 32768], P(None, None, None, ('shaft', 'ply')), may hold values from -0.3125 to 0.3125
- history_old: float32 [48, 32768], P(None, ('shaft', 'ply')), may hold values from -6 to 6
- decay_old: float32 [48, 32768], P(None, ('shaft', 'ply')), may hold values from 0.2 to 0.98
- strain_map: float32 [48, 64], replicated, may hold values from -0.75 to 0.75
- send_slot: int32 [128, 2, 32], P(('shaft', 'ply')), may hold values from 0 to 255, as said below
- arrive_place: int32 [128, 2, 32], P(('shaft', 'ply')), may hold values from 0 to 255, as said below
- arrive_count: int32 [128, 2], P(('shaft', 'ply')), may hold values from 0 to 32, as said below
Outputs:
- final_displacement: float32 [64, 4, 8192], P(None, 'ply', 'shaft')
- final_velocity: float32 [64, 4, 8192], P(None, 'ply', 'shaft')
- final_history: float32 [48, 4, 8192], P(None, 'ply', 'shaft')
Inputs may be any that keep to these rules, and one draw needn't show every extreme that they name: pattern[0, q, s] is 4, the block itself; the codes of one block are distinct; code c names the block at ply offset c // 3 - 1 and shaft offset c % 3 - 1. coupled[q, s] counts the live entries of pattern[:, q, s]. send_slot[d, r, i] for i below the matching arrival count of the receiving neighbour is the old slot on d of the i-th block that moves from d toward neighbour r; entries past the count are 0; no slot of d is named twice. arrive_place[e, r, i] for i < arrive_count[e, r] is the new place on e of the i-th block arriving from neighbour r; these places are exactly the slots that e sends away, and all other blocks of e keep their slot; entries past the count are 0. `arrive_count`: as many blocks move from e to a neighbour as from that neighbour to e; counts toward a missing neighbour are 0.
All inputs are finite; a program needn't handle non-finite values.
Results may differ from a plain program's by a relative error of at most 0.00082.
Values may be sent and summed in bfloat16 or wider, within the bound.
No kernel may reach another device: no remote copies, remote signals or barrier semaphores. Data moves between devices by JAX's collectives and lax.ppermute only.
A program may use at most 192 MiB of HBM per device.

v0:
```python
import jax
import jax.numpy as jnp
from jax import lax
from jax.sharding import PartitionSpec as P

ITERS = 4


time_step = 0.25


def padded_2(value, sides, width):
    for axis, dim in sides:
        size, length = (lax.axis_size(axis), value.shape[dim])
        up = [(i, (i + 1) % size) for i in range(size - 1)]
        down = [(j, i) for i, j in up]
        last = lax.slice_in_dim(value, length - width, length, axis=dim)
        first = lax.slice_in_dim(value, 0, width, axis=dim)
        before = lax.ppermute(last, axis, up)
        after = lax.ppermute(first, axis, down)
        value = jnp.concatenate([before, value, after], axis=dim)
    return value


def select_neighbours(padded, pattern, coupled):
    blocks = pattern.shape[-1]
    shifted = [
        padded[:, code_index // 3, code_index % 3 : code_index % 3 + blocks]
        for code_index in range(9)
    ]
    gathered = []
    for slot_index in range(pattern.shape[0]):
        picked = jnp.zeros_like(shifted[0])
        for code_index in range(9):
            picked = jnp.where(pattern[slot_index] == code_index, shifted[code_index], picked)
        gathered.append(jnp.where(slot_index < coupled, picked, jnp.zeros_like(picked)))
    return jnp.stack(gathered)


def both_rims(padded, capacity):
    return jnp.concatenate([padded[..., :capacity], padded[..., -capacity:]], -1)


def on_device(
    displacement,
    velocity,
    external,
    mass_inverse,
    pattern,
    coupled,
    stiffness_old,
    history_old,
    decay_old,
    strain_map,
    send_slot,
    arrive_place,
    arrive_count,
):
    blocks = displacement.shape[-1]
    capacity = send_slot.shape[2]
    outgoing = send_slot[0].reshape(-1)
    filled = jnp.arange(capacity, dtype=jnp.int32)[None, :] < arrive_count[0][:, None]
    target = jnp.where(filled, arrive_place[0], blocks).reshape(-1)
    placing = (
        jnp.arange(blocks + 1, dtype=jnp.int32)
        .at[target]
        .set(blocks + jnp.arange(2 * capacity, dtype=jnp.int32))[:blocks]
    )
    moving_state = jnp.concatenate(
        [jnp.take(history_old, outgoing, axis=1), jnp.take(decay_old, outgoing, axis=1)], 0
    )
    state_padded = padded_2(moving_state, (("shaft", 1),), capacity)
    state_arrived = both_rims(state_padded, capacity)
    depth = history_old.shape[0]
    history = jnp.take(jnp.concatenate([history_old, state_arrived[:depth]], 1), placing, axis=1)
    decay = jnp.take(jnp.concatenate([decay_old, state_arrived[depth:]], 1), placing, axis=1)
    stiff_buffer = jnp.take(stiffness_old, outgoing, axis=3)
    stiff_padded = padded_2(stiff_buffer, (("shaft", 3),), capacity)
    stiffness = jnp.take(
        jnp.concatenate([stiffness_old, both_rims(stiff_padded, capacity)], 3), placing, axis=3
    )
    moved = displacement[:, 0, :]
    speeds = velocity[:, 0, :]
    forcing = external[:, 0, :]
    scaling = mass_inverse[:, 0, :]
    codes = pattern[:, 0, :]
    live_count = coupled[0]
    for repeat in range(ITERS):
        rounded = moved.astype(jnp.bfloat16)[:, None, :]
        padded = padded_2(rounded, (("shaft", 2), ("ply", 1)), 1)
        neighbours = select_neighbours(padded, codes, live_count)
        force = jnp.einsum(
            "kijb,kjb->ib", stiffness, neighbours, preferred_element_type=jnp.float32
        ) + jnp.dot(strain_map.T, history, precision=lax.Precision.HIGHEST)
        speeds = speeds + time_step * (scaling * (forcing - force))
        advanced = moved + time_step * speeds
        history = decay * history + jnp.dot(
            strain_map, advanced - moved, precision=lax.Precision.HIGHEST
        )
        moved = advanced
    return (moved[:, None, :], speeds[:, None, :], history[:, None, :])


def solution(mesh):
    in_specs = (
        P(None, "ply", "shaft"),
        P(None, "ply", "shaft"),
        P(None, "ply", "shaft"),
        P(None, "ply", "shaft"),
        P(None, "ply", "shaft"),
        P("ply", "shaft"),
        P(None, None, None, ("shaft", "ply")),
        P(None, ("shaft", "ply")),
        P(None, ("shaft", "ply")),
        P(),
        P(("shaft", "ply"), None, None),
        P(("shaft", "ply"), None, None),
        P(("shaft", "ply"), None),
    )
    out_specs = (P(None, "ply", "shaft"), P(None, "ply", "shaft"), P(None, "ply", "shaft"))
    return jax.shard_map(
        on_device, mesh=mesh, in_specs=in_specs, out_specs=out_specs, check_vma=False
    )
```

profile of v0, /device:TPU:96, one launch (start us, length us, event | category | flops | bytes accessed | tf_op | source)
XLA Modules:
  0.0 238.9 jit_solution(17735958958371557575)
XLA Ops:
  1.6 4.2 %collective-permute-start.1 = (bf16[64,1,1]{2,0,1:T(8,128)(2,1)S(1)}, bf16[64,1,1]{2,0,1:T(8,128)(2,1)S(1)}, u32[]{:S(2)}, u32[]{:S(2)}) collective-permute-start(bf16[64,1,1]{2,0,1:T(8,128)(2,1)S(1)} %get-tuple-element.90), channel_id=1, source_target_pairs={{4,0},{8,4},{12,8},{16,12},{20,16},{24,20},{28,24},{32,28},{36,32}... | collective-permute-start | bytes 392 | tf_op jit(solution)/shard_map/ppermute | solution.py:20
  5.8 1.9 collective-permute-start
  9.3 29.5 %copy.70 = bf16[5,64,64,256]{2,1,0,3:T(8,128)(2,1)} copy(bf16[5,64,64,256]{3,2,1,0:T(8,128)(2,1)} %param.23) | data formatting | bytes 20971520 | tf_op args[6]
  38.9 10.6 %gather_fusion = bf16[64,5,64,64]{3,2,1,0:T(8,128)(2,1)} fusion(bf16[5,64,64,256]{2,1,0,3:T(8,128)(2,1)} %copy.70, s32[1024]{0:T(1024)S(1)} %get-tuple-element.122), kind=kCustom, calls=%fused_computation.4 | custom fusion | bytes 5243136 | tf_op jit(solution)/shard_map/jit(_take)/gather | solution.py:77
  49.4 3.0 %select_bitcast_fusion = bf16[5,64,64,64]{2,1,0,3:T(8,128)(2,1)S(1)} fusion(bf16[64,5,64,64]{3,2,1,0:T(8,128)(2,1)} %gather_fusion, pred[64]{0:T(512)(128)(4,1)S(1)} %compare_and_fusion), kind=kLoop, calls=%fused_computation.17 | loop fusion | flops 1310720 | bytes 5242944 | tf_op jit(solution)/shard_map/jit(_take)/select_n | solution.py:77
  52.4 3.6 %fusion.79 = (bf16[5,64,64,32]{2,1,0,3:T(8,128)(2,1)}, bf16[5,64,64,32]{2,1,0,3:T(8,128)(2,1)}) fusion(bf16[5,64,64,64]{2,1,0,3:T(8,128)(2,1)S(1)} %select_bitcast_fusion), kind=kLoop, calls=%fused_computation.243 | loop fusion | bytes 5242880 | tf_op jit(solution)/shard_map/slice | solution.py:17
  58.0 5.8 %collective-permute-start.5 = (bf16[5,64,64,32]{2,1,0,3:T(8,128)(2,1)}, bf16[5,64,64,32]{2,1,0,3:T(8,128)(2,1)}, u32[]{:S(2)}, u32[]{:S(2)}) collective-permute-start(bf16[5,64,64,32]{2,1,0,3:T(8,128)(2,1)} %get-tuple-element.78), channel_id=1, source_target_pairs={{4,0},{8,4},{12,8},{16,12},{20,16},{24,20},{28,24},{32,28},{36,32}... | collective-permute-start | bytes 3932168 | tf_op jit(solution)/shard_map/ppermute | solution.py:20
  65.3 1.9 collective-permute-start.6
  68.5 5.8 %collective-permute-start.7 = (f32[96,32]{0,1:T(8,128)S(1)}, f32[96,32]{0,1:T(8,128)S(1)}, u32[]{:S(2)}, u32[]{:S(2)}) collective-permute-start(f32[96,32]{0,1:T(8,128)S(1)} %get-tuple-element.79), channel_id=1, source_target_pairs={{4,0},{8,4},{12,8},{16,12},{20,16},{24,20},{28,24},{32,28},{36,32}... | collective-permute-start | bytes 36872 | tf_op jit(solution)/shard_map/ppermute | solution.py:20
  75.9 15.6 %collective-permute-done.6 = f32[96,32]{0,1:T(8,128)S(1)} collective-permute-done((f32[96,32]{0,1:T(8,128)S(1)}, f32[96,32]{0,1:T(8,128)S(1)}, u32[]{:S(2)}, u32[]{:S(2)}) %collective-permute-start.6) | collective-permute-done | bytes 12320 | tf_op jit(solution)/shard_map/ppermute | solution.py:19
  91.5 3.4 %collective-permute-start.3 = (bf16[64,1,258]{2,0,1:T(8,128)(2,1)S(1)}, bf16[64,1,258]{2,0,1:T(8,128)(2,1)S(1)}, u32[]{:S(2)}, u32[]{:S(2)}) collective-permute-start(bf16[64,1,258]{2,0,1:T(8,128)(2,1)S(1)} %pad_maximum_fusion.4), channel_id=1, source_target_pairs={{0,1},{1,2},{2,3},{4,5},{5,6},{6,7},{8,9},{9,10},{10,11},{12,13},{... | collective-permute-start | bytes 99080 | tf_op jit(solution)/shard_map/ppermute | solution.py:19
  97.8 21.5 %pad_maximum_fusion = bf16[5,64,64,320]{2,1,0,3:T(8,128)(2,1)} fusion(bf16[5,64,64,32]{2,1,0,3:T(8,128)(2,1)} %collective-permute-done.5, bf16[5,64,64,32]{2,1,0,3:T(8,128)(2,1)} %collective-permute-done.4, bf16[5,64,64,256]{2,1,0,3:T(8,128)(2,1)} %copy.70), kind=kLoop, calls=%fused_computation.15 | loop fusion | flops 13107200 | bytes 26214400 | tf_op jit(solution)/shard_map/concatenate | solution.py:80
  119.4 19.9 %gather_fusion.1 = bf16[256,5,64,64]{3,2,1,0:T(8,128)(2,1)} fusion(bf16[5,64,64,320]{2,1,0,3:T(8,128)(2,1)} %pad_maximum_fusion, s32[1024]{0:T(1024)S(1)} %pad_clamp_fusion.1), kind=kCustom, calls=%fused_computation.5 | custom fusion | bytes 20972544 | tf_op jit(solution)/shard_map/jit(_take)/gather | solution.py:79
  139.3 10.3 %fusion = f32[256,64]{1,0:T(8,128)S(1)} fusion(f32[256,64,5]{1,2,0:T(8,128)S(1)} %copy.110, bf16[256,5,64,64]{3,2,1,0:T(8,128)(2,1)} %gather_fusion.1, pred[256]{0:T(512)(128)(4,1)S(1)} %compare_and_fusion.1), kind=kLoop, calls=%fused_computation.11 | loop fusion | flops 20955136 | bytes 10879232
  150.1 1.9 collective-permute-start.8
  152.0 5.8 %collective-permute-start.9 = (bf16[64,1,1]{2,0,1:T(8,128)(2,1)S(1)}, bf16[64,1,1]{2,0,1:T(8,128)(2,1)S(1)}, u32[]{:S(2)}, u32[]{:S(2)}) collective-permute-start(bf16[64,1,1]{2,0,1:T(8,128)(2,1)S(1)} %get-tuple-element.88), channel_id=1, source_target_pairs={{4,0},{8,4},{12,8},{16,12},{20,16},{24,20},{28,24},{32,28},{36,32}... | collective-permute-start | bytes 392 | tf_op jit(solution)/shard_map/ppermute | solution.py:20
  160.6 5.0 %collective-permute-start.11 = (bf16[64,1,258]{2,0,1:T(8,128)(2,1)S(1)}, bf16[64,1,258]{2,0,1:T(8,128)(2,1)S(1)}, u32[]{:S(2)}, u32[]{:S(2)}) collective-permute-start(bf16[64,1,258]{2,0,1:T(8,128)(2,1)S(1)} %pad_maximum_fusion.5), channel_id=1, source_target_pairs={{0,1},{1,2},{2,3},{4,5},{5,6},{6,7},{8,9},{9,10},{10,11},{12,13},{... | collective-permute-start | bytes 99080 | tf_op jit(solution)/shard_map/ppermute | solution.py:19
  168.3 10.3 %fusion.1 = f32[256,64]{1,0:T(8,128)S(1)} fusion(f32[256,64,5]{1,2,0:T(8,128)S(1)} %copy.111, bf16[256,5,64,64]{3,2,1,0:T(8,128)(2,1)} %gather_fusion.1, pred[256]{0:T(512)(128)(4,1)S(1)} %compare_and_fusion.1), kind=kLoop, calls=%fused_computation.12 | loop fusion | flops 20955136 | bytes 10879232
  180.8 5.8 %collective-permute-start.13 = (bf16[64,1,1]{2,0,1:T(8,128)(2,1)S(1)}, bf16[64,1,1]{2,0,1:T(8,128)(2,1)S(1)}, u32[]{:S(2)}, u32[]{:S(2)}) collective-permute-start(bf16[64,1,1]{2,0,1:T(8,128)(2,1)S(1)} %get-tuple-element.84), channel_id=1, source_target_pairs={{4,0},{8,4},{12,8},{16,12},{20,16},{24,20},{28,24},{32,28},{36,32}... | collective-permute-start | bytes 392 | tf_op jit(solution)/shard_map/ppermute | solution.py:20
  189.3 4.9 %collective-permute-start.15 = (bf16[64,1,258]{2,0,1:T(8,128)(2,1)S(1)}, bf16[64,1,258]{2,0,1:T(8,128)(2,1)S(1)}, u32[]{:S(2)}, u32[]{:S(2)}) collective-permute-start(bf16[64,1,258]{2,0,1:T(8,128)(2,1)S(1)} %pad_maximum_fusion.6), channel_id=1, source_target_pairs={{0,1},{1,2},{2,3},{4,5},{5,6},{6,7},{8,9},{9,10},{10,11},{12,13},{... | collective-permute-start | bytes 99080 | tf_op jit(solution)/shard_map/ppermute | solution.py:19
  197.1 10.3 %fusion.2 = f32[256,64]{1,0:T(8,128)S(1)} fusion(f32[256,64,5]{1,2,0:T(8,128)S(1)} %copy.112, bf16[256,5,64,64]{3,2,1,0:T(8,128)(2,1)} %gather_fusion.1, pred[256]{0:T(512)(128)(4,1)S(1)} %compare_and_fusion.1), kind=kLoop, calls=%fused_computation.13 | loop fusion | flops 20955136 | bytes 10879232
  209.8 5.8 %collective-permute-start.17 = (bf16[64,1,1]{2,0,1:T(8,128)(2,1)S(1)}, bf16[64,1,1]{2,0,1:T(8,128)(2,1)S(1)}, u32[]{:S(2)}, u32[]{:S(2)}) collective-permute-start(bf16[64,1,1]{2,0,1:T(8,128)(2,1)S(1)} %get-tuple-element.82), channel_id=1, source_target_pairs={{4,0},{8,4},{12,8},{16,12},{20,16},{24,20},{28,24},{32,28},{36,32}... | collective-permute-start | bytes 392 | tf_op jit(solution)/shard_map/ppermute | solution.py:20
  218.4 4.9 %collective-permute-start.19 = (bf16[64,1,258]{2,0,1:T(8,128)(2,1)S(1)}, bf16[64,1,258]{2,0,1:T(8,128)(2,1)S(1)}, u32[]{:S(2)}, u32[]{:S(2)}) collective-permute-start(bf16[64,1,258]{2,0,1:T(8,128)(2,1)S(1)} %pad_maximum_fusion.7), channel_id=1, source_target_pairs={{0,1},{1,2},{2,3},{4,5},{5,6},{6,7},{8,9},{9,10},{10,11},{12,13},{... | collective-permute-start | bytes 99080 | tf_op jit(solution)/shard_map/ppermute | solution.py:19
  226.1 10.3 %fusion.3 = f32[256,64]{1,0:T(8,128)S(1)} fusion(f32[256,64,5]{1,2,0:T(8,128)S(1)} %copy.113, bf16[256,5,64,64]{3,2,1,0:T(8,128)(2,1)} %gather_fusion.1, pred[256]{0:T(512)(128)(4,1)S(1)} %compare_and_fusion.1), kind=kLoop, calls=%fused_computation.14 | loop fusion | flops 20955136 | bytes 10879232
  (138 shorter events, 35.5 us)
Async XLA Ops:
  0.6 149.1 %copy-start = (f32[48,64]{1,0:T(8,128)S(1)}, f32[48,64]{1,0:T(8,128)}, u32[]{:S(2)}) copy-start(f32[48,64]{1,0:T(8,128)} %param.26) | copy-start | bytes 36868
  1.6 66.9 %collective-permute-start.1 = (bf16[64,1,1]{2,0,1:T(8,128)(2,1)S(1)}, bf16[64,1,1]{2,0,1:T(8,128)(2,1)S(1)}, u32[]{:S(2)}, u32[]{:S(2)}) collective-permute-start(bf16[64,1,1]{2,0,1:T(8,128)(2,1)S(1)} %get-tuple-element.90), channel_id=1, source_target_pairs={{4,0},{8,4},{12,8},{16,12},{20,16},{24,20},{28,24},{32,28},{36,32}... | collective-permute-start | bytes 392 | tf_op jit(solution)/shard_map/ppermute | solution.py:20
  5.8 68.5 %collective-permute-start = (bf16[64,1,1]{2,0,1:T(8,128)(2,1)S(1)}, bf16[64,1,1]{2,0,1:T(8,128)(2,1)S(1)}, u32[]{:S(2)}, u32[]{:S(2)}) collective-permute-start(bf16[64,1,1]{2,0,1:T(8,128)(2,1)S(1)} %get-tuple-element.89), channel_id=1, source_target_pairs={{0,4},{4,8},{8,12},{12,16},{16,20},{20,24},{24,28},{28,32},{32,36}... | collective-permute-start | bytes 392 | tf_op jit(solution)/shard_map/ppermute | solution.py:19
  56.0 41.7 %collective-permute-start.4 = (bf16[5,64,64,32]{2,1,0,3:T(8,128)(2,1)}, bf16[5,64,64,32]{2,1,0,3:T(8,128)(2,1)}, u32[]{:S(2)}, u32[]{:S(2)}) collective-permute-start(bf16[5,64,64,32]{2,1,0,3:T(8,128)(2,1)} %get-tuple-element.77), channel_id=1, source_target_pairs={{0,4},{4,8},{8,12},{12,16},{16,20},{20,24},{24,28},{28,32},{32,36}... | collective-permute-start | bytes 3932168 | tf_op jit(solution)/shard_map/ppermute | solution.py:19
  58.0 39.8 %collective-permute-start.5 = (bf16[5,64,64,32]{2,1,0,3:T(8,128)(2,1)}, bf16[5,64,64,32]{2,1,0,3:T(8,128)(2,1)}, u32[]{:S(2)}, u32[]{:S(2)}) collective-permute-start(bf16[5,64,64,32]{2,1,0,3:T(8,128)(2,1)} %get-tuple-element.78), channel_id=1, source_target_pairs={{4,0},{8,4},{12,8},{16,12},{20,16},{24,20},{28,24},{32,28},{36,32}... | collective-permute-start | bytes 3932168 | tf_op jit(solution)/shard_map/ppermute | solution.py:20
  65.3 26.2 %collective-permute-start.6 = (f32[96,32]{0,1:T(8,128)S(1)}, f32[96,32]{0,1:T(8,128)S(1)}, u32[]{:S(2)}, u32[]{:S(2)}) collective-permute-start(f32[96,32]{0,1:T(8,128)S(1)} %get-tuple-element.80), channel_id=1, source_target_pairs={{0,4},{4,8},{8,12},{12,16},{16,20},{20,24},{24,28},{28,32},{32,36}... | collective-permute-start | bytes 36872 | tf_op jit(solution)/shard_map/ppermute | solution.py:19
  68.5 26.4 %collective-permute-start.7 = (f32[96,32]{0,1:T(8,128)S(1)}, f32[96,32]{0,1:T(8,128)S(1)}, u32[]{:S(2)}, u32[]{:S(2)}) collective-permute-start(f32[96,32]{0,1:T(8,128)S(1)} %get-tuple-element.79), channel_id=1, source_target_pairs={{4,0},{8,4},{12,8},{16,12},{20,16},{24,20},{28,24},{32,28},{36,32}... | collective-permute-start | bytes 36872 | tf_op jit(solution)/shard_map/ppermute | solution.py:20
  74.4 22.2 %collective-permute-start.2 = (bf16[64,1,258]{2,0,1:T(8,128)(2,1)S(1)}, bf16[64,1,258]{2,0,1:T(8,128)(2,1)S(1)}, u32[]{:S(2)}, u32[]{:S(2)}) collective-permute-start(bf16[64,1,258]{2,0,1:T(8,128)(2,1)S(1)} %pad_maximum_fusion.4), channel_id=1, source_target_pairs={{1,0},{2,1},{3,2},{5,4},{6,5},{7,6},{9,8},{10,9},{11,10},{13,12},{... | collective-permute-start | bytes 99080 | tf_op jit(solution)/shard_map/ppermute | solution.py:20
  91.5 5.2 %collective-permute-start.3 = (bf16[64,1,258]{2,0,1:T(8,128)(2,1)S(1)}, bf16[64,1,258]{2,0,1:T(8,128)(2,1)S(1)}, u32[]{:S(2)}, u32[]{:S(2)}) collective-permute-start(bf16[64,1,258]{2,0,1:T(8,128)(2,1)S(1)} %pad_maximum_fusion.4), channel_id=1, source_target_pairs={{0,1},{1,2},{2,3},{4,5},{5,6},{6,7},{8,9},{9,10},{10,11},{12,13},{... | collective-permute-start | bytes 99080 | tf_op jit(solution)/shard_map/ppermute | solution.py:19
  119.3 30.4 %copy-start.1 = (f32[64,1,256]{2,1,0:T(1,128)S(1)}, f32[64,1,256]{2,1,0:T(1,128)}, u32[]{:S(2)}) copy-start(f32[64,1,256]{2,1,0:T(1,128)} %param.19) | copy-start | bytes 196612
  119.4 30.4 %copy-start.2 = (f32[64,1,256]{2,1,0:T(1,128)S(1)}, f32[64,1,256]{2,1,0:T(1,128)}, u32[]{:S(2)}) copy-start(f32[64,1,256]{2,1,0:T(1,128)} %param.20) | copy-start | bytes 196612
  119.4 30.4 %copy-start.3 = (f32[64,1,256]{2,1,0:T(1,128)S(1)}, f32[64,1,256]{2,1,0:T(1,128)}, u32[]{:S(2)}) copy-start(f32[64,1,256]{2,1,0:T(1,128)} %param.17) | copy-start | bytes 196612
  150.1 7.9 %collective-permute-start.8 = (bf16[64,1,1]{2,0,1:T(8,128)(2,1)S(1)}, bf16[64,1,1]{2,0,1:T(8,128)(2,1)S(1)}, u32[]{:S(2)}, u32[]{:S(2)}) collective-permute-start(bf16[64,1,1]{2,0,1:T(8,128)(2,1)S(1)} %get-tuple-element.87), channel_id=1, source_target_pairs={{0,4},{4,8},{8,12},{12,16},{16,20},{20,24},{24,28},{28,32},{32,36}... | collective-permute-start | bytes 392 | tf_op jit(solution)/shard_map/ppermute | solution.py:19
  152.0 7.2 %collective-permute-start.9 = (bf16[64,1,1]{2,0,1:T(8,128)(2,1)S(1)}, bf16[64,1,1]{2,0,1:T(8,128)(2,1)S(1)}, u32[]{:S(2)}, u32[]{:S(2)}) collective-permute-start(bf16[64,1,1]{2,0,1:T(8,128)(2,1)S(1)} %get-tuple-element.88), channel_id=1, source_target_pairs={{4,0},{8,4},{12,8},{16,12},{20,16},{24,20},{28,24},{32,28},{36,32}... | collective-permute-start | bytes 392 | tf_op jit(solution)/shard_map/ppermute | solution.py:20
  159.3 6.6 %collective-permute-start.10 = (bf16[64,1,258]{2,0,1:T(8,128)(2,1)S(1)}, bf16[64,1,258]{2,0,1:T(8,128)(2,1)S(1)}, u32[]{:S(2)}, u32[]{:S(2)}) collective-permute-start(bf16[64,1,258]{2,0,1:T(8,128)(2,1)S(1)} %pad_maximum_fusion.5), channel_id=1, source_target_pairs={{1,0},{2,1},{3,2},{5,4},{6,5},{7,6},{9,8},{10,9},{11,10},{13,12},{... | collective-permute-start | bytes 99080 | tf_op jit(solution)/shard_map/ppermute | solution.py:20
  160.6 6.6 %collective-permute-start.11 = (bf16[64,1,258]{2,0,1:T(8,128)(2,1)S(1)}, bf16[64,1,258]{2,0,1:T(8,128)(2,1)S(1)}, u32[]{:S(2)}, u32[]{:S(2)}) collective-permute-start(bf16[64,1,258]{2,0,1:T(8,128)(2,1)S(1)} %pad_maximum_fusion.5), channel_id=1, source_target_pairs={{0,1},{1,2},{2,3},{4,5},{5,6},{6,7},{8,9},{9,10},{10,11},{12,13},{... | collective-permute-start | bytes 99080 | tf_op jit(solution)/shard_map/ppermute | solution.py:19
  178.8 7.7 %collective-permute-start.12 = (bf16[64,1,1]{2,0,1:T(8,128)(2,1)S(1)}, bf16[64,1,1]{2,0,1:T(8,128)(2,1)S(1)}, u32[]{:S(2)}, u32[]{:S(2)}) collective-permute-start(bf16[64,1,1]{2,0,1:T(8,128)(2,1)S(1)} %get-tuple-element.83), channel_id=1, source_target_pairs={{0,4},{4,8},{8,12},{12,16},{16,20},{20,24},{24,28},{28,32},{32,36}... | collective-permute-start | bytes 392 | tf_op jit(solution)/shard_map/ppermute | solution.py:19
  180.8 7.2 %collective-permute-start.13 = (bf16[64,1,1]{2,0,1:T(8,128)(2,1)S(1)}, bf16[64,1,1]{2,0,1:T(8,128)(2,1)S(1)}, u32[]{:S(2)}, u32[]{:S(2)}) collective-permute-start(bf16[64,1,1]{2,0,1:T(8,128)(2,1)S(1)} %get-tuple-element.84), channel_id=1, source_target_pairs={{4,0},{8,4},{12,8},{16,12},{20,16},{24,20},{28,24},{32,28},{36,32}... | collective-permute-start | bytes 392 | tf_op jit(solution)/shard_map/ppermute | solution.py:20
  188.0 6.4 %collective-permute-start.14 = (bf16[64,1,258]{2,0,1:T(8,128)(2,1)S(1)}, bf16[64,1,258]{2,0,1:T(8,128)(2,1)S(1)}, u32[]{:S(2)}, u32[]{:S(2)}) collective-permute-start(bf16[64,1,258]{2,0,1:T(8,128)(2,1)S(1)} %pad_maximum_fusion.6), channel_id=1, source_target_pairs={{1,0},{2,1},{3,2},{5,4},{6,5},{7,6},{9,8},{10,9},{11,10},{13,12},{... | collective-permute-start | bytes 99080 | tf_op jit(solution)/shard_map/ppermute | solution.py:20
  189.3 6.6 %collective-permute-start.15 = (bf16[64,1,258]{2,0,1:T(8,128)(2,1)S(1)}, bf16[64,1,258]{2,0,1:T(8,128)(2,1)S(1)}, u32[]{:S(2)}, u32[]{:S(2)}) collective-permute-start(bf16[64,1,258]{2,0,1:T(8,128)(2,1)S(1)} %pad_maximum_fusion.6), channel_id=1, source_target_pairs={{0,1},{1,2},{2,3},{4,5},{5,6},{6,7},{8,9},{9,10},{10,11},{12,13},{... | collective-permute-start | bytes 99080 | tf_op jit(solution)/shard_map/ppermute | solution.py:19
  207.9 7.9 %collective-permute-start.16 = (bf16[64,1,1]{2,0,1:T(8,128)(2,1)S(1)}, bf16[64,1,1]{2,0,1:T(8,128)(2,1)S(1)}, u32[]{:S(2)}, u32[]{:S(2)}) collective-permute-start(bf16[64,1,1]{2,0,1:T(8,128)(2,1)S(1)} %get-tuple-element.81), channel_id=1, source_target_pairs={{0,4},{4,8},{8,12},{12,16},{16,20},{20,24},{24,28},{28,32},{32,36}... | collective-permute-start | bytes 392 | tf_op jit(solution)/shard_map/ppermute | solution.py:19
  209.8 7.2 %collective-permute-start.17 = (bf16[64,1,1]{2,0,1:T(8,128)(2,1)S(1)}, bf16[64,1,1]{2,0,1:T(8,128)(2,1)S(1)}, u32[]{:S(2)}, u32[]{:S(2)}) collective-permute-start(bf16[64,1,1]{2,0,1:T(8,128)(2,1)S(1)} %get-tuple-element.82), channel_id=1, source_target_pairs={{4,0},{8,4},{12,8},{16,12},{20,16},{24,20},{28,24},{32,28},{36,32}... | collective-permute-start | bytes 392 | tf_op jit(solution)/shard_map/ppermute | solution.py:20
  217.1 6.4 %collective-permute-start.18 = (bf16[64,1,258]{2,0,1:T(8,128)(2,1)S(1)}, bf16[64,1,258]{2,0,1:T(8,128)(2,1)S(1)}, u32[]{:S(2)}, u32[]{:S(2)}) collective-permute-start(bf16[64,1,258]{2,0,1:T(8,128)(2,1)S(1)} %pad_maximum_fusion.7), channel_id=1, source_target_pairs={{1,0},{2,1},{3,2},{5,4},{6,5},{7,6},{9,8},{10,9},{11,10},{13,12},{... | collective-permute-start | bytes 99080 | tf_op jit(solution)/shard_map/ppermute | solution.py:20
  218.4 6.6 %collective-permute-start.19 = (bf16[64,1,258]{2,0,1:T(8,128)(2,1)S(1)}, bf16[64,1,258]{2,0,1:T(8,128)(2,1)S(1)}, u32[]{:S(2)}, u32[]{:S(2)}) collective-permute-start(bf16[64,1,258]{2,0,1:T(8,128)(2,1)S(1)} %pad_maximum_fusion.7), channel_id=1, source_target_pairs={{0,1},{1,2},{2,3},{4,5},{5,6},{6,7},{8,9},{9,10},{10,11},{12,13},{... | collective-permute-start | bytes 99080 | tf_op jit(solution)/shard_map/ppermute | solution.py:19
  (7 other events, 196.4 us)
where the time goes:
time: 243 us; the launch traced here: 239 us
  local copies, waits for them, and re-layouts  73.5 us (30%)
  other arithmetic  70.5 us (29%)
  starting transfers between devices  67.7 us (28%)
  waiting for transfers between devices  23.7 us (10%)
    unnamed x24, other arithmetic  43.5 us
    ppermute x10, starting transfers between devices, padded_2(): after = lax.ppermute(first, axis, down)  38.1 us
    unnamed x33, local copies, waits for them, and re-layouts  33.5 us
    ppermute x10, starting transfers between devices, padded_2(): before = lax.ppermute(last, axis, up)  29.6 us
    concatenate x1, other arithmetic, on_device(): jnp.concatenate([stiffness_old, both_rims(stiff_padded, capacity)], 3)  21.5 us
    gather x1, local copies, waits for them, and re-layouts, on_device(): jnp.take(jnp.concatenate([stiffness_old, both_rims(stiff_padded, capacity...  19.9 us
    ppermute x10, waiting for transfers between devices, padded_2(): before = lax.ppermute(last, axis, up)  19.9 us
    gather x1, local copies, waits for them, and re-layouts, on_device(): stiff_buffer = jnp.take(stiffness_old, outgoing, axis=3)  10.6 us
  transfers between devices with their start and end apart: 20, of which 7 were waited for; matrix products, arithmetic and copies ran while one was open for 23% of the time, Pallas kernels for 0%

commit v1 on v0

--- a/solution.py
+++ b/solution.py
@@ -22,6 +22,15 @@
     return value
 
 
+def shaft_exchange(lower_bound, upper_bound):
+    size = lax.axis_size("shaft")
+    up = [(i, i + 1) for i in range(size - 1)]
+    down = [(i + 1, i) for i in range(size - 1)]
+    from_lower = lax.ppermute(upper_bound, "shaft", up)
+    from_higher = lax.ppermute(lower_bound, "shaft", down)
+    return from_lower, from_higher
+
+
 def select_neighbours(padded, pattern, coupled):
     blocks = pattern.shape[-1]
     shifted = [
@@ -37,8 +46,9 @@
     return jnp.stack(gathered)
 
 
-def both_rims(padded, capacity):
-    return jnp.concatenate([padded[..., :capacity], padded[..., -capacity:]], -1)
+def block_force(stiffness, neighbours):
+    product = stiffness.astype(jnp.float32) * neighbours.astype(jnp.float32)[:, None, :, :]
+    return jnp.sum(product, axis=(0, 2))
 
 
 def on_device(
@@ -59,8 +69,27 @@
     blocks = displacement.shape[-1]
     capacity = send_slot.shape[2]
     outgoing = send_slot[0].reshape(-1)
-    filled = jnp.arange(capacity, dtype=jnp.int32)[None, :] < arrive_count[0][:, None]
-    target = jnp.where(filled, arrive_place[0], blocks).reshape(-1)
+    lanes = jnp.arange(blocks, dtype=jnp.int32)
+
+    leaving = (lanes[:, None] == outgoing[None, :]).astype(jnp.bfloat16)
+    stiff_out = jnp.einsum(
+        "kijb,bm->kijm", stiffness_old, leaving, preferred_element_type=jnp.float32
+    ).astype(jnp.bfloat16)
+    stiff_lower, stiff_higher = shaft_exchange(
+        stiff_out[..., :capacity], stiff_out[..., capacity:]
+    )
+    stiff_arrived = jnp.concatenate([stiff_lower, stiff_higher], -1)
+
+    filled = (
+        jnp.arange(capacity, dtype=jnp.int32)[None, :] < arrive_count[0][:, None]
+    ).reshape(-1)
+    places = arrive_place[0].reshape(-1)
+    arriving = (lanes[:, None] == places[None, :]) & filled[None, :]
+    is_arrival = jnp.any(arriving, axis=1)
+    arriving_bf16 = arriving.astype(jnp.bfloat16)
+    arriving_f32 = arriving.astype(jnp.float32)
+
+    target = jnp.where(filled, places, blocks)
     placing = (
         jnp.arange(blocks + 1, dtype=jnp.int32)
         .at[target]
@@ -69,16 +98,14 @@
     moving_state = jnp.concatenate(
         [jnp.take(history_old, outgoing, axis=1), jnp.take(decay_old, outgoing, axis=1)], 0
     )
-    state_padded = padded_2(moving_state, (("shaft", 1),), capacity)
-    state_arrived = both_rims(state_padded, capacity)
+    state_lower, state_higher = shaft_exchange(
+        moving_state[:, :capacity], moving_state[:, capacity:]
+    )
+    state_arrived = jnp.concatenate([state_lower, state_higher], 1)
     depth = history_old.shape[0]
     history = jnp.take(jnp.concatenate([history_old, state_arrived[:depth]], 1), placing, axis=1)
     decay = jnp.take(jnp.concatenate([decay_old, state_arrived[depth:]], 1), placing, axis=1)
-    stiff_buffer = jnp.take(stiffness_old, outgoing, axis=3)
-    stiff_padded = padded_2(stiff_buffer, (("shaft", 3),), capacity)
-    stiffness = jnp.take(
-        jnp.concatenate([stiffness_old, both_rims(stiff_padded, capacity)], 3), placing, axis=3
-    )
+
     moved = displacement[:, 0, :]
     speeds = velocity[:, 0, :]
     forcing = external[:, 0, :]
@@ -89,9 +116,17 @@
         rounded = moved.astype(jnp.bfloat16)[:, None, :]
         padded = padded_2(rounded, (("shaft", 2), ("ply", 1)), 1)
         neighbours = select_neighbours(padded, codes, live_count)
-        force = jnp.einsum(
-            "kijb,kjb->ib", stiffness, neighbours, preferred_element_type=jnp.float32
-        ) + jnp.dot(strain_map.T, history, precision=lax.Precision.HIGHEST)
+        force_old = block_force(stiffness_old, neighbours)
+        neighbours_arrived = jnp.einsum(
+            "kjb,bm->kjm", neighbours, arriving_bf16, preferred_element_type=jnp.float32
+        ).astype(jnp.bfloat16)
+        force_arrived = block_force(stiff_arrived, neighbours_arrived)
+        force_placed = jnp.dot(
+            force_arrived, arriving_f32.T, precision=lax.Precision.HIGHEST
+        )
+        force = jnp.where(is_arrival[None, :], force_placed, force_old) + jnp.dot(
+            strain_map.T, history, precision=lax.Precision.HIGHEST
+        )
         speeds = speeds + time_step * (scaling * (forcing - force))
         advanced = moved + time_step * speeds
         history = decay * history + jnp.dot(

time: 243 us -> 189 us (0.78)
  the two profiles are of different devices: /device:TPU:96 before, /device:TPU:63 now
where the time goes in v1:
time: 189 us; the launch traced here: 188 us
  other arithmetic  62.3 us (33%)
  starting transfers between devices  51.9 us (27%)
  waiting for transfers between devices  36.4 us (19%)
  matrix products  21.4 us (11%)
  local copies, waits for them, and re-layouts  14.2 us (8%)
    reduce_sum x8, other arithmetic, block_force(): return jnp.sum(product, axis=(0, 2))  41.3 us
    ppermute x8, starting transfers between devices, padded_2(): before = lax.ppermute(last, axis, up)  18.8 us
    ppermute x8, starting transfers between devices, padded_2(): after = lax.ppermute(first, axis, down)  17.8 us
    unnamed x16, other arithmetic  13.7 us
    ppermute x8, waiting for transfers between devices, padded_2(): after = lax.ppermute(first, axis, down)  13.5 us
    ppermute x2, starting transfers between devices, shaft_exchange(): from_lower = lax.ppermute(upper_bound, 'shaft', up)  11.5 us
    ppermute x2, waiting for transfers between devices, shaft_exchange(): from_lower = lax.ppermute(upper_bound, 'shaft', up)  10.2 us
    dot_general x1, matrix products, on_device(): jnp.einsum('kijb,bm->kijm', stiffness_old, leaving, preferred_element_typ...  9.23 us
  transfers between devices with their start and end apart: 20, of which 8 were waited for; matrix products, arithmetic and copies ran while one was open for 21% of the time, Pallas kernels for 0%

profile of v1, /device:TPU:63, one launch (start us, length us, event | category | flops | bytes accessed | tf_op | source)
XLA Modules:
  0.0 187.8 jit_solution(16604658466457176348)
XLA Ops:
  1.6 3.8 %collective-permute-start.2 = (bf16[64,1,1]{2,0,1:T(8,128)(2,1)S(1)}, bf16[64,1,1]{2,0,1:T(8,128)(2,1)S(1)}, u32[]{:S(2)}, u32[]{:S(2)}) collective-permute-start(bf16[64,1,1]{2,0,1:T(8,128)(2,1)S(1)} %get-tuple-element.80), channel_id=1, source_target_pairs={{0,4},{4,8},{8,12},{12,16},{16,20},{20,24},{24,28},{28,32},{32,36}... | collective-permute-start | bytes 392 | tf_op jit(solution)/shard_map/ppermute | solution.py:19
  8.1 9.2 %convert_bitcast_fusion = bf16[5,64,64,64]{2,3,1,0:T(8,128)(2,1)S(1)} fusion(bf16[5,64,64,256]{3,2,1,0:T(8,128)(2,1)} %param.23, s32[64]{0:T(128)S(1)} %eq.440), kind=kOutput, calls=%fused_computation.22 | convolution fusion | flops 672415744 | bytes 13107456 | tf_op jit(solution)/shard_map/kijb,bm->kijm/dot_general | solution.py:75
  17.3 3.4 %fusion.109 = (bf16[5,64,64,32]{2,3,1,0:T(8,128)(2,1)}, bf16[5,64,64,32]{2,3,1,0:T(8,128)(2,1)}) fusion(bf16[5,64,64,64]{2,3,1,0:T(8,128)(2,1)S(1)} %convert_bitcast_fusion), kind=kLoop, calls=%fused_computation.272 | loop fusion | bytes 5242880 | tf_op jit(solution)/shard_map/slice | solution.py:79
  20.7 5.7 %collective-permute-start = (bf16[5,64,64,32]{2,3,1,0:T(8,128)(2,1)}, bf16[5,64,64,32]{2,3,1,0:T(8,128)(2,1)S(1)}, u32[]{:S(2)}, u32[]{:S(2)}) collective-permute-start(bf16[5,64,64,32]{2,3,1,0:T(8,128)(2,1)} %get-tuple-element.68), channel_id=1, source_target_pairs={{0,4},{4,8},{8,12},{12,16},{16,20},{20,24},{24,28},{28,32},{32,36}... | collective-permute-start | bytes 3932168 | tf_op jit(solution)/shard_map/ppermute | solution.py:29
  30.0 5.7 %collective-permute-start.6 = (f32[96,32]{0,1:T(8,128)S(1)}, f32[96,32]{0,1:T(8,128)S(1)}, u32[]{:S(2)}, u32[]{:S(2)}) collective-permute-start(f32[96,32]{0,1:T(8,128)S(1)} %get-tuple-element.71), channel_id=1, source_target_pairs={{0,4},{4,8},{8,12},{12,16},{16,20},{20,24},{24,28},{28,32},{32,36}... | collective-permute-start | bytes 36872 | tf_op jit(solution)/shard_map/ppermute | solution.py:29
  45.3 10.2 %collective-permute-done.6 = f32[96,32]{0,1:T(8,128)S(1)} collective-permute-done((f32[96,32]{0,1:T(8,128)S(1)}, f32[96,32]{0,1:T(8,128)S(1)}, u32[]{:S(2)}, u32[]{:S(2)}) %collective-permute-start.6) | collective-permute-done | bytes 12320 | tf_op jit(solution)/shard_map/ppermute | solution.py:29
  56.7 5.2 %collective-permute-done.7 = f32[96,32]{0,1:T(8,128)S(1)} collective-permute-done((f32[96,32]{0,1:T(8,128)S(1)}, f32[96,32]{0,1:T(8,128)S(1)}, u32[]{:S(2)}, u32[]{:S(2)}) %collective-permute-start.7) | collective-permute-done | bytes 12320 | tf_op jit(solution)/shard_map/ppermute | solution.py:30
  70.4 6.7 %fusion = f32[64,256]{1,0:T(8,128)S(1)} fusion(bf16[5,64,64,256]{3,2,1,0:T(8,128)(2,1)} %param.23, f32[5,64,256]{2,1,0:T(8,128)S(1)} %convert_element_type.130), kind=kLoop, calls=%fused_computation.9 | loop fusion | flops 15712256 | bytes 10878976 | tf_op jit(solution)/shard_map/reduce_sum | solution.py:51
  77.1 3.6 %fusion.4 = f32[64,64]{1,0:T(8,128)S(1)} fusion(f32[5,64,64]{1,2,0:T(8,128)S(1)} %copy.47, bf16[5,64,64,32]{2,3,1,0:T(8,128)(2,1)} %collective-permute-done.1, bf16[5,64,64,32]{2,3,1,0:T(8,128)(2,1)S(1)} %collective-permute-done), kind=kLoop, calls=%fused_computation.17 | loop fusion | flops 7860224 | bytes 2719744 | tf_op jit(solution)/shard_map/reduce_sum | solution.py:51
  82.6 2.7 %collective-permute-start.8 = (bf16[64,1,1]{2,0,1:T(8,128)(2,1)S(1)}, bf16[64,1,1]{2,0,1:T(8,128)(2,1)S(1)}, u32[]{:S(2)}, u32[]{:S(2)}) collective-permute-start(bf16[64,1,1]{2,0,1:T(8,128)(2,1)S(1)} %get-tuple-element.76), channel_id=1, source_target_pairs={{0,4},{4,8},{8,12},{12,16},{16,20},{20,24},{24,28},{28,32},{32,36}... | collective-permute-start | bytes 392 | tf_op jit(solution)/shard_map/ppermute | solution.py:19
  88.3 4.2 %collective-permute-done.9 = bf16[64,1,1]{2,0,1:T(8,128)(2,1)S(1)} collective-permute-done((bf16[64,1,1]{2,0,1:T(8,128)(2,1)S(1)}, bf16[64,1,1]{2,0,1:T(8,128)(2,1)S(1)}, u32[]{:S(2)}, u32[]{:S(2)}) %collective-permute-start.9) | collective-permute-done | bytes 160 | tf_op jit(solution)/shard_map/ppermute | solution.py:20
  92.5 2.9 %collective-permute-start.10 = (bf16[64,1,258]{2,0,1:T(8,128)(2,1)S(1)}, bf16[64,1,258]{2,0,1:T(8,128)(2,1)S(1)}, u32[]{:S(2)}, u32[]{:S(2)}) collective-permute-start(bf16[64,1,258]{2,0,1:T(8,128)(2,1)S(1)} %pad_maximum_fusion.4), channel_id=1, source_target_pairs={{1,0},{2,1},{3,2},{5,4},{6,5},{7,6},{9,8},{10,9},{11,10},{13,12},{... | collective-permute-start | bytes 99080 | tf_op jit(solution)/shard_map/ppermute | solution.py:20
  97.6 2.6 %collective-permute-done.11 = bf16[64,1,258]{2,0,1:T(8,128)(2,1)S(1)} collective-permute-done((bf16[64,1,258]{2,0,1:T(8,128)(2,1)S(1)}, bf16[64,1,258]{2,0,1:T(8,128)(2,1)S(1)}, u32[]{:S(2)}, u32[]{:S(2)}) %collective-permute-start.11) | collective-permute-done | bytes 33056 | tf_op jit(solution)/shard_map/ppermute | solution.py:19
  104.9 6.7 %fusion.1 = f32[64,256]{1,0:T(8,128)S(1)} fusion(bf16[5,64,64,256]{3,2,1,0:T(8,128)(2,1)} %param.23, f32[5,64,256]{2,1,0:T(8,128)S(1)} %convert_element_type.134), kind=kLoop, calls=%fused_computation.10 | loop fusion | flops 15712256 | bytes 10878976 | tf_op jit(solution)/shard_map/reduce_sum | solution.py:51
  111.7 3.6 %fusion.5 = f32[64,64]{1,0:T(8,128)S(1)} fusion(f32[5,64,64]{1,2,0:T(8,128)S(1)} %copy.52, bf16[5,64,64,32]{2,3,1,0:T(8,128)(2,1)} %collective-permute-done.1, bf16[5,64,64,32]{2,3,1,0:T(8,128)(2,1)S(1)} %collective-permute-done), kind=kLoop, calls=%fused_computation.18 | loop fusion | flops 7860224 | bytes 2719744 | tf_op jit(solution)/shard_map/reduce_sum | solution.py:51
  116.2 3.4 %collective-permute-start.12 = (bf16[64,1,1]{2,0,1:T(8,128)(2,1)S(1)}, bf16[64,1,1]{2,0,1:T(8,128)(2,1)S(1)}, u32[]{:S(2)}, u32[]{:S(2)}) collective-permute-start(bf16[64,1,1]{2,0,1:T(8,128)(2,1)S(1)} %get-tuple-element.74), channel_id=1, source_target_pairs={{0,4},{4,8},{8,12},{12,16},{16,20},{20,24},{24,28},{28,32},{32,36}... | collective-permute-start | bytes 392 | tf_op jit(solution)/shard_map/ppermute | solution.py:19
  122.4 4.4 %collective-permute-done.13 = bf16[64,1,1]{2,0,1:T(8,128)(2,1)S(1)} collective-permute-done((bf16[64,1,1]{2,0,1:T(8,128)(2,1)S(1)}, bf16[64,1,1]{2,0,1:T(8,128)(2,1)S(1)}, u32[]{:S(2)}, u32[]{:S(2)}) %collective-permute-start.13) | collective-permute-done | bytes 160 | tf_op jit(solution)/shard_map/ppermute | solution.py:20
  126.8 2.5 %collective-permute-start.14 = (bf16[64,1,258]{2,0,1:T(8,128)(2,1)S(1)}, bf16[64,1,258]{2,0,1:T(8,128)(2,1)S(1)}, u32[]{:S(2)}, u32[]{:S(2)}) collective-permute-start(bf16[64,1,258]{2,0,1:T(8,128)(2,1)S(1)} %pad_maximum_fusion.5), channel_id=1, source_target_pairs={{1,0},{2,1},{3,2},{5,4},{6,5},{7,6},{9,8},{10,9},{11,10},{13,12},{... | collective-permute-start | bytes 99080 | tf_op jit(solution)/shard_map/ppermute | solution.py:20
  139.5 6.7 %fusion.2 = f32[64,256]{1,0:T(8,128)S(1)} fusion(bf16[5,64,64,256]{3,2,1,0:T(8,128)(2,1)} %param.23, f32[5,64,256]{2,1,0:T(8,128)S(1)} %convert_element_type.138), kind=kLoop, calls=%fused_computation.11 | loop fusion | flops 15712256 | bytes 10878976 | tf_op jit(solution)/shard_map/reduce_sum | solution.py:51
  146.2 3.6 %fusion.6 = f32[64,64]{1,0:T(8,128)S(1)} fusion(f32[5,64,64]{1,2,0:T(8,128)S(1)} %copy-done.4, bf16[5,64,64,32]{2,3,1,0:T(8,128)(2,1)} %collective-permute-done.1, bf16[5,64,64,32]{2,3,1,0:T(8,128)(2,1)S(1)} %collective-permute-done), kind=kLoop, calls=%fused_computation.19 | loop fusion | flops 7860224 | bytes 2719744 | tf_op jit(solution)/shard_map/reduce_sum | solution.py:51
  151.3 3.3 %collective-permute-start.16 = (bf16[64,1,1]{2,0,1:T(8,128)(2,1)S(1)}, bf16[64,1,1]{2,0,1:T(8,128)(2,1)S(1)}, u32[]{:S(2)}, u32[]{:S(2)}) collective-permute-start(bf16[64,1,1]{2,0,1:T(8,128)(2,1)S(1)} %get-tuple-element.72), channel_id=1, source_target_pairs={{0,4},{4,8},{8,12},{12,16},{16,20},{20,24},{24,28},{28,32},{32,36}... | collective-permute-start | bytes 392 | tf_op jit(solution)/shard_map/ppermute | solution.py:19
  156.8 5.0 %collective-permute-done.17 = bf16[64,1,1]{2,0,1:T(8,128)(2,1)S(1)} collective-permute-done((bf16[64,1,1]{2,0,1:T(8,128)(2,1)S(1)}, bf16[64,1,1]{2,0,1:T(8,128)(2,1)S(1)}, u32[]{:S(2)}, u32[]{:S(2)}) %collective-permute-start.17) | collective-permute-done | bytes 160 | tf_op jit(solution)/shard_map/ppermute | solution.py:20
  174.3 6.7 %fusion.3 = f32[64,256]{1,0:T(8,128)S(1)} fusion(bf16[5,64,64,256]{3,2,1,0:T(8,128)(2,1)} %param.23, f32[5,64,256]{2,1,0:T(8,128)S(1)} %convert_element_type.142), kind=kLoop, calls=%fused_computation.12 | loop fusion | flops 15712256 | bytes 10878976 | tf_op jit(solution)/shard_map/reduce_sum | solution.py:51
  181.1 3.6 %fusion.7 = f32[64,64]{1,0:T(8,128)S(1)} fusion(f32[5,64,64]{1,2,0:T(8,128)S(1)} %copy-done.3, bf16[5,64,64,32]{2,3,1,0:T(8,128)(2,1)} %collective-permute-done.1, bf16[5,64,64,32]{2,3,1,0:T(8,128)(2,1)S(1)} %collective-permute-done), kind=kLoop, calls=%fused_computation.20 | loop fusion | flops 7860224 | bytes 2719744 | tf_op jit(solution)/shard_map/reduce_sum | solution.py:51
  (180 shorter events, 70.8 us)
Async XLA Ops:
  0.6 62.2 %copy-start = (f32[48,64]{1,0:T(8,128)S(1)}, f32[48,64]{1,0:T(8,128)}, u32[]{:S(2)}) copy-start(f32[48,64]{1,0:T(8,128)} %param.26) | copy-start | bytes 36868
  1.6 38.0 %collective-permute-start.2 = (bf16[64,1,1]{2,0,1:T(8,128)(2,1)S(1)}, bf16[64,1,1]{2,0,1:T(8,128)(2,1)S(1)}, u32[]{:S(2)}, u32[]{:S(2)}) collective-permute-start(bf16[64,1,1]{2,0,1:T(8,128)(2,1)S(1)} %get-tuple-element.80), channel_id=1, source_target_pairs={{0,4},{4,8},{8,12},{12,16},{16,20},{20,24},{24,28},{28,32},{32,36}... | collective-permute-start | bytes 392 | tf_op jit(solution)/shard_map/ppermute | solution.py:19
  5.3 36.1 %collective-permute-start.3 = (bf16[64,1,1]{2,0,1:T(8,128)(2,1)S(1)}, bf16[64,1,1]{2,0,1:T(8,128)(2,1)S(1)}, u32[]{:S(2)}, u32[]{:S(2)}) collective-permute-start(bf16[64,1,1]{2,0,1:T(8,128)(2,1)S(1)} %get-tuple-element.81), channel_id=1, source_target_pairs={{4,0},{8,4},{12,8},{16,12},{20,16},{24,20},{28,24},{32,28},{36,32}... | collective-permute-start | bytes 392 | tf_op jit(solution)/shard_map/ppermute | solution.py:20
  20.7 56.4 %collective-permute-start = (bf16[5,64,64,32]{2,3,1,0:T(8,128)(2,1)}, bf16[5,64,64,32]{2,3,1,0:T(8,128)(2,1)S(1)}, u32[]{:S(2)}, u32[]{:S(2)}) collective-permute-start(bf16[5,64,64,32]{2,3,1,0:T(8,128)(2,1)} %get-tuple-element.68), channel_id=1, source_target_pairs={{0,4},{4,8},{8,12},{12,16},{16,20},{20,24},{24,28},{28,32},{32,36}... | collective-permute-start | bytes 3932168 | tf_op jit(solution)/shard_map/ppermute | solution.py:29
  26.5 50.7 %collective-permute-start.1 = (bf16[5,64,64,32]{2,3,1,0:T(8,128)(2,1)}, bf16[5,64,64,32]{2,3,1,0:T(8,128)(2,1)}, u32[]{:S(2)}, u32[]{:S(2)}) collective-permute-start(bf16[5,64,64,32]{2,3,1,0:T(8,128)(2,1)} %get-tuple-element.69), channel_id=1, source_target_pairs={{4,0},{8,4},{12,8},{16,12},{20,16},{24,20},{28,24},{32,28},{36,32}... | collective-permute-start | bytes 3932168 | tf_op jit(solution)/shard_map/ppermute | solution.py:30
  30.0 25.4 %collective-permute-start.6 = (f32[96,32]{0,1:T(8,128)S(1)}, f32[96,32]{0,1:T(8,128)S(1)}, u32[]{:S(2)}, u32[]{:S(2)}) collective-permute-start(f32[96,32]{0,1:T(8,128)S(1)} %get-tuple-element.71), channel_id=1, source_target_pairs={{0,4},{4,8},{8,12},{12,16},{16,20},{20,24},{24,28},{28,32},{32,36}... | collective-permute-start | bytes 36872 | tf_op jit(solution)/shard_map/ppermute | solution.py:29
  39.6 22.4 %collective-permute-start.7 = (f32[96,32]{0,1:T(8,128)S(1)}, f32[96,32]{0,1:T(8,128)S(1)}, u32[]{:S(2)}, u32[]{:S(2)}) collective-permute-start(f32[96,32]{0,1:T(8,128)S(1)} %get-tuple-element.70), channel_id=1, source_target_pairs={{4,0},{8,4},{12,8},{16,12},{20,16},{24,20},{28,24},{32,28},{36,32}... | collective-permute-start | bytes 36872 | tf_op jit(solution)/shard_map/ppermute | solution.py:30
  42.8 22.6 %collective-permute-start.4 = (bf16[64,1,258]{2,0,1:T(8,128)(2,1)}, bf16[64,1,258]{2,0,1:T(8,128)(2,1)S(1)}, u32[]{:S(2)}, u32[]{:S(2)}) collective-permute-start(bf16[64,1,258]{2,0,1:T(8,128)(2,1)} %pad_maximum_fusion.3), channel_id=1, source_target_pairs={{1,0},{2,1},{3,2},{5,4},{6,5},{7,6},{9,8},{10,9},{11,10},{13,12},{... | collective-permute-start | bytes 99080 | tf_op jit(solution)/shard_map/ppermute | solution.py:20
  55.4 10.0 %collective-permute-start.5 = (bf16[64,1,258]{2,0,1:T(8,128)(2,1)}, bf16[64,1,258]{2,0,1:T(8,128)(2,1)S(1)}, u32[]{:S(2)}, u32[]{:S(2)}) collective-permute-start(bf16[64,1,258]{2,0,1:T(8,128)(2,1)} %pad_maximum_fusion.3), channel_id=1, source_target_pairs={{0,1},{1,2},{2,3},{4,5},{5,6},{6,7},{8,9},{9,10},{10,11},{12,13},{... | collective-permute-start | bytes 99080 | tf_op jit(solution)/shard_map/ppermute | solution.py:19
  82.6 5.7 %collective-permute-start.8 = (bf16[64,1,1]{2,0,1:T(8,128)(2,1)S(1)}, bf16[64,1,1]{2,0,1:T(8,128)(2,1)S(1)}, u32[]{:S(2)}, u32[]{:S(2)}) collective-permute-start(bf16[64,1,1]{2,0,1:T(8,128)(2,1)S(1)} %get-tuple-element.76), channel_id=1, source_target_pairs={{0,4},{4,8},{8,12},{12,16},{16,20},{20,24},{24,28},{28,32},{32,36}... | collective-permute-start | bytes 392 | tf_op jit(solution)/shard_map/ppermute | solution.py:19
  85.2 7.2 %collective-permute-start.9 = (bf16[64,1,1]{2,0,1:T(8,128)(2,1)S(1)}, bf16[64,1,1]{2,0,1:T(8,128)(2,1)S(1)}, u32[]{:S(2)}, u32[]{:S(2)}) collective-permute-start(bf16[64,1,1]{2,0,1:T(8,128)(2,1)S(1)} %get-tuple-element.77), channel_id=1, source_target_pairs={{4,0},{8,4},{12,8},{16,12},{20,16},{24,20},{28,24},{32,28},{36,32}... | collective-permute-start | bytes 392 | tf_op jit(solution)/shard_map/ppermute | solution.py:20
  92.5 5.1 %collective-permute-start.10 = (bf16[64,1,258]{2,0,1:T(8,128)(2,1)S(1)}, bf16[64,1,258]{2,0,1:T(8,128)(2,1)S(1)}, u32[]{:S(2)}, u32[]{:S(2)}) collective-permute-start(bf16[64,1,258]{2,0,1:T(8,128)(2,1)S(1)} %pad_maximum_fusion.4), channel_id=1, source_target_pairs={{1,0},{2,1},{3,2},{5,4},{6,5},{7,6},{9,8},{10,9},{11,10},{13,12},{... | collective-permute-start | bytes 99080 | tf_op jit(solution)/shard_map/ppermute | solution.py:20
  95.4 4.8 %collective-permute-start.11 = (bf16[64,1,258]{2,0,1:T(8,128)(2,1)S(1)}, bf16[64,1,258]{2,0,1:T(8,128)(2,1)S(1)}, u32[]{:S(2)}, u32[]{:S(2)}) collective-permute-start(bf16[64,1,258]{2,0,1:T(8,128)(2,1)S(1)} %pad_maximum_fusion.4), channel_id=1, source_target_pairs={{0,1},{1,2},{2,3},{4,5},{5,6},{6,7},{8,9},{9,10},{10,11},{12,13},{... | collective-permute-start | bytes 99080 | tf_op jit(solution)/shard_map/ppermute | solution.py:19
  115.3 41.4 %copy-start.23 = (pred[256]{0:T(512)(128)(4,1)S(1)}, pred[256]{0:T(512)(128)(4,1)}, u32[]{:S(2)}) copy-start(pred[256]{0:T(512)(128)(4,1)} %compare_and_fusion) | copy-start | bytes 772
  116.2 6.2 %collective-permute-start.12 = (bf16[64,1,1]{2,0,1:T(8,128)(2,1)S(1)}, bf16[64,1,1]{2,0,1:T(8,128)(2,1)S(1)}, u32[]{:S(2)}, u32[]{:S(2)}) collective-permute-start(bf16[64,1,1]{2,0,1:T(8,128)(2,1)S(1)} %get-tuple-element.74), channel_id=1, source_target_pairs={{0,4},{4,8},{8,12},{12,16},{16,20},{20,24},{24,28},{28,32},{32,36}... | collective-permute-start | bytes 392 | tf_op jit(solution)/shard_map/ppermute | solution.py:19
  119.6 7.2 %collective-permute-start.13 = (bf16[64,1,1]{2,0,1:T(8,128)(2,1)S(1)}, bf16[64,1,1]{2,0,1:T(8,128)(2,1)S(1)}, u32[]{:S(2)}, u32[]{:S(2)}) collective-permute-start(bf16[64,1,1]{2,0,1:T(8,128)(2,1)S(1)} %get-tuple-element.75), channel_id=1, source_target_pairs={{4,0},{8,4},{12,8},{16,12},{20,16},{24,20},{28,24},{32,28},{36,32}... | collective-permute-start | bytes 392 | tf_op jit(solution)/shard_map/ppermute | solution.py:20
  126.8 4.9 %collective-permute-start.14 = (bf16[64,1,258]{2,0,1:T(8,128)(2,1)S(1)}, bf16[64,1,258]{2,0,1:T(8,128)(2,1)S(1)}, u32[]{:S(2)}, u32[]{:S(2)}) collective-permute-start(bf16[64,1,258]{2,0,1:T(8,128)(2,1)S(1)} %pad_maximum_fusion.5), channel_id=1, source_target_pairs={{1,0},{2,1},{3,2},{5,4},{6,5},{7,6},{9,8},{10,9},{11,10},{13,12},{... | collective-permute-start | bytes 99080 | tf_op jit(solution)/shard_map/ppermute | solution.py:20
  129.3 4.8 %collective-permute-start.15 = (bf16[64,1,258]{2,0,1:T(8,128)(2,1)S(1)}, bf16[64,1,258]{2,0,1:T(8,128)(2,1)S(1)}, u32[]{:S(2)}, u32[]{:S(2)}) collective-permute-start(bf16[64,1,258]{2,0,1:T(8,128)(2,1)S(1)} %pad_maximum_fusion.5), channel_id=1, source_target_pairs={{0,1},{1,2},{2,3},{4,5},{5,6},{6,7},{8,9},{9,10},{10,11},{12,13},{... | collective-permute-start | bytes 99080 | tf_op jit(solution)/shard_map/ppermute | solution.py:19
  135.8 36.5 %copy-start.24 = (pred[256]{0:T(512)(128)(4,1)S(1)}, pred[256]{0:T(512)(128)(4,1)}, u32[]{:S(2)}) copy-start(pred[256]{0:T(512)(128)(4,1)} %get-tuple-element.33) | copy-start | bytes 772
  135.8 36.5 %copy-start.25 = (pred[256]{0:T(512)(128)(4,1)S(1)}, pred[256]{0:T(512)(128)(4,1)}, u32[]{:S(2)}) copy-start(pred[256]{0:T(512)(128)(4,1)} %get-tuple-element.48) | copy-start | bytes 772
  151.3 5.5 %collective-permute-start.16 = (bf16[64,1,1]{2,0,1:T(8,128)(2,1)S(1)}, bf16[64,1,1]{2,0,1:T(8,128)(2,1)S(1)}, u32[]{:S(2)}, u32[]{:S(2)}) collective-permute-start(bf16[64,1,1]{2,0,1:T(8,128)(2,1)S(1)} %get-tuple-element.72), channel_id=1, source_target_pairs={{0,4},{4,8},{8,12},{12,16},{16,20},{20,24},{24,28},{28,32},{32,36}... | collective-permute-start | bytes 392 | tf_op jit(solution)/shard_map/ppermute | solution.py:19
  154.7 7.2 %collective-permute-start.17 = (bf16[64,1,1]{2,0,1:T(8,128)(2,1)S(1)}, bf16[64,1,1]{2,0,1:T(8,128)(2,1)S(1)}, u32[]{:S(2)}, u32[]{:S(2)}) collective-permute-start(bf16[64,1,1]{2,0,1:T(8,128)(2,1)S(1)} %get-tuple-element.73), channel_id=1, source_target_pairs={{4,0},{8,4},{12,8},{16,12},{20,16},{24,20},{28,24},{32,28},{36,32}... | collective-permute-start | bytes 392 | tf_op jit(solution)/shard_map/ppermute | solution.py:20
  161.9 4.6 %collective-permute-start.18 = (bf16[64,1,258]{2,0,1:T(8,128)(2,1)S(1)}, bf16[64,1,258]{2,0,1:T(8,128)(2,1)S(1)}, u32[]{:S(2)}, u32[]{:S(2)}) collective-permute-start(bf16[64,1,258]{2,0,1:T(8,128)(2,1)S(1)} %pad_maximum_fusion.6), channel_id=1, source_target_pairs={{1,0},{2,1},{3,2},{5,4},{6,5},{7,6},{9,8},{10,9},{11,10},{13,12},{... | collective-permute-start | bytes 99080 | tf_op jit(solution)/shard_map/ppermute | solution.py:20
  164.1 4.8 %collective-permute-start.19 = (bf16[64,1,258]{2,0,1:T(8,128)(2,1)S(1)}, bf16[64,1,258]{2,0,1:T(8,128)(2,1)S(1)}, u32[]{:S(2)}, u32[]{:S(2)}) collective-permute-start(bf16[64,1,258]{2,0,1:T(8,128)(2,1)S(1)} %pad_maximum_fusion.6), channel_id=1, source_target_pairs={{0,1},{1,2},{2,3},{4,5},{5,6},{6,7},{8,9},{9,10},{10,11},{12,13},{... | collective-permute-start | bytes 99080 | tf_op jit(solution)/shard_map/ppermute | solution.py:19
  (28 other events, 439.5 us)

commit v2 on v0

v2 whole, which is shorter than its diff:
```python
import jax
import jax.numpy as jnp
from jax import lax
from jax.experimental import pallas as pl
from jax.experimental.pallas import tpu as pltpu
from jax.sharding import PartitionSpec as P

ITERS = 4
ROWS = 8


time_step = 0.25


def padded_2(value, sides, width):
    for axis, dim in sides:
        size, length = (lax.axis_size(axis), value.shape[dim])
        up = [(i, (i + 1) % size) for i in range(size - 1)]
        down = [(j, i) for i, j in up]
        last = lax.slice_in_dim(value, length - width, length, axis=dim)
        first = lax.slice_in_dim(value, 0, width, axis=dim)
        before = lax.ppermute(last, axis, up)
        after = lax.ppermute(first, axis, down)
        value = jnp.concatenate([before, value, after], axis=dim)
    return value


def neighbour_exchange(axis, lower_bound, upper_bound):
    size = lax.axis_size(axis)
    up = [(i, i + 1) for i in range(size - 1)]
    down = [(i + 1, i) for i in range(size - 1)]
    from_lower = lax.ppermute(upper_bound, axis, up)
    from_higher = lax.ppermute(lower_bound, axis, down)
    return from_lower, from_higher


def gather_kernel(s_ref, lo_ref, hi_ref, out_lo_ref, out_hi_ref):
    rows, depth, blocks = s_ref.shape[1:]
    flat = s_ref[0].reshape(rows * depth, blocks)
    for pick_ref, out_ref in ((lo_ref, out_lo_ref), (hi_ref, out_hi_ref)):
        picked = jnp.dot(flat, pick_ref[...], preferred_element_type=jnp.float32)
        out_ref[0] = picked.reshape(rows, depth, -1).astype(out_ref.dtype)


def gather_leaving(stiffness, pick_lo, pick_hi):
    slots, rows_i, rows_j, blocks = stiffness.shape
    width = pick_lo.shape[1]
    out = jax.ShapeDtypeStruct((slots, rows_i, rows_j, width), stiffness.dtype)
    return pl.pallas_call(
        gather_kernel,
        grid=(slots, rows_i // ROWS),
        in_specs=[
            pl.BlockSpec((1, ROWS, rows_j, blocks), lambda k, i: (k, i, 0, 0)),
            pl.BlockSpec((blocks, width), lambda k, i: (0, 0)),
            pl.BlockSpec((blocks, width), lambda k, i: (0, 0)),
        ],
        out_specs=[
            pl.BlockSpec((1, ROWS, rows_j, width), lambda k, i: (k, i, 0, 0)),
            pl.BlockSpec((1, ROWS, rows_j, width), lambda k, i: (k, i, 0, 0)),
        ],
        out_shape=[out, out],
    )(stiffness, pick_lo, pick_hi)


def merge_kernel(s_ref, lo_ref, hi_ref, place_lo_ref, place_hi_ref, arrival_ref, out_ref):
    rows, depth, blocks = s_ref.shape[1:]
    width = lo_ref.shape[-1]
    placed = jnp.dot(
        lo_ref[0].reshape(rows * depth, width), place_lo_ref[...],
        preferred_element_type=jnp.float32,
    ) + jnp.dot(
        hi_ref[0].reshape(rows * depth, width), place_hi_ref[...],
        preferred_element_type=jnp.float32,
    )
    placed = placed.reshape(rows, depth, blocks).astype(out_ref.dtype)
    out_ref[0] = jnp.where(arrival_ref[...] > 0, placed, s_ref[0])


def merge_arrived(stiffness, arrived_lo, arrived_hi, place_lo, place_hi, arrival):
    slots, rows_i, rows_j, blocks = stiffness.shape
    width = arrived_lo.shape[-1]
    return pl.pallas_call(
        merge_kernel,
        grid=(slots, rows_i // ROWS),
        in_specs=[
            pl.BlockSpec((1, ROWS, rows_j, blocks), lambda k, i: (k, i, 0, 0)),
            pl.BlockSpec((1, ROWS, rows_j, width), lambda k, i: (k, i, 0, 0)),
            pl.BlockSpec((1, ROWS, rows_j, width), lambda k, i: (k, i, 0, 0)),
            pl.BlockSpec((width, blocks), lambda k, i: (0, 0)),
            pl.BlockSpec((width, blocks), lambda k, i: (0, 0)),
            pl.BlockSpec((1, blocks), lambda k, i: (0, 0)),
        ],
        out_specs=pl.BlockSpec((1, ROWS, rows_j, blocks), lambda k, i: (k, i, 0, 0)),
        out_shape=jax.ShapeDtypeStruct(stiffness.shape, stiffness.dtype),
    )(stiffness, arrived_lo, arrived_hi, place_lo, place_hi, arrival)


def force_kernel(s_ref, n_ref, out_ref):
    slots, rows = s_ref.shape[:2]
    for row in range(rows):
        acc = s_ref[0, row].astype(jnp.float32) * n_ref[0]
        for slot_index in range(1, slots):
            acc = acc + s_ref[slot_index, row].astype(jnp.float32) * n_ref[slot_index]
        out_ref[pl.ds(row, 1), :] = jnp.sum(acc, axis=0, keepdims=True)


def block_force(stiffness, neighbours):
    slots, rows_i, rows_j, blocks = stiffness.shape
    return pl.pallas_call(
        force_kernel,
        grid=(rows_i // ROWS,),
        in_specs=[
            pl.BlockSpec((slots, ROWS, rows_j, blocks), lambda i: (0, i, 0, 0)),
            pl.BlockSpec((slots, rows_j, blocks), lambda i: (0, 0, 0)),
        ],
        out_specs=pl.BlockSpec((ROWS, blocks), lambda i: (i, 0)),
        out_shape=jax.ShapeDtypeStruct((rows_i, blocks), jnp.float32),
        cost_estimate=pl.CostEstimate(
            flops=2 * slots * rows_i * rows_j * blocks,
            bytes_accessed=stiffness.size * 2 + neighbours.size * 4 + rows_i * blocks * 4,
            transcendentals=0,
        ),
    )(stiffness, neighbours)


def on_device(
    displacement,
    velocity,
    external,
    mass_inverse,
    pattern,
    coupled,
    stiffness_old,
    history_old,
    decay_old,
    strain_map,
    send_slot,
    arrive_place,
    arrive_count,
):
    blocks = displacement.shape[-1]
    capacity = send_slot.shape[2]
    slots = stiffness_old.shape[0]
    lanes = jnp.arange(blocks, dtype=jnp.int32)

    leave_lo = (lanes[:, None] == send_slot[0, 0][None, :]).astype(jnp.bfloat16)
    leave_hi = (lanes[:, None] == send_slot[0, 1][None, :]).astype(jnp.bfloat16)
    stiff_to_lower, stiff_to_higher = gather_leaving(stiffness_old, leave_lo, leave_hi)
    stiff_lower, stiff_higher = neighbour_exchange("shaft", stiff_to_lower, stiff_to_higher)

    count_live = jnp.arange(capacity, dtype=jnp.int32)[None, :] < arrive_count[0][:, None]
    place_lo = (arrive_place[0, 0][:, None] == lanes[None, :]) & count_live[0][:, None]
    place_hi = (arrive_place[0, 1][:, None] == lanes[None, :]) & count_live[1][:, None]
    arrival = (jnp.any(place_lo, 0) | jnp.any(place_hi, 0)).astype(jnp.int32)[None, :]
    stiffness = merge_arrived(
        stiffness_old,
        stiff_lower,
        stiff_higher,
        place_lo.astype(jnp.bfloat16),
        place_hi.astype(jnp.bfloat16),
        arrival,
    )

    outgoing = send_slot[0].reshape(-1)
    filled = count_live.reshape(-1)
    target = jnp.where(filled, arrive_place[0].reshape(-1), blocks)
    placing = (
        jnp.arange(blocks + 1, dtype=jnp.int32)
        .at[target]
        .set(blocks + jnp.arange(2 * capacity, dtype=jnp.int32))[:blocks]
    )
    moving_state = jnp.concatenate(
        [jnp.take(history_old, outgoing, axis=1), jnp.take(decay_old, outgoing, axis=1)], 0
    )
    state_lower, state_higher = neighbour_exchange(
        "shaft", moving_state[:, :capacity], moving_state[:, capacity:]
    )
    state_arrived = jnp.concatenate([state_lower, state_higher], 1)
    depth = history_old.shape[0]
    history = jnp.take(jnp.concatenate([history_old, state_arrived[:depth]], 1), placing, axis=1)
    decay = jnp.take(jnp.concatenate([decay_old, state_arrived[depth:]], 1), placing, axis=1)

    moved = displacement[:, 0, :]
    speeds = velocity[:, 0, :]
    forcing = external[:, 0, :]
    scaling = mass_inverse[:, 0, :]
    live = jnp.arange(slots, dtype=jnp.int32)[:, None] < coupled[0][None, :]
    codes = jnp.where(live, pattern[:, 0, :], 9)[:, None, :]
    for repeat in range(ITERS):
        rounded = moved.astype(jnp.bfloat16)[:, None, :]
        padded = padded_2(rounded, (("shaft", 2), ("ply", 1)), 1)
        neighbours = jnp.zeros((slots,) + moved.shape, jnp.float32)
        for code_index in range(9):
            shifted = padded[:, code_index // 3, code_index % 3 : code_index % 3 + blocks]
            neighbours = jnp.where(
                codes == code_index, shifted.astype(jnp.float32)[None], neighbours
            )
        force = block_force(stiffness, neighbours) + jnp.dot(
            strain_map.T, history, precision=lax.Precision.HIGHEST
        )
        speeds = speeds + time_step * (scaling * (forcing - force))
        advanced = moved + time_step * speeds
        history = decay * history + jnp.dot(
            strain_map, advanced - moved, precision=lax.Precision.HIGHEST
        )
        moved = advanced
    return (moved[:, None, :], speeds[:, None, :], history[:, None, :])


def solution(mesh):
    in_specs = (
        P(None, "ply", "shaft"),
        P(None, "ply", "shaft"),
        P(None, "ply", "shaft"),
        P(None, "ply", "shaft"),
        P(None, "ply", "shaft"),
        P("ply", "shaft"),
        P(None, None, None, ("shaft", "ply")),
        P(None, ("shaft", "ply")),
        P(None, ("shaft", "ply")),
        P(),
        P(("shaft", "ply"), None, None),
        P(("shaft", "ply"), None, None),
        P(("shaft", "ply"), None),
    )
    out_specs = (P(None, "ply", "shaft"), P(None, "ply", "shaft"), P(None, "ply", "shaft"))
    return jax.shard_map(
        on_device, mesh=mesh, in_specs=in_specs, out_specs=out_specs, check_vma=False
    )
```

time: 243 us -> 242 us (level)
  Pallas kernels: 0 us -> 90.7 us
  other arithmetic: 70.5 us -> 12.9 us
  local copies, waits for them, and re-layouts: 73.5 us -> 35 us
  waiting for transfers between devices: 23.7 us -> 43.9 us
  starting transfers between devices: 67.7 us -> 51 us
    pallas_call x0 -> x6, Pallas kernels: none -> 90.7 us  [the longest x4 31.9 us: block_force(): pl.pallas_call(force_kernel, grid=(rows_i // ROWS,), in_specs=[pl.BlockSp...]
    unnamed x24 -> x0, other arithmetic: 43.5 us -> none
    gather x2 -> x0, local copies, waits for them, and re-layouts: 30.5 us -> none  [the longest x1 19.9 us: on_device(): jnp.take(jnp.concatenate([stiffness_old, both_rims(stiff_padded, capacity...]
    unnamed x33 -> x59, local copies, waits for them, and re-layouts: 33.5 us -> 5.44 us
    ppermute x10 -> x8, waiting for transfers between devices: 3.86 us -> 29.6 us  [padded_2(): after = lax.ppermute(first, axis, down)]
    ppermute x10 -> x8, starting transfers between devices: 38.1 us -> 12.8 us  [padded_2(): after = lax.ppermute(first, axis, down)]
    concatenate x1 -> x0, other arithmetic: 21.5 us -> none  [on_device(): jnp.concatenate([stiffness_old, both_rims(stiff_padded, capacity)], 3)]
    ppermute x0 -> x4, starting transfers between devices: none -> 15.6 us  [the longest x2 11.7 us: neighbour_exchange(): from_higher = lax.ppermute(lower_bound, axis, down)]
  transfers between devices with their start and end apart: 20 -> 20, of which waited for: 7 -> 11; matrix products, arithmetic and copies ran while one was open for 23% -> 12% of each run, Pallas kernels for 0% -> 0%
where the time goes in v2:
time: 242 us; the launch traced here: 239 us
  Pallas kernels  90.7 us (37%)
  starting transfers between devices  51 us (21%)
  waiting for transfers between devices  43.9 us (18%)
  local copies, waits for them, and re-layouts  35 us (14%)
  other arithmetic  12.9 us (5%)
  matrix products  3.5 us (1%)
    pallas_call x4, Pallas kernels, block_force(): pl.pallas_call(force_kernel, grid=(rows_i // ROWS,), in_specs=[pl.BlockSp...  31.9 us
    pallas_call x1, Pallas kernels, merge_arrived(): pl.pallas_call(merge_kernel, grid=(slots, rows_i // ROWS), in_specs=[pl.B...  30 us
    ppermute x8, waiting for transfers between devices, padded_2(): after = lax.ppermute(first, axis, down)  29.6 us
    pallas_call x1, Pallas kernels, gather_leaving(): pl.pallas_call(gather_kernel, grid=(slots, rows_i // ROWS), in_specs=[pl....  28.7 us
    ppermute x8, starting transfers between devices, padded_2(): before = lax.ppermute(last, axis, up)  22.6 us
    ppermute x8, waiting for transfers between devices, padded_2(): before = lax.ppermute(last, axis, up)  14.3 us
    ppermute x8, starting transfers between devices, padded_2(): after = lax.ppermute(first, axis, down)  12.8 us
    ppermute x2, starting transfers between devices, neighbour_exchange(): from_higher = lax.ppermute(lower_bound, axis, down)  11.7 us
  transfers between devices with their start and end apart: 20, of which 11 were waited for; matrix products, arithmetic and copies ran while one was open for 12% of the time, Pallas kernels for 0%

profile of v2, /device:TPU:96, one launch (start us, length us, event | category | flops | bytes accessed | tf_op | source)
XLA Modules:
  0.0 238.5 jit_solution(3422860776321643035)
XLA Ops:
  2.1 28.7 %shard_map.151 = (bf16[5,64,64,32]{3,2,1,0:T(8,128)(2,1)}, bf16[5,64,64,32]{3,2,1,0:T(8,128)(2,1)}) custom-call(bf16[5,64,64,256]{3,2,1,0:T(8,128)(2,1)} %s_ref.3, bf16[256,32]{1,0:T(8,128)(2,1)} %get-tuple-element.93.lo_ref, bf16[256,32]{1,0:T(8,128)(2,1)} %get-tuple-element.94.hi_ref), custom_call_target="tpu_custom_call" | custom-call | tf_op jit(solution)/shard_map/pallas_call | solution.py:49
  30.8 4.9 %copy.40 = bf16[5,64,64,32]{2,3,1,0:T(8,128)(2,1)S(1)} copy(bf16[5,64,64,32]{3,2,1,0:T(8,128)(2,1)} %get-tuple-element.7) | data formatting | bytes 2621440 | tf_op jit(solution)/shard_map/pallas_call | solution.py:49
  37.8 6.1 %copy.41 = bf16[5,64,64,32]{2,3,1,0:T(8,128)(2,1)} copy(bf16[5,64,64,32]{3,2,1,0:T(8,128)(2,1)} %get-tuple-element.8) | data formatting | bytes 2621440 | tf_op jit(solution)/shard_map/pallas_call | solution.py:49
  43.9 5.7 %collective-permute-start.1 = (bf16[5,64,64,32]{2,3,1,0:T(8,128)(2,1)}, bf16[5,64,64,32]{2,3,1,0:T(8,128)(2,1)}, u32[]{:S(2)}, u32[]{:S(2)}) collective-permute-start(bf16[5,64,64,32]{2,3,1,0:T(8,128)(2,1)} %copy.41), channel_id=1, source_target_pairs={{4,0},{8,4},{12,8},{16,12},{20,16},{24,20},{28,24},{32,28},{36,32}... | collective-permute-start | bytes 3932168 | tf_op jit(solution)/shard_map/ppermute | solution.py:33
  51.8 2.4 %collective-permute-start.2 = (bf16[64,1,1]{2,1,0:T(2,128)(2,1)S(1)}, bf16[64,1,1]{2,1,0:T(2,128)(2,1)S(1)}, u32[]{:S(2)}, u32[]{:S(2)}) collective-permute-start(bf16[64,1,1]{2,1,0:T(2,128)(2,1)S(1)} %get-tuple-element.36), channel_id=1, source_target_pairs={{0,4},{4,8},{8,12},{12,16},{16,20},{20,24},{24,28},{28,32},{32,36}... | collective-permute-start | bytes 392 | tf_op jit(solution)/shard_map/ppermute | solution.py:22
  63.8 15.6 %collective-permute-done.3 = bf16[64,1,1]{2,1,0:T(2,128)(2,1)S(1)} collective-permute-done((bf16[64,1,1]{2,1,0:T(2,128)(2,1)S(1)}, bf16[64,1,1]{2,1,0:T(2,128)(2,1)S(1)}, u32[]{:S(2)}, u32[]{:S(2)}) %collective-permute-start.3) | collective-permute-done | bytes 160 | tf_op jit(solution)/shard_map/ppermute | solution.py:23
  79.4 5.9 %collective-permute-start.7 = (f32[96,32]{0,1:T(8,128)S(1)}, f32[96,32]{0,1:T(8,128)S(1)}, u32[]{:S(2)}, u32[]{:S(2)}) collective-permute-start(f32[96,32]{0,1:T(8,128)S(1)} %get-tuple-element.32), channel_id=1, source_target_pairs={{4,0},{8,4},{12,8},{16,12},{20,16},{24,20},{28,24},{32,28},{36,32}... | collective-permute-start | bytes 36872 | tf_op jit(solution)/shard_map/ppermute | solution.py:33
  86.2 3.4 %collective-permute-start.5 = (bf16[64,1,258]{2,1,0:T(2,128)(2,1)}, bf16[64,1,258]{2,1,0:T(2,128)(2,1)S(1)}, u32[]{:S(2)}, u32[]{:S(2)}) collective-permute-start(bf16[64,1,258]{2,1,0:T(2,128)(2,1)} %pad_maximum_fusion.2), channel_id=1, source_target_pairs={{0,1},{1,2},{2,3},{4,5},{5,6},{6,7},{8,9},{9,10},{10,11},{12,13},{... | collective-permute-start | bytes 99080 | tf_op jit(solution)/shard_map/ppermute | solution.py:22
  99.6 5.9 %copy.42.lo_ref = bf16[5,64,64,32]{3,2,1,0:T(8,128)(2,1)} copy(bf16[5,64,64,32]{2,3,1,0:T(8,128)(2,1)} %collective-permute-done) | data formatting | bytes 2621440 | tf_op jit(solution)/shard_map/ppermute | solution.py:32
  105.6 5.9 %copy.43.hi_ref = bf16[5,64,64,32]{3,2,1,0:T(8,128)(2,1)} copy(bf16[5,64,64,32]{2,3,1,0:T(8,128)(2,1)} %collective-permute-done.1) | data formatting | bytes 2621440 | tf_op jit(solution)/shard_map/ppermute | solution.py:33
  111.5 30.0 %shard_map.152.s_ref = bf16[5,64,64,256]{3,2,1,0:T(8,128)(2,1)} custom-call(bf16[5,64,64,256]{3,2,1,0:T(8,128)(2,1)} %s_ref.3, bf16[5,64,64,32]{3,2,1,0:T(8,128)(2,1)} %copy.42.lo_ref, bf16[5,64,64,32]{3,2,1,0:T(8,128)(2,1)} %copy.43.hi_ref, bf16[32,256]{1,0:T(8,128)(2,1)} %get-tuple-element.82.place_lo_ref, bf16[32,256]{1,0:T(8,128)(2,1)} %get-tuple-element.95.place_hi_ref, ...), custom_call_target="tpu_custom_call" | custom-call | tf_op jit(solution)/shard_map/pallas_call | solution.py:82
  141.6 8.0 %shard_map.153 = f32[64,256]{1,0:T(8,128)} custom-call(bf16[5,64,64,256]{3,2,1,0:T(8,128)(2,1)} %shard_map.152.s_ref, f32[5,64,256]{2,1,0:T(8,128)} %select_select_fusion.3.n_ref), custom_call_target="tpu_custom_call" | custom-call | flops 10485760 | bytes 10878976 | tf_op jit(solution)/shard_map/pallas_call | solution.py:109
  155.6 4.3 %collective-permute-done.8 = bf16[64,1,1]{2,0,1:T(8,128)(2,1)S(1)} collective-permute-done((bf16[64,1,1]{2,0,1:T(8,128)(2,1)S(1)}, bf16[64,1,1]{2,0,1:T(8,128)(2,1)S(1)}, u32[]{:S(2)}, u32[]{:S(2)}) %collective-permute-start.8) | collective-permute-done | bytes 160 | tf_op jit(solution)/shard_map/ppermute | solution.py:22
  160.0 3.4 %collective-permute-start.11 = (bf16[64,1,258]{2,0,1:T(8,128)(2,1)S(1)}, bf16[64,1,258]{2,0,1:T(8,128)(2,1)S(1)}, u32[]{:S(2)}, u32[]{:S(2)}) collective-permute-start(bf16[64,1,258]{2,0,1:T(8,128)(2,1)S(1)} %pad_maximum_fusion.5), channel_id=1, source_target_pairs={{0,1},{1,2},{2,3},{4,5},{5,6},{6,7},{8,9},{9,10},{10,11},{12,13},{... | collective-permute-start | bytes 99080 | tf_op jit(solution)/shard_map/ppermute | solution.py:22
  165.2 4.2 %collective-permute-done.10 = bf16[64,1,258]{2,0,1:T(8,128)(2,1)S(1)} collective-permute-done((bf16[64,1,258]{2,0,1:T(8,128)(2,1)S(1)}, bf16[64,1,258]{2,0,1:T(8,128)(2,1)S(1)}, u32[]{:S(2)}, u32[]{:S(2)}) %collective-permute-start.10) | collective-permute-done | bytes 33056 | tf_op jit(solution)/shard_map/ppermute | solution.py:23
  170.5 8.0 %shard_map.154 = f32[64,256]{1,0:T(8,128)} custom-call(bf16[5,64,64,256]{3,2,1,0:T(8,128)(2,1)} %shard_map.152.s_ref, f32[5,64,256]{2,1,0:T(8,128)} %select_select_fusion.2.n_ref), custom_call_target="tpu_custom_call" | custom-call | flops 10485760 | bytes 10878976 | tf_op jit(solution)/shard_map/pallas_call | solution.py:109
  184.0 4.5 %collective-permute-done.12 = bf16[64,1,1]{2,0,1:T(8,128)(2,1)S(1)} collective-permute-done((bf16[64,1,1]{2,0,1:T(8,128)(2,1)S(1)}, bf16[64,1,1]{2,0,1:T(8,128)(2,1)S(1)}, u32[]{:S(2)}, u32[]{:S(2)}) %collective-permute-start.12) | collective-permute-done | bytes 160 | tf_op jit(solution)/shard_map/ppermute | solution.py:22
  188.6 3.1 %collective-permute-start.15 = (bf16[64,1,258]{2,0,1:T(8,128)(2,1)S(1)}, bf16[64,1,258]{2,0,1:T(8,128)(2,1)S(1)}, u32[]{:S(2)}, u32[]{:S(2)}) collective-permute-start(bf16[64,1,258]{2,0,1:T(8,128)(2,1)S(1)} %pad_maximum_fusion.6), channel_id=1, source_target_pairs={{0,1},{1,2},{2,3},{4,5},{5,6},{6,7},{8,9},{9,10},{10,11},{12,13},{... | collective-permute-start | bytes 99080 | tf_op jit(solution)/shard_map/ppermute | solution.py:22
  193.6 4.2 %collective-permute-done.14 = bf16[64,1,258]{2,0,1:T(8,128)(2,1)S(1)} collective-permute-done((bf16[64,1,258]{2,0,1:T(8,128)(2,1)S(1)}, bf16[64,1,258]{2,0,1:T(8,128)(2,1)S(1)}, u32[]{:S(2)}, u32[]{:S(2)}) %collective-permute-start.14) | collective-permute-done | bytes 33056 | tf_op jit(solution)/shard_map/ppermute | solution.py:23
  198.8 8.0 %shard_map.155 = f32[64,256]{1,0:T(8,128)} custom-call(bf16[5,64,64,256]{3,2,1,0:T(8,128)(2,1)} %shard_map.152.s_ref, f32[5,64,256]{2,1,0:T(8,128)} %select_select_fusion.1.n_ref), custom_call_target="tpu_custom_call" | custom-call | flops 10485760 | bytes 10878976 | tf_op jit(solution)/shard_map/pallas_call | solution.py:109
  212.7 4.5 %collective-permute-done.16 = bf16[64,1,1]{2,0,1:T(8,128)(2,1)S(1)} collective-permute-done((bf16[64,1,1]{2,0,1:T(8,128)(2,1)S(1)}, bf16[64,1,1]{2,0,1:T(8,128)(2,1)S(1)}, u32[]{:S(2)}, u32[]{:S(2)}) %collective-permute-start.16) | collective-permute-done | bytes 160 | tf_op jit(solution)/shard_map/ppermute | solution.py:22
  217.3 3.1 %collective-permute-start.19 = (bf16[64,1,258]{2,0,1:T(8,128)(2,1)S(1)}, bf16[64,1,258]{2,0,1:T(8,128)(2,1)S(1)}, u32[]{:S(2)}, u32[]{:S(2)}) collective-permute-start(bf16[64,1,258]{2,0,1:T(8,128)(2,1)S(1)} %pad_maximum_fusion.7), channel_id=1, source_target_pairs={{0,1},{1,2},{2,3},{4,5},{5,6},{6,7},{8,9},{9,10},{10,11},{12,13},{... | collective-permute-start | bytes 99080 | tf_op jit(solution)/shard_map/ppermute | solution.py:22
  222.2 4.2 %collective-permute-done.18 = bf16[64,1,258]{2,0,1:T(8,128)(2,1)S(1)} collective-permute-done((bf16[64,1,258]{2,0,1:T(8,128)(2,1)S(1)}, bf16[64,1,258]{2,0,1:T(8,128)(2,1)S(1)}, u32[]{:S(2)}, u32[]{:S(2)}) %collective-permute-start.18) | collective-permute-done | bytes 33056 | tf_op jit(solution)/shard_map/ppermute | solution.py:23
  227.4 8.0 %shard_map.156 = f32[64,256]{1,0:T(8,128)} custom-call(bf16[5,64,64,256]{3,2,1,0:T(8,128)(2,1)} %shard_map.152.s_ref, f32[5,64,256]{2,1,0:T(8,128)} %select_select_fusion.n_ref), custom_call_target="tpu_custom_call" | custom-call | flops 10485760 | bytes 10878976 | tf_op jit(solution)/shard_map/pallas_call | solution.py:109
  (156 shorter events, 55.2 us)
Async XLA Ops:
  0.6 149.0 %copy-start = (f32[48,64]{1,0:T(8,128)S(1)}, f32[48,64]{1,0:T(8,128)}, u32[]{:S(2)}) copy-start(f32[48,64]{1,0:T(8,128)} %param.26) | copy-start | bytes 36868
  35.8 63.8 %collective-permute-start = (bf16[5,64,64,32]{2,3,1,0:T(8,128)(2,1)S(1)}, bf16[5,64,64,32]{2,3,1,0:T(8,128)(2,1)}, u32[]{:S(2)}, u32[]{:S(2)}) collective-permute-start(bf16[5,64,64,32]{2,3,1,0:T(8,128)(2,1)S(1)} %copy.40), channel_id=1, source_target_pairs={{0,4},{4,8},{8,12},{12,16},{16,20},{20,24},{24,28},{28,32},{32,36}... | collective-permute-start | bytes 3932168 | tf_op jit(solution)/shard_map/ppermute | solution.py:32
  43.9 61.6 %collective-permute-start.1 = (bf16[5,64,64,32]{2,3,1,0:T(8,128)(2,1)}, bf16[5,64,64,32]{2,3,1,0:T(8,128)(2,1)}, u32[]{:S(2)}, u32[]{:S(2)}) collective-permute-start(bf16[5,64,64,32]{2,3,1,0:T(8,128)(2,1)} %copy.41), channel_id=1, source_target_pairs={{4,0},{8,4},{12,8},{16,12},{20,16},{24,20},{28,24},{32,28},{36,32}... | collective-permute-start | bytes 3932168 | tf_op jit(solution)/shard_map/ppermute | solution.py:33
  49.9 29.5 %collective-permute-start.3 = (bf16[64,1,1]{2,1,0:T(2,128)(2,1)S(1)}, bf16[64,1,1]{2,1,0:T(2,128)(2,1)S(1)}, u32[]{:S(2)}, u32[]{:S(2)}) collective-permute-start(bf16[64,1,1]{2,1,0:T(2,128)(2,1)S(1)} %get-tuple-element.37), channel_id=1, source_target_pairs={{4,0},{8,4},{12,8},{16,12},{20,16},{24,20},{28,24},{32,28},{36,32}... | collective-permute-start | bytes 392 | tf_op jit(solution)/shard_map/ppermute | solution.py:23
  51.8 33.5 %collective-permute-start.2 = (bf16[64,1,1]{2,1,0:T(2,128)(2,1)S(1)}, bf16[64,1,1]{2,1,0:T(2,128)(2,1)S(1)}, u32[]{:S(2)}, u32[]{:S(2)}) collective-permute-start(bf16[64,1,1]{2,1,0:T(2,128)(2,1)S(1)} %get-tuple-element.36), channel_id=1, source_target_pairs={{0,4},{4,8},{8,12},{12,16},{16,20},{20,24},{24,28},{28,32},{32,36}... | collective-permute-start | bytes 392 | tf_op jit(solution)/shard_map/ppermute | solution.py:22
  57.5 33.1 %collective-permute-start.6 = (f32[96,32]{0,1:T(8,128)S(1)}, f32[96,32]{0,1:T(8,128)S(1)}, u32[]{:S(2)}, u32[]{:S(2)}) collective-permute-start(f32[96,32]{0,1:T(8,128)S(1)} %get-tuple-element.33), channel_id=1, source_target_pairs={{0,4},{4,8},{8,12},{12,16},{16,20},{20,24},{24,28},{28,32},{32,36}... | collective-permute-start | bytes 36872 | tf_op jit(solution)/shard_map/ppermute | solution.py:32
  79.4 12.6 %collective-permute-start.7 = (f32[96,32]{0,1:T(8,128)S(1)}, f32[96,32]{0,1:T(8,128)S(1)}, u32[]{:S(2)}, u32[]{:S(2)}) collective-permute-start(f32[96,32]{0,1:T(8,128)S(1)} %get-tuple-element.32), channel_id=1, source_target_pairs={{4,0},{8,4},{12,8},{16,12},{20,16},{24,20},{28,24},{32,28},{36,32}... | collective-permute-start | bytes 36872 | tf_op jit(solution)/shard_map/ppermute | solution.py:33
  86.2 9.3 %collective-permute-start.5 = (bf16[64,1,258]{2,1,0:T(2,128)(2,1)}, bf16[64,1,258]{2,1,0:T(2,128)(2,1)S(1)}, u32[]{:S(2)}, u32[]{:S(2)}) collective-permute-start(bf16[64,1,258]{2,1,0:T(2,128)(2,1)} %pad_maximum_fusion.2), channel_id=1, source_target_pairs={{0,1},{1,2},{2,3},{4,5},{5,6},{6,7},{8,9},{9,10},{10,11},{12,13},{... | collective-permute-start | bytes 99080 | tf_op jit(solution)/shard_map/ppermute | solution.py:22
  90.7 6.7 %collective-permute-start.4 = (bf16[64,1,258]{2,1,0:T(2,128)(2,1)}, bf16[64,1,258]{2,1,0:T(2,128)(2,1)S(1)}, u32[]{:S(2)}, u32[]{:S(2)}) collective-permute-start(bf16[64,1,258]{2,1,0:T(2,128)(2,1)} %pad_maximum_fusion.2), channel_id=1, source_target_pairs={{1,0},{2,1},{3,2},{5,4},{6,5},{7,6},{9,8},{10,9},{11,10},{13,12},{... | collective-permute-start | bytes 99080 | tf_op jit(solution)/shard_map/ppermute | solution.py:23
  141.5 27.9 %copy-start.7 = (pred[5,256]{1,0:T(8,128)(4,1)S(1)}, pred[5,256]{1,0:T(8,128)(4,1)}, u32[]{:S(2)}) copy-start(pred[5,256]{1,0:T(8,128)(4,1)} %get-tuple-element.105) | copy-start | bytes 3844
  141.5 27.9 %copy-start.8 = (pred[5,256]{1,0:T(8,128)(4,1)S(1)}, pred[5,256]{1,0:T(8,128)(4,1)}, u32[]{:S(2)}) copy-start(pred[5,256]{1,0:T(8,128)(4,1)} %get-tuple-element.106) | copy-start | bytes 3844
  141.6 27.9 %copy-start.9 = (pred[5,256]{1,0:T(8,128)(4,1)S(1)}, pred[5,256]{1,0:T(8,128)(4,1)}, u32[]{:S(2)}) copy-start(pred[5,256]{1,0:T(8,128)(4,1)} %get-tuple-element.107) | copy-start | bytes 3844
  150.8 4.8 %collective-permute-start.9 = (bf16[64,1,1]{2,0,1:T(8,128)(2,1)S(1)}, bf16[64,1,1]{2,0,1:T(8,128)(2,1)S(1)}, u32[]{:S(2)}, u32[]{:S(2)}) collective-permute-start(bf16[64,1,1]{2,0,1:T(8,128)(2,1)S(1)} %get-tuple-element.69), channel_id=1, source_target_pairs={{4,0},{8,4},{12,8},{16,12},{20,16},{24,20},{28,24},{32,28},{36,32}... | collective-permute-start | bytes 392 | tf_op jit(solution)/shard_map/ppermute | solution.py:23
  152.8 7.2 %collective-permute-start.8 = (bf16[64,1,1]{2,0,1:T(8,128)(2,1)S(1)}, bf16[64,1,1]{2,0,1:T(8,128)(2,1)S(1)}, u32[]{:S(2)}, u32[]{:S(2)}) collective-permute-start(bf16[64,1,1]{2,0,1:T(8,128)(2,1)S(1)} %get-tuple-element.68), channel_id=1, source_target_pairs={{0,4},{4,8},{8,12},{12,16},{16,20},{20,24},{24,28},{28,32},{32,36}... | collective-permute-start | bytes 392 | tf_op jit(solution)/shard_map/ppermute | solution.py:22
  160.0 5.1 %collective-permute-start.11 = (bf16[64,1,258]{2,0,1:T(8,128)(2,1)S(1)}, bf16[64,1,258]{2,0,1:T(8,128)(2,1)S(1)}, u32[]{:S(2)}, u32[]{:S(2)}) collective-permute-start(bf16[64,1,258]{2,0,1:T(8,128)(2,1)S(1)} %pad_maximum_fusion.5), channel_id=1, source_target_pairs={{0,1},{1,2},{2,3},{4,5},{5,6},{6,7},{8,9},{9,10},{10,11},{12,13},{... | collective-permute-start | bytes 99080 | tf_op jit(solution)/shard_map/ppermute | solution.py:22
  163.4 6.0 %collective-permute-start.10 = (bf16[64,1,258]{2,0,1:T(8,128)(2,1)S(1)}, bf16[64,1,258]{2,0,1:T(8,128)(2,1)S(1)}, u32[]{:S(2)}, u32[]{:S(2)}) collective-permute-start(bf16[64,1,258]{2,0,1:T(8,128)(2,1)S(1)} %pad_maximum_fusion.5), channel_id=1, source_target_pairs={{1,0},{2,1},{3,2},{5,4},{6,5},{7,6},{9,8},{10,9},{11,10},{13,12},{... | collective-permute-start | bytes 99080 | tf_op jit(solution)/shard_map/ppermute | solution.py:23
  179.5 4.5 %collective-permute-start.13 = (bf16[64,1,1]{2,0,1:T(8,128)(2,1)S(1)}, bf16[64,1,1]{2,0,1:T(8,128)(2,1)S(1)}, u32[]{:S(2)}, u32[]{:S(2)}) collective-permute-start(bf16[64,1,1]{2,0,1:T(8,128)(2,1)S(1)} %get-tuple-element.63), channel_id=1, source_target_pairs={{4,0},{8,4},{12,8},{16,12},{20,16},{24,20},{28,24},{32,28},{36,32}... | collective-permute-start | bytes 392 | tf_op jit(solution)/shard_map/ppermute | solution.py:23
  181.4 7.2 %collective-permute-start.12 = (bf16[64,1,1]{2,0,1:T(8,128)(2,1)S(1)}, bf16[64,1,1]{2,0,1:T(8,128)(2,1)S(1)}, u32[]{:S(2)}, u32[]{:S(2)}) collective-permute-start(bf16[64,1,1]{2,0,1:T(8,128)(2,1)S(1)} %get-tuple-element.62), channel_id=1, source_target_pairs={{0,4},{4,8},{8,12},{12,16},{16,20},{20,24},{24,28},{28,32},{32,36}... | collective-permute-start | bytes 392 | tf_op jit(solution)/shard_map/ppermute | solution.py:22
  188.6 4.9 %collective-permute-start.15 = (bf16[64,1,258]{2,0,1:T(8,128)(2,1)S(1)}, bf16[64,1,258]{2,0,1:T(8,128)(2,1)S(1)}, u32[]{:S(2)}, u32[]{:S(2)}) collective-permute-start(bf16[64,1,258]{2,0,1:T(8,128)(2,1)S(1)} %pad_maximum_fusion.6), channel_id=1, source_target_pairs={{0,1},{1,2},{2,3},{4,5},{5,6},{6,7},{8,9},{9,10},{10,11},{12,13},{... | collective-permute-start | bytes 99080 | tf_op jit(solution)/shard_map/ppermute | solution.py:22
  191.8 6.0 %collective-permute-start.14 = (bf16[64,1,258]{2,0,1:T(8,128)(2,1)S(1)}, bf16[64,1,258]{2,0,1:T(8,128)(2,1)S(1)}, u32[]{:S(2)}, u32[]{:S(2)}) collective-permute-start(bf16[64,1,258]{2,0,1:T(8,128)(2,1)S(1)} %pad_maximum_fusion.6), channel_id=1, source_target_pairs={{1,0},{2,1},{3,2},{5,4},{6,5},{7,6},{9,8},{10,9},{11,10},{13,12},{... | collective-permute-start | bytes 99080 | tf_op jit(solution)/shard_map/ppermute | solution.py:23
  208.1 4.6 %collective-permute-start.17 = (bf16[64,1,1]{2,0,1:T(8,128)(2,1)S(1)}, bf16[64,1,1]{2,0,1:T(8,128)(2,1)S(1)}, u32[]{:S(2)}, u32[]{:S(2)}) collective-permute-start(bf16[64,1,1]{2,0,1:T(8,128)(2,1)S(1)} %get-tuple-element.59), channel_id=1, source_target_pairs={{4,0},{8,4},{12,8},{16,12},{20,16},{24,20},{28,24},{32,28},{36,32}... | collective-permute-start | bytes 392 | tf_op jit(solution)/shard_map/ppermute | solution.py:23
  210.1 7.2 %collective-permute-start.16 = (bf16[64,1,1]{2,0,1:T(8,128)(2,1)S(1)}, bf16[64,1,1]{2,0,1:T(8,128)(2,1)S(1)}, u32[]{:S(2)}, u32[]{:S(2)}) collective-permute-start(bf16[64,1,1]{2,0,1:T(8,128)(2,1)S(1)} %get-tuple-element.58), channel_id=1, source_target_pairs={{0,4},{4,8},{8,12},{12,16},{16,20},{20,24},{24,28},{28,32},{32,36}... | collective-permute-start | bytes 392 | tf_op jit(solution)/shard_map/ppermute | solution.py:22
  217.3 4.8 %collective-permute-start.19 = (bf16[64,1,258]{2,0,1:T(8,128)(2,1)S(1)}, bf16[64,1,258]{2,0,1:T(8,128)(2,1)S(1)}, u32[]{:S(2)}, u32[]{:S(2)}) collective-permute-start(bf16[64,1,258]{2,0,1:T(8,128)(2,1)S(1)} %pad_maximum_fusion.7), channel_id=1, source_target_pairs={{0,1},{1,2},{2,3},{4,5},{5,6},{6,7},{8,9},{9,10},{10,11},{12,13},{... | collective-permute-start | bytes 99080 | tf_op jit(solution)/shard_map/ppermute | solution.py:22
  220.4 6.0 %collective-permute-start.18 = (bf16[64,1,258]{2,0,1:T(8,128)(2,1)S(1)}, bf16[64,1,258]{2,0,1:T(8,128)(2,1)S(1)}, u32[]{:S(2)}, u32[]{:S(2)}) collective-permute-start(bf16[64,1,258]{2,0,1:T(8,128)(2,1)S(1)} %pad_maximum_fusion.7), channel_id=1, source_target_pairs={{1,0},{2,1},{3,2},{5,4},{6,5},{7,6},{9,8},{10,9},{11,10},{13,12},{... | collective-permute-start | bytes 99080 | tf_op jit(solution)/shard_map/ppermute | solution.py:23
  (18 other events, 319.5 us)

commit v3 on v2

--- a/solution.py
+++ b/solution.py
@@ -48,15 +48,15 @@
     out = jax.ShapeDtypeStruct((slots, rows_i, rows_j, width), stiffness.dtype)
     return pl.pallas_call(
         gather_kernel,
-        grid=(slots, rows_i // ROWS),
+        grid=(slots,),
         in_specs=[
-            pl.BlockSpec((1, ROWS, rows_j, blocks), lambda k, i: (k, i, 0, 0)),
-            pl.BlockSpec((blocks, width), lambda k, i: (0, 0)),
-            pl.BlockSpec((blocks, width), lambda k, i: (0, 0)),
+            pl.BlockSpec((1, rows_i, rows_j, blocks), lambda k: (k, 0, 0, 0)),
+            pl.BlockSpec((blocks, width), lambda k: (0, 0)),
+            pl.BlockSpec((blocks, width), lambda k: (0, 0)),
         ],
         out_specs=[
-            pl.BlockSpec((1, ROWS, rows_j, width), lambda k, i: (k, i, 0, 0)),
-            pl.BlockSpec((1, ROWS, rows_j, width), lambda k, i: (k, i, 0, 0)),
+            pl.BlockSpec((1, rows_i, rows_j, width), lambda k: (k, 0, 0, 0)),
+            pl.BlockSpec((1, rows_i, rows_j, width), lambda k: (k, 0, 0, 0)),
         ],
         out_shape=[out, out],
     )(stiffness, pick_lo, pick_hi)
@@ -81,16 +81,16 @@
     width = arrived_lo.shape[-1]
     return pl.pallas_call(
         merge_kernel,
-        grid=(slots, rows_i // ROWS),
+        grid=(slots,),
         in_specs=[
-            pl.BlockSpec((1, ROWS, rows_j, blocks), lambda k, i: (k, i, 0, 0)),
-            pl.BlockSpec((1, ROWS, rows_j, width), lambda k, i: (k, i, 0, 0)),
-            pl.BlockSpec((1, ROWS, rows_j, width), lambda k, i: (k, i, 0, 0)),
-            pl.BlockSpec((width, blocks), lambda k, i: (0, 0)),
-            pl.BlockSpec((width, blocks), lambda k, i: (0, 0)),
-            pl.BlockSpec((1, blocks), lambda k, i: (0, 0)),
-        ],
-        out_specs=pl.BlockSpec((1, ROWS, rows_j, blocks), lambda k, i: (k, i, 0, 0)),
+            pl.BlockSpec((1, rows_i, rows_j, blocks), lambda k: (k, 0, 0, 0)),
+            pl.BlockSpec((1, rows_i, rows_j, width), lambda k: (k, 0, 0, 0)),
+            pl.BlockSpec((1, rows_i, rows_j, width), lambda k: (k, 0, 0, 0)),
+            pl.BlockSpec((width, blocks), lambda k: (0, 0)),
+            pl.BlockSpec((width, blocks), lambda k: (0, 0)),
+            pl.BlockSpec((1, blocks), lambda k: (0, 0)),
+        ],
+        out_specs=pl.BlockSpec((1, rows_i, rows_j, blocks), lambda k: (k, 0, 0, 0)),
         out_shape=jax.ShapeDtypeStruct(stiffness.shape, stiffness.dtype),
     )(stiffness, arrived_lo, arrived_hi, place_lo, place_hi, arrival)
 
@@ -189,13 +189,12 @@
     for repeat in range(ITERS):
         rounded = moved.astype(jnp.bfloat16)[:, None, :]
         padded = padded_2(rounded, (("shaft", 2), ("ply", 1)), 1)
-        neighbours = jnp.zeros((slots,) + moved.shape, jnp.float32)
+        neighbours = jnp.zeros((slots,) + moved.shape, jnp.bfloat16)
         for code_index in range(9):
             shifted = padded[:, code_index // 3, code_index % 3 : code_index % 3 + blocks]
-            neighbours = jnp.where(
-                codes == code_index, shifted.astype(jnp.float32)[None], neighbours
-            )
-        force = block_force(stiffness, neighbours) + jnp.dot(
+            neighbours = jnp.where(codes == code_index, shifted[None], neighbours)
+        product = stiffness.astype(jnp.float32) * neighbours.astype(jnp.float32)[:, None, :, :]
+        force = jnp.sum(product, axis=(0, 2)) + jnp.dot(
             strain_map.T, history, precision=lax.Precision.HIGHEST
         )
         speeds = speeds + time_step * (scaling * (forcing - force))

time: 242 us -> 183 us (0.76); the launches traced: 239 us -> 182 us
  Pallas kernels: 90.7 us -> 26.7 us
  other arithmetic: 12.9 us -> 21.9 us
  waiting for transfers between devices: 43.9 us -> 46.7 us
    pallas_call x6 -> x2, Pallas kernels: 90.7 us -> 26.7 us  [the longest x1 14.7 us: merge_arrived(): pl.pallas_call(merge_kernel, grid=(slots,), in_specs=[pl.BlockSpec((1, ro...]
    reduce_sum x0 -> x4, other arithmetic: none -> 15.3 us  [on_device(): jnp.sum(product, axis=(0, 2))]
    select_n x4 -> x0, other arithmetic: 4.61 us -> none  [on_device(): jnp.where(codes == code_index, shifted.astype(jnp.float32)[None], neighbo...]
    ppermute x8, waiting for transfers between devices: 29.6 us -> 32.3 us  [padded_2(): after = lax.ppermute(first, axis, down)]
    unnamed x59 -> x54, local copies, waits for them, and re-layouts: 5.44 us -> 4.24 us
  transfers between devices with their start and end apart: 20 -> 20, of which waited for: 11 -> 11; matrix products, arithmetic and copies ran while one was open for 12% -> 14% of each run, Pallas kernels for 0% -> 0%
where the time goes in v3:
time: 183 us; the launch traced here: 182 us
  starting transfers between devices  49.9 us (27%)
  waiting for transfers between devices  46.7 us (26%)
  local copies, waits for them, and re-layouts  33.6 us (18%)
  Pallas kernels  26.7 us (15%)
  other arithmetic  21.9 us (12%)
  matrix products  1.85 us (1%)
    ppermute x8, waiting for transfers between devices, padded_2(): after = lax.ppermute(first, axis, down)  32.3 us
    ppermute x8, starting transfers between devices, padded_2(): before = lax.ppermute(last, axis, up)  21.4 us
    reduce_sum x4, other arithmetic, on_device(): jnp.sum(product, axis=(0, 2))  15.3 us
    pallas_call x1, Pallas kernels, merge_arrived(): pl.pallas_call(merge_kernel, grid=(slots,), in_specs=[pl.BlockSpec((1, ro...  14.7 us
    ppermute x8, waiting for transfers between devices, padded_2(): before = lax.ppermute(last, axis, up)  14.5 us
    ppermute x8, starting transfers between devices, padded_2(): after = lax.ppermute(first, axis, down)  13 us
    pallas_call x1, Pallas kernels, gather_leaving(): pl.pallas_call(gather_kernel, grid=(slots,), in_specs=[pl.BlockSpec((1, r...  12 us
    ppermute x2, starting transfers between devices, neighbour_exchange(): from_higher = lax.ppermute(lower_bound, axis, down)  11.7 us
  transfers between devices with their start and end apart: 20, of which 11 were waited for; matrix products, arithmetic and copies ran while one was open for 14% of the time, Pallas kernels for 0%

profile of v3, /device:TPU:96, one launch (start us, length us, event | category | flops | bytes accessed | tf_op | source)
XLA Modules:
  0.0 182.1 jit_solution(15122174168646606759)
XLA Ops:
  2.1 12.0 %shard_map.151 = (bf16[5,64,64,32]{3,2,1,0:T(8,128)(2,1)}, bf16[5,64,64,32]{3,2,1,0:T(8,128)(2,1)}) custom-call(bf16[5,64,64,256]{3,2,1,0:T(8,128)(2,1)} %s_ref.3, bf16[256,32]{1,0:T(8,128)(2,1)} %get-tuple-element.91.lo_ref, bf16[256,32]{1,0:T(8,128)(2,1)} %get-tuple-element.92.hi_ref), custom_call_target="tpu_custom_call" | custom-call | tf_op jit(solution)/shard_map/pallas_call | solution.py:49
  14.2 5.0 %copy.40 = bf16[5,64,64,32]{2,3,1,0:T(8,128)(2,1)S(1)} copy(bf16[5,64,64,32]{3,2,1,0:T(8,128)(2,1)} %get-tuple-element.7) | data formatting | bytes 2621440 | tf_op jit(solution)/shard_map/pallas_call | solution.py:49
  21.0 6.1 %copy.41 = bf16[5,64,64,32]{2,3,1,0:T(8,128)(2,1)} copy(bf16[5,64,64,32]{3,2,1,0:T(8,128)(2,1)} %get-tuple-element.8) | data formatting | bytes 2621440 | tf_op jit(solution)/shard_map/pallas_call | solution.py:49
  27.2 5.7 %collective-permute-start.1 = (bf16[5,64,64,32]{2,3,1,0:T(8,128)(2,1)}, bf16[5,64,64,32]{2,3,1,0:T(8,128)(2,1)}, u32[]{:S(2)}, u32[]{:S(2)}) collective-permute-start(bf16[5,64,64,32]{2,3,1,0:T(8,128)(2,1)} %copy.41), channel_id=1, source_target_pairs={{4,0},{8,4},{12,8},{16,12},{20,16},{24,20},{28,24},{32,28},{36,32}... | collective-permute-start | bytes 3932168 | tf_op jit(solution)/shard_map/ppermute | solution.py:33
  35.0 2.4 %collective-permute-start.2 = (bf16[64,1,1]{2,1,0:T(2,128)(2,1)S(1)}, bf16[64,1,1]{2,1,0:T(2,128)(2,1)S(1)}, u32[]{:S(2)}, u32[]{:S(2)}) collective-permute-start(bf16[64,1,1]{2,1,0:T(2,128)(2,1)S(1)} %get-tuple-element.32), channel_id=1, source_target_pairs={{0,4},{4,8},{8,12},{12,16},{16,20},{20,24},{24,28},{28,32},{32,36}... | collective-permute-start | bytes 392 | tf_op jit(solution)/shard_map/ppermute | solution.py:22
  45.9 16.7 %collective-permute-done.3 = bf16[64,1,1]{2,1,0:T(2,128)(2,1)S(1)} collective-permute-done((bf16[64,1,1]{2,1,0:T(2,128)(2,1)S(1)}, bf16[64,1,1]{2,1,0:T(2,128)(2,1)S(1)}, u32[]{:S(2)}, u32[]{:S(2)}) %collective-permute-start.3) | collective-permute-done | bytes 160 | tf_op jit(solution)/shard_map/ppermute | solution.py:23
  62.6 5.9 %collective-permute-start.7 = (f32[96,32]{0,1:T(8,128)S(1)}, f32[96,32]{0,1:T(8,128)S(1)}, u32[]{:S(2)}, u32[]{:S(2)}) collective-permute-start(f32[96,32]{0,1:T(8,128)S(1)} %get-tuple-element.28), channel_id=1, source_target_pairs={{4,0},{8,4},{12,8},{16,12},{20,16},{24,20},{28,24},{32,28},{36,32}... | collective-permute-start | bytes 36872 | tf_op jit(solution)/shard_map/ppermute | solution.py:33
  69.4 3.4 %collective-permute-start.5 = (bf16[64,1,258]{2,1,0:T(2,128)(2,1)}, bf16[64,1,258]{2,1,0:T(2,128)(2,1)S(1)}, u32[]{:S(2)}, u32[]{:S(2)}) collective-permute-start(bf16[64,1,258]{2,1,0:T(2,128)(2,1)} %pad_maximum_fusion.2), channel_id=1, source_target_pairs={{0,1},{1,2},{2,3},{4,5},{5,6},{6,7},{8,9},{9,10},{10,11},{12,13},{... | collective-permute-start | bytes 99080 | tf_op jit(solution)/shard_map/ppermute | solution.py:22
  77.5 3.1 %collective-permute-done.4 = bf16[64,1,258]{2,1,0:T(2,128)(2,1)S(1)} collective-permute-done((bf16[64,1,258]{2,1,0:T(2,128)(2,1)}, bf16[64,1,258]{2,1,0:T(2,128)(2,1)S(1)}, u32[]{:S(2)}, u32[]{:S(2)}) %collective-permute-start.4) | collective-permute-done | bytes 33056 | tf_op jit(solution)/shard_map/ppermute | solution.py:23
  81.8 6.0 %copy.42.lo_ref = bf16[5,64,64,32]{3,2,1,0:T(8,128)(2,1)} copy(bf16[5,64,64,32]{2,3,1,0:T(8,128)(2,1)} %collective-permute-done) | data formatting | bytes 2621440 | tf_op jit(solution)/shard_map/ppermute | solution.py:32
  87.8 5.9 %copy.43.hi_ref = bf16[5,64,64,32]{3,2,1,0:T(8,128)(2,1)} copy(bf16[5,64,64,32]{2,3,1,0:T(8,128)(2,1)} %collective-permute-done.1) | data formatting | bytes 2621440 | tf_op jit(solution)/shard_map/ppermute | solution.py:33
  93.7 14.7 %shard_map.152 = bf16[5,64,64,256]{3,2,1,0:T(8,128)(2,1)} custom-call(bf16[5,64,64,256]{3,2,1,0:T(8,128)(2,1)} %s_ref.3, bf16[5,64,64,32]{3,2,1,0:T(8,128)(2,1)} %copy.42.lo_ref, bf16[5,64,64,32]{3,2,1,0:T(8,128)(2,1)} %copy.43.hi_ref, bf16[32,256]{1,0:T(8,128)(2,1)} %get-tuple-element.78.place_lo_ref, bf16[32,256]{1,0:T(8,128)(2,1)} %get-tuple-element.93.place_hi_ref, ...), custom_call_target="tpu_custom_call" | custom-call | tf_op jit(solution)/shard_map/pallas_call | solution.py:82
  108.5 6.9 %fusion = f32[64,256]{1,0:T(8,128)S(1)} fusion(bf16[5,64,64,256]{3,2,1,0:T(8,128)(2,1)} %shard_map.152, f32[5,64,256]{2,1,0:T(8,128)S(1)} %select_convert_fusion.3), kind=kLoop, calls=%fused_computation.9 | loop fusion | flops 15712256 | bytes 10878976 | tf_op jit(solution)/shard_map/reduce_sum | solution.py:197
  120.4 4.5 %collective-permute-done.8 = bf16[64,1,1]{2,0,1:T(8,128)(2,1)S(1)} collective-permute-done((bf16[64,1,1]{2,0,1:T(8,128)(2,1)S(1)}, bf16[64,1,1]{2,0,1:T(8,128)(2,1)S(1)}, u32[]{:S(2)}, u32[]{:S(2)}) %collective-permute-start.8) | collective-permute-done | bytes 160 | tf_op jit(solution)/shard_map/ppermute | solution.py:22
  125.0 3.4 %collective-permute-start.11 = (bf16[64,1,258]{2,0,1:T(8,128)(2,1)S(1)}, bf16[64,1,258]{2,0,1:T(8,128)(2,1)S(1)}, u32[]{:S(2)}, u32[]{:S(2)}) collective-permute-start(bf16[64,1,258]{2,0,1:T(8,128)(2,1)S(1)} %pad_maximum_fusion.5), channel_id=1, source_target_pairs={{0,1},{1,2},{2,3},{4,5},{5,6},{6,7},{8,9},{9,10},{10,11},{12,13},{... | collective-permute-start | bytes 99080 | tf_op jit(solution)/shard_map/ppermute | solution.py:22
  130.3 4.2 %collective-permute-done.10 = bf16[64,1,258]{2,0,1:T(8,128)(2,1)S(1)} collective-permute-done((bf16[64,1,258]{2,0,1:T(8,128)(2,1)S(1)}, bf16[64,1,258]{2,0,1:T(8,128)(2,1)S(1)}, u32[]{:S(2)}, u32[]{:S(2)}) %collective-permute-start.10) | collective-permute-done | bytes 33056 | tf_op jit(solution)/shard_map/ppermute | solution.py:23
  134.7 2.8 %fusion.1 = f32[64,256]{1,0:T(8,128)S(1)} fusion(bf16[5,64,64,256]{3,2,1,0:T(8,128)(2,1)S(1)} %copy-done.1, f32[5,64,256]{2,1,0:T(8,128)S(1)} %select_convert_fusion.2), kind=kLoop, calls=%fused_computation.10 | loop fusion | flops 15712256 | bytes 10878976 | tf_op jit(solution)/shard_map/reduce_sum | solution.py:197
  142.4 4.5 %collective-permute-done.12 = bf16[64,1,1]{2,0,1:T(8,128)(2,1)S(1)} collective-permute-done((bf16[64,1,1]{2,0,1:T(8,128)(2,1)S(1)}, bf16[64,1,1]{2,0,1:T(8,128)(2,1)S(1)}, u32[]{:S(2)}, u32[]{:S(2)}) %collective-permute-start.12) | collective-permute-done | bytes 160 | tf_op jit(solution)/shard_map/ppermute | solution.py:22
  147.0 3.1 %collective-permute-start.15 = (bf16[64,1,258]{2,0,1:T(8,128)(2,1)S(1)}, bf16[64,1,258]{2,0,1:T(8,128)(2,1)S(1)}, u32[]{:S(2)}, u32[]{:S(2)}) collective-permute-start(bf16[64,1,258]{2,0,1:T(8,128)(2,1)S(1)} %pad_maximum_fusion.6), channel_id=1, source_target_pairs={{0,1},{1,2},{2,3},{4,5},{5,6},{6,7},{8,9},{9,10},{10,11},{12,13},{... | collective-permute-start | bytes 99080 | tf_op jit(solution)/shard_map/ppermute | solution.py:22
  151.9 4.2 %collective-permute-done.14 = bf16[64,1,258]{2,0,1:T(8,128)(2,1)S(1)} collective-permute-done((bf16[64,1,258]{2,0,1:T(8,128)(2,1)S(1)}, bf16[64,1,258]{2,0,1:T(8,128)(2,1)S(1)}, u32[]{:S(2)}, u32[]{:S(2)}) %collective-permute-start.14) | collective-permute-done | bytes 33056 | tf_op jit(solution)/shard_map/ppermute | solution.py:23
  156.3 2.8 %fusion.2 = f32[64,256]{1,0:T(8,128)S(1)} fusion(bf16[5,64,64,256]{3,2,1,0:T(8,128)(2,1)S(1)} %copy-done.1, f32[5,64,256]{2,1,0:T(8,128)S(1)} %select_convert_fusion.1), kind=kLoop, calls=%fused_computation.11 | loop fusion | flops 15712256 | bytes 10878976 | tf_op jit(solution)/shard_map/reduce_sum | solution.py:197
  164.0 4.5 %collective-permute-done.16 = bf16[64,1,1]{2,0,1:T(8,128)(2,1)S(1)} collective-permute-done((bf16[64,1,1]{2,0,1:T(8,128)(2,1)S(1)}, bf16[64,1,1]{2,0,1:T(8,128)(2,1)S(1)}, u32[]{:S(2)}, u32[]{:S(2)}) %collective-permute-start.16) | collective-permute-done | bytes 160 | tf_op jit(solution)/shard_map/ppermute | solution.py:22
  172.4 4.2 %collective-permute-done.18 = bf16[64,1,258]{2,0,1:T(8,128)(2,1)S(1)} collective-permute-done((bf16[64,1,258]{2,0,1:T(8,128)(2,1)S(1)}, bf16[64,1,258]{2,0,1:T(8,128)(2,1)S(1)}, u32[]{:S(2)}, u32[]{:S(2)}) %collective-permute-start.18) | collective-permute-done | bytes 33056 | tf_op jit(solution)/shard_map/ppermute | solution.py:23
  176.8 2.8 %fusion.3 = f32[64,256]{1,0:T(8,128)S(1)} fusion(bf16[5,64,64,256]{3,2,1,0:T(8,128)(2,1)S(1)} %copy-done.1, f32[5,64,256]{2,1,0:T(8,128)S(1)} %select_convert_fusion), kind=kLoop, calls=%fused_computation.12 | loop fusion | flops 15712256 | bytes 10878976 | tf_op jit(solution)/shard_map/reduce_sum | solution.py:197
  (146 shorter events, 45.9 us)
Async XLA Ops:
  0.6 114.8 %copy-start = (f32[48,64]{1,0:T(8,128)S(1)}, f32[48,64]{1,0:T(8,128)}, u32[]{:S(2)}) copy-start(f32[48,64]{1,0:T(8,128)} %param.26) | copy-start | bytes 36868
  14.1 30.5 %copy-start.14 = (s32[5,1,256]{2,1,0:T(1,128)S(1)}, s32[5,1,256]{2,1,0:T(1,128)}, u32[]{:S(2)}) copy-start(s32[5,1,256]{2,1,0:T(1,128)} %param.21) | copy-start | bytes 15364
  14.1 30.5 %copy-start.15 = (s32[1,256]{1,0:T(1,128)S(1)}, s32[1,256]{1,0:T(1,128)}, u32[]{:S(2)}) copy-start(s32[1,256]{1,0:T(1,128)} %param.22) | copy-start | bytes 3076
  19.1 62.7 %collective-permute-start = (bf16[5,64,64,32]{2,3,1,0:T(8,128)(2,1)S(1)}, bf16[5,64,64,32]{2,3,1,0:T(8,128)(2,1)}, u32[]{:S(2)}, u32[]{:S(2)}) collective-permute-start(bf16[5,64,64,32]{2,3,1,0:T(8,128)(2,1)S(1)} %copy.40), channel_id=1, source_target_pairs={{0,4},{4,8},{8,12},{12,16},{16,20},{20,24},{24,28},{28,32},{32,36}... | collective-permute-start | bytes 3932168 | tf_op jit(solution)/shard_map/ppermute | solution.py:32
  27.2 60.6 %collective-permute-start.1 = (bf16[5,64,64,32]{2,3,1,0:T(8,128)(2,1)}, bf16[5,64,64,32]{2,3,1,0:T(8,128)(2,1)}, u32[]{:S(2)}, u32[]{:S(2)}) collective-permute-start(bf16[5,64,64,32]{2,3,1,0:T(8,128)(2,1)} %copy.41), channel_id=1, source_target_pairs={{4,0},{8,4},{12,8},{16,12},{20,16},{24,20},{28,24},{32,28},{36,32}... | collective-permute-start | bytes 3932168 | tf_op jit(solution)/shard_map/ppermute | solution.py:33
  33.1 29.5 %collective-permute-start.3 = (bf16[64,1,1]{2,1,0:T(2,128)(2,1)S(1)}, bf16[64,1,1]{2,1,0:T(2,128)(2,1)S(1)}, u32[]{:S(2)}, u32[]{:S(2)}) collective-permute-start(bf16[64,1,1]{2,1,0:T(2,128)(2,1)S(1)} %get-tuple-element.33), channel_id=1, source_target_pairs={{4,0},{8,4},{12,8},{16,12},{20,16},{24,20},{28,24},{32,28},{36,32}... | collective-permute-start | bytes 392 | tf_op jit(solution)/shard_map/ppermute | solution.py:23
  35.0 33.5 %collective-permute-start.2 = (bf16[64,1,1]{2,1,0:T(2,128)(2,1)S(1)}, bf16[64,1,1]{2,1,0:T(2,128)(2,1)S(1)}, u32[]{:S(2)}, u32[]{:S(2)}) collective-permute-start(bf16[64,1,1]{2,1,0:T(2,128)(2,1)S(1)} %get-tuple-element.32), channel_id=1, source_target_pairs={{0,4},{4,8},{8,12},{12,16},{16,20},{20,24},{24,28},{28,32},{32,36}... | collective-permute-start | bytes 392 | tf_op jit(solution)/shard_map/ppermute | solution.py:22
  40.8 33.1 %collective-permute-start.6 = (f32[96,32]{0,1:T(8,128)S(1)}, f32[96,32]{0,1:T(8,128)S(1)}, u32[]{:S(2)}, u32[]{:S(2)}) collective-permute-start(f32[96,32]{0,1:T(8,128)S(1)} %get-tuple-element.29), channel_id=1, source_target_pairs={{0,4},{4,8},{8,12},{12,16},{16,20},{20,24},{24,28},{28,32},{32,36}... | collective-permute-start | bytes 36872 | tf_op jit(solution)/shard_map/ppermute | solution.py:32
  44.7 49.0 %copy-start.6 = (pred[5,256]{1,0:T(8,128)(4,1)}, pred[5,256]{1,0:T(8,128)(4,1)S(1)}, u32[]{:S(2)}) copy-start(pred[5,256]{1,0:T(8,128)(4,1)S(1)} %get-tuple-element.100) | copy-start | bytes 3844
  62.6 12.5 %collective-permute-start.7 = (f32[96,32]{0,1:T(8,128)S(1)}, f32[96,32]{0,1:T(8,128)S(1)}, u32[]{:S(2)}, u32[]{:S(2)}) collective-permute-start(f32[96,32]{0,1:T(8,128)S(1)} %get-tuple-element.28), channel_id=1, source_target_pairs={{4,0},{8,4},{12,8},{16,12},{20,16},{24,20},{28,24},{32,28},{36,32}... | collective-permute-start | bytes 36872 | tf_op jit(solution)/shard_map/ppermute | solution.py:33
  69.4 7.7 %collective-permute-start.5 = (bf16[64,1,258]{2,1,0:T(2,128)(2,1)}, bf16[64,1,258]{2,1,0:T(2,128)(2,1)S(1)}, u32[]{:S(2)}, u32[]{:S(2)}) collective-permute-start(bf16[64,1,258]{2,1,0:T(2,128)(2,1)} %pad_maximum_fusion.2), channel_id=1, source_target_pairs={{0,1},{1,2},{2,3},{4,5},{5,6},{6,7},{8,9},{9,10},{10,11},{12,13},{... | collective-permute-start | bytes 99080 | tf_op jit(solution)/shard_map/ppermute | solution.py:22
  73.8 6.7 %collective-permute-start.4 = (bf16[64,1,258]{2,1,0:T(2,128)(2,1)}, bf16[64,1,258]{2,1,0:T(2,128)(2,1)S(1)}, u32[]{:S(2)}, u32[]{:S(2)}) collective-permute-start(bf16[64,1,258]{2,1,0:T(2,128)(2,1)} %pad_maximum_fusion.2), channel_id=1, source_target_pairs={{1,0},{2,1},{3,2},{5,4},{6,5},{7,6},{9,8},{10,9},{11,10},{13,12},{... | collective-permute-start | bytes 99080 | tf_op jit(solution)/shard_map/ppermute | solution.py:23
  115.9 4.5 %collective-permute-start.9 = (bf16[64,1,1]{2,0,1:T(8,128)(2,1)S(1)}, bf16[64,1,1]{2,0,1:T(8,128)(2,1)S(1)}, u32[]{:S(2)}, u32[]{:S(2)}) collective-permute-start(bf16[64,1,1]{2,0,1:T(8,128)(2,1)S(1)} %get-tuple-element.65), channel_id=1, source_target_pairs={{4,0},{8,4},{12,8},{16,12},{20,16},{24,20},{28,24},{32,28},{36,32}... | collective-permute-start | bytes 392 | tf_op jit(solution)/shard_map/ppermute | solution.py:23
  117.8 7.2 %collective-permute-start.8 = (bf16[64,1,1]{2,0,1:T(8,128)(2,1)S(1)}, bf16[64,1,1]{2,0,1:T(8,128)(2,1)S(1)}, u32[]{:S(2)}, u32[]{:S(2)}) collective-permute-start(bf16[64,1,1]{2,0,1:T(8,128)(2,1)S(1)} %get-tuple-element.64), channel_id=1, source_target_pairs={{0,4},{4,8},{8,12},{12,16},{16,20},{20,24},{24,28},{28,32},{32,36}... | collective-permute-start | bytes 392 | tf_op jit(solution)/shard_map/ppermute | solution.py:22
  125.0 5.1 %collective-permute-start.11 = (bf16[64,1,258]{2,0,1:T(8,128)(2,1)S(1)}, bf16[64,1,258]{2,0,1:T(8,128)(2,1)S(1)}, u32[]{:S(2)}, u32[]{:S(2)}) collective-permute-start(bf16[64,1,258]{2,0,1:T(8,128)(2,1)S(1)} %pad_maximum_fusion.5), channel_id=1, source_target_pairs={{0,1},{1,2},{2,3},{4,5},{5,6},{6,7},{8,9},{9,10},{10,11},{12,13},{... | collective-permute-start | bytes 99080 | tf_op jit(solution)/shard_map/ppermute | solution.py:22
  128.4 6.0 %collective-permute-start.10 = (bf16[64,1,258]{2,0,1:T(8,128)(2,1)S(1)}, bf16[64,1,258]{2,0,1:T(8,128)(2,1)S(1)}, u32[]{:S(2)}, u32[]{:S(2)}) collective-permute-start(bf16[64,1,258]{2,0,1:T(8,128)(2,1)S(1)} %pad_maximum_fusion.5), channel_id=1, source_target_pairs={{1,0},{2,1},{3,2},{5,4},{6,5},{7,6},{9,8},{10,9},{11,10},{13,12},{... | collective-permute-start | bytes 99080 | tf_op jit(solution)/shard_map/ppermute | solution.py:23
  137.8 4.5 %collective-permute-start.13 = (bf16[64,1,1]{2,0,1:T(8,128)(2,1)S(1)}, bf16[64,1,1]{2,0,1:T(8,128)(2,1)S(1)}, u32[]{:S(2)}, u32[]{:S(2)}) collective-permute-start(bf16[64,1,1]{2,0,1:T(8,128)(2,1)S(1)} %get-tuple-element.59), channel_id=1, source_target_pairs={{4,0},{8,4},{12,8},{16,12},{20,16},{24,20},{28,24},{32,28},{36,32}... | collective-permute-start | bytes 392 | tf_op jit(solution)/shard_map/ppermute | solution.py:23
  139.8 7.2 %collective-permute-start.12 = (bf16[64,1,1]{2,0,1:T(8,128)(2,1)S(1)}, bf16[64,1,1]{2,0,1:T(8,128)(2,1)S(1)}, u32[]{:S(2)}, u32[]{:S(2)}) collective-permute-start(bf16[64,1,1]{2,0,1:T(8,128)(2,1)S(1)} %get-tuple-element.58), channel_id=1, source_target_pairs={{0,4},{4,8},{8,12},{12,16},{16,20},{20,24},{24,28},{28,32},{32,36}... | collective-permute-start | bytes 392 | tf_op jit(solution)/shard_map/ppermute | solution.py:22
  147.0 4.8 %collective-permute-start.15 = (bf16[64,1,258]{2,0,1:T(8,128)(2,1)S(1)}, bf16[64,1,258]{2,0,1:T(8,128)(2,1)S(1)}, u32[]{:S(2)}, u32[]{:S(2)}) collective-permute-start(bf16[64,1,258]{2,0,1:T(8,128)(2,1)S(1)} %pad_maximum_fusion.6), channel_id=1, source_target_pairs={{0,1},{1,2},{2,3},{4,5},{5,6},{6,7},{8,9},{9,10},{10,11},{12,13},{... | collective-permute-start | bytes 99080 | tf_op jit(solution)/shard_map/ppermute | solution.py:22
  150.1 6.0 %collective-permute-start.14 = (bf16[64,1,258]{2,0,1:T(8,128)(2,1)S(1)}, bf16[64,1,258]{2,0,1:T(8,128)(2,1)S(1)}, u32[]{:S(2)}, u32[]{:S(2)}) collective-permute-start(bf16[64,1,258]{2,0,1:T(8,128)(2,1)S(1)} %pad_maximum_fusion.6), channel_id=1, source_target_pairs={{1,0},{2,1},{3,2},{5,4},{6,5},{7,6},{9,8},{10,9},{11,10},{13,12},{... | collective-permute-start | bytes 99080 | tf_op jit(solution)/shard_map/ppermute | solution.py:23
  159.5 4.5 %collective-permute-start.17 = (bf16[64,1,1]{2,0,1:T(8,128)(2,1)S(1)}, bf16[64,1,1]{2,0,1:T(8,128)(2,1)S(1)}, u32[]{:S(2)}, u32[]{:S(2)}) collective-permute-start(bf16[64,1,1]{2,0,1:T(8,128)(2,1)S(1)} %get-tuple-element.55), channel_id=1, source_target_pairs={{4,0},{8,4},{12,8},{16,12},{20,16},{24,20},{28,24},{32,28},{36,32}... | collective-permute-start | bytes 392 | tf_op jit(solution)/shard_map/ppermute | solution.py:23
  161.4 7.2 %collective-permute-start.16 = (bf16[64,1,1]{2,0,1:T(8,128)(2,1)S(1)}, bf16[64,1,1]{2,0,1:T(8,128)(2,1)S(1)}, u32[]{:S(2)}, u32[]{:S(2)}) collective-permute-start(bf16[64,1,1]{2,0,1:T(8,128)(2,1)S(1)} %get-tuple-element.54), channel_id=1, source_target_pairs={{0,4},{4,8},{8,12},{12,16},{16,20},{20,24},{24,28},{28,32},{32,36}... | collective-permute-start | bytes 392 | tf_op jit(solution)/shard_map/ppermute | solution.py:22
  168.7 3.7 %collective-permute-start.19 = (bf16[64,1,258]{2,0,1:T(8,128)(2,1)S(1)}, bf16[64,1,258]{2,0,1:T(8,128)(2,1)S(1)}, u32[]{:S(2)}, u32[]{:S(2)}) collective-permute-start(bf16[64,1,258]{2,0,1:T(8,128)(2,1)S(1)} %pad_maximum_fusion.7), channel_id=1, source_target_pairs={{0,1},{1,2},{2,3},{4,5},{5,6},{6,7},{8,9},{9,10},{10,11},{12,13},{... | collective-permute-start | bytes 99080 | tf_op jit(solution)/shard_map/ppermute | solution.py:22
  170.6 6.0 %collective-permute-start.18 = (bf16[64,1,258]{2,0,1:T(8,128)(2,1)S(1)}, bf16[64,1,258]{2,0,1:T(8,128)(2,1)S(1)}, u32[]{:S(2)}, u32[]{:S(2)}) collective-permute-start(bf16[64,1,258]{2,0,1:T(8,128)(2,1)S(1)} %pad_maximum_fusion.7), channel_id=1, source_target_pairs={{1,0},{2,1},{3,2},{5,4},{6,5},{7,6},{9,8},{10,9},{11,10},{13,12},{... | collective-permute-start | bytes 99080 | tf_op jit(solution)/shard_map/ppermute | solution.py:23
  (15 other events, 295.9 us)

commit v4 on v3

--- a/solution.py
+++ b/solution.py
@@ -35,62 +35,56 @@
 
 
 def gather_kernel(s_ref, lo_ref, hi_ref, out_lo_ref, out_hi_ref):
-    rows, depth, blocks = s_ref.shape[1:]
-    flat = s_ref[0].reshape(rows * depth, blocks)
+    flat = s_ref[0]
     for pick_ref, out_ref in ((lo_ref, out_lo_ref), (hi_ref, out_hi_ref)):
-        picked = jnp.dot(flat, pick_ref[...], preferred_element_type=jnp.float32)
-        out_ref[0] = picked.reshape(rows, depth, -1).astype(out_ref.dtype)
+        picked = lax.dot_general(
+            pick_ref[...], flat, (((1,), (1,)), ((), ())), preferred_element_type=jnp.float32
+        )
+        out_ref[0] = picked.astype(out_ref.dtype)
 
 
 def gather_leaving(stiffness, pick_lo, pick_hi):
-    slots, rows_i, rows_j, blocks = stiffness.shape
-    width = pick_lo.shape[1]
-    out = jax.ShapeDtypeStruct((slots, rows_i, rows_j, width), stiffness.dtype)
+    slots, depth, blocks = stiffness.shape
+    width = pick_lo.shape[0]
+    out = jax.ShapeDtypeStruct((slots, width, depth), stiffness.dtype)
     return pl.pallas_call(
         gather_kernel,
         grid=(slots,),
         in_specs=[
-            pl.BlockSpec((1, rows_i, rows_j, blocks), lambda k: (k, 0, 0, 0)),
-            pl.BlockSpec((blocks, width), lambda k: (0, 0)),
-            pl.BlockSpec((blocks, width), lambda k: (0, 0)),
+            pl.BlockSpec((1, depth, blocks), lambda k: (k, 0, 0)),
+            pl.BlockSpec((width, blocks), lambda k: (0, 0)),
+            pl.BlockSpec((width, blocks), lambda k: (0, 0)),
         ],
         out_specs=[
-            pl.BlockSpec((1, rows_i, rows_j, width), lambda k: (k, 0, 0, 0)),
-            pl.BlockSpec((1, rows_i, rows_j, width), lambda k: (k, 0, 0, 0)),
+            pl.BlockSpec((1, width, depth), lambda k: (k, 0, 0)),
+            pl.BlockSpec((1, width, depth), lambda k: (k, 0, 0)),
         ],
         out_shape=[out, out],
     )(stiffness, pick_lo, pick_hi)
 
 
 def merge_kernel(s_ref, lo_ref, hi_ref, place_lo_ref, place_hi_ref, arrival_ref, out_ref):
-    rows, depth, blocks = s_ref.shape[1:]
-    width = lo_ref.shape[-1]
     placed = jnp.dot(
-        lo_ref[0].reshape(rows * depth, width), place_lo_ref[...],
-        preferred_element_type=jnp.float32,
-    ) + jnp.dot(
-        hi_ref[0].reshape(rows * depth, width), place_hi_ref[...],
-        preferred_element_type=jnp.float32,
-    )
-    placed = placed.reshape(rows, depth, blocks).astype(out_ref.dtype)
-    out_ref[0] = jnp.where(arrival_ref[...] > 0, placed, s_ref[0])
+        lo_ref[0].T, place_lo_ref[...], preferred_element_type=jnp.float32
+    ) + jnp.dot(hi_ref[0].T, place_hi_ref[...], preferred_element_type=jnp.float32)
+    out_ref[0] = jnp.where(arrival_ref[...] > 0, placed.astype(out_ref.dtype), s_ref[0])
 
 
 def merge_arrived(stiffness, arrived_lo, arrived_hi, place_lo, place_hi, arrival):
-    slots, rows_i, rows_j, blocks = stiffness.shape
-    width = arrived_lo.shape[-1]
+    slots, depth, blocks = stiffness.shape
+    width = arrived_lo.shape[1]
     return pl.pallas_call(
         merge_kernel,
         grid=(slots,),
         in_specs=[
-            pl.BlockSpec((1, rows_i, rows_j, blocks), lambda k: (k, 0, 0, 0)),
-            pl.BlockSpec((1, rows_i, rows_j, width), lambda k: (k, 0, 0, 0)),
-            pl.BlockSpec((1, rows_i, rows_j, width), lambda k: (k, 0, 0, 0)),
+            pl.BlockSpec((1, depth, blocks), lambda k: (k, 0, 0)),
+            pl.BlockSpec((1, width, depth), lambda k: (k, 0, 0)),
+            pl.BlockSpec((1, width, depth), lambda k: (k, 0, 0)),
             pl.BlockSpec((width, blocks), lambda k: (0, 0)),
             pl.BlockSpec((width, blocks), lambda k: (0, 0)),
             pl.BlockSpec((1, blocks), lambda k: (0, 0)),
         ],
-        out_specs=pl.BlockSpec((1, rows_i, rows_j, blocks), lambda k: (k, 0, 0, 0)),
+        out_specs=pl.BlockSpec((1, depth, blocks), lambda k: (k, 0, 0)),
         out_shape=jax.ShapeDtypeStruct(stiffness.shape, stiffness.dtype),
     )(stiffness, arrived_lo, arrived_hi, place_lo, place_hi, arrival)
 
@@ -143,9 +137,11 @@
     slots = stiffness_old.shape[0]
     lanes = jnp.arange(blocks, dtype=jnp.int32)
 
-    leave_lo = (lanes[:, None] == send_slot[0, 0][None, :]).astype(jnp.bfloat16)
-    leave_hi = (lanes[:, None] == send_slot[0, 1][None, :]).astype(jnp.bfloat16)
-    stiff_to_lower, stiff_to_higher = gather_leaving(stiffness_old, leave_lo, leave_hi)
+    slots, rows_i, rows_j, _ = stiffness_old.shape
+    stiff_flat = stiffness_old.reshape(slots, rows_i * rows_j, blocks)
+    leave_lo = (send_slot[0, 0][:, None] == lanes[None, :]).astype(jnp.bfloat16)
+    leave_hi = (send_slot[0, 1][:, None] == lanes[None, :]).astype(jnp.bfloat16)
+    stiff_to_lower, stiff_to_higher = gather_leaving(stiff_flat, leave_lo, leave_hi)
     stiff_lower, stiff_higher = neighbour_exchange("shaft", stiff_to_lower, stiff_to_higher)
 
     count_live = jnp.arange(capacity, dtype=jnp.int32)[None, :] < arrive_count[0][:, None]
@@ -153,13 +149,13 @@
     place_hi = (arrive_place[0, 1][:, None] == lanes[None, :]) & count_live[1][:, None]
     arrival = (jnp.any(place_lo, 0) | jnp.any(place_hi, 0)).astype(jnp.int32)[None, :]
     stiffness = merge_arrived(
-        stiffness_old,
+        stiff_flat,
         stiff_lower,
         stiff_higher,
         place_lo.astype(jnp.bfloat16),
         place_hi.astype(jnp.bfloat16),
         arrival,
-    )
+    ).reshape(stiffness_old.shape)
 
     outgoing = send_slot[0].reshape(-1)
     filled = count_live.reshape(-1)

time: 183 us -> 167 us (0.913)
  waiting for transfers between devices: 46.7 us -> 20.9 us
  other arithmetic: 21.9 us -> 39.9 us
  local copies, waits for them, and re-layouts: 33.6 us -> 16.3 us
  starting transfers between devices: 49.9 us -> 61.5 us
  Pallas kernels: 26.7 us -> 22.6 us
    ppermute x8, starting transfers between devices: 13 us -> 28.6 us  [padded_2(): after = lax.ppermute(first, axis, down)]
    reduce_sum x4 -> x8, other arithmetic: 15.3 us -> 30.3 us  [on_device(): jnp.sum(product, axis=(0, 2))]
    ppermute x8, waiting for transfers between devices: 32.3 us -> 18.1 us  [padded_2(): after = lax.ppermute(first, axis, down)]
    ppermute x8, waiting for transfers between devices: 14.5 us -> 0.6 us  [padded_2(): before = lax.ppermute(last, axis, up)]
    ppermute x2 -> x0, local copies, waits for them, and re-layouts: 11.9 us -> none  [the longest x1 5.98 us: neighbour_exchange(): from_lower = lax.ppermute(upper_bound, axis, up)]
    pallas_call x2 -> x0, local copies, waits for them, and re-layouts: 11.1 us -> none  [gather_leaving(): pl.pallas_call(gather_kernel, grid=(slots,), in_specs=[pl.BlockSpec((1, r...]
    pallas_call x2, Pallas kernels: 26.7 us -> 22.6 us  [the longest x1 12.9 us: merge_arrived(): pl.pallas_call(merge_kernel, grid=(slots,), in_specs=[pl.BlockSpec((1, de...]
    ppermute x2, starting transfers between devices: 11.7 us -> 7.66 us  [neighbour_exchange(): from_higher = lax.ppermute(lower_bound, axis, down)]
  transfers between devices with their start and end apart: 20 -> 20, of which waited for: 11 -> 11; matrix products, arithmetic and copies ran while one was open for 14% -> 12% of each run, Pallas kernels for 0% -> 6%
where the time goes in v4:
time: 167 us; the launch traced here: 166 us
  starting transfers between devices  61.5 us (37%)
  other arithmetic  39.9 us (24%)
  Pallas kernels  22.6 us (14%)
  waiting for transfers between devices  20.9 us (13%)
  local copies, waits for them, and re-layouts  16.3 us (10%)
  matrix products  3 us (2%)
    reduce_sum x8, other arithmetic, on_device(): jnp.sum(product, axis=(0, 2))  30.3 us
    ppermute x8, starting transfers between devices, padded_2(): after = lax.ppermute(first, axis, down)  28.6 us
    ppermute x8, starting transfers between devices, padded_2(): before = lax.ppermute(last, axis, up)  20.9 us
    ppermute x8, waiting for transfers between devices, padded_2(): after = lax.ppermute(first, axis, down)  18.1 us
    pallas_call x1, Pallas kernels, merge_arrived(): pl.pallas_call(merge_kernel, grid=(slots,), in_specs=[pl.BlockSpec((1, de...  12.9 us
    pallas_call x1, Pallas kernels, gather_leaving(): pl.pallas_call(gather_kernel, grid=(slots,), in_specs=[pl.BlockSpec((1, d...  9.73 us
    unnamed x52, local copies, waits for them, and re-layouts  8.14 us
    ppermute x2, starting transfers between devices, neighbour_exchange(): from_higher = lax.ppermute(lower_bound, axis, down)  7.66 us
  transfers between devices with their start and end apart: 20, of which 11 were waited for; matrix products, arithmetic and copies ran while one was open for 12% of the time, Pallas kernels for 6%

profile of v4, /device:TPU:96, one launch (start us, length us, event | category | flops | bytes accessed | tf_op | source)
XLA Modules:
  0.0 165.7 jit_solution(6813971369179973630)
XLA Ops:
  1.7 1.9 %collective-permute-start.2 = (bf16[64,1,1]{2,1,0:T(2,128)(2,1)S(1)}, bf16[64,1,1]{2,1,0:T(2,128)(2,1)S(1)}, u32[]{:S(2)}, u32[]{:S(2)}) collective-permute-start(bf16[64,1,1]{2,1,0:T(2,128)(2,1)S(1)} %get-tuple-element.32), channel_id=1, source_target_pairs={{0,4},{4,8},{8,12},{12,16},{16,20},{20,24},{24,28},{28,32},{32,36}... | collective-permute-start | bytes 392 | tf_op jit(solution)/shard_map/ppermute | solution.py:22
  3.7 5.8 %collective-permute-start.3 = (bf16[64,1,1]{2,1,0:T(2,128)(2,1)S(1)}, bf16[64,1,1]{2,1,0:T(2,128)(2,1)S(1)}, u32[]{:S(2)}, u32[]{:S(2)}) collective-permute-start(bf16[64,1,1]{2,1,0:T(2,128)(2,1)S(1)} %get-tuple-element.33), channel_id=1, source_target_pairs={{4,0},{8,4},{12,8},{16,12},{20,16},{24,20},{28,24},{32,28},{36,32}... | collective-permute-start | bytes 392 | tf_op jit(solution)/shard_map/ppermute | solution.py:23
  15.8 1.9 %collective-permute-start.7 = (f32[96,32]{0,1:T(8,128)S(1)}, f32[96,32]{0,1:T(8,128)S(1)}, u32[]{:S(2)}, u32[]{:S(2)}) collective-permute-start(f32[96,32]{0,1:T(8,128)S(1)} %get-tuple-element.28), channel_id=1, source_target_pairs={{4,0},{8,4},{12,8},{16,12},{20,16},{24,20},{28,24},{32,28},{36,32}... | collective-permute-start | bytes 36872 | tf_op jit(solution)/shard_map/ppermute | solution.py:33
  17.7 2.4 %collective-permute-start.6 = (f32[96,32]{0,1:T(8,128)S(1)}, f32[96,32]{0,1:T(8,128)S(1)}, u32[]{:S(2)}, u32[]{:S(2)}) collective-permute-start(f32[96,32]{0,1:T(8,128)S(1)} %get-tuple-element.29), channel_id=1, source_target_pairs={{0,4},{4,8},{8,12},{12,16},{16,20},{20,24},{24,28},{28,32},{32,36}... | collective-permute-start | bytes 36872 | tf_op jit(solution)/shard_map/ppermute | solution.py:32
  21.6 9.7 %shard_map.151 = (bf16[5,32,4096]{2,1,0:T(8,128)(2,1)}, bf16[5,32,4096]{2,1,0:T(8,128)(2,1)}) custom-call(bf16[5,4096,256]{2,1,0:T(8,128)(2,1)} %bitcast.245, bf16[32,256]{1,0:T(8,128)(2,1)} %get-tuple-element.91.lo_ref, bf16[32,256]{1,0:T(8,128)(2,1)} %get-tuple-element.92.hi_ref), custom_call_target="tpu_custom_call" | custom-call | tf_op jit(solution)/shard_map/pallas_call | solution.py:50
  37.5 5.7 %collective-permute-start.1 = (bf16[5,32,4096]{2,1,0:T(8,128)(2,1)}, bf16[5,32,4096]{2,1,0:T(8,128)(2,1)S(1)}, u32[]{:S(2)}, u32[]{:S(2)}) collective-permute-start(bf16[5,32,4096]{2,1,0:T(8,128)(2,1)} %get-tuple-element.8), channel_id=1, source_target_pairs={{4,0},{8,4},{12,8},{16,12},{20,16},{24,20},{28,24},{32,28},{36,32}... | collective-permute-start | bytes 3932168 | tf_op jit(solution)/shard_map/ppermute | solution.py:33
  44.1 3.4 %collective-permute-start.5 = (bf16[64,1,258]{2,1,0:T(2,128)(2,1)}, bf16[64,1,258]{2,1,0:T(2,128)(2,1)S(1)}, u32[]{:S(2)}, u32[]{:S(2)}) collective-permute-start(bf16[64,1,258]{2,1,0:T(2,128)(2,1)} %pad_maximum_fusion.2), channel_id=1, source_target_pairs={{0,1},{1,2},{2,3},{4,5},{5,6},{6,7},{8,9},{9,10},{10,11},{12,13},{... | collective-permute-start | bytes 99080 | tf_op jit(solution)/shard_map/ppermute | solution.py:22
  52.6 2.6 %collective-permute-done.4 = bf16[64,1,258]{2,1,0:T(2,128)(2,1)S(1)} collective-permute-done((bf16[64,1,258]{2,1,0:T(2,128)(2,1)}, bf16[64,1,258]{2,1,0:T(2,128)(2,1)S(1)}, u32[]{:S(2)}, u32[]{:S(2)}) %collective-permute-start.4) | collective-permute-done | bytes 33056 | tf_op jit(solution)/shard_map/ppermute | solution.py:23
  56.5 2.2 %collective-permute-done.1.hi_ref = bf16[5,32,4096]{2,1,0:T(8,128)(2,1)S(1)} collective-permute-done((bf16[5,32,4096]{2,1,0:T(8,128)(2,1)}, bf16[5,32,4096]{2,1,0:T(8,128)(2,1)S(1)}, u32[]{:S(2)}, u32[]{:S(2)}) %collective-permute-start.1) | collective-permute-done | bytes 1310752 | tf_op jit(solution)/shard_map/ppermute | solution.py:33
  59.8 12.9 %shard_map.152 = bf16[5,4096,256]{2,1,0:T(8,128)(2,1)} custom-call(bf16[5,4096,256]{2,1,0:T(8,128)(2,1)} %bitcast.246, bf16[5,32,4096]{2,1,0:T(8,128)(2,1)} %copy-done.1, bf16[5,32,4096]{2,1,0:T(8,128)(2,1)} %copy-done.2, bf16[32,256]{1,0:T(8,128)(2,1)} %get-tuple-element.78.place_lo_ref, bf16[32,256]{1,0:T(8,128)(2,1)} %get-tuple-element.93.place_hi_ref, ...), custom_call_target="tpu_custom_call" | custom-call | tf_op jit(solution)/shard_map/pallas_call | solution.py:76
  72.7 7.1 %fusion = f32[4096,256]{1,0:T(8,128)S(1)} fusion(bf16[5,4096,256]{2,1,0:T(8,128)(2,1)} %shard_map.152, f32[5,64,256]{2,1,0:T(8,128)S(1)} %select_convert_fusion.3), kind=kLoop, calls=%fused_computation.9 | loop fusion | flops 14680064 | bytes 15007744 | tf_op jit(solution)/shard_map/reduce_sum | solution.py:193
  82.7 5.8 %collective-permute-start.9 = (bf16[64,1,1]{2,0,1:T(8,128)(2,1)S(1)}, bf16[64,1,1]{2,0,1:T(8,128)(2,1)S(1)}, u32[]{:S(2)}, u32[]{:S(2)}) collective-permute-start(bf16[64,1,1]{2,0,1:T(8,128)(2,1)S(1)} %get-tuple-element.65), channel_id=1, source_target_pairs={{4,0},{8,4},{12,8},{16,12},{20,16},{24,20},{28,24},{32,28},{36,32}... | collective-permute-start | bytes 392 | tf_op jit(solution)/shard_map/ppermute | solution.py:23
  90.1 3.4 %collective-permute-start.11 = (bf16[64,1,258]{2,0,1:T(8,128)(2,1)S(1)}, bf16[64,1,258]{2,0,1:T(8,128)(2,1)S(1)}, u32[]{:S(2)}, u32[]{:S(2)}) collective-permute-start(bf16[64,1,258]{2,0,1:T(8,128)(2,1)S(1)} %pad_maximum_fusion.5), channel_id=1, source_target_pairs={{0,1},{1,2},{2,3},{4,5},{5,6},{6,7},{8,9},{9,10},{10,11},{12,13},{... | collective-permute-start | bytes 99080 | tf_op jit(solution)/shard_map/ppermute | solution.py:22
  95.3 4.2 %collective-permute-done.10 = bf16[64,1,258]{2,0,1:T(8,128)(2,1)S(1)} collective-permute-done((bf16[64,1,258]{2,0,1:T(8,128)(2,1)S(1)}, bf16[64,1,258]{2,0,1:T(8,128)(2,1)S(1)}, u32[]{:S(2)}, u32[]{:S(2)}) %collective-permute-start.10) | collective-permute-done | bytes 33056 | tf_op jit(solution)/shard_map/ppermute | solution.py:23
  100.4 7.0 %fusion.1 = f32[4096,256]{1,0:T(8,128)S(1)} fusion(bf16[5,4096,256]{2,1,0:T(8,128)(2,1)} %shard_map.152, f32[5,64,256]{2,1,0:T(8,128)S(1)} %select_convert_fusion.2), kind=kLoop, calls=%fused_computation.10 | loop fusion | flops 14680064 | bytes 15007744 | tf_op jit(solution)/shard_map/reduce_sum | solution.py:193
  108.3 1.9 %collective-permute-start.12 = (bf16[64,1,1]{2,0,1:T(8,128)(2,1)S(1)}, bf16[64,1,1]{2,0,1:T(8,128)(2,1)S(1)}, u32[]{:S(2)}, u32[]{:S(2)}) collective-permute-start(bf16[64,1,1]{2,0,1:T(8,128)(2,1)S(1)} %get-tuple-element.58), channel_id=1, source_target_pairs={{0,4},{4,8},{8,12},{12,16},{16,20},{20,24},{24,28},{28,32},{32,36}... | collective-permute-start | bytes 392 | tf_op jit(solution)/shard_map/ppermute | solution.py:22
  110.3 5.8 %collective-permute-start.13 = (bf16[64,1,1]{2,0,1:T(8,128)(2,1)S(1)}, bf16[64,1,1]{2,0,1:T(8,128)(2,1)S(1)}, u32[]{:S(2)}, u32[]{:S(2)}) collective-permute-start(bf16[64,1,1]{2,0,1:T(8,128)(2,1)S(1)} %get-tuple-element.59), channel_id=1, source_target_pairs={{4,0},{8,4},{12,8},{16,12},{20,16},{24,20},{28,24},{32,28},{36,32}... | collective-permute-start | bytes 392 | tf_op jit(solution)/shard_map/ppermute | solution.py:23
  117.5 3.4 %collective-permute-start.15 = (bf16[64,1,258]{2,0,1:T(8,128)(2,1)S(1)}, bf16[64,1,258]{2,0,1:T(8,128)(2,1)S(1)}, u32[]{:S(2)}, u32[]{:S(2)}) collective-permute-start(bf16[64,1,258]{2,0,1:T(8,128)(2,1)S(1)} %pad_maximum_fusion.6), channel_id=1, source_target_pairs={{0,1},{1,2},{2,3},{4,5},{5,6},{6,7},{8,9},{9,10},{10,11},{12,13},{... | collective-permute-start | bytes 99080 | tf_op jit(solution)/shard_map/ppermute | solution.py:22
  122.8 4.2 %collective-permute-done.14 = bf16[64,1,258]{2,0,1:T(8,128)(2,1)S(1)} collective-permute-done((bf16[64,1,258]{2,0,1:T(8,128)(2,1)S(1)}, bf16[64,1,258]{2,0,1:T(8,128)(2,1)S(1)}, u32[]{:S(2)}, u32[]{:S(2)}) %collective-permute-start.14) | collective-permute-done | bytes 33056 | tf_op jit(solution)/shard_map/ppermute | solution.py:23
  127.9 7.0 %fusion.2 = f32[4096,256]{1,0:T(8,128)S(1)} fusion(bf16[5,4096,256]{2,1,0:T(8,128)(2,1)} %shard_map.152, f32[5,64,256]{2,1,0:T(8,128)S(1)} %select_convert_fusion.1), kind=kLoop, calls=%fused_computation.11 | loop fusion | flops 14680064 | bytes 15007744 | tf_op jit(solution)/shard_map/reduce_sum | solution.py:193
  137.7 5.8 %collective-permute-start.17 = (bf16[64,1,1]{2,0,1:T(8,128)(2,1)S(1)}, bf16[64,1,1]{2,0,1:T(8,128)(2,1)S(1)}, u32[]{:S(2)}, u32[]{:S(2)}) collective-permute-start(bf16[64,1,1]{2,0,1:T(8,128)(2,1)S(1)} %get-tuple-element.55), channel_id=1, source_target_pairs={{4,0},{8,4},{12,8},{16,12},{20,16},{24,20},{28,24},{32,28},{36,32}... | collective-permute-start | bytes 392 | tf_op jit(solution)/shard_map/ppermute | solution.py:23
  145.0 3.1 %collective-permute-start.19 = (bf16[64,1,258]{2,0,1:T(8,128)(2,1)S(1)}, bf16[64,1,258]{2,0,1:T(8,128)(2,1)S(1)}, u32[]{:S(2)}, u32[]{:S(2)}) collective-permute-start(bf16[64,1,258]{2,0,1:T(8,128)(2,1)S(1)} %pad_maximum_fusion.7), channel_id=1, source_target_pairs={{0,1},{1,2},{2,3},{4,5},{5,6},{6,7},{8,9},{9,10},{10,11},{12,13},{... | collective-permute-start | bytes 99080 | tf_op jit(solution)/shard_map/ppermute | solution.py:22
  149.9 4.2 %collective-permute-done.18 = bf16[64,1,258]{2,0,1:T(8,128)(2,1)S(1)} collective-permute-done((bf16[64,1,258]{2,0,1:T(8,128)(2,1)S(1)}, bf16[64,1,258]{2,0,1:T(8,128)(2,1)S(1)}, u32[]{:S(2)}, u32[]{:S(2)}) %collective-permute-start.18) | collective-permute-done | bytes 33056 | tf_op jit(solution)/shard_map/ppermute | solution.py:23
  155.0 7.0 %fusion.3 = f32[4096,256]{1,0:T(8,128)S(1)} fusion(bf16[5,4096,256]{2,1,0:T(8,128)(2,1)} %shard_map.152, f32[5,64,256]{2,1,0:T(8,128)S(1)} %select_convert_fusion), kind=kLoop, calls=%fused_computation.12 | loop fusion | flops 14680064 | bytes 15007744 | tf_op jit(solution)/shard_map/reduce_sum | solution.py:193
  (144 shorter events, 46.1 us)
Async XLA Ops:
  0.6 79.8 %copy-start = (f32[48,64]{1,0:T(8,128)S(1)}, f32[48,64]{1,0:T(8,128)}, u32[]{:S(2)}) copy-start(f32[48,64]{1,0:T(8,128)} %param.26) | copy-start | bytes 36868
  0.7 34.4 %copy-start.16 = (s32[1,256]{1,0:T(1,128)S(1)}, s32[1,256]{1,0:T(1,128)}, u32[]{:S(2)}) copy-start(s32[1,256]{1,0:T(1,128)} %param.22) | copy-start | bytes 3076
  0.7 34.3 %copy-start.15 = (s32[5,1,256]{2,1,0:T(1,128)S(1)}, s32[5,1,256]{2,1,0:T(1,128)}, u32[]{:S(2)}) copy-start(s32[5,1,256]{2,1,0:T(1,128)} %param.21) | copy-start | bytes 15364
  1.7 35.7 %collective-permute-start.2 = (bf16[64,1,1]{2,1,0:T(2,128)(2,1)S(1)}, bf16[64,1,1]{2,1,0:T(2,128)(2,1)S(1)}, u32[]{:S(2)}, u32[]{:S(2)}) collective-permute-start(bf16[64,1,1]{2,1,0:T(2,128)(2,1)S(1)} %get-tuple-element.32), channel_id=1, source_target_pairs={{0,4},{4,8},{8,12},{12,16},{16,20},{20,24},{24,28},{28,32},{32,36}... | collective-permute-start | bytes 392 | tf_op jit(solution)/shard_map/ppermute | solution.py:22
  3.7 39.6 %collective-permute-start.3 = (bf16[64,1,1]{2,1,0:T(2,128)(2,1)S(1)}, bf16[64,1,1]{2,1,0:T(2,128)(2,1)S(1)}, u32[]{:S(2)}, u32[]{:S(2)}) collective-permute-start(bf16[64,1,1]{2,1,0:T(2,128)(2,1)S(1)} %get-tuple-element.33), channel_id=1, source_target_pairs={{4,0},{8,4},{12,8},{16,12},{20,16},{24,20},{28,24},{32,28},{36,32}... | collective-permute-start | bytes 392 | tf_op jit(solution)/shard_map/ppermute | solution.py:23
  14.4 36.3 %copy-start.14 = (s32[1024]{0:T(1024)}, s32[1024]{0:T(1024)S(1)}, u32[]{:S(2)}) copy-start(s32[1024]{0:T(1024)S(1)} %get-tuple-element.111) | copy-start | bytes 12292
  15.8 34.0 %collective-permute-start.7 = (f32[96,32]{0,1:T(8,128)S(1)}, f32[96,32]{0,1:T(8,128)S(1)}, u32[]{:S(2)}, u32[]{:S(2)}) collective-permute-start(f32[96,32]{0,1:T(8,128)S(1)} %get-tuple-element.28), channel_id=1, source_target_pairs={{4,0},{8,4},{12,8},{16,12},{20,16},{24,20},{28,24},{32,28},{36,32}... | collective-permute-start | bytes 36872 | tf_op jit(solution)/shard_map/ppermute | solution.py:33
  17.7 30.8 %collective-permute-start.6 = (f32[96,32]{0,1:T(8,128)S(1)}, f32[96,32]{0,1:T(8,128)S(1)}, u32[]{:S(2)}, u32[]{:S(2)}) collective-permute-start(f32[96,32]{0,1:T(8,128)S(1)} %get-tuple-element.29), channel_id=1, source_target_pairs={{0,4},{4,8},{8,12},{12,16},{16,20},{20,24},{24,28},{28,32},{32,36}... | collective-permute-start | bytes 36872 | tf_op jit(solution)/shard_map/ppermute | solution.py:32
  31.3 25.2 %collective-permute-start = (bf16[5,32,4096]{2,1,0:T(8,128)(2,1)}, bf16[5,32,4096]{2,1,0:T(8,128)(2,1)S(1)}, u32[]{:S(2)}, u32[]{:S(2)}) collective-permute-start(bf16[5,32,4096]{2,1,0:T(8,128)(2,1)} %get-tuple-element.7), channel_id=1, source_target_pairs={{0,4},{4,8},{8,12},{12,16},{16,20},{20,24},{24,28},{28,32},{32,36}... | collective-permute-start | bytes 3932168 | tf_op jit(solution)/shard_map/ppermute | solution.py:32
  37.5 21.2 %collective-permute-start.1 = (bf16[5,32,4096]{2,1,0:T(8,128)(2,1)}, bf16[5,32,4096]{2,1,0:T(8,128)(2,1)S(1)}, u32[]{:S(2)}, u32[]{:S(2)}) collective-permute-start(bf16[5,32,4096]{2,1,0:T(8,128)(2,1)} %get-tuple-element.8), channel_id=1, source_target_pairs={{4,0},{8,4},{12,8},{16,12},{20,16},{24,20},{28,24},{32,28},{36,32}... | collective-permute-start | bytes 3932168 | tf_op jit(solution)/shard_map/ppermute | solution.py:33
  44.1 8.2 %collective-permute-start.5 = (bf16[64,1,258]{2,1,0:T(2,128)(2,1)}, bf16[64,1,258]{2,1,0:T(2,128)(2,1)S(1)}, u32[]{:S(2)}, u32[]{:S(2)}) collective-permute-start(bf16[64,1,258]{2,1,0:T(2,128)(2,1)} %pad_maximum_fusion.2), channel_id=1, source_target_pairs={{0,1},{1,2},{2,3},{4,5},{5,6},{6,7},{8,9},{9,10},{10,11},{12,13},{... | collective-permute-start | bytes 99080 | tf_op jit(solution)/shard_map/ppermute | solution.py:22
  48.5 6.7 %collective-permute-start.4 = (bf16[64,1,258]{2,1,0:T(2,128)(2,1)}, bf16[64,1,258]{2,1,0:T(2,128)(2,1)S(1)}, u32[]{:S(2)}, u32[]{:S(2)}) collective-permute-start(bf16[64,1,258]{2,1,0:T(2,128)(2,1)} %pad_maximum_fusion.2), channel_id=1, source_target_pairs={{1,0},{2,1},{3,2},{5,4},{6,5},{7,6},{9,8},{10,9},{11,10},{13,12},{... | collective-permute-start | bytes 99080 | tf_op jit(solution)/shard_map/ppermute | solution.py:23
  80.8 7.9 %collective-permute-start.8 = (bf16[64,1,1]{2,0,1:T(8,128)(2,1)S(1)}, bf16[64,1,1]{2,0,1:T(8,128)(2,1)S(1)}, u32[]{:S(2)}, u32[]{:S(2)}) collective-permute-start(bf16[64,1,1]{2,0,1:T(8,128)(2,1)S(1)} %get-tuple-element.64), channel_id=1, source_target_pairs={{0,4},{4,8},{8,12},{12,16},{16,20},{20,24},{24,28},{28,32},{32,36}... | collective-permute-start | bytes 392 | tf_op jit(solution)/shard_map/ppermute | solution.py:22
  82.7 7.2 %collective-permute-start.9 = (bf16[64,1,1]{2,0,1:T(8,128)(2,1)S(1)}, bf16[64,1,1]{2,0,1:T(8,128)(2,1)S(1)}, u32[]{:S(2)}, u32[]{:S(2)}) collective-permute-start(bf16[64,1,1]{2,0,1:T(8,128)(2,1)S(1)} %get-tuple-element.65), channel_id=1, source_target_pairs={{4,0},{8,4},{12,8},{16,12},{20,16},{24,20},{28,24},{32,28},{36,32}... | collective-permute-start | bytes 392 | tf_op jit(solution)/shard_map/ppermute | solution.py:23
  90.1 5.1 %collective-permute-start.11 = (bf16[64,1,258]{2,0,1:T(8,128)(2,1)S(1)}, bf16[64,1,258]{2,0,1:T(8,128)(2,1)S(1)}, u32[]{:S(2)}, u32[]{:S(2)}) collective-permute-start(bf16[64,1,258]{2,0,1:T(8,128)(2,1)S(1)} %pad_maximum_fusion.5), channel_id=1, source_target_pairs={{0,1},{1,2},{2,3},{4,5},{5,6},{6,7},{8,9},{9,10},{10,11},{12,13},{... | collective-permute-start | bytes 99080 | tf_op jit(solution)/shard_map/ppermute | solution.py:22
  93.5 6.0 %collective-permute-start.10 = (bf16[64,1,258]{2,0,1:T(8,128)(2,1)S(1)}, bf16[64,1,258]{2,0,1:T(8,128)(2,1)S(1)}, u32[]{:S(2)}, u32[]{:S(2)}) collective-permute-start(bf16[64,1,258]{2,0,1:T(8,128)(2,1)S(1)} %pad_maximum_fusion.5), channel_id=1, source_target_pairs={{1,0},{2,1},{3,2},{5,4},{6,5},{7,6},{9,8},{10,9},{11,10},{13,12},{... | collective-permute-start | bytes 99080 | tf_op jit(solution)/shard_map/ppermute | solution.py:23
  108.3 8.5 %collective-permute-start.12 = (bf16[64,1,1]{2,0,1:T(8,128)(2,1)S(1)}, bf16[64,1,1]{2,0,1:T(8,128)(2,1)S(1)}, u32[]{:S(2)}, u32[]{:S(2)}) collective-permute-start(bf16[64,1,1]{2,0,1:T(8,128)(2,1)S(1)} %get-tuple-element.58), channel_id=1, source_target_pairs={{0,4},{4,8},{8,12},{12,16},{16,20},{20,24},{24,28},{28,32},{32,36}... | collective-permute-start | bytes 392 | tf_op jit(solution)/shard_map/ppermute | solution.py:22
  110.3 7.2 %collective-permute-start.13 = (bf16[64,1,1]{2,0,1:T(8,128)(2,1)S(1)}, bf16[64,1,1]{2,0,1:T(8,128)(2,1)S(1)}, u32[]{:S(2)}, u32[]{:S(2)}) collective-permute-start(bf16[64,1,1]{2,0,1:T(8,128)(2,1)S(1)} %get-tuple-element.59), channel_id=1, source_target_pairs={{4,0},{8,4},{12,8},{16,12},{20,16},{24,20},{28,24},{32,28},{36,32}... | collective-permute-start | bytes 392 | tf_op jit(solution)/shard_map/ppermute | solution.py:23
  117.5 5.1 %collective-permute-start.15 = (bf16[64,1,258]{2,0,1:T(8,128)(2,1)S(1)}, bf16[64,1,258]{2,0,1:T(8,128)(2,1)S(1)}, u32[]{:S(2)}, u32[]{:S(2)}) collective-permute-start(bf16[64,1,258]{2,0,1:T(8,128)(2,1)S(1)} %pad_maximum_fusion.6), channel_id=1, source_target_pairs={{0,1},{1,2},{2,3},{4,5},{5,6},{6,7},{8,9},{9,10},{10,11},{12,13},{... | collective-permute-start | bytes 99080 | tf_op jit(solution)/shard_map/ppermute | solution.py:22
  120.9 6.0 %collective-permute-start.14 = (bf16[64,1,258]{2,0,1:T(8,128)(2,1)S(1)}, bf16[64,1,258]{2,0,1:T(8,128)(2,1)S(1)}, u32[]{:S(2)}, u32[]{:S(2)}) collective-permute-start(bf16[64,1,258]{2,0,1:T(8,128)(2,1)S(1)} %pad_maximum_fusion.6), channel_id=1, source_target_pairs={{1,0},{2,1},{3,2},{5,4},{6,5},{7,6},{9,8},{10,9},{11,10},{13,12},{... | collective-permute-start | bytes 99080 | tf_op jit(solution)/shard_map/ppermute | solution.py:23
  135.8 7.9 %collective-permute-start.16 = (bf16[64,1,1]{2,0,1:T(8,128)(2,1)S(1)}, bf16[64,1,1]{2,0,1:T(8,128)(2,1)S(1)}, u32[]{:S(2)}, u32[]{:S(2)}) collective-permute-start(bf16[64,1,1]{2,0,1:T(8,128)(2,1)S(1)} %get-tuple-element.54), channel_id=1, source_target_pairs={{0,4},{4,8},{8,12},{12,16},{16,20},{20,24},{24,28},{28,32},{32,36}... | collective-permute-start | bytes 392 | tf_op jit(solution)/shard_map/ppermute | solution.py:22
  137.7 7.2 %collective-permute-start.17 = (bf16[64,1,1]{2,0,1:T(8,128)(2,1)S(1)}, bf16[64,1,1]{2,0,1:T(8,128)(2,1)S(1)}, u32[]{:S(2)}, u32[]{:S(2)}) collective-permute-start(bf16[64,1,1]{2,0,1:T(8,128)(2,1)S(1)} %get-tuple-element.55), channel_id=1, source_target_pairs={{4,0},{8,4},{12,8},{16,12},{20,16},{24,20},{28,24},{32,28},{36,32}... | collective-permute-start | bytes 392 | tf_op jit(solution)/shard_map/ppermute | solution.py:23
  145.0 4.8 %collective-permute-start.19 = (bf16[64,1,258]{2,0,1:T(8,128)(2,1)S(1)}, bf16[64,1,258]{2,0,1:T(8,128)(2,1)S(1)}, u32[]{:S(2)}, u32[]{:S(2)}) collective-permute-start(bf16[64,1,258]{2,0,1:T(8,128)(2,1)S(1)} %pad_maximum_fusion.7), channel_id=1, source_target_pairs={{0,1},{1,2},{2,3},{4,5},{5,6},{6,7},{8,9},{9,10},{10,11},{12,13},{... | collective-permute-start | bytes 99080 | tf_op jit(solution)/shard_map/ppermute | solution.py:22
  148.1 6.0 %collective-permute-start.18 = (bf16[64,1,258]{2,0,1:T(8,128)(2,1)S(1)}, bf16[64,1,258]{2,0,1:T(8,128)(2,1)S(1)}, u32[]{:S(2)}, u32[]{:S(2)}) collective-permute-start(bf16[64,1,258]{2,0,1:T(8,128)(2,1)S(1)} %pad_maximum_fusion.7), channel_id=1, source_target_pairs={{1,0},{2,1},{3,2},{5,4},{6,5},{7,6},{9,8},{10,9},{11,10},{13,12},{... | collective-permute-start | bytes 99080 | tf_op jit(solution)/shard_map/ppermute | solution.py:23
  (14 other events, 216.4 us)

commit v5 on v4

--- a/solution.py
+++ b/solution.py
@@ -67,24 +67,26 @@
     placed = jnp.dot(
         lo_ref[0].T, place_lo_ref[...], preferred_element_type=jnp.float32
     ) + jnp.dot(hi_ref[0].T, place_hi_ref[...], preferred_element_type=jnp.float32)
-    out_ref[0] = jnp.where(arrival_ref[...] > 0, placed.astype(out_ref.dtype), s_ref[0])
+    placed = placed.astype(out_ref.dtype).reshape(s_ref.shape[1:])
+    out_ref[0] = jnp.where(arrival_ref[...] > 0, placed, s_ref[0])
 
 
 def merge_arrived(stiffness, arrived_lo, arrived_hi, place_lo, place_hi, arrival):
-    slots, depth, blocks = stiffness.shape
+    slots, rows_i, rows_j, blocks = stiffness.shape
+    depth = rows_i * rows_j
     width = arrived_lo.shape[1]
     return pl.pallas_call(
         merge_kernel,
         grid=(slots,),
         in_specs=[
-            pl.BlockSpec((1, depth, blocks), lambda k: (k, 0, 0)),
+            pl.BlockSpec((1, rows_i, rows_j, blocks), lambda k: (k, 0, 0, 0)),
             pl.BlockSpec((1, width, depth), lambda k: (k, 0, 0)),
             pl.BlockSpec((1, width, depth), lambda k: (k, 0, 0)),
             pl.BlockSpec((width, blocks), lambda k: (0, 0)),
             pl.BlockSpec((width, blocks), lambda k: (0, 0)),
             pl.BlockSpec((1, blocks), lambda k: (0, 0)),
         ],
-        out_specs=pl.BlockSpec((1, depth, blocks), lambda k: (k, 0, 0)),
+        out_specs=pl.BlockSpec((1, rows_i, rows_j, blocks), lambda k: (k, 0, 0, 0)),
         out_shape=jax.ShapeDtypeStruct(stiffness.shape, stiffness.dtype),
     )(stiffness, arrived_lo, arrived_hi, place_lo, place_hi, arrival)
 
@@ -149,13 +151,13 @@
     place_hi = (arrive_place[0, 1][:, None] == lanes[None, :]) & count_live[1][:, None]
     arrival = (jnp.any(place_lo, 0) | jnp.any(place_hi, 0)).astype(jnp.int32)[None, :]
     stiffness = merge_arrived(
-        stiff_flat,
+        stiffness_old,
         stiff_lower,
         stiff_higher,
         place_lo.astype(jnp.bfloat16),
         place_hi.astype(jnp.bfloat16),
         arrival,
-    ).reshape(stiffness_old.shape)
+    )
 
     outgoing = send_slot[0].reshape(-1)
     filled = count_live.reshape(-1)

time: 167 us -> 144 us (0.86)
  other arithmetic: 39.9 us -> 21.3 us
  starting transfers between devices: 61.5 us -> 49.9 us
  waiting for transfers between devices: 20.9 us -> 31.2 us
  local copies, waits for them, and re-layouts: 16.3 us -> 14.3 us
    ppermute x8, starting transfers between devices: 28.6 us -> 13 us  [padded_2(): after = lax.ppermute(first, axis, down)]
    reduce_sum x8 -> x4, other arithmetic: 30.3 us -> 15.3 us  [on_device(): jnp.sum(product, axis=(0, 2))]
    ppermute x8, waiting for transfers between devices: 0.6 us -> 14.5 us  [padded_2(): before = lax.ppermute(last, axis, up)]
    ppermute x2, starting transfers between devices: 7.66 us -> 11.7 us  [neighbour_exchange(): from_higher = lax.ppermute(lower_bound, axis, down)]
    ppermute x2, waiting for transfers between devices: 2.19 us -> 0.01 us  [neighbour_exchange(): from_higher = lax.ppermute(lower_bound, axis, down)]
    convert_element_type x4, other arithmetic: 3.4 us -> 1.32 us  [on_device(): neighbours.astype(jnp.float32)[:, None, :, :]]
    unnamed x52 -> x64, local copies, waits for them, and re-layouts: 8.14 us -> 7.57 us
  transfers between devices with their start and end apart: 20 -> 20, of which waited for: 11 -> 11; matrix products, arithmetic and copies ran while one was open for 12% -> 10% of each run, Pallas kernels for 6% -> 0%
where the time goes in v5:
time: 144 us; the launch traced here: 143 us
  starting transfers between devices  49.9 us (35%)
  waiting for transfers between devices  31.2 us (22%)
  Pallas kernels  22.5 us (16%)
  other arithmetic  21.3 us (15%)
  local copies, waits for them, and re-layouts  14.3 us (10%)
  matrix products  1.85 us (1%)
  between operations  1.5 us (1%)
    ppermute x8, starting transfers between devices, padded_2(): before = lax.ppermute(last, axis, up)  21.4 us
    ppermute x8, waiting for transfers between devices, padded_2(): after = lax.ppermute(first, axis, down)  16.7 us
    reduce_sum x4, other arithmetic, on_device(): jnp.sum(product, axis=(0, 2))  15.3 us
    ppermute x8, waiting for transfers between devices, padded_2(): before = lax.ppermute(last, axis, up)  14.5 us
    ppermute x8, starting transfers between devices, padded_2(): after = lax.ppermute(first, axis, down)  13 us
    pallas_call x1, Pallas kernels, merge_arrived(): pl.pallas_call(merge_kernel, grid=(slots,), in_specs=[pl.BlockSpec((1, ro...  12.9 us
    ppermute x2, starting transfers between devices, neighbour_exchange(): from_higher = lax.ppermute(lower_bound, axis, down)  11.7 us
    pallas_call x1, Pallas kernels, gather_leaving(): pl.pallas_call(gather_kernel, grid=(slots,), in_specs=[pl.BlockSpec((1, d...  9.69 us
  transfers between devices with their start and end apart: 20, of which 11 were waited for; matrix products, arithmetic and copies ran while one was open for 10% of the time, Pallas kernels for 0%

profile of v5, /device:TPU:96, one launch (start us, length us, event | category | flops | bytes accessed | tf_op | source)
XLA Modules:
  0.0 142.6 jit_solution(16772808084890952408)
XLA Ops:
  2.2 9.7 %shard_map.151 = (bf16[5,32,4096]{2,1,0:T(8,128)(2,1)}, bf16[5,32,4096]{2,1,0:T(8,128)(2,1)}) custom-call(bf16[5,4096,256]{2,1,0:T(8,128)(2,1)} %bitcast.228, bf16[32,256]{1,0:T(8,128)(2,1)} %get-tuple-element.91.lo_ref, bf16[32,256]{1,0:T(8,128)(2,1)} %get-tuple-element.92.hi_ref), custom_call_target="tpu_custom_call" | custom-call | tf_op jit(solution)/shard_map/pallas_call | solution.py:50
  13.8 5.8 %collective-permute-start.1 = (bf16[5,32,4096]{2,1,0:T(8,128)(2,1)}, bf16[5,32,4096]{2,1,0:T(8,128)(2,1)S(1)}, u32[]{:S(2)}, u32[]{:S(2)}) collective-permute-start(bf16[5,32,4096]{2,1,0:T(8,128)(2,1)} %get-tuple-element.8), channel_id=1, source_target_pairs={{4,0},{8,4},{12,8},{16,12},{20,16},{24,20},{28,24},{32,28},{36,32}... | collective-permute-start | bytes 3932168 | tf_op jit(solution)/shard_map/ppermute | solution.py:33
  19.7 1.9 %collective-permute-start.3 = (bf16[64,1,1]{2,1,0:T(2,128)(2,1)S(1)}, bf16[64,1,1]{2,1,0:T(2,128)(2,1)S(1)}, u32[]{:S(2)}, u32[]{:S(2)}) collective-permute-start(bf16[64,1,1]{2,1,0:T(2,128)(2,1)S(1)} %get-tuple-element.33), channel_id=1, source_target_pairs={{4,0},{8,4},{12,8},{16,12},{20,16},{24,20},{28,24},{32,28},{36,32}... | collective-permute-start | bytes 392 | tf_op jit(solution)/shard_map/ppermute | solution.py:23
  21.6 2.4 %collective-permute-start.2 = (bf16[64,1,1]{2,1,0:T(2,128)(2,1)S(1)}, bf16[64,1,1]{2,1,0:T(2,128)(2,1)S(1)}, u32[]{:S(2)}, u32[]{:S(2)}) collective-permute-start(bf16[64,1,1]{2,1,0:T(2,128)(2,1)S(1)} %get-tuple-element.32), channel_id=1, source_target_pairs={{0,4},{4,8},{8,12},{12,16},{16,20},{20,24},{24,28},{28,32},{32,36}... | collective-permute-start | bytes 392 | tf_op jit(solution)/shard_map/ppermute | solution.py:22
  35.2 5.9 %collective-permute-start.7 = (f32[96,32]{0,1:T(8,128)S(1)}, f32[96,32]{0,1:T(8,128)S(1)}, u32[]{:S(2)}, u32[]{:S(2)}) collective-permute-start(f32[96,32]{0,1:T(8,128)S(1)} %get-tuple-element.28), channel_id=1, source_target_pairs={{4,0},{8,4},{12,8},{16,12},{20,16},{24,20},{28,24},{32,28},{36,32}... | collective-permute-start | bytes 36872 | tf_op jit(solution)/shard_map/ppermute | solution.py:33
  42.0 3.4 %collective-permute-start.5 = (bf16[64,1,258]{2,1,0:T(2,128)(2,1)}, bf16[64,1,258]{2,1,0:T(2,128)(2,1)S(1)}, u32[]{:S(2)}, u32[]{:S(2)}) collective-permute-start(bf16[64,1,258]{2,1,0:T(2,128)(2,1)} %pad_maximum_fusion.2), channel_id=1, source_target_pairs={{0,1},{1,2},{2,3},{4,5},{5,6},{6,7},{8,9},{9,10},{10,11},{12,13},{... | collective-permute-start | bytes 99080 | tf_op jit(solution)/shard_map/ppermute | solution.py:22
  50.4 2.7 %collective-permute-done.4 = bf16[64,1,258]{2,1,0:T(2,128)(2,1)S(1)} collective-permute-done((bf16[64,1,258]{2,1,0:T(2,128)(2,1)}, bf16[64,1,258]{2,1,0:T(2,128)(2,1)S(1)}, u32[]{:S(2)}, u32[]{:S(2)}) %collective-permute-start.4) | collective-permute-done | bytes 33056 | tf_op jit(solution)/shard_map/ppermute | solution.py:23
  56.0 12.9 %shard_map.152 = bf16[5,64,64,256]{3,2,1,0:T(8,128)(2,1)} custom-call(bf16[5,64,64,256]{3,2,1,0:T(8,128)(2,1)} %s_ref.1, bf16[5,32,4096]{2,1,0:T(8,128)(2,1)} %copy-done.2, bf16[5,32,4096]{2,1,0:T(8,128)(2,1)} %copy-done.3, bf16[32,256]{1,0:T(8,128)(2,1)} %get-tuple-element.78.place_lo_ref, bf16[32,256]{1,0:T(8,128)(2,1)} %get-tuple-element.93.place_hi_ref, ...), custom_call_target="tpu_custom_call" | custom-call | tf_op jit(solution)/shard_map/pallas_call | solution.py:78
  69.0 6.9 %fusion = f32[64,256]{1,0:T(8,128)S(1)} fusion(bf16[5,64,64,256]{3,2,1,0:T(8,128)(2,1)} %shard_map.152, f32[5,64,256]{2,1,0:T(8,128)S(1)} %select_convert_fusion.3), kind=kLoop, calls=%fused_computation.9 | loop fusion | flops 15712256 | bytes 10878976 | tf_op jit(solution)/shard_map/reduce_sum | solution.py:195
  78.2 2.4 %collective-permute-start.8 = (bf16[64,1,1]{2,0,1:T(8,128)(2,1)S(1)}, bf16[64,1,1]{2,0,1:T(8,128)(2,1)S(1)}, u32[]{:S(2)}, u32[]{:S(2)}) collective-permute-start(bf16[64,1,1]{2,0,1:T(8,128)(2,1)S(1)} %get-tuple-element.64), channel_id=1, source_target_pairs={{0,4},{4,8},{8,12},{12,16},{16,20},{20,24},{24,28},{28,32},{32,36}... | collective-permute-start | bytes 392 | tf_op jit(solution)/shard_map/ppermute | solution.py:22
  80.8 4.6 %collective-permute-done.8 = bf16[64,1,1]{2,0,1:T(8,128)(2,1)S(1)} collective-permute-done((bf16[64,1,1]{2,0,1:T(8,128)(2,1)S(1)}, bf16[64,1,1]{2,0,1:T(8,128)(2,1)S(1)}, u32[]{:S(2)}, u32[]{:S(2)}) %collective-permute-start.8) | collective-permute-done | bytes 160 | tf_op jit(solution)/shard_map/ppermute | solution.py:22
  85.5 3.4 %collective-permute-start.11 = (bf16[64,1,258]{2,0,1:T(8,128)(2,1)S(1)}, bf16[64,1,258]{2,0,1:T(8,128)(2,1)S(1)}, u32[]{:S(2)}, u32[]{:S(2)}) collective-permute-start(bf16[64,1,258]{2,0,1:T(8,128)(2,1)S(1)} %pad_maximum_fusion.5), channel_id=1, source_target_pairs={{0,1},{1,2},{2,3},{4,5},{5,6},{6,7},{8,9},{9,10},{10,11},{12,13},{... | collective-permute-start | bytes 99080 | tf_op jit(solution)/shard_map/ppermute | solution.py:22
  90.7 4.2 %collective-permute-done.10 = bf16[64,1,258]{2,0,1:T(8,128)(2,1)S(1)} collective-permute-done((bf16[64,1,258]{2,0,1:T(8,128)(2,1)S(1)}, bf16[64,1,258]{2,0,1:T(8,128)(2,1)S(1)}, u32[]{:S(2)}, u32[]{:S(2)}) %collective-permute-start.10) | collective-permute-done | bytes 33056 | tf_op jit(solution)/shard_map/ppermute | solution.py:23
  95.2 2.8 %fusion.1 = f32[64,256]{1,0:T(8,128)S(1)} fusion(bf16[5,64,64,256]{3,2,1,0:T(8,128)(2,1)S(1)} %copy-done.1, f32[5,64,256]{2,1,0:T(8,128)S(1)} %select_convert_fusion.2), kind=kLoop, calls=%fused_computation.10 | loop fusion | flops 15712256 | bytes 10878976 | tf_op jit(solution)/shard_map/reduce_sum | solution.py:195
  100.2 2.4 %collective-permute-start.12 = (bf16[64,1,1]{2,0,1:T(8,128)(2,1)S(1)}, bf16[64,1,1]{2,0,1:T(8,128)(2,1)S(1)}, u32[]{:S(2)}, u32[]{:S(2)}) collective-permute-start(bf16[64,1,1]{2,0,1:T(8,128)(2,1)S(1)} %get-tuple-element.58), channel_id=1, source_target_pairs={{0,4},{4,8},{8,12},{12,16},{16,20},{20,24},{24,28},{28,32},{32,36}... | collective-permute-start | bytes 392 | tf_op jit(solution)/shard_map/ppermute | solution.py:22
  102.9 4.5 %collective-permute-done.12 = bf16[64,1,1]{2,0,1:T(8,128)(2,1)S(1)} collective-permute-done((bf16[64,1,1]{2,0,1:T(8,128)(2,1)S(1)}, bf16[64,1,1]{2,0,1:T(8,128)(2,1)S(1)}, u32[]{:S(2)}, u32[]{:S(2)}) %collective-permute-start.12) | collective-permute-done | bytes 160 | tf_op jit(solution)/shard_map/ppermute | solution.py:22
  107.5 3.1 %collective-permute-start.15 = (bf16[64,1,258]{2,0,1:T(8,128)(2,1)S(1)}, bf16[64,1,258]{2,0,1:T(8,128)(2,1)S(1)}, u32[]{:S(2)}, u32[]{:S(2)}) collective-permute-start(bf16[64,1,258]{2,0,1:T(8,128)(2,1)S(1)} %pad_maximum_fusion.6), channel_id=1, source_target_pairs={{0,1},{1,2},{2,3},{4,5},{5,6},{6,7},{8,9},{9,10},{10,11},{12,13},{... | collective-permute-start | bytes 99080 | tf_op jit(solution)/shard_map/ppermute | solution.py:22
  112.4 4.2 %collective-permute-done.14 = bf16[64,1,258]{2,0,1:T(8,128)(2,1)S(1)} collective-permute-done((bf16[64,1,258]{2,0,1:T(8,128)(2,1)S(1)}, bf16[64,1,258]{2,0,1:T(8,128)(2,1)S(1)}, u32[]{:S(2)}, u32[]{:S(2)}) %collective-permute-start.14) | collective-permute-done | bytes 33056 | tf_op jit(solution)/shard_map/ppermute | solution.py:23
  116.8 2.8 %fusion.2 = f32[64,256]{1,0:T(8,128)S(1)} fusion(bf16[5,64,64,256]{3,2,1,0:T(8,128)(2,1)S(1)} %copy-done.1, f32[5,64,256]{2,1,0:T(8,128)S(1)} %select_convert_fusion.1), kind=kLoop, calls=%fused_computation.11 | loop fusion | flops 15712256 | bytes 10878976 | tf_op jit(solution)/shard_map/reduce_sum | solution.py:195
  121.9 2.4 %collective-permute-start.16 = (bf16[64,1,1]{2,0,1:T(8,128)(2,1)S(1)}, bf16[64,1,1]{2,0,1:T(8,128)(2,1)S(1)}, u32[]{:S(2)}, u32[]{:S(2)}) collective-permute-start(bf16[64,1,1]{2,0,1:T(8,128)(2,1)S(1)} %get-tuple-element.54), channel_id=1, source_target_pairs={{0,4},{4,8},{8,12},{12,16},{16,20},{20,24},{24,28},{28,32},{32,36}... | collective-permute-start | bytes 392 | tf_op jit(solution)/shard_map/ppermute | solution.py:22
  124.5 4.5 %collective-permute-done.16 = bf16[64,1,1]{2,0,1:T(8,128)(2,1)S(1)} collective-permute-done((bf16[64,1,1]{2,0,1:T(8,128)(2,1)S(1)}, bf16[64,1,1]{2,0,1:T(8,128)(2,1)S(1)}, u32[]{:S(2)}, u32[]{:S(2)}) %collective-permute-start.16) | collective-permute-done | bytes 160 | tf_op jit(solution)/shard_map/ppermute | solution.py:22
  129.1 1.9 %collective-permute-start.19 = (bf16[64,1,258]{2,0,1:T(8,128)(2,1)S(1)}, bf16[64,1,258]{2,0,1:T(8,128)(2,1)S(1)}, u32[]{:S(2)}, u32[]{:S(2)}) collective-permute-start(bf16[64,1,258]{2,0,1:T(8,128)(2,1)S(1)} %pad_maximum_fusion.7), channel_id=1, source_target_pairs={{0,1},{1,2},{2,3},{4,5},{5,6},{6,7},{8,9},{9,10},{10,11},{12,13},{... | collective-permute-start | bytes 99080 | tf_op jit(solution)/shard_map/ppermute | solution.py:22
  132.9 4.2 %collective-permute-done.18 = bf16[64,1,258]{2,0,1:T(8,128)(2,1)S(1)} collective-permute-done((bf16[64,1,258]{2,0,1:T(8,128)(2,1)S(1)}, bf16[64,1,258]{2,0,1:T(8,128)(2,1)S(1)}, u32[]{:S(2)}, u32[]{:S(2)}) %collective-permute-start.18) | collective-permute-done | bytes 33056 | tf_op jit(solution)/shard_map/ppermute | solution.py:23
  137.3 2.8 %fusion.3 = f32[64,256]{1,0:T(8,128)S(1)} fusion(bf16[5,64,64,256]{3,2,1,0:T(8,128)(2,1)S(1)} %copy-done.1, f32[5,64,256]{2,1,0:T(8,128)S(1)} %select_convert_fusion), kind=kLoop, calls=%fused_computation.12 | loop fusion | flops 15712256 | bytes 10878976 | tf_op jit(solution)/shard_map/reduce_sum | solution.py:195
  (152 shorter events, 39.4 us)
Async XLA Ops:
  0.6 75.2 %copy-start = (f32[48,64]{1,0:T(8,128)S(1)}, f32[48,64]{1,0:T(8,128)}, u32[]{:S(2)}) copy-start(f32[48,64]{1,0:T(8,128)} %param.26) | copy-start | bytes 36868
  0.7 30.5 %copy-start.19 = (s32[5,1,256]{2,1,0:T(1,128)S(1)}, s32[5,1,256]{2,1,0:T(1,128)}, u32[]{:S(2)}) copy-start(s32[5,1,256]{2,1,0:T(1,128)} %param.21) | copy-start | bytes 15364
  0.7 30.5 %copy-start.20 = (s32[1,256]{1,0:T(1,128)S(1)}, s32[1,256]{1,0:T(1,128)}, u32[]{:S(2)}) copy-start(s32[1,256]{1,0:T(1,128)} %param.22) | copy-start | bytes 3076
  11.9 42.5 %collective-permute-start = (bf16[5,32,4096]{2,1,0:T(8,128)(2,1)}, bf16[5,32,4096]{2,1,0:T(8,128)(2,1)S(1)}, u32[]{:S(2)}, u32[]{:S(2)}) collective-permute-start(bf16[5,32,4096]{2,1,0:T(8,128)(2,1)} %get-tuple-element.7), channel_id=1, source_target_pairs={{0,4},{4,8},{8,12},{12,16},{16,20},{20,24},{24,28},{28,32},{32,36}... | collective-permute-start | bytes 3932168 | tf_op jit(solution)/shard_map/ppermute | solution.py:32
  13.8 40.6 %collective-permute-start.1 = (bf16[5,32,4096]{2,1,0:T(8,128)(2,1)}, bf16[5,32,4096]{2,1,0:T(8,128)(2,1)S(1)}, u32[]{:S(2)}, u32[]{:S(2)}) collective-permute-start(bf16[5,32,4096]{2,1,0:T(8,128)(2,1)} %get-tuple-element.8), channel_id=1, source_target_pairs={{4,0},{8,4},{12,8},{16,12},{20,16},{24,20},{28,24},{32,28},{36,32}... | collective-permute-start | bytes 3932168 | tf_op jit(solution)/shard_map/ppermute | solution.py:33
  19.7 15.5 %collective-permute-start.3 = (bf16[64,1,1]{2,1,0:T(2,128)(2,1)S(1)}, bf16[64,1,1]{2,1,0:T(2,128)(2,1)S(1)}, u32[]{:S(2)}, u32[]{:S(2)}) collective-permute-start(bf16[64,1,1]{2,1,0:T(2,128)(2,1)S(1)} %get-tuple-element.33), channel_id=1, source_target_pairs={{4,0},{8,4},{12,8},{16,12},{20,16},{24,20},{28,24},{32,28},{36,32}... | collective-permute-start | bytes 392 | tf_op jit(solution)/shard_map/ppermute | solution.py:23
  21.6 19.5 %collective-permute-start.2 = (bf16[64,1,1]{2,1,0:T(2,128)(2,1)S(1)}, bf16[64,1,1]{2,1,0:T(2,128)(2,1)S(1)}, u32[]{:S(2)}, u32[]{:S(2)}) collective-permute-start(bf16[64,1,1]{2,1,0:T(2,128)(2,1)S(1)} %get-tuple-element.32), channel_id=1, source_target_pairs={{0,4},{4,8},{8,12},{12,16},{16,20},{20,24},{24,28},{28,32},{32,36}... | collective-permute-start | bytes 392 | tf_op jit(solution)/shard_map/ppermute | solution.py:22
  26.8 19.6 %collective-permute-start.6 = (f32[96,32]{0,1:T(8,128)S(1)}, f32[96,32]{0,1:T(8,128)S(1)}, u32[]{:S(2)}, u32[]{:S(2)}) collective-permute-start(f32[96,32]{0,1:T(8,128)S(1)} %get-tuple-element.29), channel_id=1, source_target_pairs={{0,4},{4,8},{8,12},{12,16},{16,20},{20,24},{24,28},{28,32},{32,36}... | collective-permute-start | bytes 36872 | tf_op jit(solution)/shard_map/ppermute | solution.py:32
  35.2 12.5 %collective-permute-start.7 = (f32[96,32]{0,1:T(8,128)S(1)}, f32[96,32]{0,1:T(8,128)S(1)}, u32[]{:S(2)}, u32[]{:S(2)}) collective-permute-start(f32[96,32]{0,1:T(8,128)S(1)} %get-tuple-element.28), channel_id=1, source_target_pairs={{4,0},{8,4},{12,8},{16,12},{20,16},{24,20},{28,24},{32,28},{36,32}... | collective-permute-start | bytes 36872 | tf_op jit(solution)/shard_map/ppermute | solution.py:33
  42.0 8.1 %collective-permute-start.5 = (bf16[64,1,258]{2,1,0:T(2,128)(2,1)}, bf16[64,1,258]{2,1,0:T(2,128)(2,1)S(1)}, u32[]{:S(2)}, u32[]{:S(2)}) collective-permute-start(bf16[64,1,258]{2,1,0:T(2,128)(2,1)} %pad_maximum_fusion.2), channel_id=1, source_target_pairs={{0,1},{1,2},{2,3},{4,5},{5,6},{6,7},{8,9},{9,10},{10,11},{12,13},{... | collective-permute-start | bytes 99080 | tf_op jit(solution)/shard_map/ppermute | solution.py:22
  46.4 6.7 %collective-permute-start.4 = (bf16[64,1,258]{2,1,0:T(2,128)(2,1)}, bf16[64,1,258]{2,1,0:T(2,128)(2,1)S(1)}, u32[]{:S(2)}, u32[]{:S(2)}) collective-permute-start(bf16[64,1,258]{2,1,0:T(2,128)(2,1)} %pad_maximum_fusion.2), channel_id=1, source_target_pairs={{1,0},{2,1},{3,2},{5,4},{6,5},{7,6},{9,8},{10,9},{11,10},{13,12},{... | collective-permute-start | bytes 99080 | tf_op jit(solution)/shard_map/ppermute | solution.py:23
  68.9 26.2 %copy-start.1 = (bf16[5,64,64,256]{3,2,1,0:T(8,128)(2,1)S(1)}, bf16[5,64,64,256]{3,2,1,0:T(8,128)(2,1)}, u32[]{:S(2)}) copy-start(bf16[5,64,64,256]{3,2,1,0:T(8,128)(2,1)} %shard_map.152) | copy-start | bytes 31457284
  76.3 4.5 %collective-permute-start.9 = (bf16[64,1,1]{2,0,1:T(8,128)(2,1)S(1)}, bf16[64,1,1]{2,0,1:T(8,128)(2,1)S(1)}, u32[]{:S(2)}, u32[]{:S(2)}) collective-permute-start(bf16[64,1,1]{2,0,1:T(8,128)(2,1)S(1)} %get-tuple-element.65), channel_id=1, source_target_pairs={{4,0},{8,4},{12,8},{16,12},{20,16},{24,20},{28,24},{32,28},{36,32}... | collective-permute-start | bytes 392 | tf_op jit(solution)/shard_map/ppermute | solution.py:23
  78.2 7.2 %collective-permute-start.8 = (bf16[64,1,1]{2,0,1:T(8,128)(2,1)S(1)}, bf16[64,1,1]{2,0,1:T(8,128)(2,1)S(1)}, u32[]{:S(2)}, u32[]{:S(2)}) collective-permute-start(bf16[64,1,1]{2,0,1:T(8,128)(2,1)S(1)} %get-tuple-element.64), channel_id=1, source_target_pairs={{0,4},{4,8},{8,12},{12,16},{16,20},{20,24},{24,28},{28,32},{32,36}... | collective-permute-start | bytes 392 | tf_op jit(solution)/shard_map/ppermute | solution.py:22
  85.5 5.1 %collective-permute-start.11 = (bf16[64,1,258]{2,0,1:T(8,128)(2,1)S(1)}, bf16[64,1,258]{2,0,1:T(8,128)(2,1)S(1)}, u32[]{:S(2)}, u32[]{:S(2)}) collective-permute-start(bf16[64,1,258]{2,0,1:T(8,128)(2,1)S(1)} %pad_maximum_fusion.5), channel_id=1, source_target_pairs={{0,1},{1,2},{2,3},{4,5},{5,6},{6,7},{8,9},{9,10},{10,11},{12,13},{... | collective-permute-start | bytes 99080 | tf_op jit(solution)/shard_map/ppermute | solution.py:22
  88.9 6.0 %collective-permute-start.10 = (bf16[64,1,258]{2,0,1:T(8,128)(2,1)S(1)}, bf16[64,1,258]{2,0,1:T(8,128)(2,1)S(1)}, u32[]{:S(2)}, u32[]{:S(2)}) collective-permute-start(bf16[64,1,258]{2,0,1:T(8,128)(2,1)S(1)} %pad_maximum_fusion.5), channel_id=1, source_target_pairs={{1,0},{2,1},{3,2},{5,4},{6,5},{7,6},{9,8},{10,9},{11,10},{13,12},{... | collective-permute-start | bytes 99080 | tf_op jit(solution)/shard_map/ppermute | solution.py:23
  98.3 4.5 %collective-permute-start.13 = (bf16[64,1,1]{2,0,1:T(8,128)(2,1)S(1)}, bf16[64,1,1]{2,0,1:T(8,128)(2,1)S(1)}, u32[]{:S(2)}, u32[]{:S(2)}) collective-permute-start(bf16[64,1,1]{2,0,1:T(8,128)(2,1)S(1)} %get-tuple-element.59), channel_id=1, source_target_pairs={{4,0},{8,4},{12,8},{16,12},{20,16},{24,20},{28,24},{32,28},{36,32}... | collective-permute-start | bytes 392 | tf_op jit(solution)/shard_map/ppermute | solution.py:23
  100.2 7.2 %collective-permute-start.12 = (bf16[64,1,1]{2,0,1:T(8,128)(2,1)S(1)}, bf16[64,1,1]{2,0,1:T(8,128)(2,1)S(1)}, u32[]{:S(2)}, u32[]{:S(2)}) collective-permute-start(bf16[64,1,1]{2,0,1:T(8,128)(2,1)S(1)} %get-tuple-element.58), channel_id=1, source_target_pairs={{0,4},{4,8},{8,12},{12,16},{16,20},{20,24},{24,28},{28,32},{32,36}... | collective-permute-start | bytes 392 | tf_op jit(solution)/shard_map/ppermute | solution.py:22
  107.5 4.8 %collective-permute-start.15 = (bf16[64,1,258]{2,0,1:T(8,128)(2,1)S(1)}, bf16[64,1,258]{2,0,1:T(8,128)(2,1)S(1)}, u32[]{:S(2)}, u32[]{:S(2)}) collective-permute-start(bf16[64,1,258]{2,0,1:T(8,128)(2,1)S(1)} %pad_maximum_fusion.6), channel_id=1, source_target_pairs={{0,1},{1,2},{2,3},{4,5},{5,6},{6,7},{8,9},{9,10},{10,11},{12,13},{... | collective-permute-start | bytes 99080 | tf_op jit(solution)/shard_map/ppermute | solution.py:22
  110.6 6.0 %collective-permute-start.14 = (bf16[64,1,258]{2,0,1:T(8,128)(2,1)S(1)}, bf16[64,1,258]{2,0,1:T(8,128)(2,1)S(1)}, u32[]{:S(2)}, u32[]{:S(2)}) collective-permute-start(bf16[64,1,258]{2,0,1:T(8,128)(2,1)S(1)} %pad_maximum_fusion.6), channel_id=1, source_target_pairs={{1,0},{2,1},{3,2},{5,4},{6,5},{7,6},{9,8},{10,9},{11,10},{13,12},{... | collective-permute-start | bytes 99080 | tf_op jit(solution)/shard_map/ppermute | solution.py:23
  120.0 4.5 %collective-permute-start.17 = (bf16[64,1,1]{2,0,1:T(8,128)(2,1)S(1)}, bf16[64,1,1]{2,0,1:T(8,128)(2,1)S(1)}, u32[]{:S(2)}, u32[]{:S(2)}) collective-permute-start(bf16[64,1,1]{2,0,1:T(8,128)(2,1)S(1)} %get-tuple-element.55), channel_id=1, source_target_pairs={{4,0},{8,4},{12,8},{16,12},{20,16},{24,20},{28,24},{32,28},{36,32}... | collective-permute-start | bytes 392 | tf_op jit(solution)/shard_map/ppermute | solution.py:23
  121.9 7.2 %collective-permute-start.16 = (bf16[64,1,1]{2,0,1:T(8,128)(2,1)S(1)}, bf16[64,1,1]{2,0,1:T(8,128)(2,1)S(1)}, u32[]{:S(2)}, u32[]{:S(2)}) collective-permute-start(bf16[64,1,1]{2,0,1:T(8,128)(2,1)S(1)} %get-tuple-element.54), channel_id=1, source_target_pairs={{0,4},{4,8},{8,12},{12,16},{16,20},{20,24},{24,28},{28,32},{32,36}... | collective-permute-start | bytes 392 | tf_op jit(solution)/shard_map/ppermute | solution.py:22
  129.1 3.7 %collective-permute-start.19 = (bf16[64,1,258]{2,0,1:T(8,128)(2,1)S(1)}, bf16[64,1,258]{2,0,1:T(8,128)(2,1)S(1)}, u32[]{:S(2)}, u32[]{:S(2)}) collective-permute-start(bf16[64,1,258]{2,0,1:T(8,128)(2,1)S(1)} %pad_maximum_fusion.7), channel_id=1, source_target_pairs={{0,1},{1,2},{2,3},{4,5},{5,6},{6,7},{8,9},{9,10},{10,11},{12,13},{... | collective-permute-start | bytes 99080 | tf_op jit(solution)/shard_map/ppermute | solution.py:22
  131.1 6.0 %collective-permute-start.18 = (bf16[64,1,258]{2,0,1:T(8,128)(2,1)S(1)}, bf16[64,1,258]{2,0,1:T(8,128)(2,1)S(1)}, u32[]{:S(2)}, u32[]{:S(2)}) collective-permute-start(bf16[64,1,258]{2,0,1:T(8,128)(2,1)S(1)} %pad_maximum_fusion.7), channel_id=1, source_target_pairs={{1,0},{2,1},{3,2},{5,4},{6,5},{7,6},{9,8},{10,9},{11,10},{13,12},{... | collective-permute-start | bytes 99080 | tf_op jit(solution)/shard_map/ppermute | solution.py:23
  (20 other events, 358.4 us)

commit v6 on v5

--- a/solution.py
+++ b/solution.py
@@ -23,6 +23,17 @@
         after = lax.ppermute(first, axis, down)
         value = jnp.concatenate([before, value, after], axis=dim)
     return value
+
+
+def ply_rows(row):
+    size = lax.axis_size("ply")
+    here = lax.axis_index("ply")
+    gathered = lax.all_gather(row, "ply")
+    lower = lax.dynamic_index_in_dim(gathered, jnp.maximum(here - 1, 0), 0, keepdims=False)
+    upper = lax.dynamic_index_in_dim(gathered, jnp.minimum(here + 1, size - 1), 0, keepdims=False)
+    lower = jnp.where(here > 0, lower, jnp.zeros_like(lower))
+    upper = jnp.where(here < size - 1, upper, jnp.zeros_like(upper))
+    return jnp.stack([lower, row, upper], 1)
 
 
 def neighbour_exchange(axis, lower_bound, upper_bound):
@@ -186,7 +197,7 @@
     codes = jnp.where(live, pattern[:, 0, :], 9)[:, None, :]
     for repeat in range(ITERS):
         rounded = moved.astype(jnp.bfloat16)[:, None, :]
-        padded = padded_2(rounded, (("shaft", 2), ("ply", 1)), 1)
+        padded = ply_rows(padded_2(rounded, (("shaft", 2),), 1)[:, 0, :])
         neighbours = jnp.zeros((slots,) + moved.shape, jnp.bfloat16)
         for code_index in range(9):
             shifted = padded[:, code_index // 3, code_index % 3 : code_index % 3 + blocks]

time: 144 us -> 157 us (1.090)
  blocking collectives: 0 us -> 49.4 us
  starting transfers between devices: 49.9 us -> 32.7 us
  waiting for transfers between devices: 31.2 us -> 17.4 us
  local copies, waits for them, and re-layouts: 14.3 us -> 11 us
    all_gather x0 -> x4, blocking collectives: none -> 49.4 us  [ply_rows(): gathered = lax.all_gather(row, 'ply')]
    ppermute x8 -> x4, waiting for transfers between devices: 16.7 us -> 3.77 us  [padded_2(): after = lax.ppermute(first, axis, down)]
    ppermute x8 -> x4, starting transfers between devices: 21.4 us -> 9.63 us  [padded_2(): before = lax.ppermute(last, axis, up)]
    ppermute x8 -> x4, starting transfers between devices: 13 us -> 7.64 us  [padded_2(): after = lax.ppermute(first, axis, down)]
    unnamed x64 -> x73, local copies, waits for them, and re-layouts: 7.57 us -> 4.71 us
    ppermute x8 -> x4, waiting for transfers between devices: 14.5 us -> 13.6 us  [padded_2(): before = lax.ppermute(last, axis, up)]
  transfers between devices with their start and end apart: 20 -> 12, of which waited for: 11 -> 4; matrix products, arithmetic and copies ran while one was open for 10% -> 6% of each run, Pallas kernels for 0% -> 0%
where the time goes in v6:
time: 157 us; the launch traced here: 156 us
  blocking collectives  49.4 us (31%)
  starting transfers between devices  32.7 us (21%)
  Pallas kernels  22.5 us (14%)
  other arithmetic  20 us (13%)
  waiting for transfers between devices  17.4 us (11%)
  local copies, waits for them, and re-layouts  11 us (7%)
  matrix products  1.85 us (1%)
    all_gather x4, blocking collectives, ply_rows(): gathered = lax.all_gather(row, 'ply')  49.4 us
    reduce_sum x4, other arithmetic, on_device(): jnp.sum(product, axis=(0, 2))  15.3 us
    ppermute x4, waiting for transfers between devices, padded_2(): before = lax.ppermute(last, axis, up)  13.6 us
    pallas_call x1, Pallas kernels, merge_arrived(): pl.pallas_call(merge_kernel, grid=(slots,), in_specs=[pl.BlockSpec((1, ro...  12.8 us
    ppermute x2, starting transfers between devices, neighbour_exchange(): from_higher = lax.ppermute(lower_bound, axis, down)  11.7 us
    pallas_call x1, Pallas kernels, gather_leaving(): pl.pallas_call(gather_kernel, grid=(slots,), in_specs=[pl.BlockSpec((1, d...  9.7 us
    ppermute x4, starting transfers between devices, padded_2(): before = lax.ppermute(last, axis, up)  9.63 us
    ppermute x4, starting transfers between devices, padded_2(): after = lax.ppermute(first, axis, down)  7.64 us
  transfers between devices with their start and end apart: 12, of which 4 were waited for; matrix products, arithmetic and copies ran while one was open for 6% of the time, Pallas kernels for 0%

profile of v6, /device:TPU:96, one launch (start us, length us, event | category | flops | bytes accessed | tf_op | source)
XLA Modules:
  0.0 156.5 jit_solution(1664855508836882135)
XLA Ops:
  2.2 9.7 %shard_map.151 = (bf16[5,32,4096]{2,1,0:T(8,128)(2,1)}, bf16[5,32,4096]{2,1,0:T(8,128)(2,1)}) custom-call(bf16[5,4096,256]{2,1,0:T(8,128)(2,1)} %bitcast.248, bf16[32,256]{1,0:T(8,128)(2,1)} %get-tuple-element.104.lo_ref, bf16[32,256]{1,0:T(8,128)(2,1)} %get-tuple-element.105.hi_ref), custom_call_target="tpu_custom_call" | custom-call | tf_op jit(solution)/shard_map/pallas_call | solution.py:61
  13.8 5.8 %collective-permute-start.1 = (bf16[5,32,4096]{2,1,0:T(8,128)(2,1)}, bf16[5,32,4096]{2,1,0:T(8,128)(2,1)S(1)}, u32[]{:S(2)}, u32[]{:S(2)}) collective-permute-start(bf16[5,32,4096]{2,1,0:T(8,128)(2,1)} %get-tuple-element.8), channel_id=1, source_target_pairs={{4,0},{8,4},{12,8},{16,12},{20,16},{24,20},{28,24},{32,28},{36,32}... | collective-permute-start | bytes 3932168 | tf_op jit(solution)/shard_map/ppermute | solution.py:44
  19.7 1.9 %collective-permute-start.3 = (bf16[64,1,1]{2,0,1:T(8,128)(2,1)S(1)}, bf16[64,1,1]{2,0,1:T(8,128)(2,1)S(1)}, u32[]{:S(2)}, u32[]{:S(2)}) collective-permute-start(bf16[64,1,1]{2,0,1:T(8,128)(2,1)S(1)} %get-tuple-element.78), channel_id=1, source_target_pairs={{4,0},{8,4},{12,8},{16,12},{20,16},{24,20},{28,24},{32,28},{36,32}... | collective-permute-start | bytes 392 | tf_op jit(solution)/shard_map/ppermute | solution.py:23
  21.6 2.4 %collective-permute-start.2 = (bf16[64,1,1]{2,0,1:T(8,128)(2,1)S(1)}, bf16[64,1,1]{2,0,1:T(8,128)(2,1)S(1)}, u32[]{:S(2)}, u32[]{:S(2)}) collective-permute-start(bf16[64,1,1]{2,0,1:T(8,128)(2,1)S(1)} %get-tuple-element.77), channel_id=1, source_target_pairs={{0,4},{4,8},{8,12},{12,16},{16,20},{20,24},{24,28},{28,32},{32,36}... | collective-permute-start | bytes 392 | tf_op jit(solution)/shard_map/ppermute | solution.py:22
  27.4 1.9 %collective-permute-start.4 = (f32[96,32]{0,1:T(8,128)}, f32[96,32]{0,1:T(8,128)}, u32[]{:S(2)}, u32[]{:S(2)}) collective-permute-start(f32[96,32]{0,1:T(8,128)} %get-tuple-element.34), channel_id=1, source_target_pairs={{0,4},{4,8},{8,12},{12,16},{16,20},{20,24},{24,28},{28,32},{32,36}... | collective-permute-start | bytes 36872 | tf_op jit(solution)/shard_map/ppermute | solution.py:43
  31.3 3.8 %collective-permute-done.3 = bf16[64,1,1]{2,0,1:T(8,128)(2,1)S(1)} collective-permute-done((bf16[64,1,1]{2,0,1:T(8,128)(2,1)S(1)}, bf16[64,1,1]{2,0,1:T(8,128)(2,1)S(1)}, u32[]{:S(2)}, u32[]{:S(2)}) %collective-permute-start.3) | collective-permute-done | bytes 160 | tf_op jit(solution)/shard_map/ppermute | solution.py:23
  35.0 5.9 %collective-permute-start.5 = (f32[96,32]{0,1:T(8,128)}, f32[96,32]{0,1:T(8,128)S(1)}, u32[]{:S(2)}, u32[]{:S(2)}) collective-permute-start(f32[96,32]{0,1:T(8,128)} %get-tuple-element.33), channel_id=1, source_target_pairs={{4,0},{8,4},{12,8},{16,12},{20,16},{24,20},{28,24},{32,28},{36,32}... | collective-permute-start | bytes 36872 | tf_op jit(solution)/shard_map/ppermute | solution.py:44
  41.2 12.5 %all-gather = bf16[256,1,258]{2,0,1:T(8,128)(2,1)S(1)} all-gather(bf16[64,1,258]{2,0,1:T(8,128)(2,1)S(1)} %pad_maximum_fusion.2), channel_id=2, replica_groups=mesh['shaft'=32,'ply'=4] {'ply'}, dimensions={0}, use_global_device_ids=true | all-gather | bytes 165120 | tf_op jit(solution)/shard_map/all_gather | solution.py:31
  58.7 12.8 %shard_map.152 = bf16[5,64,64,256]{3,2,1,0:T(8,128)(2,1)} custom-call(bf16[5,64,64,256]{3,2,1,0:T(8,128)(2,1)} %s_ref.1, bf16[5,32,4096]{2,1,0:T(8,128)(2,1)} %copy-done.2, bf16[5,32,4096]{2,1,0:T(8,128)(2,1)} %copy-done.3, bf16[32,256]{1,0:T(8,128)(2,1)} %get-tuple-element.91.place_lo_ref, bf16[32,256]{1,0:T(8,128)(2,1)} %get-tuple-element.106.place_hi_ref, ...), custom_call_target="tpu_custom_call" | custom-call | tf_op jit(solution)/shard_map/pallas_call | solution.py:89
  71.7 6.9 %fusion = f32[64,256]{1,0:T(8,128)S(1)} fusion(bf16[5,64,64,256]{3,2,1,0:T(8,128)(2,1)} %shard_map.152, f32[5,64,256]{2,1,0:T(8,128)S(1)} %select_convert_fusion.3), kind=kLoop, calls=%fused_computation.9 | loop fusion | flops 15712256 | bytes 10878976 | tf_op jit(solution)/shard_map/reduce_sum | solution.py:206
  79.0 1.9 %collective-permute-start.7 = (bf16[64,1,1]{2,0,1:T(8,128)(2,1)S(1)}, bf16[64,1,1]{2,0,1:T(8,128)(2,1)S(1)}, u32[]{:S(2)}, u32[]{:S(2)}) collective-permute-start(bf16[64,1,1]{2,0,1:T(8,128)(2,1)S(1)} %get-tuple-element.74), channel_id=1, source_target_pairs={{4,0},{8,4},{12,8},{16,12},{20,16},{24,20},{28,24},{32,28},{36,32}... | collective-permute-start | bytes 392 | tf_op jit(solution)/shard_map/ppermute | solution.py:23
  80.9 2.4 %collective-permute-start.6 = (bf16[64,1,1]{2,0,1:T(8,128)(2,1)S(1)}, bf16[64,1,1]{2,0,1:T(8,128)(2,1)S(1)}, u32[]{:S(2)}, u32[]{:S(2)}) collective-permute-start(bf16[64,1,1]{2,0,1:T(8,128)(2,1)S(1)} %get-tuple-element.73), channel_id=1, source_target_pairs={{0,4},{4,8},{8,12},{12,16},{16,20},{20,24},{24,28},{28,32},{32,36}... | collective-permute-start | bytes 392 | tf_op jit(solution)/shard_map/ppermute | solution.py:22
  83.5 4.6 %collective-permute-done.6 = bf16[64,1,1]{2,0,1:T(8,128)(2,1)S(1)} collective-permute-done((bf16[64,1,1]{2,0,1:T(8,128)(2,1)S(1)}, bf16[64,1,1]{2,0,1:T(8,128)(2,1)S(1)}, u32[]{:S(2)}, u32[]{:S(2)}) %collective-permute-start.6) | collective-permute-done | bytes 160 | tf_op jit(solution)/shard_map/ppermute | solution.py:22
  88.2 12.2 %all-gather.1 = bf16[256,1,258]{2,0,1:T(8,128)(2,1)S(1)} all-gather(bf16[64,1,258]{2,0,1:T(8,128)(2,1)S(1)} %pad_maximum_fusion.3), channel_id=3, replica_groups=mesh['shaft'=32,'ply'=4] {'ply'}, dimensions={0}, use_global_device_ids=true | all-gather | bytes 165120 | tf_op jit(solution)/shard_map/all_gather | solution.py:31
  100.9 2.8 %fusion.1 = f32[64,256]{1,0:T(8,128)S(1)} fusion(bf16[5,64,64,256]{3,2,1,0:T(8,128)(2,1)S(1)} %copy-done.1, f32[5,64,256]{2,1,0:T(8,128)S(1)} %select_convert_fusion.2), kind=kLoop, calls=%fused_computation.10 | loop fusion | flops 15712256 | bytes 10878976 | tf_op jit(solution)/shard_map/reduce_sum | solution.py:206
  104.1 1.9 %collective-permute-start.9 = (bf16[64,1,1]{2,0,1:T(8,128)(2,1)S(1)}, bf16[64,1,1]{2,0,1:T(8,128)(2,1)S(1)}, u32[]{:S(2)}, u32[]{:S(2)}) collective-permute-start(bf16[64,1,1]{2,0,1:T(8,128)(2,1)S(1)} %get-tuple-element.68), channel_id=1, source_target_pairs={{4,0},{8,4},{12,8},{16,12},{20,16},{24,20},{28,24},{32,28},{36,32}... | collective-permute-start | bytes 392 | tf_op jit(solution)/shard_map/ppermute | solution.py:23
  106.0 2.4 %collective-permute-start.8 = (bf16[64,1,1]{2,0,1:T(8,128)(2,1)S(1)}, bf16[64,1,1]{2,0,1:T(8,128)(2,1)S(1)}, u32[]{:S(2)}, u32[]{:S(2)}) collective-permute-start(bf16[64,1,1]{2,0,1:T(8,128)(2,1)S(1)} %get-tuple-element.67), channel_id=1, source_target_pairs={{0,4},{4,8},{8,12},{12,16},{16,20},{20,24},{24,28},{28,32},{32,36}... | collective-permute-start | bytes 392 | tf_op jit(solution)/shard_map/ppermute | solution.py:22
  108.6 4.5 %collective-permute-done.8 = bf16[64,1,1]{2,0,1:T(8,128)(2,1)S(1)} collective-permute-done((bf16[64,1,1]{2,0,1:T(8,128)(2,1)S(1)}, bf16[64,1,1]{2,0,1:T(8,128)(2,1)S(1)}, u32[]{:S(2)}, u32[]{:S(2)}) %collective-permute-start.8) | collective-permute-done | bytes 160 | tf_op jit(solution)/shard_map/ppermute | solution.py:22
  113.3 12.4 %all-gather.2 = bf16[256,1,258]{2,0,1:T(8,128)(2,1)S(1)} all-gather(bf16[64,1,258]{2,0,1:T(8,128)(2,1)S(1)} %pad_maximum_fusion.4), channel_id=4, replica_groups=mesh['shaft'=32,'ply'=4] {'ply'}, dimensions={0}, use_global_device_ids=true | all-gather | bytes 165120 | tf_op jit(solution)/shard_map/all_gather | solution.py:31
  126.1 2.8 %fusion.2 = f32[64,256]{1,0:T(8,128)S(1)} fusion(bf16[5,64,64,256]{3,2,1,0:T(8,128)(2,1)S(1)} %copy-done.1, f32[5,64,256]{2,1,0:T(8,128)S(1)} %select_convert_fusion.1), kind=kLoop, calls=%fused_computation.11 | loop fusion | flops 15712256 | bytes 10878976 | tf_op jit(solution)/shard_map/reduce_sum | solution.py:206
  131.2 2.4 %collective-permute-start.10 = (bf16[64,1,1]{2,0,1:T(8,128)(2,1)S(1)}, bf16[64,1,1]{2,0,1:T(8,128)(2,1)S(1)}, u32[]{:S(2)}, u32[]{:S(2)}) collective-permute-start(bf16[64,1,1]{2,0,1:T(8,128)(2,1)S(1)} %get-tuple-element.63), channel_id=1, source_target_pairs={{0,4},{4,8},{8,12},{12,16},{16,20},{20,24},{24,28},{28,32},{32,36}... | collective-permute-start | bytes 392 | tf_op jit(solution)/shard_map/ppermute | solution.py:22
  133.8 4.5 %collective-permute-done.10 = bf16[64,1,1]{2,0,1:T(8,128)(2,1)S(1)} collective-permute-done((bf16[64,1,1]{2,0,1:T(8,128)(2,1)S(1)}, bf16[64,1,1]{2,0,1:T(8,128)(2,1)S(1)}, u32[]{:S(2)}, u32[]{:S(2)}) %collective-permute-start.10) | collective-permute-done | bytes 160 | tf_op jit(solution)/shard_map/ppermute | solution.py:22
  138.4 12.2 %all-gather.3 = bf16[256,1,258]{2,0,1:T(8,128)(2,1)S(1)} all-gather(bf16[64,1,258]{2,0,1:T(8,128)(2,1)S(1)} %pad_maximum_fusion.5), channel_id=5, replica_groups=mesh['shaft'=32,'ply'=4] {'ply'}, dimensions={0}, use_global_device_ids=true | all-gather | bytes 165120 | tf_op jit(solution)/shard_map/all_gather | solution.py:31
  151.1 2.8 %fusion.3 = f32[64,256]{1,0:T(8,128)S(1)} fusion(bf16[5,64,64,256]{3,2,1,0:T(8,128)(2,1)S(1)} %copy-done.1, f32[5,64,256]{2,1,0:T(8,128)S(1)} %select_convert_fusion), kind=kLoop, calls=%fused_computation.12 | loop fusion | flops 15712256 | bytes 10878976 | tf_op jit(solution)/shard_map/reduce_sum | solution.py:206
  (152 shorter events, 21.4 us)
Async XLA Ops:
  0.6 78.0 %copy-start = (f32[48,64]{1,0:T(8,128)S(1)}, f32[48,64]{1,0:T(8,128)}, u32[]{:S(2)}) copy-start(f32[48,64]{1,0:T(8,128)} %param.26) | copy-start | bytes 36868
  0.7 29.1 %copy-start.26 = (s32[5,1,256]{2,1,0:T(1,128)S(1)}, s32[5,1,256]{2,1,0:T(1,128)}, u32[]{:S(2)}) copy-start(s32[5,1,256]{2,1,0:T(1,128)} %param.21) | copy-start | bytes 15364
  0.7 29.1 %copy-start.27 = (s32[1,256]{1,0:T(1,128)S(1)}, s32[1,256]{1,0:T(1,128)}, u32[]{:S(2)}) copy-start(s32[1,256]{1,0:T(1,128)} %param.22) | copy-start | bytes 3076
  11.9 45.2 %collective-permute-start = (bf16[5,32,4096]{2,1,0:T(8,128)(2,1)}, bf16[5,32,4096]{2,1,0:T(8,128)(2,1)S(1)}, u32[]{:S(2)}, u32[]{:S(2)}) collective-permute-start(bf16[5,32,4096]{2,1,0:T(8,128)(2,1)} %get-tuple-element.7), channel_id=1, source_target_pairs={{0,4},{4,8},{8,12},{12,16},{16,20},{20,24},{24,28},{28,32},{32,36}... | collective-permute-start | bytes 3932168 | tf_op jit(solution)/shard_map/ppermute | solution.py:43
  13.8 43.3 %collective-permute-start.1 = (bf16[5,32,4096]{2,1,0:T(8,128)(2,1)}, bf16[5,32,4096]{2,1,0:T(8,128)(2,1)S(1)}, u32[]{:S(2)}, u32[]{:S(2)}) collective-permute-start(bf16[5,32,4096]{2,1,0:T(8,128)(2,1)} %get-tuple-element.8), channel_id=1, source_target_pairs={{4,0},{8,4},{12,8},{16,12},{20,16},{24,20},{28,24},{32,28},{36,32}... | collective-permute-start | bytes 3932168 | tf_op jit(solution)/shard_map/ppermute | solution.py:44
  19.7 15.4 %collective-permute-start.3 = (bf16[64,1,1]{2,0,1:T(8,128)(2,1)S(1)}, bf16[64,1,1]{2,0,1:T(8,128)(2,1)S(1)}, u32[]{:S(2)}, u32[]{:S(2)}) collective-permute-start(bf16[64,1,1]{2,0,1:T(8,128)(2,1)S(1)} %get-tuple-element.78), channel_id=1, source_target_pairs={{4,0},{8,4},{12,8},{16,12},{20,16},{24,20},{28,24},{32,28},{36,32}... | collective-permute-start | bytes 392 | tf_op jit(solution)/shard_map/ppermute | solution.py:23
  21.6 19.4 %collective-permute-start.2 = (bf16[64,1,1]{2,0,1:T(8,128)(2,1)S(1)}, bf16[64,1,1]{2,0,1:T(8,128)(2,1)S(1)}, u32[]{:S(2)}, u32[]{:S(2)}) collective-permute-start(bf16[64,1,1]{2,0,1:T(8,128)(2,1)S(1)} %get-tuple-element.77), channel_id=1, source_target_pairs={{0,4},{4,8},{8,12},{12,16},{16,20},{20,24},{24,28},{28,32},{32,36}... | collective-permute-start | bytes 392 | tf_op jit(solution)/shard_map/ppermute | solution.py:22
  27.4 26.6 %collective-permute-start.4 = (f32[96,32]{0,1:T(8,128)}, f32[96,32]{0,1:T(8,128)}, u32[]{:S(2)}, u32[]{:S(2)}) collective-permute-start(f32[96,32]{0,1:T(8,128)} %get-tuple-element.34), channel_id=1, source_target_pairs={{0,4},{4,8},{8,12},{12,16},{16,20},{20,24},{24,28},{28,32},{32,36}... | collective-permute-start | bytes 36872 | tf_op jit(solution)/shard_map/ppermute | solution.py:43
  31.2 25.0 %copy-start.17 = (pred[5,256]{1,0:T(8,128)(4,1)}, pred[5,256]{1,0:T(8,128)(4,1)S(1)}, u32[]{:S(2)}) copy-start(pred[5,256]{1,0:T(8,128)(4,1)S(1)} %get-tuple-element.113) | copy-start | bytes 3844
  35.0 19.6 %collective-permute-start.5 = (f32[96,32]{0,1:T(8,128)}, f32[96,32]{0,1:T(8,128)S(1)}, u32[]{:S(2)}, u32[]{:S(2)}) collective-permute-start(f32[96,32]{0,1:T(8,128)} %get-tuple-element.33), channel_id=1, source_target_pairs={{4,0},{8,4},{12,8},{16,12},{20,16},{24,20},{28,24},{32,28},{36,32}... | collective-permute-start | bytes 36872 | tf_op jit(solution)/shard_map/ppermute | solution.py:44
  71.6 29.2 %copy-start.10 = (pred[5,256]{1,0:T(8,128)(4,1)S(1)}, pred[5,256]{1,0:T(8,128)(4,1)}, u32[]{:S(2)}) copy-start(pred[5,256]{1,0:T(8,128)(4,1)} %copy-done.9) | copy-start | bytes 3844
  71.6 29.2 %copy-start.12 = (pred[5,256]{1,0:T(8,128)(4,1)S(1)}, pred[5,256]{1,0:T(8,128)(4,1)}, u32[]{:S(2)}) copy-start(pred[5,256]{1,0:T(8,128)(4,1)} %copy-done.11) | copy-start | bytes 3844
  71.6 29.2 %copy-start.14 = (pred[5,256]{1,0:T(8,128)(4,1)S(1)}, pred[5,256]{1,0:T(8,128)(4,1)}, u32[]{:S(2)}) copy-start(pred[5,256]{1,0:T(8,128)(4,1)} %copy-done.13) | copy-start | bytes 3844
  71.6 29.2 %copy-start.16 = (pred[5,256]{1,0:T(8,128)(4,1)S(1)}, pred[5,256]{1,0:T(8,128)(4,1)}, u32[]{:S(2)}) copy-start(pred[5,256]{1,0:T(8,128)(4,1)} %copy-done.15) | copy-start | bytes 3844
  71.6 29.2 %copy-start.18 = (pred[5,256]{1,0:T(8,128)(4,1)S(1)}, pred[5,256]{1,0:T(8,128)(4,1)}, u32[]{:S(2)}) copy-start(pred[5,256]{1,0:T(8,128)(4,1)} %copy-done.17) | copy-start | bytes 3844
  71.6 29.2 %copy-start.20 = (pred[5,256]{1,0:T(8,128)(4,1)S(1)}, pred[5,256]{1,0:T(8,128)(4,1)}, u32[]{:S(2)}) copy-start(pred[5,256]{1,0:T(8,128)(4,1)} %copy-done.19) | copy-start | bytes 3844
  71.6 29.2 %copy-start.22 = (pred[5,256]{1,0:T(8,128)(4,1)S(1)}, pred[5,256]{1,0:T(8,128)(4,1)}, u32[]{:S(2)}) copy-start(pred[5,256]{1,0:T(8,128)(4,1)} %copy-done.21) | copy-start | bytes 3844
  71.6 29.3 %copy-start.1 = (bf16[5,64,64,256]{3,2,1,0:T(8,128)(2,1)S(1)}, bf16[5,64,64,256]{3,2,1,0:T(8,128)(2,1)}, u32[]{:S(2)}) copy-start(bf16[5,64,64,256]{3,2,1,0:T(8,128)(2,1)} %shard_map.152) | copy-start | bytes 31457284
  79.0 4.5 %collective-permute-start.7 = (bf16[64,1,1]{2,0,1:T(8,128)(2,1)S(1)}, bf16[64,1,1]{2,0,1:T(8,128)(2,1)S(1)}, u32[]{:S(2)}, u32[]{:S(2)}) collective-permute-start(bf16[64,1,1]{2,0,1:T(8,128)(2,1)S(1)} %get-tuple-element.74), channel_id=1, source_target_pairs={{4,0},{8,4},{12,8},{16,12},{20,16},{24,20},{28,24},{32,28},{36,32}... | collective-permute-start | bytes 392 | tf_op jit(solution)/shard_map/ppermute | solution.py:23
  80.9 7.2 %collective-permute-start.6 = (bf16[64,1,1]{2,0,1:T(8,128)(2,1)S(1)}, bf16[64,1,1]{2,0,1:T(8,128)(2,1)S(1)}, u32[]{:S(2)}, u32[]{:S(2)}) collective-permute-start(bf16[64,1,1]{2,0,1:T(8,128)(2,1)S(1)} %get-tuple-element.73), channel_id=1, source_target_pairs={{0,4},{4,8},{8,12},{12,16},{16,20},{20,24},{24,28},{28,32},{32,36}... | collective-permute-start | bytes 392 | tf_op jit(solution)/shard_map/ppermute | solution.py:22
  104.1 4.5 %collective-permute-start.9 = (bf16[64,1,1]{2,0,1:T(8,128)(2,1)S(1)}, bf16[64,1,1]{2,0,1:T(8,128)(2,1)S(1)}, u32[]{:S(2)}, u32[]{:S(2)}) collective-permute-start(bf16[64,1,1]{2,0,1:T(8,128)(2,1)S(1)} %get-tuple-element.68), channel_id=1, source_target_pairs={{4,0},{8,4},{12,8},{16,12},{20,16},{24,20},{28,24},{32,28},{36,32}... | collective-permute-start | bytes 392 | tf_op jit(solution)/shard_map/ppermute | solution.py:23
  106.0 7.2 %collective-permute-start.8 = (bf16[64,1,1]{2,0,1:T(8,128)(2,1)S(1)}, bf16[64,1,1]{2,0,1:T(8,128)(2,1)S(1)}, u32[]{:S(2)}, u32[]{:S(2)}) collective-permute-start(bf16[64,1,1]{2,0,1:T(8,128)(2,1)S(1)} %get-tuple-element.67), channel_id=1, source_target_pairs={{0,4},{4,8},{8,12},{12,16},{16,20},{20,24},{24,28},{28,32},{32,36}... | collective-permute-start | bytes 392 | tf_op jit(solution)/shard_map/ppermute | solution.py:22
  129.3 4.5 %collective-permute-start.11 = (bf16[64,1,1]{2,0,1:T(8,128)(2,1)S(1)}, bf16[64,1,1]{2,0,1:T(8,128)(2,1)S(1)}, u32[]{:S(2)}, u32[]{:S(2)}) collective-permute-start(bf16[64,1,1]{2,0,1:T(8,128)(2,1)S(1)} %get-tuple-element.64), channel_id=1, source_target_pairs={{4,0},{8,4},{12,8},{16,12},{20,16},{24,20},{28,24},{32,28},{36,32}... | collective-permute-start | bytes 392 | tf_op jit(solution)/shard_map/ppermute | solution.py:23
  131.2 7.2 %collective-permute-start.10 = (bf16[64,1,1]{2,0,1:T(8,128)(2,1)S(1)}, bf16[64,1,1]{2,0,1:T(8,128)(2,1)S(1)}, u32[]{:S(2)}, u32[]{:S(2)}) collective-permute-start(bf16[64,1,1]{2,0,1:T(8,128)(2,1)S(1)} %get-tuple-element.63), channel_id=1, source_target_pairs={{0,4},{4,8},{8,12},{12,16},{16,20},{20,24},{24,28},{28,32},{32,36}... | collective-permute-start | bytes 392 | tf_op jit(solution)/shard_map/ppermute | solution.py:22
  (19 other events, 319.7 us)

commit v7 on v5

--- a/solution.py
+++ b/solution.py
@@ -34,60 +34,55 @@
     return from_lower, from_higher
 
 
-def gather_kernel(s_ref, lo_ref, hi_ref, out_lo_ref, out_hi_ref):
-    flat = s_ref[0]
-    for pick_ref, out_ref in ((lo_ref, out_lo_ref), (hi_ref, out_hi_ref)):
-        picked = lax.dot_general(
-            pick_ref[...], flat, (((1,), (1,)), ((), ())), preferred_element_type=jnp.float32
-        )
-        out_ref[0] = picked.astype(out_ref.dtype)
-
-
-def gather_leaving(stiffness, pick_lo, pick_hi):
+def gather_kernel(s_ref, pick_ref, out_lo_ref, out_hi_ref):
+    width = out_lo_ref.shape[0]
+    picked = jnp.dot(s_ref[0], pick_ref[...], preferred_element_type=jnp.float32).T
+    out_lo_ref[...] = picked[:width].astype(out_lo_ref.dtype)
+    out_hi_ref[...] = picked[width : 2 * width].astype(out_hi_ref.dtype)
+
+
+def gather_leaving(stiffness, slot_index, pick, width):
     slots, depth, blocks = stiffness.shape
-    width = pick_lo.shape[0]
-    out = jax.ShapeDtypeStruct((slots, width, depth), stiffness.dtype)
+    out = jax.ShapeDtypeStruct((width, depth), stiffness.dtype)
     return pl.pallas_call(
         gather_kernel,
-        grid=(slots,),
+        grid=(1,),
         in_specs=[
-            pl.BlockSpec((1, depth, blocks), lambda k: (k, 0, 0)),
-            pl.BlockSpec((width, blocks), lambda k: (0, 0)),
-            pl.BlockSpec((width, blocks), lambda k: (0, 0)),
+            pl.BlockSpec((1, depth, blocks), lambda g: (slot_index, 0, 0)),
+            pl.BlockSpec(pick.shape, lambda g: (0, 0)),
         ],
         out_specs=[
-            pl.BlockSpec((1, width, depth), lambda k: (k, 0, 0)),
-            pl.BlockSpec((1, width, depth), lambda k: (k, 0, 0)),
+            pl.BlockSpec((width, depth), lambda g: (0, 0)),
+            pl.BlockSpec((width, depth), lambda g: (0, 0)),
         ],
         out_shape=[out, out],
-    )(stiffness, pick_lo, pick_hi)
+    )(stiffness, pick)
 
 
 def merge_kernel(s_ref, lo_ref, hi_ref, place_lo_ref, place_hi_ref, arrival_ref, out_ref):
     placed = jnp.dot(
-        lo_ref[0].T, place_lo_ref[...], preferred_element_type=jnp.float32
-    ) + jnp.dot(hi_ref[0].T, place_hi_ref[...], preferred_element_type=jnp.float32)
-    placed = placed.astype(out_ref.dtype).reshape(s_ref.shape[1:])
-    out_ref[0] = jnp.where(arrival_ref[...] > 0, placed, s_ref[0])
-
-
-def merge_arrived(stiffness, arrived_lo, arrived_hi, place_lo, place_hi, arrival):
+        lo_ref[...].T, place_lo_ref[...], preferred_element_type=jnp.float32
+    ) + jnp.dot(hi_ref[...].T, place_hi_ref[...], preferred_element_type=jnp.float32)
+    placed = placed.astype(out_ref.dtype).reshape(out_ref.shape)
+    out_ref[...] = jnp.where(arrival_ref[...] > 0, placed, s_ref[0])
+
+
+def merge_arrived(stiffness, slot_index, arrived_lo, arrived_hi, place_lo, place_hi, arrival):
     slots, rows_i, rows_j, blocks = stiffness.shape
-    depth = rows_i * rows_j
-    width = arrived_lo.shape[1]
+    width, depth = arrived_lo.shape
     return pl.pallas_call(
         merge_kernel,
-        grid=(slots,),
+        grid=(1,),
         in_specs=[
-            pl.BlockSpec((1, rows_i, rows_j, blocks), lambda k: (k, 0, 0, 0)),
-            pl.BlockSpec((1, width, depth), lambda k: (k, 0, 0)),
-            pl.BlockSpec((1, width, depth), lambda k: (k, 0, 0)),
-            pl.BlockSpec((width, blocks), lambda k: (0, 0)),
-            pl.BlockSpec((width, blocks), lambda k: (0, 0)),
-            pl.BlockSpec((1, blocks), lambda k: (0, 0)),
-        ],
-        out_specs=pl.BlockSpec((1, rows_i, rows_j, blocks), lambda k: (k, 0, 0, 0)),
-        out_shape=jax.ShapeDtypeStruct(stiffness.shape, stiffness.dtype),
+            pl.BlockSpec((1, rows_i, rows_j, blocks), lambda g: (slot_index, 0, 0, 0)),
+            pl.BlockSpec((width, depth), lambda g: (0, 0)),
+            pl.BlockSpec((width, depth), lambda g: (0, 0)),
+            pl.BlockSpec((width, blocks), lambda g: (0, 0)),
+            pl.BlockSpec((width, blocks), lambda g: (0, 0)),
+            pl.BlockSpec((1, blocks), lambda g: (0, 0)),
+        ],
+        out_specs=pl.BlockSpec((rows_i, rows_j, blocks), lambda g: (0, 0, 0)),
+        out_shape=jax.ShapeDtypeStruct((rows_i, rows_j, blocks), stiffness.dtype),
     )(stiffness, arrived_lo, arrived_hi, place_lo, place_hi, arrival)
 
 
@@ -141,23 +136,32 @@
 
     slots, rows_i, rows_j, _ = stiffness_old.shape
     stiff_flat = stiffness_old.reshape(slots, rows_i * rows_j, blocks)
-    leave_lo = (send_slot[0, 0][:, None] == lanes[None, :]).astype(jnp.bfloat16)
-    leave_hi = (send_slot[0, 1][:, None] == lanes[None, :]).astype(jnp.bfloat16)
-    stiff_to_lower, stiff_to_higher = gather_leaving(stiff_flat, leave_lo, leave_hi)
-    stiff_lower, stiff_higher = neighbour_exchange("shaft", stiff_to_lower, stiff_to_higher)
+    picks = jnp.arange(128, dtype=jnp.int32)
+    leaving = jnp.concatenate([send_slot[0, 0], send_slot[0, 1]])
+    pick = (
+        (lanes[:, None] == jnp.pad(leaving, (0, 128 - 2 * capacity))[None, :])
+        & (picks < 2 * capacity)[None, :]
+    ).astype(jnp.bfloat16)
 
     count_live = jnp.arange(capacity, dtype=jnp.int32)[None, :] < arrive_count[0][:, None]
     place_lo = (arrive_place[0, 0][:, None] == lanes[None, :]) & count_live[0][:, None]
     place_hi = (arrive_place[0, 1][:, None] == lanes[None, :]) & count_live[1][:, None]
     arrival = (jnp.any(place_lo, 0) | jnp.any(place_hi, 0)).astype(jnp.int32)[None, :]
-    stiffness = merge_arrived(
-        stiffness_old,
-        stiff_lower,
-        stiff_higher,
-        place_lo.astype(jnp.bfloat16),
-        place_hi.astype(jnp.bfloat16),
-        arrival,
-    )
+    stiffness = []
+    for slot_index in range(slots):
+        to_lower, to_higher = gather_leaving(stiff_flat, slot_index, pick, capacity)
+        arrived_lo, arrived_hi = neighbour_exchange("shaft", to_lower, to_higher)
+        stiffness.append(
+            merge_arrived(
+                stiffness_old,
+                slot_index,
+                arrived_lo,
+                arrived_hi,
+                place_lo.astype(jnp.bfloat16),
+                place_hi.astype(jnp.bfloat16),
+                arrival,
+            )
+        )
 
     outgoing = send_slot[0].reshape(-1)
     filled = count_live.reshape(-1)
@@ -191,8 +195,13 @@
         for code_index in range(9):
             shifted = padded[:, code_index // 3, code_index % 3 : code_index % 3 + blocks]
             neighbours = jnp.where(codes == code_index, shifted[None], neighbours)
-        product = stiffness.astype(jnp.float32) * neighbours.astype(jnp.float32)[:, None, :, :]
-        force = jnp.sum(product, axis=(0, 2)) + jnp.dot(
+        product = None
+        for slot_index in range(slots):
+            term = stiffness[slot_index].astype(jnp.float32) * neighbours[slot_index].astype(
+                jnp.float32
+            )[None, :, :]
+            product = term if product is None else product + term
+        force = jnp.sum(product, axis=1) + jnp.dot(
             strain_map.T, history, precision=lax.Precision.HIGHEST
         )
         speeds = speeds + time_step * (scaling * (forcing - force))

time: 144 us -> 193 us (1.34)
  starting transfers between devices: 49.9 us -> 81.1 us
  Pallas kernels: 22.5 us -> 37.9 us
  waiting for transfers between devices: 31.2 us -> 38.7 us
  other arithmetic: 21.3 us -> 18.9 us
  local copies, waits for them, and re-layouts: 14.3 us -> 12 us
    ppermute x2 -> x6, starting transfers between devices: 11.7 us -> 31 us  [neighbour_exchange(): from_higher = lax.ppermute(lower_bound, axis, down)]
    pallas_call x2 -> x10, Pallas kernels: 22.5 us -> 37.9 us  [the longest x5 21.8 us: merge_arrived(): pl.pallas_call(merge_kernel, grid=(1,), in_specs=[pl.BlockSpec((1, rows_i...]
    ppermute x2 -> x6, starting transfers between devices: 3.82 us -> 11.5 us  [neighbour_exchange(): from_lower = lax.ppermute(upper_bound, axis, up)]
    ppermute x2 -> x6, waiting for transfers between devices: 0.01 us -> 4.63 us  [neighbour_exchange(): from_lower = lax.ppermute(upper_bound, axis, up)]
    ppermute x8, starting transfers between devices: 13 us -> 16.9 us  [padded_2(): after = lax.ppermute(first, axis, down)]
    unnamed x64 -> x72, local copies, waits for them, and re-layouts: 7.57 us -> 5.97 us
  transfers between devices with their start and end apart: 20 -> 28, of which waited for: 11 -> 13; matrix products, arithmetic and copies ran while one was open for 10% -> 4% of each run, Pallas kernels for 0% -> 16%
where the time goes in v7:
time: 193 us; the launch traced here: 192 us
  starting transfers between devices  81.1 us (42%)
  waiting for transfers between devices  38.7 us (20%)
  Pallas kernels  37.9 us (20%)
  other arithmetic  18.9 us (10%)
  local copies, waits for them, and re-layouts  12 us (6%)
    ppermute x6, starting transfers between devices, neighbour_exchange(): from_higher = lax.ppermute(lower_bound, axis, down)  31 us
    pallas_call x5, Pallas kernels, merge_arrived(): pl.pallas_call(merge_kernel, grid=(1,), in_specs=[pl.BlockSpec((1, rows_i...  21.8 us
    ppermute x8, starting transfers between devices, padded_2(): before = lax.ppermute(last, axis, up)  21.8 us
    ppermute x8, waiting for transfers between devices, padded_2(): after = lax.ppermute(first, axis, down)  17.8 us
    ppermute x8, starting transfers between devices, padded_2(): after = lax.ppermute(first, axis, down)  16.9 us
    pallas_call x5, Pallas kernels, gather_leaving(): pl.pallas_call(gather_kernel, grid=(1,), in_specs=[pl.BlockSpec((1, depth...  16.1 us
    ppermute x8, waiting for transfers between devices, padded_2(): before = lax.ppermute(last, axis, up)  14.9 us
    reduce_sum x4, other arithmetic, on_device(): jnp.sum(product, axis=1)  14.8 us
  transfers between devices with their start and end apart: 28, of which 13 were waited for; matrix products, arithmetic and copies ran while one was open for 4% of the time, Pallas kernels for 16%

profile of v7, /device:TPU:96, one launch (start us, length us, event | category | flops | bytes accessed | tf_op | source)
XLA Modules:
  0.0 192.0 jit_solution(5848226111430046876)
XLA Ops:
  7.3 5.9 %collective-permute-start.1 = (bf16[32,4096]{1,0:T(8,128)(2,1)}, bf16[32,4096]{1,0:T(8,128)(2,1)S(1)}, u32[]{:S(2)}, u32[]{:S(2)}) collective-permute-start(bf16[32,4096]{1,0:T(8,128)(2,1)} %get-tuple-element.16), channel_id=1, source_target_pairs={{4,0},{8,4},{12,8},{16,12},{20,16},{24,20},{28,24},{32,28},{36,32}... | collective-permute-start | bytes 786440 | tf_op jit(solution)/shard_map/ppermute | solution.py:33
  18.5 5.8 %collective-permute-start.3 = (bf16[64,1,1]{2,1,0:T(2,128)(2,1)S(1)}, bf16[64,1,1]{2,1,0:T(2,128)(2,1)S(1)}, u32[]{:S(2)}, u32[]{:S(2)}) collective-permute-start(bf16[64,1,1]{2,1,0:T(2,128)(2,1)S(1)} %get-tuple-element.69), channel_id=1, source_target_pairs={{4,0},{8,4},{12,8},{16,12},{20,16},{24,20},{28,24},{32,28},{36,32}... | collective-permute-start | bytes 392 | tf_op jit(solution)/shard_map/ppermute | solution.py:23
  32.6 3.3 %shard_map.159 = (bf16[32,4096]{1,0:T(8,128)(2,1)}, bf16[32,4096]{1,0:T(8,128)(2,1)}) custom-call(bf16[5,4096,256]{2,1,0:T(8,128)(2,1)} %bitcast.332, bf16[256,128]{1,0:T(8,128)(2,1)} %fusion.46.pick_ref), custom_call_target="tpu_custom_call" | custom-call | tf_op jit(solution)/shard_map/pallas_call | solution.py:47
  40.1 5.7 %collective-permute-start.7 = (bf16[32,4096]{1,0:T(8,128)(2,1)S(1)}, bf16[32,4096]{1,0:T(8,128)(2,1)S(1)}, u32[]{:S(2)}, u32[]{:S(2)}) collective-permute-start(bf16[32,4096]{1,0:T(8,128)(2,1)S(1)} %copy-done.26), channel_id=1, source_target_pairs={{4,0},{8,4},{12,8},{16,12},{20,16},{24,20},{28,24},{32,28},{36,32}... | collective-permute-start | bytes 786440 | tf_op jit(solution)/shard_map/ppermute | solution.py:33
  48.4 4.6 %collective-permute-done.14 = f32[96,32]{0,1:T(8,128)S(1)} collective-permute-done((f32[96,32]{0,1:T(8,128)S(1)}, f32[96,32]{0,1:T(8,128)S(1)}, u32[]{:S(2)}, u32[]{:S(2)}) %collective-permute-start.14) | collective-permute-done | bytes 12320 | tf_op jit(solution)/shard_map/ppermute | solution.py:32
  56.4 3.4 %collective-permute-start.5 = (bf16[64,1,258]{2,1,0:T(2,128)(2,1)S(1)}, bf16[64,1,258]{2,1,0:T(2,128)(2,1)S(1)}, u32[]{:S(2)}, u32[]{:S(2)}) collective-permute-start(bf16[64,1,258]{2,1,0:T(2,128)(2,1)S(1)} %pad_maximum_fusion.2), channel_id=1, source_target_pairs={{0,1},{1,2},{2,3},{4,5},{5,6},{6,7},{8,9},{9,10},{10,11},{12,13},{... | collective-permute-start | bytes 99080 | tf_op jit(solution)/shard_map/ppermute | solution.py:22
  63.6 5.3 %collective-permute-done.4 = bf16[64,1,258]{2,1,0:T(2,128)(2,1)S(1)} collective-permute-done((bf16[64,1,258]{2,1,0:T(2,128)(2,1)S(1)}, bf16[64,1,258]{2,1,0:T(2,128)(2,1)S(1)}, u32[]{:S(2)}, u32[]{:S(2)}) %collective-permute-start.4) | collective-permute-done | bytes 33056 | tf_op jit(solution)/shard_map/ppermute | solution.py:23
  71.1 5.8 %collective-permute-start.9 = (bf16[32,4096]{1,0:T(8,128)(2,1)}, bf16[32,4096]{1,0:T(8,128)(2,1)S(1)}, u32[]{:S(2)}, u32[]{:S(2)}) collective-permute-start(bf16[32,4096]{1,0:T(8,128)(2,1)} %get-tuple-element.20), channel_id=1, source_target_pairs={{4,0},{8,4},{12,8},{16,12},{20,16},{24,20},{28,24},{32,28},{36,32}... | collective-permute-start | bytes 786440 | tf_op jit(solution)/shard_map/ppermute | solution.py:33
  78.8 5.8 %collective-permute-start.11 = (bf16[32,4096]{1,0:T(8,128)(2,1)}, bf16[32,4096]{1,0:T(8,128)(2,1)S(1)}, u32[]{:S(2)}, u32[]{:S(2)}) collective-permute-start(bf16[32,4096]{1,0:T(8,128)(2,1)} %get-tuple-element.22), channel_id=1, source_target_pairs={{4,0},{8,4},{12,8},{16,12},{20,16},{24,20},{28,24},{32,28},{36,32}... | collective-permute-start | bytes 786440 | tf_op jit(solution)/shard_map/ppermute | solution.py:33
  86.6 5.9 %collective-permute-start.13 = (bf16[32,4096]{1,0:T(8,128)(2,1)}, bf16[32,4096]{1,0:T(8,128)(2,1)S(1)}, u32[]{:S(2)}, u32[]{:S(2)}) collective-permute-start(bf16[32,4096]{1,0:T(8,128)(2,1)} %get-tuple-element.24), channel_id=1, source_target_pairs={{4,0},{8,4},{12,8},{16,12},{20,16},{24,20},{28,24},{32,28},{36,32}... | collective-permute-start | bytes 786440 | tf_op jit(solution)/shard_map/ppermute | solution.py:33
  92.7 4.3 %shard_map.152 = bf16[64,64,256]{2,1,0:T(8,128)(2,1)} custom-call(bf16[5,64,64,256]{3,2,1,0:T(8,128)(2,1)} %s_ref.9, bf16[32,4096]{1,0:T(8,128)(2,1)} %copy-done.9, bf16[32,4096]{1,0:T(8,128)(2,1)} %copy-done.10, bf16[32,256]{1,0:T(8,128)(2,1)} %get-tuple-element.114.place_lo_ref, bf16[32,256]{1,0:T(8,128)(2,1)} %get-tuple-element.127.place_hi_ref, ...), custom_call_target="tpu_custom_call" | custom-call | tf_op jit(solution)/shard_map/pallas_call | solution.py:73
  97.0 4.4 %shard_map.154 = bf16[64,64,256]{2,1,0:T(8,128)(2,1)} custom-call(bf16[5,64,64,256]{3,2,1,0:T(8,128)(2,1)} %s_ref.9, bf16[32,4096]{1,0:T(8,128)(2,1)} %copy-done.11, bf16[32,4096]{1,0:T(8,128)(2,1)} %copy-done.12, bf16[32,256]{1,0:T(8,128)(2,1)} %get-tuple-element.114.place_lo_ref, bf16[32,256]{1,0:T(8,128)(2,1)} %get-tuple-element.127.place_hi_ref, ...), custom_call_target="tpu_custom_call" | custom-call | tf_op jit(solution)/shard_map/pallas_call | solution.py:73
  102.1 4.4 %shard_map.156 = bf16[64,64,256]{2,1,0:T(8,128)(2,1)} custom-call(bf16[5,64,64,256]{3,2,1,0:T(8,128)(2,1)} %s_ref.9, bf16[32,4096]{1,0:T(8,128)(2,1)} %copy-done.13, bf16[32,4096]{1,0:T(8,128)(2,1)} %copy-done.15, bf16[32,256]{1,0:T(8,128)(2,1)} %get-tuple-element.114.place_lo_ref, bf16[32,256]{1,0:T(8,128)(2,1)} %get-tuple-element.127.place_hi_ref, ...), custom_call_target="tpu_custom_call" | custom-call | tf_op jit(solution)/shard_map/pallas_call | solution.py:73
  107.9 4.4 %shard_map.158 = bf16[64,64,256]{2,1,0:T(8,128)(2,1)} custom-call(bf16[5,64,64,256]{3,2,1,0:T(8,128)(2,1)} %s_ref.9, bf16[32,4096]{1,0:T(8,128)(2,1)} %copy-done.14, bf16[32,4096]{1,0:T(8,128)(2,1)} %copy-done.17, bf16[32,256]{1,0:T(8,128)(2,1)} %get-tuple-element.114.place_lo_ref, bf16[32,256]{1,0:T(8,128)(2,1)} %get-tuple-element.127.place_hi_ref, ...), custom_call_target="tpu_custom_call" | custom-call | tf_op jit(solution)/shard_map/pallas_call | solution.py:73
  113.7 4.3 %shard_map.160 = bf16[64,64,256]{2,1,0:T(8,128)(2,1)} custom-call(bf16[5,64,64,256]{3,2,1,0:T(8,128)(2,1)} %s_ref.9, bf16[32,4096]{1,0:T(8,128)(2,1)} %copy-done.16, bf16[32,4096]{1,0:T(8,128)(2,1)} %copy-done.18, bf16[32,256]{1,0:T(8,128)(2,1)} %get-tuple-element.114.place_lo_ref, bf16[32,256]{1,0:T(8,128)(2,1)} %get-tuple-element.127.place_hi_ref, ...), custom_call_target="tpu_custom_call" | custom-call | tf_op jit(solution)/shard_map/pallas_call | solution.py:73
  118.1 6.4 %fusion.4 = f32[64,256]{1,0:T(8,128)S(1)} fusion(bf16[64,64,256]{2,1,0:T(8,128)(2,1)S(1)} %copy-done.1, bf16[64,64,256]{2,1,0:T(8,128)(2,1)} %shard_map.154, bf16[64,64,256]{2,1,0:T(8,128)(2,1)} %shard_map.156, bf16[64,64,256]{2,1,0:T(8,128)(2,1)} %shard_map.158, bf16[64,64,256]{2,1,0:T(8,128)(2,1)} %shard_map.160, f32[64,256]{1,0:T(8,128)S(1)} %get-tuple-element.54, ...), kind=kLoop, calls=%fused_computation.29 | loop fusion | flops 15712256 | bytes 10878976 | tf_op jit(solution)/shard_map/reduce_sum | solution.py:204
  129.4 4.5 %collective-permute-done.16 = bf16[64,1,1]{2,0,1:T(8,128)(2,1)S(1)} collective-permute-done((bf16[64,1,1]{2,0,1:T(8,128)(2,1)S(1)}, bf16[64,1,1]{2,0,1:T(8,128)(2,1)S(1)}, u32[]{:S(2)}, u32[]{:S(2)}) %collective-permute-start.16) | collective-permute-done | bytes 160 | tf_op jit(solution)/shard_map/ppermute | solution.py:22
  134.1 3.9 %collective-permute-start.19 = (bf16[64,1,258]{2,0,1:T(8,128)(2,1)S(1)}, bf16[64,1,258]{2,0,1:T(8,128)(2,1)S(1)}, u32[]{:S(2)}, u32[]{:S(2)}) collective-permute-start(bf16[64,1,258]{2,0,1:T(8,128)(2,1)S(1)} %pad_maximum_fusion.5), channel_id=1, source_target_pairs={{0,1},{1,2},{2,3},{4,5},{5,6},{6,7},{8,9},{9,10},{10,11},{12,13},{... | collective-permute-start | bytes 99080 | tf_op jit(solution)/shard_map/ppermute | solution.py:22
  139.8 4.2 %collective-permute-done.18 = bf16[64,1,258]{2,0,1:T(8,128)(2,1)S(1)} collective-permute-done((bf16[64,1,258]{2,0,1:T(8,128)(2,1)S(1)}, bf16[64,1,258]{2,0,1:T(8,128)(2,1)S(1)}, u32[]{:S(2)}, u32[]{:S(2)}) %collective-permute-start.18) | collective-permute-done | bytes 33056 | tf_op jit(solution)/shard_map/ppermute | solution.py:23
  152.0 4.5 %collective-permute-done.20 = bf16[64,1,1]{2,0,1:T(8,128)(2,1)S(1)} collective-permute-done((bf16[64,1,1]{2,0,1:T(8,128)(2,1)S(1)}, bf16[64,1,1]{2,0,1:T(8,128)(2,1)S(1)}, u32[]{:S(2)}, u32[]{:S(2)}) %collective-permute-start.20) | collective-permute-done | bytes 160 | tf_op jit(solution)/shard_map/ppermute | solution.py:22
  156.6 3.4 %collective-permute-start.23 = (bf16[64,1,258]{2,0,1:T(8,128)(2,1)S(1)}, bf16[64,1,258]{2,0,1:T(8,128)(2,1)S(1)}, u32[]{:S(2)}, u32[]{:S(2)}) collective-permute-start(bf16[64,1,258]{2,0,1:T(8,128)(2,1)S(1)} %pad_maximum_fusion.6), channel_id=1, source_target_pairs={{0,1},{1,2},{2,3},{4,5},{5,6},{6,7},{8,9},{9,10},{10,11},{12,13},{... | collective-permute-start | bytes 99080 | tf_op jit(solution)/shard_map/ppermute | solution.py:22
  161.8 4.2 %collective-permute-done.22 = bf16[64,1,258]{2,0,1:T(8,128)(2,1)S(1)} collective-permute-done((bf16[64,1,258]{2,0,1:T(8,128)(2,1)S(1)}, bf16[64,1,258]{2,0,1:T(8,128)(2,1)S(1)}, u32[]{:S(2)}, u32[]{:S(2)}) %collective-permute-start.22) | collective-permute-done | bytes 33056 | tf_op jit(solution)/shard_map/ppermute | solution.py:23
  173.9 4.5 %collective-permute-done.24 = bf16[64,1,1]{2,0,1:T(8,128)(2,1)S(1)} collective-permute-done((bf16[64,1,1]{2,0,1:T(8,128)(2,1)S(1)}, bf16[64,1,1]{2,0,1:T(8,128)(2,1)S(1)}, u32[]{:S(2)}, u32[]{:S(2)}) %collective-permute-start.24) | collective-permute-done | bytes 160 | tf_op jit(solution)/shard_map/ppermute | solution.py:22
  182.3 4.2 %collective-permute-done.26 = bf16[64,1,258]{2,0,1:T(8,128)(2,1)S(1)} collective-permute-done((bf16[64,1,258]{2,0,1:T(8,128)(2,1)S(1)}, bf16[64,1,258]{2,0,1:T(8,128)(2,1)S(1)}, u32[]{:S(2)}, u32[]{:S(2)}) %collective-permute-start.26) | collective-permute-done | bytes 33056 | tf_op jit(solution)/shard_map/ppermute | solution.py:23
  (191 shorter events, 77.4 us)
Async XLA Ops:
  5.4 65.7 %collective-permute-start = (bf16[32,4096]{1,0:T(8,128)(2,1)}, bf16[32,4096]{1,0:T(8,128)(2,1)S(1)}, u32[]{:S(2)}, u32[]{:S(2)}) collective-permute-start(bf16[32,4096]{1,0:T(8,128)(2,1)} %get-tuple-element.15), channel_id=1, source_target_pairs={{0,4},{4,8},{8,12},{12,16},{16,20},{20,24},{24,28},{28,32},{32,36}... | collective-permute-start | bytes 786440 | tf_op jit(solution)/shard_map/ppermute | solution.py:32
  7.3 69.6 %collective-permute-start.1 = (bf16[32,4096]{1,0:T(8,128)(2,1)}, bf16[32,4096]{1,0:T(8,128)(2,1)S(1)}, u32[]{:S(2)}, u32[]{:S(2)}) collective-permute-start(bf16[32,4096]{1,0:T(8,128)(2,1)} %get-tuple-element.16), channel_id=1, source_target_pairs={{4,0},{8,4},{12,8},{16,12},{20,16},{24,20},{28,24},{32,28},{36,32}... | collective-permute-start | bytes 786440 | tf_op jit(solution)/shard_map/ppermute | solution.py:33
  16.4 62.4 %collective-permute-start.6 = (bf16[32,4096]{1,0:T(8,128)(2,1)}, bf16[32,4096]{1,0:T(8,128)(2,1)S(1)}, u32[]{:S(2)}, u32[]{:S(2)}) collective-permute-start(bf16[32,4096]{1,0:T(8,128)(2,1)} %get-tuple-element.17), channel_id=1, source_target_pairs={{0,4},{4,8},{8,12},{12,16},{16,20},{20,24},{24,28},{28,32},{32,36}... | collective-permute-start | bytes 786440 | tf_op jit(solution)/shard_map/ppermute | solution.py:32
  18.5 21.6 %collective-permute-start.3 = (bf16[64,1,1]{2,1,0:T(2,128)(2,1)S(1)}, bf16[64,1,1]{2,1,0:T(2,128)(2,1)S(1)}, u32[]{:S(2)}, u32[]{:S(2)}) collective-permute-start(bf16[64,1,1]{2,1,0:T(2,128)(2,1)S(1)} %get-tuple-element.69), channel_id=1, source_target_pairs={{4,0},{8,4},{12,8},{16,12},{20,16},{24,20},{28,24},{32,28},{36,32}... | collective-permute-start | bytes 392 | tf_op jit(solution)/shard_map/ppermute | solution.py:23
  24.2 21.6 %collective-permute-start.2 = (bf16[64,1,1]{2,1,0:T(2,128)(2,1)S(1)}, bf16[64,1,1]{2,1,0:T(2,128)(2,1)S(1)}, u32[]{:S(2)}, u32[]{:S(2)}) collective-permute-start(bf16[64,1,1]{2,1,0:T(2,128)(2,1)S(1)} %get-tuple-element.68), channel_id=1, source_target_pairs={{0,4},{4,8},{8,12},{12,16},{16,20},{20,24},{24,28},{28,32},{32,36}... | collective-permute-start | bytes 392 | tf_op jit(solution)/shard_map/ppermute | solution.py:22
  40.1 44.5 %collective-permute-start.7 = (bf16[32,4096]{1,0:T(8,128)(2,1)S(1)}, bf16[32,4096]{1,0:T(8,128)(2,1)S(1)}, u32[]{:S(2)}, u32[]{:S(2)}) collective-permute-start(bf16[32,4096]{1,0:T(8,128)(2,1)S(1)} %copy-done.26), channel_id=1, source_target_pairs={{4,0},{8,4},{12,8},{16,12},{20,16},{24,20},{28,24},{32,28},{36,32}... | collective-permute-start | bytes 786440 | tf_op jit(solution)/shard_map/ppermute | solution.py:33
  45.9 7.2 %collective-permute-start.14 = (f32[96,32]{0,1:T(8,128)S(1)}, f32[96,32]{0,1:T(8,128)S(1)}, u32[]{:S(2)}, u32[]{:S(2)}) collective-permute-start(f32[96,32]{0,1:T(8,128)S(1)} %get-tuple-element.65), channel_id=1, source_target_pairs={{0,4},{4,8},{8,12},{12,16},{16,20},{20,24},{24,28},{28,32},{32,36}... | collective-permute-start | bytes 36872 | tf_op jit(solution)/shard_map/ppermute | solution.py:32
  56.4 5.6 %collective-permute-start.5 = (bf16[64,1,258]{2,1,0:T(2,128)(2,1)S(1)}, bf16[64,1,258]{2,1,0:T(2,128)(2,1)S(1)}, u32[]{:S(2)}, u32[]{:S(2)}) collective-permute-start(bf16[64,1,258]{2,1,0:T(2,128)(2,1)S(1)} %pad_maximum_fusion.2), channel_id=1, source_target_pairs={{0,1},{1,2},{2,3},{4,5},{5,6},{6,7},{8,9},{9,10},{10,11},{12,13},{... | collective-permute-start | bytes 99080 | tf_op jit(solution)/shard_map/ppermute | solution.py:22
  62.0 6.9 %collective-permute-start.4 = (bf16[64,1,258]{2,1,0:T(2,128)(2,1)S(1)}, bf16[64,1,258]{2,1,0:T(2,128)(2,1)S(1)}, u32[]{:S(2)}, u32[]{:S(2)}) collective-permute-start(bf16[64,1,258]{2,1,0:T(2,128)(2,1)S(1)} %pad_maximum_fusion.2), channel_id=1, source_target_pairs={{1,0},{2,1},{3,2},{5,4},{6,5},{7,6},{9,8},{10,9},{11,10},{13,12},{... | collective-permute-start | bytes 99080 | tf_op jit(solution)/shard_map/ppermute | solution.py:23
  68.9 17.7 %collective-permute-start.8 = (bf16[32,4096]{1,0:T(8,128)(2,1)}, bf16[32,4096]{1,0:T(8,128)(2,1)S(1)}, u32[]{:S(2)}, u32[]{:S(2)}) collective-permute-start(bf16[32,4096]{1,0:T(8,128)(2,1)} %get-tuple-element.19), channel_id=1, source_target_pairs={{0,4},{4,8},{8,12},{12,16},{16,20},{20,24},{24,28},{28,32},{32,36}... | collective-permute-start | bytes 786440 | tf_op jit(solution)/shard_map/ppermute | solution.py:32
  71.1 30.3 %collective-permute-start.9 = (bf16[32,4096]{1,0:T(8,128)(2,1)}, bf16[32,4096]{1,0:T(8,128)(2,1)S(1)}, u32[]{:S(2)}, u32[]{:S(2)}) collective-permute-start(bf16[32,4096]{1,0:T(8,128)(2,1)} %get-tuple-element.20), channel_id=1, source_target_pairs={{4,0},{8,4},{12,8},{16,12},{20,16},{24,20},{28,24},{32,28},{36,32}... | collective-permute-start | bytes 786440 | tf_op jit(solution)/shard_map/ppermute | solution.py:33
  76.9 29.6 %collective-permute-start.10 = (bf16[32,4096]{1,0:T(8,128)(2,1)}, bf16[32,4096]{1,0:T(8,128)(2,1)S(1)}, u32[]{:S(2)}, u32[]{:S(2)}) collective-permute-start(bf16[32,4096]{1,0:T(8,128)(2,1)} %get-tuple-element.21), channel_id=1, source_target_pairs={{0,4},{4,8},{8,12},{12,16},{16,20},{20,24},{24,28},{28,32},{32,36}... | collective-permute-start | bytes 786440 | tf_op jit(solution)/shard_map/ppermute | solution.py:32
  78.8 27.6 %collective-permute-start.11 = (bf16[32,4096]{1,0:T(8,128)(2,1)}, bf16[32,4096]{1,0:T(8,128)(2,1)S(1)}, u32[]{:S(2)}, u32[]{:S(2)}) collective-permute-start(bf16[32,4096]{1,0:T(8,128)(2,1)} %get-tuple-element.22), channel_id=1, source_target_pairs={{4,0},{8,4},{12,8},{16,12},{20,16},{24,20},{28,24},{32,28},{36,32}... | collective-permute-start | bytes 786440 | tf_op jit(solution)/shard_map/ppermute | solution.py:33
  84.6 27.7 %collective-permute-start.12 = (bf16[32,4096]{1,0:T(8,128)(2,1)}, bf16[32,4096]{1,0:T(8,128)(2,1)S(1)}, u32[]{:S(2)}, u32[]{:S(2)}) collective-permute-start(bf16[32,4096]{1,0:T(8,128)(2,1)} %get-tuple-element.23), channel_id=1, source_target_pairs={{0,4},{4,8},{8,12},{12,16},{16,20},{20,24},{24,28},{28,32},{32,36}... | collective-permute-start | bytes 786440 | tf_op jit(solution)/shard_map/ppermute | solution.py:32
  86.6 25.7 %collective-permute-start.13 = (bf16[32,4096]{1,0:T(8,128)(2,1)}, bf16[32,4096]{1,0:T(8,128)(2,1)S(1)}, u32[]{:S(2)}, u32[]{:S(2)}) collective-permute-start(bf16[32,4096]{1,0:T(8,128)(2,1)} %get-tuple-element.24), channel_id=1, source_target_pairs={{4,0},{8,4},{12,8},{16,12},{20,16},{24,20},{28,24},{32,28},{36,32}... | collective-permute-start | bytes 786440 | tf_op jit(solution)/shard_map/ppermute | solution.py:33
  126.8 7.2 %collective-permute-start.16 = (bf16[64,1,1]{2,0,1:T(8,128)(2,1)S(1)}, bf16[64,1,1]{2,0,1:T(8,128)(2,1)S(1)}, u32[]{:S(2)}, u32[]{:S(2)}) collective-permute-start(bf16[64,1,1]{2,0,1:T(8,128)(2,1)S(1)} %get-tuple-element.100), channel_id=1, source_target_pairs={{0,4},{4,8},{8,12},{12,16},{16,20},{20,24},{24,28},{28,32},{32,36}... | collective-permute-start | bytes 392 | tf_op jit(solution)/shard_map/ppermute | solution.py:22
  134.1 5.7 %collective-permute-start.19 = (bf16[64,1,258]{2,0,1:T(8,128)(2,1)S(1)}, bf16[64,1,258]{2,0,1:T(8,128)(2,1)S(1)}, u32[]{:S(2)}, u32[]{:S(2)}) collective-permute-start(bf16[64,1,258]{2,0,1:T(8,128)(2,1)S(1)} %pad_maximum_fusion.5), channel_id=1, source_target_pairs={{0,1},{1,2},{2,3},{4,5},{5,6},{6,7},{8,9},{9,10},{10,11},{12,13},{... | collective-permute-start | bytes 99080 | tf_op jit(solution)/shard_map/ppermute | solution.py:22
  138.0 6.0 %collective-permute-start.18 = (bf16[64,1,258]{2,0,1:T(8,128)(2,1)S(1)}, bf16[64,1,258]{2,0,1:T(8,128)(2,1)S(1)}, u32[]{:S(2)}, u32[]{:S(2)}) collective-permute-start(bf16[64,1,258]{2,0,1:T(8,128)(2,1)S(1)} %pad_maximum_fusion.5), channel_id=1, source_target_pairs={{1,0},{2,1},{3,2},{5,4},{6,5},{7,6},{9,8},{10,9},{11,10},{13,12},{... | collective-permute-start | bytes 99080 | tf_op jit(solution)/shard_map/ppermute | solution.py:23
  149.3 7.2 %collective-permute-start.20 = (bf16[64,1,1]{2,0,1:T(8,128)(2,1)S(1)}, bf16[64,1,1]{2,0,1:T(8,128)(2,1)S(1)}, u32[]{:S(2)}, u32[]{:S(2)}) collective-permute-start(bf16[64,1,1]{2,0,1:T(8,128)(2,1)S(1)} %get-tuple-element.94), channel_id=1, source_target_pairs={{0,4},{4,8},{8,12},{12,16},{16,20},{20,24},{24,28},{28,32},{32,36}... | collective-permute-start | bytes 392 | tf_op jit(solution)/shard_map/ppermute | solution.py:22
  156.6 5.1 %collective-permute-start.23 = (bf16[64,1,258]{2,0,1:T(8,128)(2,1)S(1)}, bf16[64,1,258]{2,0,1:T(8,128)(2,1)S(1)}, u32[]{:S(2)}, u32[]{:S(2)}) collective-permute-start(bf16[64,1,258]{2,0,1:T(8,128)(2,1)S(1)} %pad_maximum_fusion.6), channel_id=1, source_target_pairs={{0,1},{1,2},{2,3},{4,5},{5,6},{6,7},{8,9},{9,10},{10,11},{12,13},{... | collective-permute-start | bytes 99080 | tf_op jit(solution)/shard_map/ppermute | solution.py:22
  160.0 6.0 %collective-permute-start.22 = (bf16[64,1,258]{2,0,1:T(8,128)(2,1)S(1)}, bf16[64,1,258]{2,0,1:T(8,128)(2,1)S(1)}, u32[]{:S(2)}, u32[]{:S(2)}) collective-permute-start(bf16[64,1,258]{2,0,1:T(8,128)(2,1)S(1)} %pad_maximum_fusion.6), channel_id=1, source_target_pairs={{1,0},{2,1},{3,2},{5,4},{6,5},{7,6},{9,8},{10,9},{11,10},{13,12},{... | collective-permute-start | bytes 99080 | tf_op jit(solution)/shard_map/ppermute | solution.py:23
  169.4 4.5 %collective-permute-start.25 = (bf16[64,1,1]{2,0,1:T(8,128)(2,1)S(1)}, bf16[64,1,1]{2,0,1:T(8,128)(2,1)S(1)}, u32[]{:S(2)}, u32[]{:S(2)}) collective-permute-start(bf16[64,1,1]{2,0,1:T(8,128)(2,1)S(1)} %get-tuple-element.91), channel_id=1, source_target_pairs={{4,0},{8,4},{12,8},{16,12},{20,16},{24,20},{28,24},{32,28},{36,32}... | collective-permute-start | bytes 392 | tf_op jit(solution)/shard_map/ppermute | solution.py:23
  171.3 7.2 %collective-permute-start.24 = (bf16[64,1,1]{2,0,1:T(8,128)(2,1)S(1)}, bf16[64,1,1]{2,0,1:T(8,128)(2,1)S(1)}, u32[]{:S(2)}, u32[]{:S(2)}) collective-permute-start(bf16[64,1,1]{2,0,1:T(8,128)(2,1)S(1)} %get-tuple-element.90), channel_id=1, source_target_pairs={{0,4},{4,8},{8,12},{12,16},{16,20},{20,24},{24,28},{28,32},{32,36}... | collective-permute-start | bytes 392 | tf_op jit(solution)/shard_map/ppermute | solution.py:22
  180.5 6.0 %collective-permute-start.26 = (bf16[64,1,258]{2,0,1:T(8,128)(2,1)S(1)}, bf16[64,1,258]{2,0,1:T(8,128)(2,1)S(1)}, u32[]{:S(2)}, u32[]{:S(2)}) collective-permute-start(bf16[64,1,258]{2,0,1:T(8,128)(2,1)S(1)} %pad_maximum_fusion.7), channel_id=1, source_target_pairs={{1,0},{2,1},{3,2},{5,4},{6,5},{7,6},{9,8},{10,9},{11,10},{13,12},{... | collective-permute-start | bytes 99080 | tf_op jit(solution)/shard_map/ppermute | solution.py:23
  (32 other events, 404.3 us)

commit v8 on v5

--- a/solution.py
+++ b/solution.py
@@ -7,6 +7,7 @@
 
 ITERS = 4
 ROWS = 8
+SPLIT = 4
 
 
 time_step = 0.25
@@ -49,24 +50,25 @@
     out = jax.ShapeDtypeStruct((slots, width, depth), stiffness.dtype)
     return pl.pallas_call(
         gather_kernel,
-        grid=(slots,),
+        grid=(slots, SPLIT),
         in_specs=[
-            pl.BlockSpec((1, depth, blocks), lambda k: (k, 0, 0)),
-            pl.BlockSpec((width, blocks), lambda k: (0, 0)),
-            pl.BlockSpec((width, blocks), lambda k: (0, 0)),
+            pl.BlockSpec((1, depth // SPLIT, blocks), lambda k, r: (k, r, 0)),
+            pl.BlockSpec((width, blocks), lambda k, r: (0, 0)),
+            pl.BlockSpec((width, blocks), lambda k, r: (0, 0)),
         ],
         out_specs=[
-            pl.BlockSpec((1, width, depth), lambda k: (k, 0, 0)),
-            pl.BlockSpec((1, width, depth), lambda k: (k, 0, 0)),
+            pl.BlockSpec((1, width, depth // SPLIT), lambda k, r: (k, 0, r)),
+            pl.BlockSpec((1, width, depth // SPLIT), lambda k, r: (k, 0, r)),
         ],
         out_shape=[out, out],
     )(stiffness, pick_lo, pick_hi)
 
 
 def merge_kernel(s_ref, lo_ref, hi_ref, place_lo_ref, place_hi_ref, arrival_ref, out_ref):
-    placed = jnp.dot(
-        lo_ref[0].T, place_lo_ref[...], preferred_element_type=jnp.float32
-    ) + jnp.dot(hi_ref[0].T, place_hi_ref[...], preferred_element_type=jnp.float32)
+    lhs_rows = (((0,), (0,)), ((), ()))
+    placed = lax.dot_general(
+        lo_ref[0], place_lo_ref[...], lhs_rows, preferred_element_type=jnp.float32
+    ) + lax.dot_general(hi_ref[0], place_hi_ref[...], lhs_rows, preferred_element_type=jnp.float32)
     placed = placed.astype(out_ref.dtype).reshape(s_ref.shape[1:])
     out_ref[0] = jnp.where(arrival_ref[...] > 0, placed, s_ref[0])
 
@@ -77,16 +79,16 @@
     width = arrived_lo.shape[1]
     return pl.pallas_call(
         merge_kernel,
-        grid=(slots,),
+        grid=(slots, SPLIT),
         in_specs=[
-            pl.BlockSpec((1, rows_i, rows_j, blocks), lambda k: (k, 0, 0, 0)),
-            pl.BlockSpec((1, width, depth), lambda k: (k, 0, 0)),
-            pl.BlockSpec((1, width, depth), lambda k: (k, 0, 0)),
-            pl.BlockSpec((width, blocks), lambda k: (0, 0)),
-            pl.BlockSpec((width, blocks), lambda k: (0, 0)),
-            pl.BlockSpec((1, blocks), lambda k: (0, 0)),
-        ],
-        out_specs=pl.BlockSpec((1, rows_i, rows_j, blocks), lambda k: (k, 0, 0, 0)),
+            pl.BlockSpec((1, rows_i // SPLIT, rows_j, blocks), lambda k, r: (k, r, 0, 0)),
+            pl.BlockSpec((1, width, depth // SPLIT), lambda k, r: (k, 0, r)),
+            pl.BlockSpec((1, width, depth // SPLIT), lambda k, r: (k, 0, r)),
+            pl.BlockSpec((width, blocks), lambda k, r: (0, 0)),
+            pl.BlockSpec((width, blocks), lambda k, r: (0, 0)),
+            pl.BlockSpec((1, blocks), lambda k, r: (0, 0)),
+        ],
+        out_specs=pl.BlockSpec((1, rows_i // SPLIT, rows_j, blocks), lambda k, r: (k, r, 0, 0)),
         out_shape=jax.ShapeDtypeStruct(stiffness.shape, stiffness.dtype),
     )(stiffness, arrived_lo, arrived_hi, place_lo, place_hi, arrival)
 

time: 144 us -> 157 us (1.090)
  Pallas kernels: 22.5 us -> 35.6 us
    pallas_call x2, Pallas kernels: 22.5 us -> 35.6 us  [the longest x1 19 us: merge_arrived(): pl.pallas_call(merge_kernel, grid=(slots, SPLIT), in_specs=[pl.BlockSpec(...]
  transfers between devices with their start and end apart: 20 -> 20, of which waited for: 11 -> 11; matrix products, arithmetic and copies ran while one was open for 10% -> 9% of each run, Pallas kernels for 0% -> 0%
where the time goes in v8:
time: 157 us; the launch traced here: 156 us
  starting transfers between devices  49.9 us (32%)
  Pallas kernels  35.6 us (23%)
  waiting for transfers between devices  31.2 us (20%)
  other arithmetic  21.3 us (14%)
  local copies, waits for them, and re-layouts  14.3 us (9%)
  matrix products  1.85 us (1%)
    ppermute x8, starting transfers between devices, padded_2(): before = lax.ppermute(last, axis, up)  21.4 us
    pallas_call x1, Pallas kernels, merge_arrived(): pl.pallas_call(merge_kernel, grid=(slots, SPLIT), in_specs=[pl.BlockSpec(...  19 us
    ppermute x8, waiting for transfers between devices, padded_2(): after = lax.ppermute(first, axis, down)  16.7 us
    pallas_call x1, Pallas kernels, gather_leaving(): pl.pallas_call(gather_kernel, grid=(slots, SPLIT), in_specs=[pl.BlockSpec...  16.5 us
    reduce_sum x4, other arithmetic, on_device(): jnp.sum(product, axis=(0, 2))  15.3 us
    ppermute x8, waiting for transfers between devices, padded_2(): before = lax.ppermute(last, axis, up)  14.5 us
    ppermute x8, starting transfers between devices, padded_2(): after = lax.ppermute(first, axis, down)  13 us
    ppermute x2, starting transfers between devices, neighbour_exchange(): from_higher = lax.ppermute(lower_bound, axis, down)  11.7 us
  transfers between devices with their start and end apart: 20, of which 11 were waited for; matrix products, arithmetic and copies ran while one was open for 9% of the time, Pallas kernels for 0%

profile of v8, /device:TPU:96, one launch (start us, length us, event | category | flops | bytes accessed | tf_op | source)
XLA Modules:
  0.0 155.6 jit_solution(2985306203117972237)
XLA Ops:
  2.2 16.5 %shard_map.151 = (bf16[5,32,4096]{2,1,0:T(8,128)(2,1)}, bf16[5,32,4096]{2,1,0:T(8,128)(2,1)}) custom-call(bf16[5,4096,256]{2,1,0:T(8,128)(2,1)} %bitcast.228, bf16[32,256]{1,0:T(8,128)(2,1)} %get-tuple-element.91.lo_ref, bf16[32,256]{1,0:T(8,128)(2,1)} %get-tuple-element.92.hi_ref), custom_call_target="tpu_custom_call" | custom-call | tf_op jit(solution)/shard_map/pallas_call | solution.py:51
  20.6 5.8 %collective-permute-start.1 = (bf16[5,32,4096]{2,1,0:T(8,128)(2,1)}, bf16[5,32,4096]{2,1,0:T(8,128)(2,1)S(1)}, u32[]{:S(2)}, u32[]{:S(2)}) collective-permute-start(bf16[5,32,4096]{2,1,0:T(8,128)(2,1)} %get-tuple-element.8), channel_id=1, source_target_pairs={{4,0},{8,4},{12,8},{16,12},{20,16},{24,20},{28,24},{32,28},{36,32}... | collective-permute-start | bytes 3932168 | tf_op jit(solution)/shard_map/ppermute | solution.py:34
  26.6 1.9 %collective-permute-start.3 = (bf16[64,1,1]{2,1,0:T(2,128)(2,1)S(1)}, bf16[64,1,1]{2,1,0:T(2,128)(2,1)S(1)}, u32[]{:S(2)}, u32[]{:S(2)}) collective-permute-start(bf16[64,1,1]{2,1,0:T(2,128)(2,1)S(1)} %get-tuple-element.33), channel_id=1, source_target_pairs={{4,0},{8,4},{12,8},{16,12},{20,16},{24,20},{28,24},{32,28},{36,32}... | collective-permute-start | bytes 392 | tf_op jit(solution)/shard_map/ppermute | solution.py:24
  28.5 2.4 %collective-permute-start.2 = (bf16[64,1,1]{2,1,0:T(2,128)(2,1)S(1)}, bf16[64,1,1]{2,1,0:T(2,128)(2,1)S(1)}, u32[]{:S(2)}, u32[]{:S(2)}) collective-permute-start(bf16[64,1,1]{2,1,0:T(2,128)(2,1)S(1)} %get-tuple-element.32), channel_id=1, source_target_pairs={{0,4},{4,8},{8,12},{12,16},{16,20},{20,24},{24,28},{28,32},{32,36}... | collective-permute-start | bytes 392 | tf_op jit(solution)/shard_map/ppermute | solution.py:23
  42.1 5.9 %collective-permute-start.7 = (f32[96,32]{0,1:T(8,128)S(1)}, f32[96,32]{0,1:T(8,128)S(1)}, u32[]{:S(2)}, u32[]{:S(2)}) collective-permute-start(f32[96,32]{0,1:T(8,128)S(1)} %get-tuple-element.28), channel_id=1, source_target_pairs={{4,0},{8,4},{12,8},{16,12},{20,16},{24,20},{28,24},{32,28},{36,32}... | collective-permute-start | bytes 36872 | tf_op jit(solution)/shard_map/ppermute | solution.py:34
  48.9 3.4 %collective-permute-start.5 = (bf16[64,1,258]{2,1,0:T(2,128)(2,1)}, bf16[64,1,258]{2,1,0:T(2,128)(2,1)S(1)}, u32[]{:S(2)}, u32[]{:S(2)}) collective-permute-start(bf16[64,1,258]{2,1,0:T(2,128)(2,1)} %pad_maximum_fusion.2), channel_id=1, source_target_pairs={{0,1},{1,2},{2,3},{4,5},{5,6},{6,7},{8,9},{9,10},{10,11},{12,13},{... | collective-permute-start | bytes 99080 | tf_op jit(solution)/shard_map/ppermute | solution.py:23
  57.2 2.7 %collective-permute-done.4 = bf16[64,1,258]{2,1,0:T(2,128)(2,1)S(1)} collective-permute-done((bf16[64,1,258]{2,1,0:T(2,128)(2,1)}, bf16[64,1,258]{2,1,0:T(2,128)(2,1)S(1)}, u32[]{:S(2)}, u32[]{:S(2)}) %collective-permute-start.4) | collective-permute-done | bytes 33056 | tf_op jit(solution)/shard_map/ppermute | solution.py:24
  62.8 19.0 %shard_map.152 = bf16[5,64,64,256]{3,2,1,0:T(8,128)(2,1)} custom-call(bf16[5,64,64,256]{3,2,1,0:T(8,128)(2,1)} %s_ref.1, bf16[5,32,4096]{2,1,0:T(8,128)(2,1)} %copy-done.2, bf16[5,32,4096]{2,1,0:T(8,128)(2,1)} %copy-done.3, bf16[32,256]{1,0:T(8,128)(2,1)} %get-tuple-element.78.place_lo_ref, bf16[32,256]{1,0:T(8,128)(2,1)} %get-tuple-element.93.place_hi_ref, ...), custom_call_target="tpu_custom_call" | custom-call | tf_op jit(solution)/shard_map/pallas_call | solution.py:80
  82.0 6.9 %fusion = f32[64,256]{1,0:T(8,128)S(1)} fusion(bf16[5,64,64,256]{3,2,1,0:T(8,128)(2,1)} %shard_map.152, f32[5,64,256]{2,1,0:T(8,128)S(1)} %select_convert_fusion.3), kind=kLoop, calls=%fused_computation.9 | loop fusion | flops 15712256 | bytes 10878976 | tf_op jit(solution)/shard_map/reduce_sum | solution.py:197
  91.2 2.4 %collective-permute-start.8 = (bf16[64,1,1]{2,0,1:T(8,128)(2,1)S(1)}, bf16[64,1,1]{2,0,1:T(8,128)(2,1)S(1)}, u32[]{:S(2)}, u32[]{:S(2)}) collective-permute-start(bf16[64,1,1]{2,0,1:T(8,128)(2,1)S(1)} %get-tuple-element.64), channel_id=1, source_target_pairs={{0,4},{4,8},{8,12},{12,16},{16,20},{20,24},{24,28},{28,32},{32,36}... | collective-permute-start | bytes 392 | tf_op jit(solution)/shard_map/ppermute | solution.py:23
  93.9 4.6 %collective-permute-done.8 = bf16[64,1,1]{2,0,1:T(8,128)(2,1)S(1)} collective-permute-done((bf16[64,1,1]{2,0,1:T(8,128)(2,1)S(1)}, bf16[64,1,1]{2,0,1:T(8,128)(2,1)S(1)}, u32[]{:S(2)}, u32[]{:S(2)}) %collective-permute-start.8) | collective-permute-done | bytes 160 | tf_op jit(solution)/shard_map/ppermute | solution.py:23
  98.5 3.4 %collective-permute-start.11 = (bf16[64,1,258]{2,0,1:T(8,128)(2,1)S(1)}, bf16[64,1,258]{2,0,1:T(8,128)(2,1)S(1)}, u32[]{:S(2)}, u32[]{:S(2)}) collective-permute-start(bf16[64,1,258]{2,0,1:T(8,128)(2,1)S(1)} %pad_maximum_fusion.5), channel_id=1, source_target_pairs={{0,1},{1,2},{2,3},{4,5},{5,6},{6,7},{8,9},{9,10},{10,11},{12,13},{... | collective-permute-start | bytes 99080 | tf_op jit(solution)/shard_map/ppermute | solution.py:23
  103.7 4.2 %collective-permute-done.10 = bf16[64,1,258]{2,0,1:T(8,128)(2,1)S(1)} collective-permute-done((bf16[64,1,258]{2,0,1:T(8,128)(2,1)S(1)}, bf16[64,1,258]{2,0,1:T(8,128)(2,1)S(1)}, u32[]{:S(2)}, u32[]{:S(2)}) %collective-permute-start.10) | collective-permute-done | bytes 33056 | tf_op jit(solution)/shard_map/ppermute | solution.py:24
  108.2 2.8 %fusion.1 = f32[64,256]{1,0:T(8,128)S(1)} fusion(bf16[5,64,64,256]{3,2,1,0:T(8,128)(2,1)S(1)} %copy-done.1, f32[5,64,256]{2,1,0:T(8,128)S(1)} %select_convert_fusion.2), kind=kLoop, calls=%fused_computation.10 | loop fusion | flops 15712256 | bytes 10878976 | tf_op jit(solution)/shard_map/reduce_sum | solution.py:197
  113.3 2.4 %collective-permute-start.12 = (bf16[64,1,1]{2,0,1:T(8,128)(2,1)S(1)}, bf16[64,1,1]{2,0,1:T(8,128)(2,1)S(1)}, u32[]{:S(2)}, u32[]{:S(2)}) collective-permute-start(bf16[64,1,1]{2,0,1:T(8,128)(2,1)S(1)} %get-tuple-element.58), channel_id=1, source_target_pairs={{0,4},{4,8},{8,12},{12,16},{16,20},{20,24},{24,28},{28,32},{32,36}... | collective-permute-start | bytes 392 | tf_op jit(solution)/shard_map/ppermute | solution.py:23
  115.9 4.5 %collective-permute-done.12 = bf16[64,1,1]{2,0,1:T(8,128)(2,1)S(1)} collective-permute-done((bf16[64,1,1]{2,0,1:T(8,128)(2,1)S(1)}, bf16[64,1,1]{2,0,1:T(8,128)(2,1)S(1)}, u32[]{:S(2)}, u32[]{:S(2)}) %collective-permute-start.12) | collective-permute-done | bytes 160 | tf_op jit(solution)/shard_map/ppermute | solution.py:23
  120.5 3.1 %collective-permute-start.15 = (bf16[64,1,258]{2,0,1:T(8,128)(2,1)S(1)}, bf16[64,1,258]{2,0,1:T(8,128)(2,1)S(1)}, u32[]{:S(2)}, u32[]{:S(2)}) collective-permute-start(bf16[64,1,258]{2,0,1:T(8,128)(2,1)S(1)} %pad_maximum_fusion.6), channel_id=1, source_target_pairs={{0,1},{1,2},{2,3},{4,5},{5,6},{6,7},{8,9},{9,10},{10,11},{12,13},{... | collective-permute-start | bytes 99080 | tf_op jit(solution)/shard_map/ppermute | solution.py:23
  125.5 4.2 %collective-permute-done.14 = bf16[64,1,258]{2,0,1:T(8,128)(2,1)S(1)} collective-permute-done((bf16[64,1,258]{2,0,1:T(8,128)(2,1)S(1)}, bf16[64,1,258]{2,0,1:T(8,128)(2,1)S(1)}, u32[]{:S(2)}, u32[]{:S(2)}) %collective-permute-start.14) | collective-permute-done | bytes 33056 | tf_op jit(solution)/shard_map/ppermute | solution.py:24
  129.8 2.8 %fusion.2 = f32[64,256]{1,0:T(8,128)S(1)} fusion(bf16[5,64,64,256]{3,2,1,0:T(8,128)(2,1)S(1)} %copy-done.1, f32[5,64,256]{2,1,0:T(8,128)S(1)} %select_convert_fusion.1), kind=kLoop, calls=%fused_computation.11 | loop fusion | flops 15712256 | bytes 10878976 | tf_op jit(solution)/shard_map/reduce_sum | solution.py:197
  134.9 2.4 %collective-permute-start.16 = (bf16[64,1,1]{2,0,1:T(8,128)(2,1)S(1)}, bf16[64,1,1]{2,0,1:T(8,128)(2,1)S(1)}, u32[]{:S(2)}, u32[]{:S(2)}) collective-permute-start(bf16[64,1,1]{2,0,1:T(8,128)(2,1)S(1)} %get-tuple-element.54), channel_id=1, source_target_pairs={{0,4},{4,8},{8,12},{12,16},{16,20},{20,24},{24,28},{28,32},{32,36}... | collective-permute-start | bytes 392 | tf_op jit(solution)/shard_map/ppermute | solution.py:23
  137.5 4.5 %collective-permute-done.16 = bf16[64,1,1]{2,0,1:T(8,128)(2,1)S(1)} collective-permute-done((bf16[64,1,1]{2,0,1:T(8,128)(2,1)S(1)}, bf16[64,1,1]{2,0,1:T(8,128)(2,1)S(1)}, u32[]{:S(2)}, u32[]{:S(2)}) %collective-permute-start.16) | collective-permute-done | bytes 160 | tf_op jit(solution)/shard_map/ppermute | solution.py:23
  142.2 1.9 %collective-permute-start.19 = (bf16[64,1,258]{2,0,1:T(8,128)(2,1)S(1)}, bf16[64,1,258]{2,0,1:T(8,128)(2,1)S(1)}, u32[]{:S(2)}, u32[]{:S(2)}) collective-permute-start(bf16[64,1,258]{2,0,1:T(8,128)(2,1)S(1)} %pad_maximum_fusion.7), channel_id=1, source_target_pairs={{0,1},{1,2},{2,3},{4,5},{5,6},{6,7},{8,9},{9,10},{10,11},{12,13},{... | collective-permute-start | bytes 99080 | tf_op jit(solution)/shard_map/ppermute | solution.py:23
  145.9 4.2 %collective-permute-done.18 = bf16[64,1,258]{2,0,1:T(8,128)(2,1)S(1)} collective-permute-done((bf16[64,1,258]{2,0,1:T(8,128)(2,1)S(1)}, bf16[64,1,258]{2,0,1:T(8,128)(2,1)S(1)}, u32[]{:S(2)}, u32[]{:S(2)}) %collective-permute-start.18) | collective-permute-done | bytes 33056 | tf_op jit(solution)/shard_map/ppermute | solution.py:24
  150.3 2.8 %fusion.3 = f32[64,256]{1,0:T(8,128)S(1)} fusion(bf16[5,64,64,256]{3,2,1,0:T(8,128)(2,1)S(1)} %copy-done.1, f32[5,64,256]{2,1,0:T(8,128)S(1)} %select_convert_fusion), kind=kLoop, calls=%fused_computation.12 | loop fusion | flops 15712256 | bytes 10878976 | tf_op jit(solution)/shard_map/reduce_sum | solution.py:197
  (152 shorter events, 39.4 us)
Async XLA Ops:
  0.6 88.3 %copy-start = (f32[48,64]{1,0:T(8,128)S(1)}, f32[48,64]{1,0:T(8,128)}, u32[]{:S(2)}) copy-start(f32[48,64]{1,0:T(8,128)} %param.26) | copy-start | bytes 36868
  0.7 31.5 %copy-start.17 = (f32[48,256]{1,0:T(8,128)S(1)}, f32[48,256]{1,0:T(8,128)}, u32[]{:S(2)}) copy-start(f32[48,256]{1,0:T(8,128)} %param.24) | copy-start | bytes 147460
  0.7 37.4 %copy-start.19 = (s32[5,1,256]{2,1,0:T(1,128)S(1)}, s32[5,1,256]{2,1,0:T(1,128)}, u32[]{:S(2)}) copy-start(s32[5,1,256]{2,1,0:T(1,128)} %param.21) | copy-start | bytes 15364
  0.7 37.4 %copy-start.20 = (s32[1,256]{1,0:T(1,128)S(1)}, s32[1,256]{1,0:T(1,128)}, u32[]{:S(2)}) copy-start(s32[1,256]{1,0:T(1,128)} %param.22) | copy-start | bytes 3076
  18.7 42.5 %collective-permute-start = (bf16[5,32,4096]{2,1,0:T(8,128)(2,1)}, bf16[5,32,4096]{2,1,0:T(8,128)(2,1)S(1)}, u32[]{:S(2)}, u32[]{:S(2)}) collective-permute-start(bf16[5,32,4096]{2,1,0:T(8,128)(2,1)} %get-tuple-element.7), channel_id=1, source_target_pairs={{0,4},{4,8},{8,12},{12,16},{16,20},{20,24},{24,28},{28,32},{32,36}... | collective-permute-start | bytes 3932168 | tf_op jit(solution)/shard_map/ppermute | solution.py:33
  20.6 40.6 %collective-permute-start.1 = (bf16[5,32,4096]{2,1,0:T(8,128)(2,1)}, bf16[5,32,4096]{2,1,0:T(8,128)(2,1)S(1)}, u32[]{:S(2)}, u32[]{:S(2)}) collective-permute-start(bf16[5,32,4096]{2,1,0:T(8,128)(2,1)} %get-tuple-element.8), channel_id=1, source_target_pairs={{4,0},{8,4},{12,8},{16,12},{20,16},{24,20},{28,24},{32,28},{36,32}... | collective-permute-start | bytes 3932168 | tf_op jit(solution)/shard_map/ppermute | solution.py:34
  26.6 15.5 %collective-permute-start.3 = (bf16[64,1,1]{2,1,0:T(2,128)(2,1)S(1)}, bf16[64,1,1]{2,1,0:T(2,128)(2,1)S(1)}, u32[]{:S(2)}, u32[]{:S(2)}) collective-permute-start(bf16[64,1,1]{2,1,0:T(2,128)(2,1)S(1)} %get-tuple-element.33), channel_id=1, source_target_pairs={{4,0},{8,4},{12,8},{16,12},{20,16},{24,20},{28,24},{32,28},{36,32}... | collective-permute-start | bytes 392 | tf_op jit(solution)/shard_map/ppermute | solution.py:24
  28.5 19.5 %collective-permute-start.2 = (bf16[64,1,1]{2,1,0:T(2,128)(2,1)S(1)}, bf16[64,1,1]{2,1,0:T(2,128)(2,1)S(1)}, u32[]{:S(2)}, u32[]{:S(2)}) collective-permute-start(bf16[64,1,1]{2,1,0:T(2,128)(2,1)S(1)} %get-tuple-element.32), channel_id=1, source_target_pairs={{0,4},{4,8},{8,12},{12,16},{16,20},{20,24},{24,28},{28,32},{32,36}... | collective-permute-start | bytes 392 | tf_op jit(solution)/shard_map/ppermute | solution.py:23
  33.7 19.6 %collective-permute-start.6 = (f32[96,32]{0,1:T(8,128)S(1)}, f32[96,32]{0,1:T(8,128)S(1)}, u32[]{:S(2)}, u32[]{:S(2)}) collective-permute-start(f32[96,32]{0,1:T(8,128)S(1)} %get-tuple-element.29), channel_id=1, source_target_pairs={{0,4},{4,8},{8,12},{12,16},{16,20},{20,24},{24,28},{28,32},{32,36}... | collective-permute-start | bytes 36872 | tf_op jit(solution)/shard_map/ppermute | solution.py:33
  42.1 12.5 %collective-permute-start.7 = (f32[96,32]{0,1:T(8,128)S(1)}, f32[96,32]{0,1:T(8,128)S(1)}, u32[]{:S(2)}, u32[]{:S(2)}) collective-permute-start(f32[96,32]{0,1:T(8,128)S(1)} %get-tuple-element.28), channel_id=1, source_target_pairs={{4,0},{8,4},{12,8},{16,12},{20,16},{24,20},{28,24},{32,28},{36,32}... | collective-permute-start | bytes 36872 | tf_op jit(solution)/shard_map/ppermute | solution.py:34
  48.9 8.1 %collective-permute-start.5 = (bf16[64,1,258]{2,1,0:T(2,128)(2,1)}, bf16[64,1,258]{2,1,0:T(2,128)(2,1)S(1)}, u32[]{:S(2)}, u32[]{:S(2)}) collective-permute-start(bf16[64,1,258]{2,1,0:T(2,128)(2,1)} %pad_maximum_fusion.2), channel_id=1, source_target_pairs={{0,1},{1,2},{2,3},{4,5},{5,6},{6,7},{8,9},{9,10},{10,11},{12,13},{... | collective-permute-start | bytes 99080 | tf_op jit(solution)/shard_map/ppermute | solution.py:23
  53.3 6.7 %collective-permute-start.4 = (bf16[64,1,258]{2,1,0:T(2,128)(2,1)}, bf16[64,1,258]{2,1,0:T(2,128)(2,1)S(1)}, u32[]{:S(2)}, u32[]{:S(2)}) collective-permute-start(bf16[64,1,258]{2,1,0:T(2,128)(2,1)} %pad_maximum_fusion.2), channel_id=1, source_target_pairs={{1,0},{2,1},{3,2},{5,4},{6,5},{7,6},{9,8},{10,9},{11,10},{13,12},{... | collective-permute-start | bytes 99080 | tf_op jit(solution)/shard_map/ppermute | solution.py:24
  89.3 4.5 %collective-permute-start.9 = (bf16[64,1,1]{2,0,1:T(8,128)(2,1)S(1)}, bf16[64,1,1]{2,0,1:T(8,128)(2,1)S(1)}, u32[]{:S(2)}, u32[]{:S(2)}) collective-permute-start(bf16[64,1,1]{2,0,1:T(8,128)(2,1)S(1)} %get-tuple-element.65), channel_id=1, source_target_pairs={{4,0},{8,4},{12,8},{16,12},{20,16},{24,20},{28,24},{32,28},{36,32}... | collective-permute-start | bytes 392 | tf_op jit(solution)/shard_map/ppermute | solution.py:24
  91.2 7.2 %collective-permute-start.8 = (bf16[64,1,1]{2,0,1:T(8,128)(2,1)S(1)}, bf16[64,1,1]{2,0,1:T(8,128)(2,1)S(1)}, u32[]{:S(2)}, u32[]{:S(2)}) collective-permute-start(bf16[64,1,1]{2,0,1:T(8,128)(2,1)S(1)} %get-tuple-element.64), channel_id=1, source_target_pairs={{0,4},{4,8},{8,12},{12,16},{16,20},{20,24},{24,28},{28,32},{32,36}... | collective-permute-start | bytes 392 | tf_op jit(solution)/shard_map/ppermute | solution.py:23
  98.5 5.1 %collective-permute-start.11 = (bf16[64,1,258]{2,0,1:T(8,128)(2,1)S(1)}, bf16[64,1,258]{2,0,1:T(8,128)(2,1)S(1)}, u32[]{:S(2)}, u32[]{:S(2)}) collective-permute-start(bf16[64,1,258]{2,0,1:T(8,128)(2,1)S(1)} %pad_maximum_fusion.5), channel_id=1, source_target_pairs={{0,1},{1,2},{2,3},{4,5},{5,6},{6,7},{8,9},{9,10},{10,11},{12,13},{... | collective-permute-start | bytes 99080 | tf_op jit(solution)/shard_map/ppermute | solution.py:23
  101.9 6.0 %collective-permute-start.10 = (bf16[64,1,258]{2,0,1:T(8,128)(2,1)S(1)}, bf16[64,1,258]{2,0,1:T(8,128)(2,1)S(1)}, u32[]{:S(2)}, u32[]{:S(2)}) collective-permute-start(bf16[64,1,258]{2,0,1:T(8,128)(2,1)S(1)} %pad_maximum_fusion.5), channel_id=1, source_target_pairs={{1,0},{2,1},{3,2},{5,4},{6,5},{7,6},{9,8},{10,9},{11,10},{13,12},{... | collective-permute-start | bytes 99080 | tf_op jit(solution)/shard_map/ppermute | solution.py:24
  111.3 4.5 %collective-permute-start.13 = (bf16[64,1,1]{2,0,1:T(8,128)(2,1)S(1)}, bf16[64,1,1]{2,0,1:T(8,128)(2,1)S(1)}, u32[]{:S(2)}, u32[]{:S(2)}) collective-permute-start(bf16[64,1,1]{2,0,1:T(8,128)(2,1)S(1)} %get-tuple-element.59), channel_id=1, source_target_pairs={{4,0},{8,4},{12,8},{16,12},{20,16},{24,20},{28,24},{32,28},{36,32}... | collective-permute-start | bytes 392 | tf_op jit(solution)/shard_map/ppermute | solution.py:24
  113.3 7.2 %collective-permute-start.12 = (bf16[64,1,1]{2,0,1:T(8,128)(2,1)S(1)}, bf16[64,1,1]{2,0,1:T(8,128)(2,1)S(1)}, u32[]{:S(2)}, u32[]{:S(2)}) collective-permute-start(bf16[64,1,1]{2,0,1:T(8,128)(2,1)S(1)} %get-tuple-element.58), channel_id=1, source_target_pairs={{0,4},{4,8},{8,12},{12,16},{16,20},{20,24},{24,28},{28,32},{32,36}... | collective-permute-start | bytes 392 | tf_op jit(solution)/shard_map/ppermute | solution.py:23
  120.5 4.8 %collective-permute-start.15 = (bf16[64,1,258]{2,0,1:T(8,128)(2,1)S(1)}, bf16[64,1,258]{2,0,1:T(8,128)(2,1)S(1)}, u32[]{:S(2)}, u32[]{:S(2)}) collective-permute-start(bf16[64,1,258]{2,0,1:T(8,128)(2,1)S(1)} %pad_maximum_fusion.6), channel_id=1, source_target_pairs={{0,1},{1,2},{2,3},{4,5},{5,6},{6,7},{8,9},{9,10},{10,11},{12,13},{... | collective-permute-start | bytes 99080 | tf_op jit(solution)/shard_map/ppermute | solution.py:23
  123.6 6.0 %collective-permute-start.14 = (bf16[64,1,258]{2,0,1:T(8,128)(2,1)S(1)}, bf16[64,1,258]{2,0,1:T(8,128)(2,1)S(1)}, u32[]{:S(2)}, u32[]{:S(2)}) collective-permute-start(bf16[64,1,258]{2,0,1:T(8,128)(2,1)S(1)} %pad_maximum_fusion.6), channel_id=1, source_target_pairs={{1,0},{2,1},{3,2},{5,4},{6,5},{7,6},{9,8},{10,9},{11,10},{13,12},{... | collective-permute-start | bytes 99080 | tf_op jit(solution)/shard_map/ppermute | solution.py:24
  133.0 4.5 %collective-permute-start.17 = (bf16[64,1,1]{2,0,1:T(8,128)(2,1)S(1)}, bf16[64,1,1]{2,0,1:T(8,128)(2,1)S(1)}, u32[]{:S(2)}, u32[]{:S(2)}) collective-permute-start(bf16[64,1,1]{2,0,1:T(8,128)(2,1)S(1)} %get-tuple-element.55), channel_id=1, source_target_pairs={{4,0},{8,4},{12,8},{16,12},{20,16},{24,20},{28,24},{32,28},{36,32}... | collective-permute-start | bytes 392 | tf_op jit(solution)/shard_map/ppermute | solution.py:24
  134.9 7.2 %collective-permute-start.16 = (bf16[64,1,1]{2,0,1:T(8,128)(2,1)S(1)}, bf16[64,1,1]{2,0,1:T(8,128)(2,1)S(1)}, u32[]{:S(2)}, u32[]{:S(2)}) collective-permute-start(bf16[64,1,1]{2,0,1:T(8,128)(2,1)S(1)} %get-tuple-element.54), channel_id=1, source_target_pairs={{0,4},{4,8},{8,12},{12,16},{16,20},{20,24},{24,28},{28,32},{32,36}... | collective-permute-start | bytes 392 | tf_op jit(solution)/shard_map/ppermute | solution.py:23
  142.2 3.7 %collective-permute-start.19 = (bf16[64,1,258]{2,0,1:T(8,128)(2,1)S(1)}, bf16[64,1,258]{2,0,1:T(8,128)(2,1)S(1)}, u32[]{:S(2)}, u32[]{:S(2)}) collective-permute-start(bf16[64,1,258]{2,0,1:T(8,128)(2,1)S(1)} %pad_maximum_fusion.7), channel_id=1, source_target_pairs={{0,1},{1,2},{2,3},{4,5},{5,6},{6,7},{8,9},{9,10},{10,11},{12,13},{... | collective-permute-start | bytes 99080 | tf_op jit(solution)/shard_map/ppermute | solution.py:23
  144.1 6.0 %collective-permute-start.18 = (bf16[64,1,258]{2,0,1:T(8,128)(2,1)S(1)}, bf16[64,1,258]{2,0,1:T(8,128)(2,1)S(1)}, u32[]{:S(2)}, u32[]{:S(2)}) collective-permute-start(bf16[64,1,258]{2,0,1:T(8,128)(2,1)S(1)} %pad_maximum_fusion.7), channel_id=1, source_target_pairs={{1,0},{2,1},{3,2},{5,4},{6,5},{7,6},{9,8},{10,9},{11,10},{13,12},{... | collective-permute-start | bytes 99080 | tf_op jit(solution)/shard_map/ppermute | solution.py:24
  (20 other events, 394.2 us)

commit v9 on v5

--- a/solution.py
+++ b/solution.py
@@ -23,6 +23,30 @@
         after = lax.ppermute(first, axis, down)
         value = jnp.concatenate([before, value, after], axis=dim)
     return value
+
+
+def halo(rounded):
+    shafts, plies = lax.axis_size("shaft"), lax.axis_size("ply")
+
+    def receive(value, shaft_offset, ply_offset):
+        perm = [
+            (a * plies + q, (a - shaft_offset) * plies + q - ply_offset)
+            for a in range(shafts)
+            for q in range(plies)
+            if 0 <= a - shaft_offset < shafts and 0 <= q - ply_offset < plies
+        ]
+        return lax.ppermute(value, ("shaft", "ply"), perm)
+
+    first, last = rounded[:, :1], rounded[:, -1:]
+    rows = []
+    for ply_offset in (-1, 0, 1):
+        middle = rounded if ply_offset == 0 else receive(rounded, 0, ply_offset)
+        rows.append(
+            jnp.concatenate(
+                [receive(last, -1, ply_offset), middle, receive(first, 1, ply_offset)], 1
+            )
+        )
+    return jnp.stack(rows, 1)
 
 
 def neighbour_exchange(axis, lower_bound, upper_bound):
@@ -185,8 +209,7 @@
     live = jnp.arange(slots, dtype=jnp.int32)[:, None] < coupled[0][None, :]
     codes = jnp.where(live, pattern[:, 0, :], 9)[:, None, :]
     for repeat in range(ITERS):
-        rounded = moved.astype(jnp.bfloat16)[:, None, :]
-        padded = padded_2(rounded, (("shaft", 2), ("ply", 1)), 1)
+        padded = halo(moved.astype(jnp.bfloat16))
         neighbours = jnp.zeros((slots,) + moved.shape, jnp.bfloat16)
         for code_index in range(9):
             shifted = padded[:, code_index // 3, code_index % 3 : code_index % 3 + blocks]

time: 144 us -> 209 us (1.45); the launches traced: 143 us -> 205 us
  starting transfers between devices: 49.9 us -> 88.9 us
  waiting for transfers between devices: 31.2 us -> 55.2 us
    ppermute x16 -> x32, starting transfers between devices: 34.4 us -> 76.1 us  [receive(): return lax.ppermute(value, ('shaft', 'ply'), perm)]
    ppermute x2, waiting for transfers between devices: 0.01 us -> 16.4 us  [neighbour_exchange(): from_lower = lax.ppermute(upper_bound, axis, up)]
    ppermute x2, starting transfers between devices: 11.7 us -> 7.63 us  [neighbour_exchange(): from_higher = lax.ppermute(lower_bound, axis, down)]
    ppermute x2, waiting for transfers between devices: 0.01 us -> 3.86 us  [neighbour_exchange(): from_higher = lax.ppermute(lower_bound, axis, down)]
    ppermute x16 -> x32, waiting for transfers between devices: 31.2 us -> 34.9 us  [receive(): return lax.ppermute(value, ('shaft', 'ply'), perm)]
    unnamed x64 -> x28, local copies, waits for them, and re-layouts: 7.57 us -> 5.9 us
  transfers between devices with their start and end apart: 20 -> 36, of which waited for: 11 -> 11; matrix products, arithmetic and copies ran while one was open for 10% -> 8% of each run, Pallas kernels for 0% -> 5%
where the time goes in v9:
time: 209 us; the launch traced here: 205 us
  starting transfers between devices  88.9 us (43%)
  waiting for transfers between devices  55.2 us (26%)
  Pallas kernels  22.6 us (11%)
  other arithmetic  20.8 us (10%)
  local copies, waits for them, and re-layouts  14.3 us (7%)
    ppermute x32, starting transfers between devices, receive(): return lax.ppermute(value, ('shaft', 'ply'), perm)  76.1 us
    ppermute x32, waiting for transfers between devices, receive(): return lax.ppermute(value, ('shaft', 'ply'), perm)  34.9 us
    ppermute x2, waiting for transfers between devices, neighbour_exchange(): from_lower = lax.ppermute(upper_bound, axis, up)  16.4 us
    reduce_sum x4, other arithmetic, on_device(): jnp.sum(product, axis=(0, 2))  15 us
    pallas_call x1, Pallas kernels, merge_arrived(): pl.pallas_call(merge_kernel, grid=(slots,), in_specs=[pl.BlockSpec((1, ro...  12.9 us
    pallas_call x1, Pallas kernels, gather_leaving(): pl.pallas_call(gather_kernel, grid=(slots,), in_specs=[pl.BlockSpec((1, d...  9.7 us
    ppermute x2, starting transfers between devices, neighbour_exchange(): from_higher = lax.ppermute(lower_bound, axis, down)  7.63 us
    unnamed x28, local copies, waits for them, and re-layouts  5.9 us
  transfers between devices with their start and end apart: 36, of which 11 were waited for; matrix products, arithmetic and copies ran while one was open for 8% of the time, Pallas kernels for 5%

profile of v9, /device:TPU:96, one launch (start us, length us, event | category | flops | bytes accessed | tf_op | source)
XLA Modules:
  0.0 205.2 jit_solution(9925331005764766967)
XLA Ops:
  1.5 3.4 %collective-permute-start.8 = (bf16[64,256]{1,0:T(8,128)(2,1)S(1)}, bf16[64,256]{1,0:T(8,128)(2,1)S(1)}, u32[]{:S(2)}, u32[]{:S(2)}) collective-permute-start(bf16[64,256]{1,0:T(8,128)(2,1)S(1)} %bitcast.259), channel_id=1, source_target_pairs={{0,1},{1,2},{2,3},{4,5},{5,6},{6,7},{8,9},{9,10},{10,11},{12,13},{... | collective-permute-start | bytes 98312 | tf_op jit(solution)/shard_map/ppermute | solution.py:38
  5.0 4.8 %collective-permute-start.9 = (bf16[64,1]{1,0:T(8,128)(2,1)S(1)}, bf16[64,1]{1,0:T(8,128)(2,1)S(1)}, u32[]{:S(2)}, u32[]{:S(2)}) collective-permute-start(bf16[64,1]{1,0:T(8,128)(2,1)S(1)} %get-tuple-element.69), channel_id=1, source_target_pairs={{4,1},{5,2},{6,3},{8,5},{9,6},{10,7},{12,9},{13,10},{14,11},{16,13... | collective-permute-start | bytes 392 | tf_op jit(solution)/shard_map/ppermute | solution.py:38
  9.8 3.0 %collective-permute-start.6 = (bf16[64,1]{1,0:T(8,128)(2,1)S(1)}, bf16[64,1]{1,0:T(8,128)(2,1)S(1)}, u32[]{:S(2)}, u32[]{:S(2)}) collective-permute-start(bf16[64,1]{1,0:T(8,128)(2,1)S(1)} %get-tuple-element.69), channel_id=1, source_target_pairs={{4,0},{5,1},{6,2},{7,3},{8,4},{9,5},{10,6},{11,7},{12,8},{13,9},{1... | collective-permute-start | bytes 392 | tf_op jit(solution)/shard_map/ppermute | solution.py:38
  28.1 9.7 %shard_map.151 = (bf16[5,32,4096]{2,1,0:T(8,128)(2,1)}, bf16[5,32,4096]{2,1,0:T(8,128)(2,1)}) custom-call(bf16[5,4096,256]{2,1,0:T(8,128)(2,1)} %bitcast.257, bf16[32,256]{1,0:T(8,128)(2,1)} %get-tuple-element.95.lo_ref, bf16[32,256]{1,0:T(8,128)(2,1)} %get-tuple-element.96.hi_ref), custom_call_target="tpu_custom_call" | custom-call | tf_op jit(solution)/shard_map/pallas_call | solution.py:74
  39.8 3.3 %collective-permute-start.10 = (f32[96,32]{0,1:T(8,128)S(1)}, f32[96,32]{0,1:T(8,128)S(1)}, u32[]{:S(2)}, u32[]{:S(2)}) collective-permute-start(f32[96,32]{0,1:T(8,128)S(1)} %get-tuple-element.23), channel_id=1, source_target_pairs={{0,4},{4,8},{8,12},{12,16},{16,20},{20,24},{24,28},{28,32},{32,36}... | collective-permute-start | bytes 36872 | tf_op jit(solution)/shard_map/ppermute | solution.py:56
  43.3 16.4 %collective-permute-done.10 = f32[96,32]{0,1:T(8,128)S(1)} collective-permute-done((f32[96,32]{0,1:T(8,128)S(1)}, f32[96,32]{0,1:T(8,128)S(1)}, u32[]{:S(2)}, u32[]{:S(2)}) %collective-permute-start.10) | collective-permute-done | bytes 12320 | tf_op jit(solution)/shard_map/ppermute | solution.py:56
  63.0 5.7 %collective-permute-start.1 = (bf16[5,32,4096]{2,1,0:T(8,128)(2,1)}, bf16[5,32,4096]{2,1,0:T(8,128)(2,1)S(1)}, u32[]{:S(2)}, u32[]{:S(2)}) collective-permute-start(bf16[5,32,4096]{2,1,0:T(8,128)(2,1)} %get-tuple-element.8), channel_id=1, source_target_pairs={{4,0},{8,4},{12,8},{16,12},{20,16},{24,20},{28,24},{32,28},{36,32}... | collective-permute-start | bytes 3932168 | tf_op jit(solution)/shard_map/ppermute | solution.py:57
  76.0 5.5 %collective-permute-done.2 = bf16[64,1]{1,0:T(8,128)(2,1)S(1)} collective-permute-done((bf16[64,1]{1,0:T(8,128)(2,1)S(1)}, bf16[64,1]{1,0:T(8,128)(2,1)S(1)}, u32[]{:S(2)}, u32[]{:S(2)}) %collective-permute-start.2) | collective-permute-done | bytes 160 | tf_op jit(solution)/shard_map/ppermute | solution.py:38
  85.5 12.9 %shard_map.152 = bf16[5,64,64,256]{3,2,1,0:T(8,128)(2,1)} custom-call(bf16[5,64,64,256]{3,2,1,0:T(8,128)(2,1)} %s_ref.1, bf16[5,32,4096]{2,1,0:T(8,128)(2,1)} %copy-done.2, bf16[5,32,4096]{2,1,0:T(8,128)(2,1)} %copy-done.3, bf16[32,256]{1,0:T(8,128)(2,1)} %get-tuple-element.82.place_lo_ref, bf16[32,256]{1,0:T(8,128)(2,1)} %get-tuple-element.97.place_hi_ref, ...), custom_call_target="tpu_custom_call" | custom-call | tf_op jit(solution)/shard_map/pallas_call | solution.py:102
  98.4 6.9 %fusion = f32[64,256]{1,0:T(8,128)S(1)} fusion(bf16[5,64,64,256]{3,2,1,0:T(8,128)(2,1)} %shard_map.152, f32[5,64,256]{2,1,0:T(8,128)S(1)} %select_convert_fusion.3), kind=kLoop, calls=%fused_computation.9 | loop fusion | flops 15712256 | bytes 10878976 | tf_op jit(solution)/shard_map/reduce_sum | solution.py:218
  108.4 5.1 %collective-permute-start.19 = (bf16[64,1]{1,0:T(8,128)(2,1)S(1)}, bf16[64,1]{1,0:T(8,128)(2,1)S(1)}, u32[]{:S(2)}, u32[]{:S(2)}) collective-permute-start(bf16[64,1]{1,0:T(8,128)(2,1)S(1)} %get-tuple-element.67), channel_id=1, source_target_pairs={{4,1},{5,2},{6,3},{8,5},{9,6},{10,7},{12,9},{13,10},{14,11},{16,13... | collective-permute-start | bytes 392 | tf_op jit(solution)/shard_map/ppermute | solution.py:38
  120.8 3.6 %collective-permute-done.15 = bf16[64,1]{1,0:T(8,128)(2,1)S(1)} collective-permute-done((bf16[64,1]{1,0:T(8,128)(2,1)S(1)}, bf16[64,1]{1,0:T(8,128)(2,1)S(1)}, u32[]{:S(2)}, u32[]{:S(2)}) %collective-permute-start.15) | collective-permute-done | bytes 160 | tf_op jit(solution)/shard_map/ppermute | solution.py:38
  127.5 6.5 %collective-permute-done.12 = bf16[64,1]{1,0:T(8,128)(2,1)S(1)} collective-permute-done((bf16[64,1]{1,0:T(8,128)(2,1)S(1)}, bf16[64,1]{1,0:T(8,128)(2,1)S(1)}, u32[]{:S(2)}, u32[]{:S(2)}) %collective-permute-start.12) | collective-permute-done | bytes 160 | tf_op jit(solution)/shard_map/ppermute | solution.py:38
  134.4 2.7 %fusion.1 = f32[64,256]{1,0:T(8,128)S(1)} fusion(bf16[5,64,64,256]{3,2,1,0:T(8,128)(2,1)S(1)} %copy-done.1, f32[5,64,256]{2,1,0:T(8,128)S(1)} %select_convert_fusion.2), kind=kLoop, calls=%fused_computation.10 | loop fusion | flops 15712256 | bytes 10878976 | tf_op jit(solution)/shard_map/reduce_sum | solution.py:218
  137.4 4.7 %collective-permute-start.26 = (bf16[64,256]{1,0:T(8,128)(2,1)S(1)}, bf16[64,256]{1,0:T(8,128)(2,1)S(1)}, u32[]{:S(2)}, u32[]{:S(2)}) collective-permute-start(bf16[64,256]{1,0:T(8,128)(2,1)S(1)} %get-tuple-element.92), channel_id=1, source_target_pairs={{0,1},{1,2},{2,3},{4,5},{5,6},{6,7},{8,9},{9,10},{10,11},{12,13},{... | collective-permute-start | bytes 98312 | tf_op jit(solution)/shard_map/ppermute | solution.py:38
  145.4 4.7 %collective-permute-start.25 = (bf16[64,1]{1,0:T(8,128)(2,1)S(1)}, bf16[64,1]{1,0:T(8,128)(2,1)S(1)}, u32[]{:S(2)}, u32[]{:S(2)}) collective-permute-start(bf16[64,1]{1,0:T(8,128)(2,1)S(1)} %get-tuple-element.62), channel_id=1, source_target_pairs={{0,5},{1,6},{2,7},{4,9},{5,10},{6,11},{8,13},{9,14},{10,15},{12,17... | collective-permute-start | bytes 392 | tf_op jit(solution)/shard_map/ppermute | solution.py:38
  150.0 3.3 %collective-permute-start.23 = (bf16[64,1]{1,0:T(8,128)(2,1)S(1)}, bf16[64,1]{1,0:T(8,128)(2,1)S(1)}, u32[]{:S(2)}, u32[]{:S(2)}) collective-permute-start(bf16[64,1]{1,0:T(8,128)(2,1)S(1)} %get-tuple-element.62), channel_id=1, source_target_pairs={{0,4},{1,5},{2,6},{3,7},{4,8},{5,9},{6,10},{7,11},{8,12},{9,13},{1... | collective-permute-start | bytes 392 | tf_op jit(solution)/shard_map/ppermute | solution.py:38
  160.2 6.5 %collective-permute-done.20 = bf16[64,1]{1,0:T(8,128)(2,1)S(1)} collective-permute-done((bf16[64,1]{1,0:T(8,128)(2,1)S(1)}, bf16[64,1]{1,0:T(8,128)(2,1)S(1)}, u32[]{:S(2)}, u32[]{:S(2)}) %collective-permute-start.20) | collective-permute-done | bytes 160 | tf_op jit(solution)/shard_map/ppermute | solution.py:38
  167.1 2.7 %fusion.2 = f32[64,256]{1,0:T(8,128)S(1)} fusion(bf16[5,64,64,256]{3,2,1,0:T(8,128)(2,1)S(1)} %copy-done.1, f32[5,64,256]{2,1,0:T(8,128)S(1)} %select_convert_fusion.1), kind=kLoop, calls=%fused_computation.11 | loop fusion | flops 15712256 | bytes 10878976 | tf_op jit(solution)/shard_map/reduce_sum | solution.py:218
  170.1 4.9 %collective-permute-start.34 = (bf16[64,256]{1,0:T(8,128)(2,1)S(1)}, bf16[64,256]{1,0:T(8,128)(2,1)S(1)}, u32[]{:S(2)}, u32[]{:S(2)}) collective-permute-start(bf16[64,256]{1,0:T(8,128)(2,1)S(1)} %get-tuple-element.18), channel_id=1, source_target_pairs={{0,1},{1,2},{2,3},{4,5},{5,6},{6,7},{8,9},{9,10},{10,11},{12,13},{... | collective-permute-start | bytes 98312 | tf_op jit(solution)/shard_map/ppermute | solution.py:38
  178.3 4.7 %collective-permute-start.33 = (bf16[64,1]{1,0:T(8,128)(2,1)S(1)}, bf16[64,1]{1,0:T(8,128)(2,1)S(1)}, u32[]{:S(2)}, u32[]{:S(2)}) collective-permute-start(bf16[64,1]{1,0:T(8,128)(2,1)S(1)} %get-tuple-element.60), channel_id=1, source_target_pairs={{0,5},{1,6},{2,7},{4,9},{5,10},{6,11},{8,13},{9,14},{10,15},{12,17... | collective-permute-start | bytes 392 | tf_op jit(solution)/shard_map/ppermute | solution.py:38
  182.9 3.1 %collective-permute-start.31 = (bf16[64,1]{1,0:T(8,128)(2,1)S(1)}, bf16[64,1]{1,0:T(8,128)(2,1)S(1)}, u32[]{:S(2)}, u32[]{:S(2)}) collective-permute-start(bf16[64,1]{1,0:T(8,128)(2,1)S(1)} %get-tuple-element.60), channel_id=1, source_target_pairs={{0,4},{1,5},{2,6},{3,7},{4,8},{5,9},{6,10},{7,11},{8,12},{9,13},{1... | collective-permute-start | bytes 392 | tf_op jit(solution)/shard_map/ppermute | solution.py:38
  193.1 6.5 %collective-permute-done.28 = bf16[64,1]{1,0:T(8,128)(2,1)S(1)} collective-permute-done((bf16[64,1]{1,0:T(8,128)(2,1)S(1)}, bf16[64,1]{1,0:T(8,128)(2,1)S(1)}, u32[]{:S(2)}, u32[]{:S(2)}) %collective-permute-start.28) | collective-permute-done | bytes 160 | tf_op jit(solution)/shard_map/ppermute | solution.py:38
  200.0 2.7 %fusion.3 = f32[64,256]{1,0:T(8,128)S(1)} fusion(bf16[5,64,64,256]{3,2,1,0:T(8,128)(2,1)S(1)} %copy-done.1, f32[5,64,256]{2,1,0:T(8,128)S(1)} %select_convert_fusion), kind=kLoop, calls=%fused_computation.12 | loop fusion | flops 15712256 | bytes 10878976 | tf_op jit(solution)/shard_map/reduce_sum | solution.py:218
  (155 shorter events, 70.3 us)
Async XLA Ops:
  1.5 71.9 %collective-permute-start.8 = (bf16[64,256]{1,0:T(8,128)(2,1)S(1)}, bf16[64,256]{1,0:T(8,128)(2,1)S(1)}, u32[]{:S(2)}, u32[]{:S(2)}) collective-permute-start(bf16[64,256]{1,0:T(8,128)(2,1)S(1)} %bitcast.259), channel_id=1, source_target_pairs={{0,1},{1,2},{2,3},{4,5},{5,6},{6,7},{8,9},{9,10},{10,11},{12,13},{... | collective-permute-start | bytes 98312 | tf_op jit(solution)/shard_map/ppermute | solution.py:38
  5.0 65.8 %collective-permute-start.9 = (bf16[64,1]{1,0:T(8,128)(2,1)S(1)}, bf16[64,1]{1,0:T(8,128)(2,1)S(1)}, u32[]{:S(2)}, u32[]{:S(2)}) collective-permute-start(bf16[64,1]{1,0:T(8,128)(2,1)S(1)} %get-tuple-element.69), channel_id=1, source_target_pairs={{4,1},{5,2},{6,3},{8,5},{9,6},{10,7},{12,9},{13,10},{14,11},{16,13... | collective-permute-start | bytes 392 | tf_op jit(solution)/shard_map/ppermute | solution.py:38
  9.8 28.0 %collective-permute-start.6 = (bf16[64,1]{1,0:T(8,128)(2,1)S(1)}, bf16[64,1]{1,0:T(8,128)(2,1)S(1)}, u32[]{:S(2)}, u32[]{:S(2)}) collective-permute-start(bf16[64,1]{1,0:T(8,128)(2,1)S(1)} %get-tuple-element.69), channel_id=1, source_target_pairs={{4,0},{5,1},{6,2},{7,3},{8,4},{9,5},{10,6},{11,7},{12,8},{13,9},{1... | collective-permute-start | bytes 392 | tf_op jit(solution)/shard_map/ppermute | solution.py:38
  12.9 59.2 %collective-permute-start.7 = (bf16[64,1]{1,0:T(8,128)(2,1)S(1)}, bf16[64,1]{1,0:T(8,128)(2,1)S(1)}, u32[]{:S(2)}, u32[]{:S(2)}) collective-permute-start(bf16[64,1]{1,0:T(8,128)(2,1)S(1)} %get-tuple-element.68), channel_id=1, source_target_pairs={{0,5},{1,6},{2,7},{4,9},{5,10},{6,11},{8,13},{9,14},{10,15},{12,17... | collective-permute-start | bytes 392 | tf_op jit(solution)/shard_map/ppermute | solution.py:38
  15.0 24.8 %collective-permute-start.5 = (bf16[64,1]{1,0:T(8,128)(2,1)S(1)}, bf16[64,1]{1,0:T(8,128)(2,1)S(1)}, u32[]{:S(2)}, u32[]{:S(2)}) collective-permute-start(bf16[64,1]{1,0:T(8,128)(2,1)S(1)} %get-tuple-element.68), channel_id=1, source_target_pairs={{0,4},{1,5},{2,6},{3,7},{4,8},{5,9},{6,10},{7,11},{8,12},{9,13},{1... | collective-permute-start | bytes 392 | tf_op jit(solution)/shard_map/ppermute | solution.py:38
  37.8 44.1 %collective-permute-start = (bf16[5,32,4096]{2,1,0:T(8,128)(2,1)}, bf16[5,32,4096]{2,1,0:T(8,128)(2,1)S(1)}, u32[]{:S(2)}, u32[]{:S(2)}) collective-permute-start(bf16[5,32,4096]{2,1,0:T(8,128)(2,1)} %get-tuple-element.7), channel_id=1, source_target_pairs={{0,4},{4,8},{8,12},{12,16},{16,20},{20,24},{24,28},{28,32},{32,36}... | collective-permute-start | bytes 3932168 | tf_op jit(solution)/shard_map/ppermute | solution.py:56
  39.8 19.9 %collective-permute-start.10 = (f32[96,32]{0,1:T(8,128)S(1)}, f32[96,32]{0,1:T(8,128)S(1)}, u32[]{:S(2)}, u32[]{:S(2)}) collective-permute-start(f32[96,32]{0,1:T(8,128)S(1)} %get-tuple-element.23), channel_id=1, source_target_pairs={{0,4},{4,8},{8,12},{12,16},{16,20},{20,24},{24,28},{28,32},{32,36}... | collective-permute-start | bytes 36872 | tf_op jit(solution)/shard_map/ppermute | solution.py:56
  63.0 21.3 %collective-permute-start.1 = (bf16[5,32,4096]{2,1,0:T(8,128)(2,1)}, bf16[5,32,4096]{2,1,0:T(8,128)(2,1)S(1)}, u32[]{:S(2)}, u32[]{:S(2)}) collective-permute-start(bf16[5,32,4096]{2,1,0:T(8,128)(2,1)} %get-tuple-element.8), channel_id=1, source_target_pairs={{4,0},{8,4},{12,8},{16,12},{20,16},{24,20},{28,24},{32,28},{36,32}... | collective-permute-start | bytes 3932168 | tf_op jit(solution)/shard_map/ppermute | solution.py:57
  72.1 9.4 %collective-permute-start.3 = (bf16[64,256]{1,0:T(8,128)(2,1)S(1)}, bf16[64,256]{1,0:T(8,128)(2,1)S(1)}, u32[]{:S(2)}, u32[]{:S(2)}) collective-permute-start(bf16[64,256]{1,0:T(8,128)(2,1)S(1)} %bitcast.262), channel_id=1, source_target_pairs={{1,0},{2,1},{3,2},{5,4},{6,5},{7,6},{9,8},{10,9},{11,10},{13,12},{... | collective-permute-start | bytes 98312 | tf_op jit(solution)/shard_map/ppermute | solution.py:38
  73.4 8.1 %collective-permute-start.2 = (bf16[64,1]{1,0:T(8,128)(2,1)S(1)}, bf16[64,1]{1,0:T(8,128)(2,1)S(1)}, u32[]{:S(2)}, u32[]{:S(2)}) collective-permute-start(bf16[64,1]{1,0:T(8,128)(2,1)S(1)} %get-tuple-element.68), channel_id=1, source_target_pairs={{1,4},{2,5},{3,6},{5,8},{6,9},{7,10},{9,12},{10,13},{11,14},{13,16... | collective-permute-start | bytes 392 | tf_op jit(solution)/shard_map/ppermute | solution.py:38
  105.7 21.6 %collective-permute-start.18 = (bf16[64,256]{1,0:T(8,128)(2,1)S(1)}, bf16[64,256]{1,0:T(8,128)(2,1)S(1)}, u32[]{:S(2)}, u32[]{:S(2)}) collective-permute-start(bf16[64,256]{1,0:T(8,128)(2,1)S(1)} %get-tuple-element.20), channel_id=1, source_target_pairs={{0,1},{1,2},{2,3},{4,5},{5,6},{6,7},{8,9},{9,10},{10,11},{12,13},{... | collective-permute-start | bytes 98312 | tf_op jit(solution)/shard_map/ppermute | solution.py:38
  108.4 17.6 %collective-permute-start.19 = (bf16[64,1]{1,0:T(8,128)(2,1)S(1)}, bf16[64,1]{1,0:T(8,128)(2,1)S(1)}, u32[]{:S(2)}, u32[]{:S(2)}) collective-permute-start(bf16[64,1]{1,0:T(8,128)(2,1)S(1)} %get-tuple-element.67), channel_id=1, source_target_pairs={{4,1},{5,2},{6,3},{8,5},{9,6},{10,7},{12,9},{13,10},{14,11},{16,13... | collective-permute-start | bytes 392 | tf_op jit(solution)/shard_map/ppermute | solution.py:38
  115.4 11.9 %collective-permute-start.17 = (bf16[64,1]{1,0:T(8,128)(2,1)S(1)}, bf16[64,1]{1,0:T(8,128)(2,1)S(1)}, u32[]{:S(2)}, u32[]{:S(2)}) collective-permute-start(bf16[64,1]{1,0:T(8,128)(2,1)S(1)} %get-tuple-element.66), channel_id=1, source_target_pairs={{0,5},{1,6},{2,7},{4,9},{5,10},{6,11},{8,13},{9,14},{10,15},{12,17... | collective-permute-start | bytes 392 | tf_op jit(solution)/shard_map/ppermute | solution.py:38
  124.5 9.6 %collective-permute-start.13 = (bf16[64,256]{1,0:T(8,128)(2,1)S(1)}, bf16[64,256]{1,0:T(8,128)(2,1)S(1)}, u32[]{:S(2)}, u32[]{:S(2)}) collective-permute-start(bf16[64,256]{1,0:T(8,128)(2,1)S(1)} %get-tuple-element.20), channel_id=1, source_target_pairs={{1,0},{2,1},{3,2},{5,4},{6,5},{7,6},{9,8},{10,9},{11,10},{13,12},{... | collective-permute-start | bytes 98312 | tf_op jit(solution)/shard_map/ppermute | solution.py:38
  137.4 22.6 %collective-permute-start.26 = (bf16[64,256]{1,0:T(8,128)(2,1)S(1)}, bf16[64,256]{1,0:T(8,128)(2,1)S(1)}, u32[]{:S(2)}, u32[]{:S(2)}) collective-permute-start(bf16[64,256]{1,0:T(8,128)(2,1)S(1)} %get-tuple-element.92), channel_id=1, source_target_pairs={{0,1},{1,2},{2,3},{4,5},{5,6},{6,7},{8,9},{9,10},{10,11},{12,13},{... | collective-permute-start | bytes 98312 | tf_op jit(solution)/shard_map/ppermute | solution.py:38
  142.1 16.5 %collective-permute-start.27 = (bf16[64,1]{1,0:T(8,128)(2,1)S(1)}, bf16[64,1]{1,0:T(8,128)(2,1)S(1)}, u32[]{:S(2)}, u32[]{:S(2)}) collective-permute-start(bf16[64,1]{1,0:T(8,128)(2,1)S(1)} %get-tuple-element.63), channel_id=1, source_target_pairs={{4,1},{5,2},{6,3},{8,5},{9,6},{10,7},{12,9},{13,10},{14,11},{16,13... | collective-permute-start | bytes 392 | tf_op jit(solution)/shard_map/ppermute | solution.py:38
  143.4 10.1 %collective-permute-start.24 = (bf16[64,1]{1,0:T(8,128)(2,1)S(1)}, bf16[64,1]{1,0:T(8,128)(2,1)S(1)}, u32[]{:S(2)}, u32[]{:S(2)}) collective-permute-start(bf16[64,1]{1,0:T(8,128)(2,1)S(1)} %get-tuple-element.63), channel_id=1, source_target_pairs={{4,0},{5,1},{6,2},{7,3},{8,4},{9,5},{10,6},{11,7},{12,8},{13,9},{1... | collective-permute-start | bytes 392 | tf_op jit(solution)/shard_map/ppermute | solution.py:38
  145.4 14.6 %collective-permute-start.25 = (bf16[64,1]{1,0:T(8,128)(2,1)S(1)}, bf16[64,1]{1,0:T(8,128)(2,1)S(1)}, u32[]{:S(2)}, u32[]{:S(2)}) collective-permute-start(bf16[64,1]{1,0:T(8,128)(2,1)S(1)} %get-tuple-element.62), channel_id=1, source_target_pairs={{0,5},{1,6},{2,7},{4,9},{5,10},{6,11},{8,13},{9,14},{10,15},{12,17... | collective-permute-start | bytes 392 | tf_op jit(solution)/shard_map/ppermute | solution.py:38
  157.2 9.6 %collective-permute-start.21 = (bf16[64,256]{1,0:T(8,128)(2,1)S(1)}, bf16[64,256]{1,0:T(8,128)(2,1)S(1)}, u32[]{:S(2)}, u32[]{:S(2)}) collective-permute-start(bf16[64,256]{1,0:T(8,128)(2,1)S(1)} %get-tuple-element.92), channel_id=1, source_target_pairs={{1,0},{2,1},{3,2},{5,4},{6,5},{7,6},{9,8},{10,9},{11,10},{13,12},{... | collective-permute-start | bytes 98312 | tf_op jit(solution)/shard_map/ppermute | solution.py:38
  170.1 22.8 %collective-permute-start.34 = (bf16[64,256]{1,0:T(8,128)(2,1)S(1)}, bf16[64,256]{1,0:T(8,128)(2,1)S(1)}, u32[]{:S(2)}, u32[]{:S(2)}) collective-permute-start(bf16[64,256]{1,0:T(8,128)(2,1)S(1)} %get-tuple-element.18), channel_id=1, source_target_pairs={{0,1},{1,2},{2,3},{4,5},{5,6},{6,7},{8,9},{9,10},{10,11},{12,13},{... | collective-permute-start | bytes 98312 | tf_op jit(solution)/shard_map/ppermute | solution.py:38
  175.0 16.5 %collective-permute-start.35 = (bf16[64,1]{1,0:T(8,128)(2,1)S(1)}, bf16[64,1]{1,0:T(8,128)(2,1)S(1)}, u32[]{:S(2)}, u32[]{:S(2)}) collective-permute-start(bf16[64,1]{1,0:T(8,128)(2,1)S(1)} %get-tuple-element.61), channel_id=1, source_target_pairs={{4,1},{5,2},{6,3},{8,5},{9,6},{10,7},{12,9},{13,10},{14,11},{16,13... | collective-permute-start | bytes 392 | tf_op jit(solution)/shard_map/ppermute | solution.py:38
  176.3 9.9 %collective-permute-start.32 = (bf16[64,1]{1,0:T(8,128)(2,1)S(1)}, bf16[64,1]{1,0:T(8,128)(2,1)S(1)}, u32[]{:S(2)}, u32[]{:S(2)}) collective-permute-start(bf16[64,1]{1,0:T(8,128)(2,1)S(1)} %get-tuple-element.61), channel_id=1, source_target_pairs={{4,0},{5,1},{6,2},{7,3},{8,4},{9,5},{10,6},{11,7},{12,8},{13,9},{1... | collective-permute-start | bytes 392 | tf_op jit(solution)/shard_map/ppermute | solution.py:38
  178.3 14.6 %collective-permute-start.33 = (bf16[64,1]{1,0:T(8,128)(2,1)S(1)}, bf16[64,1]{1,0:T(8,128)(2,1)S(1)}, u32[]{:S(2)}, u32[]{:S(2)}) collective-permute-start(bf16[64,1]{1,0:T(8,128)(2,1)S(1)} %get-tuple-element.60), channel_id=1, source_target_pairs={{0,5},{1,6},{2,7},{4,9},{5,10},{6,11},{8,13},{9,14},{10,15},{12,17... | collective-permute-start | bytes 392 | tf_op jit(solution)/shard_map/ppermute | solution.py:38
  190.1 9.6 %collective-permute-start.29 = (bf16[64,256]{1,0:T(8,128)(2,1)S(1)}, bf16[64,256]{1,0:T(8,128)(2,1)S(1)}, u32[]{:S(2)}, u32[]{:S(2)}) collective-permute-start(bf16[64,256]{1,0:T(8,128)(2,1)S(1)} %get-tuple-element.18), channel_id=1, source_target_pairs={{1,0},{2,1},{3,2},{5,4},{6,5},{7,6},{9,8},{10,9},{11,10},{13,12},{... | collective-permute-start | bytes 98312 | tf_op jit(solution)/shard_map/ppermute | solution.py:38
  (20 other events, 254.4 us)

commit v10 on v5

--- a/solution.py
+++ b/solution.py
@@ -35,12 +35,13 @@
 
 
 def gather_kernel(s_ref, lo_ref, hi_ref, out_lo_ref, out_hi_ref):
-    flat = s_ref[0]
-    for pick_ref, out_ref in ((lo_ref, out_lo_ref), (hi_ref, out_hi_ref)):
-        picked = lax.dot_general(
-            pick_ref[...], flat, (((1,), (1,)), ((), ())), preferred_element_type=jnp.float32
-        )
-        out_ref[0] = picked.astype(out_ref.dtype)
+    width = lo_ref.shape[0]
+    pick = jnp.concatenate([lo_ref[...], hi_ref[...]], 0)
+    picked = lax.dot_general(
+        pick, s_ref[0], (((1,), (1,)), ((), ())), preferred_element_type=jnp.float32
+    )
+    out_lo_ref[0] = picked[:width].astype(out_lo_ref.dtype)
+    out_hi_ref[0] = picked[width:].astype(out_hi_ref.dtype)
 
 
 def gather_leaving(stiffness, pick_lo, pick_hi):
@@ -64,9 +65,9 @@
 
 
 def merge_kernel(s_ref, lo_ref, hi_ref, place_lo_ref, place_hi_ref, arrival_ref, out_ref):
-    placed = jnp.dot(
-        lo_ref[0].T, place_lo_ref[...], preferred_element_type=jnp.float32
-    ) + jnp.dot(hi_ref[0].T, place_hi_ref[...], preferred_element_type=jnp.float32)
+    arrived = jnp.concatenate([lo_ref[0], hi_ref[0]], 0)
+    place = jnp.concatenate([place_lo_ref[...], place_hi_ref[...]], 0)
+    placed = jnp.dot(arrived.T, place, preferred_element_type=jnp.float32)
     placed = placed.astype(out_ref.dtype).reshape(s_ref.shape[1:])
     out_ref[0] = jnp.where(arrival_ref[...] > 0, placed, s_ref[0])
 

time: 144 us -> 141 us (0.979)
  Pallas kernels: 22.5 us -> 20.1 us
where the time goes in v10:
time: 141 us; the launch traced here: 140 us
  starting transfers between devices  49.9 us (35%)
  waiting for transfers between devices  31.4 us (22%)
  other arithmetic  21.3 us (15%)
  Pallas kernels  20.1 us (14%)
  local copies, waits for them, and re-layouts  14.3 us (10%)
  matrix products  1.85 us (1%)
  between operations  1.5 us (1%)
    ppermute x8, starting transfers between devices, padded_2(): before = lax.ppermute(last, axis, up)  21.4 us
    ppermute x8, waiting for transfers between devices, padded_2(): after = lax.ppermute(first, axis, down)  16.9 us
    reduce_sum x4, other arithmetic, on_device(): jnp.sum(product, axis=(0, 2))  15.3 us
    ppermute x8, waiting for transfers between devices, padded_2(): before = lax.ppermute(last, axis, up)  14.5 us
    ppermute x8, starting transfers between devices, padded_2(): after = lax.ppermute(first, axis, down)  13 us
    pallas_call x1, Pallas kernels, merge_arrived(): pl.pallas_call(merge_kernel, grid=(slots,), in_specs=[pl.BlockSpec((1, ro...  11.7 us
    ppermute x2, starting transfers between devices, neighbour_exchange(): from_higher = lax.ppermute(lower_bound, axis, down)  11.7 us
    pallas_call x1, Pallas kernels, gather_leaving(): pl.pallas_call(gather_kernel, grid=(slots,), in_specs=[pl.BlockSpec((1, d...  8.46 us
  transfers between devices with their start and end apart: 20, of which 11 were waited for; matrix products, arithmetic and copies ran while one was open for 10% of the time, Pallas kernels for 0%

profile of v10, /device:TPU:96, one launch (start us, length us, event | category | flops | bytes accessed | tf_op | source)
XLA Modules:
  0.0 140.4 jit_solution(16432477370208149388)
XLA Ops:
  2.2 8.5 %shard_map.151 = (bf16[5,32,4096]{2,1,0:T(8,128)(2,1)}, bf16[5,32,4096]{2,1,0:T(8,128)(2,1)}) custom-call(bf16[5,4096,256]{2,1,0:T(8,128)(2,1)} %bitcast.228, bf16[32,256]{1,0:T(8,128)(2,1)} %get-tuple-element.91.lo_ref, bf16[32,256]{1,0:T(8,128)(2,1)} %get-tuple-element.92.hi_ref), custom_call_target="tpu_custom_call" | custom-call | tf_op jit(solution)/shard_map/pallas_call | solution.py:51
  12.6 5.8 %collective-permute-start.1 = (bf16[5,32,4096]{2,1,0:T(8,128)(2,1)}, bf16[5,32,4096]{2,1,0:T(8,128)(2,1)S(1)}, u32[]{:S(2)}, u32[]{:S(2)}) collective-permute-start(bf16[5,32,4096]{2,1,0:T(8,128)(2,1)} %get-tuple-element.8), channel_id=1, source_target_pairs={{4,0},{8,4},{12,8},{16,12},{20,16},{24,20},{28,24},{32,28},{36,32}... | collective-permute-start | bytes 3932168 | tf_op jit(solution)/shard_map/ppermute | solution.py:33
  18.5 1.9 %collective-permute-start.3 = (bf16[64,1,1]{2,1,0:T(2,128)(2,1)S(1)}, bf16[64,1,1]{2,1,0:T(2,128)(2,1)S(1)}, u32[]{:S(2)}, u32[]{:S(2)}) collective-permute-start(bf16[64,1,1]{2,1,0:T(2,128)(2,1)S(1)} %get-tuple-element.33), channel_id=1, source_target_pairs={{4,0},{8,4},{12,8},{16,12},{20,16},{24,20},{28,24},{32,28},{36,32}... | collective-permute-start | bytes 392 | tf_op jit(solution)/shard_map/ppermute | solution.py:23
  20.4 2.4 %collective-permute-start.2 = (bf16[64,1,1]{2,1,0:T(2,128)(2,1)S(1)}, bf16[64,1,1]{2,1,0:T(2,128)(2,1)S(1)}, u32[]{:S(2)}, u32[]{:S(2)}) collective-permute-start(bf16[64,1,1]{2,1,0:T(2,128)(2,1)S(1)} %get-tuple-element.32), channel_id=1, source_target_pairs={{0,4},{4,8},{8,12},{12,16},{16,20},{20,24},{24,28},{28,32},{32,36}... | collective-permute-start | bytes 392 | tf_op jit(solution)/shard_map/ppermute | solution.py:22
  34.0 5.9 %collective-permute-start.7 = (f32[96,32]{0,1:T(8,128)S(1)}, f32[96,32]{0,1:T(8,128)S(1)}, u32[]{:S(2)}, u32[]{:S(2)}) collective-permute-start(f32[96,32]{0,1:T(8,128)S(1)} %get-tuple-element.28), channel_id=1, source_target_pairs={{4,0},{8,4},{12,8},{16,12},{20,16},{24,20},{28,24},{32,28},{36,32}... | collective-permute-start | bytes 36872 | tf_op jit(solution)/shard_map/ppermute | solution.py:33
  40.8 3.4 %collective-permute-start.5 = (bf16[64,1,258]{2,1,0:T(2,128)(2,1)}, bf16[64,1,258]{2,1,0:T(2,128)(2,1)S(1)}, u32[]{:S(2)}, u32[]{:S(2)}) collective-permute-start(bf16[64,1,258]{2,1,0:T(2,128)(2,1)} %pad_maximum_fusion.2), channel_id=1, source_target_pairs={{0,1},{1,2},{2,3},{4,5},{5,6},{6,7},{8,9},{9,10},{10,11},{12,13},{... | collective-permute-start | bytes 99080 | tf_op jit(solution)/shard_map/ppermute | solution.py:22
  49.2 2.7 %collective-permute-done.4 = bf16[64,1,258]{2,1,0:T(2,128)(2,1)S(1)} collective-permute-done((bf16[64,1,258]{2,1,0:T(2,128)(2,1)}, bf16[64,1,258]{2,1,0:T(2,128)(2,1)S(1)}, u32[]{:S(2)}, u32[]{:S(2)}) %collective-permute-start.4) | collective-permute-done | bytes 33056 | tf_op jit(solution)/shard_map/ppermute | solution.py:23
  54.8 11.7 %shard_map.152 = bf16[5,64,64,256]{3,2,1,0:T(8,128)(2,1)} custom-call(bf16[5,64,64,256]{3,2,1,0:T(8,128)(2,1)} %s_ref.1, bf16[5,32,4096]{2,1,0:T(8,128)(2,1)} %copy-done.2, bf16[5,32,4096]{2,1,0:T(8,128)(2,1)} %copy-done.3, bf16[32,256]{1,0:T(8,128)(2,1)} %get-tuple-element.78.place_lo_ref, bf16[32,256]{1,0:T(8,128)(2,1)} %get-tuple-element.93.place_hi_ref, ...), custom_call_target="tpu_custom_call" | custom-call | tf_op jit(solution)/shard_map/pallas_call | solution.py:79
  66.6 6.9 %fusion = f32[64,256]{1,0:T(8,128)S(1)} fusion(bf16[5,64,64,256]{3,2,1,0:T(8,128)(2,1)} %shard_map.152, f32[5,64,256]{2,1,0:T(8,128)S(1)} %select_convert_fusion.3), kind=kLoop, calls=%fused_computation.9 | loop fusion | flops 15712256 | bytes 10878976 | tf_op jit(solution)/shard_map/reduce_sum | solution.py:196
  75.8 2.4 %collective-permute-start.8 = (bf16[64,1,1]{2,0,1:T(8,128)(2,1)S(1)}, bf16[64,1,1]{2,0,1:T(8,128)(2,1)S(1)}, u32[]{:S(2)}, u32[]{:S(2)}) collective-permute-start(bf16[64,1,1]{2,0,1:T(8,128)(2,1)S(1)} %get-tuple-element.64), channel_id=1, source_target_pairs={{0,4},{4,8},{8,12},{12,16},{16,20},{20,24},{24,28},{28,32},{32,36}... | collective-permute-start | bytes 392 | tf_op jit(solution)/shard_map/ppermute | solution.py:22
  78.4 4.6 %collective-permute-done.8 = bf16[64,1,1]{2,0,1:T(8,128)(2,1)S(1)} collective-permute-done((bf16[64,1,1]{2,0,1:T(8,128)(2,1)S(1)}, bf16[64,1,1]{2,0,1:T(8,128)(2,1)S(1)}, u32[]{:S(2)}, u32[]{:S(2)}) %collective-permute-start.8) | collective-permute-done | bytes 160 | tf_op jit(solution)/shard_map/ppermute | solution.py:22
  83.1 3.4 %collective-permute-start.11 = (bf16[64,1,258]{2,0,1:T(8,128)(2,1)S(1)}, bf16[64,1,258]{2,0,1:T(8,128)(2,1)S(1)}, u32[]{:S(2)}, u32[]{:S(2)}) collective-permute-start(bf16[64,1,258]{2,0,1:T(8,128)(2,1)S(1)} %pad_maximum_fusion.5), channel_id=1, source_target_pairs={{0,1},{1,2},{2,3},{4,5},{5,6},{6,7},{8,9},{9,10},{10,11},{12,13},{... | collective-permute-start | bytes 99080 | tf_op jit(solution)/shard_map/ppermute | solution.py:22
  88.3 4.2 %collective-permute-done.10 = bf16[64,1,258]{2,0,1:T(8,128)(2,1)S(1)} collective-permute-done((bf16[64,1,258]{2,0,1:T(8,128)(2,1)S(1)}, bf16[64,1,258]{2,0,1:T(8,128)(2,1)S(1)}, u32[]{:S(2)}, u32[]{:S(2)}) %collective-permute-start.10) | collective-permute-done | bytes 33056 | tf_op jit(solution)/shard_map/ppermute | solution.py:23
  92.8 2.8 %fusion.1 = f32[64,256]{1,0:T(8,128)S(1)} fusion(bf16[5,64,64,256]{3,2,1,0:T(8,128)(2,1)S(1)} %copy-done.1, f32[5,64,256]{2,1,0:T(8,128)S(1)} %select_convert_fusion.2), kind=kLoop, calls=%fused_computation.10 | loop fusion | flops 15712256 | bytes 10878976 | tf_op jit(solution)/shard_map/reduce_sum | solution.py:196
  97.8 2.4 %collective-permute-start.12 = (bf16[64,1,1]{2,0,1:T(8,128)(2,1)S(1)}, bf16[64,1,1]{2,0,1:T(8,128)(2,1)S(1)}, u32[]{:S(2)}, u32[]{:S(2)}) collective-permute-start(bf16[64,1,1]{2,0,1:T(8,128)(2,1)S(1)} %get-tuple-element.58), channel_id=1, source_target_pairs={{0,4},{4,8},{8,12},{12,16},{16,20},{20,24},{24,28},{28,32},{32,36}... | collective-permute-start | bytes 392 | tf_op jit(solution)/shard_map/ppermute | solution.py:22
  100.4 4.5 %collective-permute-done.12 = bf16[64,1,1]{2,0,1:T(8,128)(2,1)S(1)} collective-permute-done((bf16[64,1,1]{2,0,1:T(8,128)(2,1)S(1)}, bf16[64,1,1]{2,0,1:T(8,128)(2,1)S(1)}, u32[]{:S(2)}, u32[]{:S(2)}) %collective-permute-start.12) | collective-permute-done | bytes 160 | tf_op jit(solution)/shard_map/ppermute | solution.py:22
  105.1 3.1 %collective-permute-start.15 = (bf16[64,1,258]{2,0,1:T(8,128)(2,1)S(1)}, bf16[64,1,258]{2,0,1:T(8,128)(2,1)S(1)}, u32[]{:S(2)}, u32[]{:S(2)}) collective-permute-start(bf16[64,1,258]{2,0,1:T(8,128)(2,1)S(1)} %pad_maximum_fusion.6), channel_id=1, source_target_pairs={{0,1},{1,2},{2,3},{4,5},{5,6},{6,7},{8,9},{9,10},{10,11},{12,13},{... | collective-permute-start | bytes 99080 | tf_op jit(solution)/shard_map/ppermute | solution.py:22
  110.0 4.3 %collective-permute-done.14 = bf16[64,1,258]{2,0,1:T(8,128)(2,1)S(1)} collective-permute-done((bf16[64,1,258]{2,0,1:T(8,128)(2,1)S(1)}, bf16[64,1,258]{2,0,1:T(8,128)(2,1)S(1)}, u32[]{:S(2)}, u32[]{:S(2)}) %collective-permute-start.14) | collective-permute-done | bytes 33056 | tf_op jit(solution)/shard_map/ppermute | solution.py:23
  114.6 2.8 %fusion.2 = f32[64,256]{1,0:T(8,128)S(1)} fusion(bf16[5,64,64,256]{3,2,1,0:T(8,128)(2,1)S(1)} %copy-done.1, f32[5,64,256]{2,1,0:T(8,128)S(1)} %select_convert_fusion.1), kind=kLoop, calls=%fused_computation.11 | loop fusion | flops 15712256 | bytes 10878976 | tf_op jit(solution)/shard_map/reduce_sum | solution.py:196
  119.7 2.4 %collective-permute-start.16 = (bf16[64,1,1]{2,0,1:T(8,128)(2,1)S(1)}, bf16[64,1,1]{2,0,1:T(8,128)(2,1)S(1)}, u32[]{:S(2)}, u32[]{:S(2)}) collective-permute-start(bf16[64,1,1]{2,0,1:T(8,128)(2,1)S(1)} %get-tuple-element.54), channel_id=1, source_target_pairs={{0,4},{4,8},{8,12},{12,16},{16,20},{20,24},{24,28},{28,32},{32,36}... | collective-permute-start | bytes 392 | tf_op jit(solution)/shard_map/ppermute | solution.py:22
  122.3 4.5 %collective-permute-done.16 = bf16[64,1,1]{2,0,1:T(8,128)(2,1)S(1)} collective-permute-done((bf16[64,1,1]{2,0,1:T(8,128)(2,1)S(1)}, bf16[64,1,1]{2,0,1:T(8,128)(2,1)S(1)}, u32[]{:S(2)}, u32[]{:S(2)}) %collective-permute-start.16) | collective-permute-done | bytes 160 | tf_op jit(solution)/shard_map/ppermute | solution.py:22
  126.9 1.9 %collective-permute-start.19 = (bf16[64,1,258]{2,0,1:T(8,128)(2,1)S(1)}, bf16[64,1,258]{2,0,1:T(8,128)(2,1)S(1)}, u32[]{:S(2)}, u32[]{:S(2)}) collective-permute-start(bf16[64,1,258]{2,0,1:T(8,128)(2,1)S(1)} %pad_maximum_fusion.7), channel_id=1, source_target_pairs={{0,1},{1,2},{2,3},{4,5},{5,6},{6,7},{8,9},{9,10},{10,11},{12,13},{... | collective-permute-start | bytes 99080 | tf_op jit(solution)/shard_map/ppermute | solution.py:22
  130.7 4.2 %collective-permute-done.18 = bf16[64,1,258]{2,0,1:T(8,128)(2,1)S(1)} collective-permute-done((bf16[64,1,258]{2,0,1:T(8,128)(2,1)S(1)}, bf16[64,1,258]{2,0,1:T(8,128)(2,1)S(1)}, u32[]{:S(2)}, u32[]{:S(2)}) %collective-permute-start.18) | collective-permute-done | bytes 33056 | tf_op jit(solution)/shard_map/ppermute | solution.py:23
  135.0 2.8 %fusion.3 = f32[64,256]{1,0:T(8,128)S(1)} fusion(bf16[5,64,64,256]{3,2,1,0:T(8,128)(2,1)S(1)} %copy-done.1, f32[5,64,256]{2,1,0:T(8,128)S(1)} %select_convert_fusion), kind=kLoop, calls=%fused_computation.12 | loop fusion | flops 15712256 | bytes 10878976 | tf_op jit(solution)/shard_map/reduce_sum | solution.py:196
  (152 shorter events, 39.4 us)
Async XLA Ops:
  0.6 72.8 %copy-start = (f32[48,64]{1,0:T(8,128)S(1)}, f32[48,64]{1,0:T(8,128)}, u32[]{:S(2)}) copy-start(f32[48,64]{1,0:T(8,128)} %param.26) | copy-start | bytes 36868
  0.7 29.3 %copy-start.19 = (s32[5,1,256]{2,1,0:T(1,128)S(1)}, s32[5,1,256]{2,1,0:T(1,128)}, u32[]{:S(2)}) copy-start(s32[5,1,256]{2,1,0:T(1,128)} %param.21) | copy-start | bytes 15364
  0.7 29.3 %copy-start.20 = (s32[1,256]{1,0:T(1,128)S(1)}, s32[1,256]{1,0:T(1,128)}, u32[]{:S(2)}) copy-start(s32[1,256]{1,0:T(1,128)} %param.22) | copy-start | bytes 3076
  10.6 42.5 %collective-permute-start = (bf16[5,32,4096]{2,1,0:T(8,128)(2,1)}, bf16[5,32,4096]{2,1,0:T(8,128)(2,1)S(1)}, u32[]{:S(2)}, u32[]{:S(2)}) collective-permute-start(bf16[5,32,4096]{2,1,0:T(8,128)(2,1)} %get-tuple-element.7), channel_id=1, source_target_pairs={{0,4},{4,8},{8,12},{12,16},{16,20},{20,24},{24,28},{28,32},{32,36}... | collective-permute-start | bytes 3932168 | tf_op jit(solution)/shard_map/ppermute | solution.py:32
  12.6 40.6 %collective-permute-start.1 = (bf16[5,32,4096]{2,1,0:T(8,128)(2,1)}, bf16[5,32,4096]{2,1,0:T(8,128)(2,1)S(1)}, u32[]{:S(2)}, u32[]{:S(2)}) collective-permute-start(bf16[5,32,4096]{2,1,0:T(8,128)(2,1)} %get-tuple-element.8), channel_id=1, source_target_pairs={{4,0},{8,4},{12,8},{16,12},{20,16},{24,20},{28,24},{32,28},{36,32}... | collective-permute-start | bytes 3932168 | tf_op jit(solution)/shard_map/ppermute | solution.py:33
  18.5 15.5 %collective-permute-start.3 = (bf16[64,1,1]{2,1,0:T(2,128)(2,1)S(1)}, bf16[64,1,1]{2,1,0:T(2,128)(2,1)S(1)}, u32[]{:S(2)}, u32[]{:S(2)}) collective-permute-start(bf16[64,1,1]{2,1,0:T(2,128)(2,1)S(1)} %get-tuple-element.33), channel_id=1, source_target_pairs={{4,0},{8,4},{12,8},{16,12},{20,16},{24,20},{28,24},{32,28},{36,32}... | collective-permute-start | bytes 392 | tf_op jit(solution)/shard_map/ppermute | solution.py:23
  20.4 19.5 %collective-permute-start.2 = (bf16[64,1,1]{2,1,0:T(2,128)(2,1)S(1)}, bf16[64,1,1]{2,1,0:T(2,128)(2,1)S(1)}, u32[]{:S(2)}, u32[]{:S(2)}) collective-permute-start(bf16[64,1,1]{2,1,0:T(2,128)(2,1)S(1)} %get-tuple-element.32), channel_id=1, source_target_pairs={{0,4},{4,8},{8,12},{12,16},{16,20},{20,24},{24,28},{28,32},{32,36}... | collective-permute-start | bytes 392 | tf_op jit(solution)/shard_map/ppermute | solution.py:22
  25.6 19.6 %collective-permute-start.6 = (f32[96,32]{0,1:T(8,128)S(1)}, f32[96,32]{0,1:T(8,128)S(1)}, u32[]{:S(2)}, u32[]{:S(2)}) collective-permute-start(f32[96,32]{0,1:T(8,128)S(1)} %get-tuple-element.29), channel_id=1, source_target_pairs={{0,4},{4,8},{8,12},{12,16},{16,20},{20,24},{24,28},{28,32},{32,36}... | collective-permute-start | bytes 36872 | tf_op jit(solution)/shard_map/ppermute | solution.py:32
  34.0 12.5 %collective-permute-start.7 = (f32[96,32]{0,1:T(8,128)S(1)}, f32[96,32]{0,1:T(8,128)S(1)}, u32[]{:S(2)}, u32[]{:S(2)}) collective-permute-start(f32[96,32]{0,1:T(8,128)S(1)} %get-tuple-element.28), channel_id=1, source_target_pairs={{4,0},{8,4},{12,8},{16,12},{20,16},{24,20},{28,24},{32,28},{36,32}... | collective-permute-start | bytes 36872 | tf_op jit(solution)/shard_map/ppermute | solution.py:33
  40.8 8.1 %collective-permute-start.5 = (bf16[64,1,258]{2,1,0:T(2,128)(2,1)}, bf16[64,1,258]{2,1,0:T(2,128)(2,1)S(1)}, u32[]{:S(2)}, u32[]{:S(2)}) collective-permute-start(bf16[64,1,258]{2,1,0:T(2,128)(2,1)} %pad_maximum_fusion.2), channel_id=1, source_target_pairs={{0,1},{1,2},{2,3},{4,5},{5,6},{6,7},{8,9},{9,10},{10,11},{12,13},{... | collective-permute-start | bytes 99080 | tf_op jit(solution)/shard_map/ppermute | solution.py:22
  45.2 6.7 %collective-permute-start.4 = (bf16[64,1,258]{2,1,0:T(2,128)(2,1)}, bf16[64,1,258]{2,1,0:T(2,128)(2,1)S(1)}, u32[]{:S(2)}, u32[]{:S(2)}) collective-permute-start(bf16[64,1,258]{2,1,0:T(2,128)(2,1)} %pad_maximum_fusion.2), channel_id=1, source_target_pairs={{1,0},{2,1},{3,2},{5,4},{6,5},{7,6},{9,8},{10,9},{11,10},{13,12},{... | collective-permute-start | bytes 99080 | tf_op jit(solution)/shard_map/ppermute | solution.py:23
  66.5 26.2 %copy-start.1 = (bf16[5,64,64,256]{3,2,1,0:T(8,128)(2,1)S(1)}, bf16[5,64,64,256]{3,2,1,0:T(8,128)(2,1)}, u32[]{:S(2)}) copy-start(bf16[5,64,64,256]{3,2,1,0:T(8,128)(2,1)} %shard_map.152) | copy-start | bytes 31457284
  73.9 4.5 %collective-permute-start.9 = (bf16[64,1,1]{2,0,1:T(8,128)(2,1)S(1)}, bf16[64,1,1]{2,0,1:T(8,128)(2,1)S(1)}, u32[]{:S(2)}, u32[]{:S(2)}) collective-permute-start(bf16[64,1,1]{2,0,1:T(8,128)(2,1)S(1)} %get-tuple-element.65), channel_id=1, source_target_pairs={{4,0},{8,4},{12,8},{16,12},{20,16},{24,20},{28,24},{32,28},{36,32}... | collective-permute-start | bytes 392 | tf_op jit(solution)/shard_map/ppermute | solution.py:23
  75.8 7.2 %collective-permute-start.8 = (bf16[64,1,1]{2,0,1:T(8,128)(2,1)S(1)}, bf16[64,1,1]{2,0,1:T(8,128)(2,1)S(1)}, u32[]{:S(2)}, u32[]{:S(2)}) collective-permute-start(bf16[64,1,1]{2,0,1:T(8,128)(2,1)S(1)} %get-tuple-element.64), channel_id=1, source_target_pairs={{0,4},{4,8},{8,12},{12,16},{16,20},{20,24},{24,28},{28,32},{32,36}... | collective-permute-start | bytes 392 | tf_op jit(solution)/shard_map/ppermute | solution.py:22
  83.1 5.1 %collective-permute-start.11 = (bf16[64,1,258]{2,0,1:T(8,128)(2,1)S(1)}, bf16[64,1,258]{2,0,1:T(8,128)(2,1)S(1)}, u32[]{:S(2)}, u32[]{:S(2)}) collective-permute-start(bf16[64,1,258]{2,0,1:T(8,128)(2,1)S(1)} %pad_maximum_fusion.5), channel_id=1, source_target_pairs={{0,1},{1,2},{2,3},{4,5},{5,6},{6,7},{8,9},{9,10},{10,11},{12,13},{... | collective-permute-start | bytes 99080 | tf_op jit(solution)/shard_map/ppermute | solution.py:22
  86.5 6.0 %collective-permute-start.10 = (bf16[64,1,258]{2,0,1:T(8,128)(2,1)S(1)}, bf16[64,1,258]{2,0,1:T(8,128)(2,1)S(1)}, u32[]{:S(2)}, u32[]{:S(2)}) collective-permute-start(bf16[64,1,258]{2,0,1:T(8,128)(2,1)S(1)} %pad_maximum_fusion.5), channel_id=1, source_target_pairs={{1,0},{2,1},{3,2},{5,4},{6,5},{7,6},{9,8},{10,9},{11,10},{13,12},{... | collective-permute-start | bytes 99080 | tf_op jit(solution)/shard_map/ppermute | solution.py:23
  95.9 4.5 %collective-permute-start.13 = (bf16[64,1,1]{2,0,1:T(8,128)(2,1)S(1)}, bf16[64,1,1]{2,0,1:T(8,128)(2,1)S(1)}, u32[]{:S(2)}, u32[]{:S(2)}) collective-permute-start(bf16[64,1,1]{2,0,1:T(8,128)(2,1)S(1)} %get-tuple-element.59), channel_id=1, source_target_pairs={{4,0},{8,4},{12,8},{16,12},{20,16},{24,20},{28,24},{32,28},{36,32}... | collective-permute-start | bytes 392 | tf_op jit(solution)/shard_map/ppermute | solution.py:23
  97.8 7.2 %collective-permute-start.12 = (bf16[64,1,1]{2,0,1:T(8,128)(2,1)S(1)}, bf16[64,1,1]{2,0,1:T(8,128)(2,1)S(1)}, u32[]{:S(2)}, u32[]{:S(2)}) collective-permute-start(bf16[64,1,1]{2,0,1:T(8,128)(2,1)S(1)} %get-tuple-element.58), channel_id=1, source_target_pairs={{0,4},{4,8},{8,12},{12,16},{16,20},{20,24},{24,28},{28,32},{32,36}... | collective-permute-start | bytes 392 | tf_op jit(solution)/shard_map/ppermute | solution.py:22
  105.1 4.9 %collective-permute-start.15 = (bf16[64,1,258]{2,0,1:T(8,128)(2,1)S(1)}, bf16[64,1,258]{2,0,1:T(8,128)(2,1)S(1)}, u32[]{:S(2)}, u32[]{:S(2)}) collective-permute-start(bf16[64,1,258]{2,0,1:T(8,128)(2,1)S(1)} %pad_maximum_fusion.6), channel_id=1, source_target_pairs={{0,1},{1,2},{2,3},{4,5},{5,6},{6,7},{8,9},{9,10},{10,11},{12,13},{... | collective-permute-start | bytes 99080 | tf_op jit(solution)/shard_map/ppermute | solution.py:22
  108.2 6.2 %collective-permute-start.14 = (bf16[64,1,258]{2,0,1:T(8,128)(2,1)S(1)}, bf16[64,1,258]{2,0,1:T(8,128)(2,1)S(1)}, u32[]{:S(2)}, u32[]{:S(2)}) collective-permute-start(bf16[64,1,258]{2,0,1:T(8,128)(2,1)S(1)} %pad_maximum_fusion.6), channel_id=1, source_target_pairs={{1,0},{2,1},{3,2},{5,4},{6,5},{7,6},{9,8},{10,9},{11,10},{13,12},{... | collective-permute-start | bytes 99080 | tf_op jit(solution)/shard_map/ppermute | solution.py:23
  117.7 4.5 %collective-permute-start.17 = (bf16[64,1,1]{2,0,1:T(8,128)(2,1)S(1)}, bf16[64,1,1]{2,0,1:T(8,128)(2,1)S(1)}, u32[]{:S(2)}, u32[]{:S(2)}) collective-permute-start(bf16[64,1,1]{2,0,1:T(8,128)(2,1)S(1)} %get-tuple-element.55), channel_id=1, source_target_pairs={{4,0},{8,4},{12,8},{16,12},{20,16},{24,20},{28,24},{32,28},{36,32}... | collective-permute-start | bytes 392 | tf_op jit(solution)/shard_map/ppermute | solution.py:23
  119.7 7.2 %collective-permute-start.16 = (bf16[64,1,1]{2,0,1:T(8,128)(2,1)S(1)}, bf16[64,1,1]{2,0,1:T(8,128)(2,1)S(1)}, u32[]{:S(2)}, u32[]{:S(2)}) collective-permute-start(bf16[64,1,1]{2,0,1:T(8,128)(2,1)S(1)} %get-tuple-element.54), channel_id=1, source_target_pairs={{0,4},{4,8},{8,12},{12,16},{16,20},{20,24},{24,28},{28,32},{32,36}... | collective-permute-start | bytes 392 | tf_op jit(solution)/shard_map/ppermute | solution.py:22
  126.9 3.7 %collective-permute-start.19 = (bf16[64,1,258]{2,0,1:T(8,128)(2,1)S(1)}, bf16[64,1,258]{2,0,1:T(8,128)(2,1)S(1)}, u32[]{:S(2)}, u32[]{:S(2)}) collective-permute-start(bf16[64,1,258]{2,0,1:T(8,128)(2,1)S(1)} %pad_maximum_fusion.7), channel_id=1, source_target_pairs={{0,1},{1,2},{2,3},{4,5},{5,6},{6,7},{8,9},{9,10},{10,11},{12,13},{... | collective-permute-start | bytes 99080 | tf_op jit(solution)/shard_map/ppermute | solution.py:22
  128.8 6.0 %collective-permute-start.18 = (bf16[64,1,258]{2,0,1:T(8,128)(2,1)S(1)}, bf16[64,1,258]{2,0,1:T(8,128)(2,1)S(1)}, u32[]{:S(2)}, u32[]{:S(2)}) collective-permute-start(bf16[64,1,258]{2,0,1:T(8,128)(2,1)S(1)} %pad_maximum_fusion.7), channel_id=1, source_target_pairs={{1,0},{2,1},{3,2},{5,4},{6,5},{7,6},{9,8},{10,9},{11,10},{13,12},{... | collective-permute-start | bytes 99080 | tf_op jit(solution)/shard_map/ppermute | solution.py:23
  (20 other events, 351.0 us)

commit v11 on v10

--- a/solution.py
+++ b/solution.py
@@ -160,6 +160,31 @@
         arrival,
     )
 
+    place_all = jnp.concatenate([place_lo, place_hi], 0)
+    arrived_all = jnp.concatenate([stiff_lower, stiff_higher], 1)
+    rows_i, rows_j = stiffness_old.shape[1:3]
+    segments = (
+        jnp.arange(rows_i * rows_j, dtype=jnp.int32)[:, None] // rows_j
+        == jnp.arange(rows_i, dtype=jnp.int32)[None, :]
+    ).astype(jnp.float32)
+
+    def first_force(neighbours):
+        own = jnp.sum(
+            stiffness_old.astype(jnp.float32) * neighbours.astype(jnp.float32)[:, None, :, :],
+            axis=(0, 2),
+        )
+        picked = jnp.einsum(
+            "kjb,mb->kmj", neighbours, place_all.astype(jnp.bfloat16),
+            preferred_element_type=jnp.float32,
+        )
+        spread = jnp.tile(picked, (1, 1, rows_i))
+        partial = jnp.sum(arrived_all.astype(jnp.float32) * spread, axis=0)
+        per_block = jnp.dot(partial, segments, precision=lax.Precision.HIGHEST)
+        placed = jnp.dot(
+            per_block.T, place_all.astype(jnp.float32), precision=lax.Precision.HIGHEST
+        )
+        return jnp.where(arrival > 0, placed, own)
+
     outgoing = send_slot[0].reshape(-1)
     filled = count_live.reshape(-1)
     target = jnp.where(filled, arrive_place[0].reshape(-1), blocks)
@@ -192,10 +217,15 @@
         for code_index in range(9):
             shifted = padded[:, code_index // 3, code_index % 3 : code_index % 3 + blocks]
             neighbours = jnp.where(codes == code_index, shifted[None], neighbours)
-        product = stiffness.astype(jnp.float32) * neighbours.astype(jnp.float32)[:, None, :, :]
-        force = jnp.sum(product, axis=(0, 2)) + jnp.dot(
-            strain_map.T, history, precision=lax.Precision.HIGHEST
-        )
+        if repeat == 0:
+            force = first_force(neighbours) + jnp.dot(
+                strain_map.T, history, precision=lax.Precision.HIGHEST
+            )
+        else:
+            product = stiffness.astype(jnp.float32) * neighbours.astype(jnp.float32)[:, None, :, :]
+            force = jnp.sum(product, axis=(0, 2)) + jnp.dot(
+                strain_map.T, history, precision=lax.Precision.HIGHEST
+            )
         speeds = speeds + time_step * (scaling * (forcing - force))
         advanced = moved + time_step * speeds
         history = decay * history + jnp.dot(

time: 141 us -> 158 us (1.12)
  other arithmetic: 21.3 us -> 29.3 us
  local copies, waits for them, and re-layouts: 14.3 us -> 19.3 us
  starting transfers between devices: 49.9 us -> 54.3 us
  waiting for transfers between devices: 31.4 us -> 29.3 us
    reduce_sum x0 -> x2, other arithmetic: none -> 12.1 us  [the longest x1 6.7 us: first_force(): jnp.sum(stiffness_old.astype(jnp.float32) * neighbours.astype(jnp.float32...]
    concatenate x0 -> x2, local copies, waits for them, and re-layouts: none -> 8.68 us  [on_device(): arrived_all = jnp.concatenate([stiff_lower, stiff_higher], 1)]
    unnamed x64 -> x42, local copies, waits for them, and re-layouts: 7.57 us -> 2.41 us
    ppermute x8, starting transfers between devices: 13 us -> 17.5 us  [padded_2(): after = lax.ppermute(first, axis, down)]
    ppermute x8, waiting for transfers between devices: 14.5 us -> 10.4 us  [padded_2(): before = lax.ppermute(last, axis, up)]
    ppermute x2, waiting for transfers between devices: 0.01 us -> 3.52 us  [neighbour_exchange(): from_lower = lax.ppermute(upper_bound, axis, up)]
    reduce_sum x4 -> x3, other arithmetic: 15.3 us -> 12.3 us  [on_device(): jnp.sum(product, axis=(0, 2))]
    reduce_sum x0 -> x1, local copies, waits for them, and re-layouts: none -> 2.12 us  [first_force(): partial = jnp.sum(arrived_all.astype(jnp.float32) * spread, axis=0)]
  transfers between devices with their start and end apart: 20 -> 20, of which waited for: 11 -> 10; matrix products, arithmetic and copies ran while one was open for 10% -> 13% of each run, Pallas kernels for 0% -> 13%
where the time goes in v11:
time: 158 us; the launch traced here: 157 us
  starting transfers between devices  54.3 us (34%)
  other arithmetic  29.3 us (19%)
  waiting for transfers between devices  29.3 us (19%)
  Pallas kernels  20.1 us (13%)
  local copies, waits for them, and re-layouts  19.3 us (12%)
  matrix products  3.33 us (2%)
    ppermute x8, starting transfers between devices, padded_2(): before = lax.ppermute(last, axis, up)  21.4 us
    ppermute x8, starting transfers between devices, padded_2(): after = lax.ppermute(first, axis, down)  17.5 us
    ppermute x8, waiting for transfers between devices, padded_2(): after = lax.ppermute(first, axis, down)  15.4 us
    reduce_sum x3, other arithmetic, on_device(): jnp.sum(product, axis=(0, 2))  12.3 us
    pallas_call x1, Pallas kernels, merge_arrived(): pl.pallas_call(merge_kernel, grid=(slots,), in_specs=[pl.BlockSpec((1, ro...  11.7 us
    ppermute x2, starting transfers between devices, neighbour_exchange(): from_higher = lax.ppermute(lower_bound, axis, down)  11.5 us
    ppermute x8, waiting for transfers between devices, padded_2(): before = lax.ppermute(last, axis, up)  10.4 us
    concatenate x2, local copies, waits for them, and re-layouts, on_device(): arrived_all = jnp.concatenate([stiff_lower, stiff_higher], 1)  8.68 us
  transfers between devices with their start and end apart: 20, of which 10 were waited for; matrix products, arithmetic and copies ran while one was open for 13% of the time, Pallas kernels for 13%

profile of v11, /device:TPU:96, one launch (start us, length us, event | category | flops | bytes accessed | tf_op | source)
XLA Modules:
  0.0 157.1 jit_solution(11416678697631439435)
XLA Ops:
  1.8 4.2 %collective-permute-start.3 = (bf16[64,1,1]{2,1,0:T(2,128)(2,1)S(1)}, bf16[64,1,1]{2,1,0:T(2,128)(2,1)S(1)}, u32[]{:S(2)}, u32[]{:S(2)}) collective-permute-start(bf16[64,1,1]{2,1,0:T(2,128)(2,1)S(1)} %get-tuple-element.35), channel_id=1, source_target_pairs={{4,0},{8,4},{12,8},{16,12},{20,16},{24,20},{28,24},{32,28},{36,32}... | collective-permute-start | bytes 392 | tf_op jit(solution)/shard_map/ppermute | solution.py:23
  9.4 8.4 %shard_map.151 = (bf16[5,32,4096]{2,1,0:T(8,128)(2,1)}, bf16[5,32,4096]{2,1,0:T(8,128)(2,1)}) custom-call(bf16[5,4096,256]{2,1,0:T(8,128)(2,1)} %bitcast.236, bf16[32,256]{1,0:T(8,128)(2,1)} %get-tuple-element.113.lo_ref, bf16[32,256]{1,0:T(8,128)(2,1)} %get-tuple-element.114.hi_ref), custom_call_target="tpu_custom_call" | custom-call | tf_op jit(solution)/shard_map/pallas_call | solution.py:51
  17.8 5.7 %collective-permute-start.1 = (bf16[5,32,4096]{2,1,0:T(8,128)(2,1)}, bf16[5,32,4096]{2,1,0:T(8,128)(2,1)}, u32[]{:S(2)}, u32[]{:S(2)}) collective-permute-start(bf16[5,32,4096]{2,1,0:T(8,128)(2,1)} %get-tuple-element.8), channel_id=1, source_target_pairs={{4,0},{8,4},{12,8},{16,12},{20,16},{24,20},{28,24},{32,28},{36,32}... | collective-permute-start | bytes 3932168 | tf_op jit(solution)/shard_map/ppermute | solution.py:33
  31.6 5.7 %collective-permute-start.7 = (f32[96,32]{0,1:T(8,128)S(1)}, f32[96,32]{0,1:T(8,128)S(1)}, u32[]{:S(2)}, u32[]{:S(2)}) collective-permute-start(f32[96,32]{0,1:T(8,128)S(1)} %get-tuple-element.30), channel_id=1, source_target_pairs={{4,0},{8,4},{12,8},{16,12},{20,16},{24,20},{28,24},{32,28},{36,32}... | collective-permute-start | bytes 36872 | tf_op jit(solution)/shard_map/ppermute | solution.py:33
  37.7 3.4 %collective-permute-start.5 = (bf16[64,1,258]{2,1,0:T(2,128)(2,1)S(1)}, bf16[64,1,258]{2,1,0:T(2,128)(2,1)S(1)}, u32[]{:S(2)}, u32[]{:S(2)}) collective-permute-start(bf16[64,1,258]{2,1,0:T(2,128)(2,1)S(1)} %pad_maximum_fusion.2), channel_id=1, source_target_pairs={{0,1},{1,2},{2,3},{4,5},{5,6},{6,7},{8,9},{9,10},{10,11},{12,13},{... | collective-permute-start | bytes 99080 | tf_op jit(solution)/shard_map/ppermute | solution.py:22
  41.4 3.5 %collective-permute-done.6 = f32[96,32]{0,1:T(8,128)S(1)} collective-permute-done((f32[96,32]{0,1:T(8,128)S(1)}, f32[96,32]{0,1:T(8,128)S(1)}, u32[]{:S(2)}, u32[]{:S(2)}) %collective-permute-start.6) | collective-permute-done | bytes 12320 | tf_op jit(solution)/shard_map/ppermute | solution.py:32
  48.5 3.0 %collective-permute-done.4 = bf16[64,1,258]{2,1,0:T(2,128)(2,1)S(1)} collective-permute-done((bf16[64,1,258]{2,1,0:T(2,128)(2,1)S(1)}, bf16[64,1,258]{2,1,0:T(2,128)(2,1)S(1)}, u32[]{:S(2)}, u32[]{:S(2)}) %collective-permute-start.4) | collective-permute-done | bytes 33056 | tf_op jit(solution)/shard_map/ppermute | solution.py:23
  52.1 6.7 %multiply_reduce_fusion = f32[64,256]{1,0:T(8,128)S(1)} fusion(bf16[5,64,64,256]{3,2,1,0:T(8,128)(2,1)} %s_ref.1, f32[5,64,256]{2,1,0:T(8,128)S(1)} %get-tuple-element.22), kind=kLoop, calls=%fused_computation.11 | loop fusion | flops 15712256 | bytes 10878976 | tf_op jit(solution)/shard_map/reduce_sum | solution.py:172
  58.9 3.9 %concatenate.66 = bf16[1,5,1,32,64,64]{5,4,3,1,2,0:T(8,128)(2,1)S(1)} reshape(bf16[5,32,4096]{2,1,0:T(8,128)(2,1)} %collective-permute-done.1.hi_ref) | data formatting | bytes 2621440 | tf_op jit(solution)/shard_map/concatenate | solution.py:164
  62.7 4.8 %concatenate.65 = bf16[1,5,1,32,64,64]{5,4,3,1,2,0:T(8,128)(2,1)} reshape(bf16[5,32,4096]{2,1,0:T(8,128)(2,1)} %collective-permute-done.lo_ref) | data formatting | bytes 2621440 | tf_op jit(solution)/shard_map/concatenate | solution.py:164
  67.6 5.4 %multiply_reduce_fusion.1 = f32[64,64,64]{2,1,0:T(8,128)} fusion(bf16[1,5,1,32,64,64]{5,4,3,1,2,0:T(8,128)(2,1)S(1)} %concatenate.66, bf16[1,5,1,32,64,64]{5,4,3,1,2,0:T(8,128)(2,1)} %concatenate.65, f32[5,64,64]{2,1,0:T(8,128)S(1)} %convolution_bitcast_fusion), kind=kLoop, calls=%fused_computation.12 | loop fusion | flops 4980736 | bytes 3751936 | tf_op jit(solution)/shard_map/reduce_sum | solution.py:181
  78.7 2.4 %collective-permute-start.8 = (bf16[64,1,1]{2,0,1:T(8,128)(2,1)S(1)}, bf16[64,1,1]{2,0,1:T(8,128)(2,1)S(1)}, u32[]{:S(2)}, u32[]{:S(2)}) collective-permute-start(bf16[64,1,1]{2,0,1:T(8,128)(2,1)S(1)} %get-tuple-element.66), channel_id=1, source_target_pairs={{0,4},{4,8},{8,12},{12,16},{16,20},{20,24},{24,28},{28,32},{32,36}... | collective-permute-start | bytes 392 | tf_op jit(solution)/shard_map/ppermute | solution.py:22
  81.3 11.7 %shard_map.152 = bf16[5,64,64,256]{3,2,1,0:T(8,128)(2,1)} custom-call(bf16[5,64,64,256]{3,2,1,0:T(8,128)(2,1)} %s_ref.1, bf16[5,32,4096]{2,1,0:T(8,128)(2,1)} %collective-permute-done.lo_ref, bf16[5,32,4096]{2,1,0:T(8,128)(2,1)} %collective-permute-done.1.hi_ref, bf16[32,256]{1,0:T(8,128)(2,1)} %get-tuple-element.117.place_lo_ref, ...), custom_call_target="tpu_custom_call" | custom-call | tf_op jit(solution)/shard_map/pallas_call | solution.py:79
  93.1 3.7 %collective-permute-start.11 = (bf16[64,1,258]{2,0,1:T(8,128)(2,1)S(1)}, bf16[64,1,258]{2,0,1:T(8,128)(2,1)S(1)}, u32[]{:S(2)}, u32[]{:S(2)}) collective-permute-start(bf16[64,1,258]{2,0,1:T(8,128)(2,1)S(1)} %pad_maximum_fusion.5), channel_id=1, source_target_pairs={{0,1},{1,2},{2,3},{4,5},{5,6},{6,7},{8,9},{9,10},{10,11},{12,13},{... | collective-permute-start | bytes 99080 | tf_op jit(solution)/shard_map/ppermute | solution.py:22
  98.6 4.2 %collective-permute-done.10 = bf16[64,1,258]{2,0,1:T(8,128)(2,1)S(1)} collective-permute-done((bf16[64,1,258]{2,0,1:T(8,128)(2,1)S(1)}, bf16[64,1,258]{2,0,1:T(8,128)(2,1)S(1)}, u32[]{:S(2)}, u32[]{:S(2)}) %collective-permute-start.10) | collective-permute-done | bytes 33056 | tf_op jit(solution)/shard_map/ppermute | solution.py:23
  103.0 6.7 %fusion = f32[64,256]{1,0:T(8,128)S(1)} fusion(bf16[5,64,64,256]{3,2,1,0:T(8,128)(2,1)} %shard_map.152, f32[5,64,256]{2,1,0:T(8,128)S(1)} %select_convert_fusion.2), kind=kLoop, calls=%fused_computation.8 | loop fusion | flops 15712256 | bytes 10878976 | tf_op jit(solution)/shard_map/reduce_sum | solution.py:226
  110.0 4.0 %collective-permute-start.13 = (bf16[64,1,1]{2,0,1:T(8,128)(2,1)S(1)}, bf16[64,1,1]{2,0,1:T(8,128)(2,1)S(1)}, u32[]{:S(2)}, u32[]{:S(2)}) collective-permute-start(bf16[64,1,1]{2,0,1:T(8,128)(2,1)S(1)} %get-tuple-element.61), channel_id=1, source_target_pairs={{4,0},{8,4},{12,8},{16,12},{20,16},{24,20},{28,24},{32,28},{36,32}... | collective-permute-start | bytes 392 | tf_op jit(solution)/shard_map/ppermute | solution.py:23
  116.2 5.0 %collective-permute-done.12 = bf16[64,1,1]{2,0,1:T(8,128)(2,1)S(1)} collective-permute-done((bf16[64,1,1]{2,0,1:T(8,128)(2,1)S(1)}, bf16[64,1,1]{2,0,1:T(8,128)(2,1)S(1)}, u32[]{:S(2)}, u32[]{:S(2)}) %collective-permute-start.12) | collective-permute-done | bytes 160 | tf_op jit(solution)/shard_map/ppermute | solution.py:22
  121.3 3.4 %collective-permute-start.15 = (bf16[64,1,258]{2,0,1:T(8,128)(2,1)S(1)}, bf16[64,1,258]{2,0,1:T(8,128)(2,1)S(1)}, u32[]{:S(2)}, u32[]{:S(2)}) collective-permute-start(bf16[64,1,258]{2,0,1:T(8,128)(2,1)S(1)} %pad_maximum_fusion.6), channel_id=1, source_target_pairs={{0,1},{1,2},{2,3},{4,5},{5,6},{6,7},{8,9},{9,10},{10,11},{12,13},{... | collective-permute-start | bytes 99080 | tf_op jit(solution)/shard_map/ppermute | solution.py:22
  126.5 4.2 %collective-permute-done.14 = bf16[64,1,258]{2,0,1:T(8,128)(2,1)S(1)} collective-permute-done((bf16[64,1,258]{2,0,1:T(8,128)(2,1)S(1)}, bf16[64,1,258]{2,0,1:T(8,128)(2,1)S(1)}, u32[]{:S(2)}, u32[]{:S(2)}) %collective-permute-start.14) | collective-permute-done | bytes 33056 | tf_op jit(solution)/shard_map/ppermute | solution.py:23
  130.9 2.8 %fusion.1 = f32[64,256]{1,0:T(8,128)S(1)} fusion(bf16[5,64,64,256]{3,2,1,0:T(8,128)(2,1)S(1)} %copy-done.1, f32[5,64,256]{2,1,0:T(8,128)S(1)} %select_convert_fusion.1), kind=kLoop, calls=%fused_computation.9 | loop fusion | flops 15712256 | bytes 10878976 | tf_op jit(solution)/shard_map/reduce_sum | solution.py:226
  138.6 4.5 %collective-permute-done.16 = bf16[64,1,1]{2,0,1:T(8,128)(2,1)S(1)} collective-permute-done((bf16[64,1,1]{2,0,1:T(8,128)(2,1)S(1)}, bf16[64,1,1]{2,0,1:T(8,128)(2,1)S(1)}, u32[]{:S(2)}, u32[]{:S(2)}) %collective-permute-start.16) | collective-permute-done | bytes 160 | tf_op jit(solution)/shard_map/ppermute | solution.py:22
  147.4 4.2 %collective-permute-done.18 = bf16[64,1,258]{2,0,1:T(8,128)(2,1)S(1)} collective-permute-done((bf16[64,1,258]{2,0,1:T(8,128)(2,1)S(1)}, bf16[64,1,258]{2,0,1:T(8,128)(2,1)S(1)}, u32[]{:S(2)}, u32[]{:S(2)}) %collective-permute-start.18) | collective-permute-done | bytes 33056 | tf_op jit(solution)/shard_map/ppermute | solution.py:23
  151.8 2.8 %fusion.2 = f32[64,256]{1,0:T(8,128)S(1)} fusion(bf16[5,64,64,256]{3,2,1,0:T(8,128)(2,1)S(1)} %copy-done.1, f32[5,64,256]{2,1,0:T(8,128)S(1)} %select_convert_fusion), kind=kLoop, calls=%fused_computation.10 | loop fusion | flops 15712256 | bytes 10878976 | tf_op jit(solution)/shard_map/reduce_sum | solution.py:226
  (138 shorter events, 41.5 us)
Async XLA Ops:
  0.6 75.7 %copy-start = (f32[48,64]{1,0:T(8,128)S(1)}, f32[48,64]{1,0:T(8,128)}, u32[]{:S(2)}) copy-start(f32[48,64]{1,0:T(8,128)} %param.26) | copy-start | bytes 36868
  0.7 29.5 %copy-start.8 = (s32[5,1,256]{2,1,0:T(1,128)S(1)}, s32[5,1,256]{2,1,0:T(1,128)}, u32[]{:S(2)}) copy-start(s32[5,1,256]{2,1,0:T(1,128)} %param.21) | copy-start | bytes 15364
  0.7 29.5 %copy-start.9 = (s32[1,256]{1,0:T(1,128)S(1)}, s32[1,256]{1,0:T(1,128)}, u32[]{:S(2)}) copy-start(s32[1,256]{1,0:T(1,128)} %param.22) | copy-start | bytes 3076
  1.8 29.9 %collective-permute-start.3 = (bf16[64,1,1]{2,1,0:T(2,128)(2,1)S(1)}, bf16[64,1,1]{2,1,0:T(2,128)(2,1)S(1)}, u32[]{:S(2)}, u32[]{:S(2)}) collective-permute-start(bf16[64,1,1]{2,1,0:T(2,128)(2,1)S(1)} %get-tuple-element.35), channel_id=1, source_target_pairs={{4,0},{8,4},{12,8},{16,12},{20,16},{24,20},{28,24},{32,28},{36,32}... | collective-permute-start | bytes 392 | tf_op jit(solution)/shard_map/ppermute | solution.py:23
  6.0 31.4 %collective-permute-start.2 = (bf16[64,1,1]{2,1,0:T(2,128)(2,1)S(1)}, bf16[64,1,1]{2,1,0:T(2,128)(2,1)S(1)}, u32[]{:S(2)}, u32[]{:S(2)}) collective-permute-start(bf16[64,1,1]{2,1,0:T(2,128)(2,1)S(1)} %get-tuple-element.34), channel_id=1, source_target_pairs={{0,4},{4,8},{8,12},{12,16},{16,20},{20,24},{24,28},{28,32},{32,36}... | collective-permute-start | bytes 392 | tf_op jit(solution)/shard_map/ppermute | solution.py:22
  17.8 41.1 %collective-permute-start.1 = (bf16[5,32,4096]{2,1,0:T(8,128)(2,1)}, bf16[5,32,4096]{2,1,0:T(8,128)(2,1)}, u32[]{:S(2)}, u32[]{:S(2)}) collective-permute-start(bf16[5,32,4096]{2,1,0:T(8,128)(2,1)} %get-tuple-element.8), channel_id=1, source_target_pairs={{4,0},{8,4},{12,8},{16,12},{20,16},{24,20},{28,24},{32,28},{36,32}... | collective-permute-start | bytes 3932168 | tf_op jit(solution)/shard_map/ppermute | solution.py:33
  23.5 39.2 %collective-permute-start = (bf16[5,32,4096]{2,1,0:T(8,128)(2,1)}, bf16[5,32,4096]{2,1,0:T(8,128)(2,1)}, u32[]{:S(2)}, u32[]{:S(2)}) collective-permute-start(bf16[5,32,4096]{2,1,0:T(8,128)(2,1)} %get-tuple-element.7), channel_id=1, source_target_pairs={{0,4},{4,8},{8,12},{12,16},{16,20},{20,24},{24,28},{28,32},{32,36}... | collective-permute-start | bytes 3932168 | tf_op jit(solution)/shard_map/ppermute | solution.py:32
  28.2 16.7 %collective-permute-start.6 = (f32[96,32]{0,1:T(8,128)S(1)}, f32[96,32]{0,1:T(8,128)S(1)}, u32[]{:S(2)}, u32[]{:S(2)}) collective-permute-start(f32[96,32]{0,1:T(8,128)S(1)} %get-tuple-element.31), channel_id=1, source_target_pairs={{0,4},{4,8},{8,12},{12,16},{16,20},{20,24},{24,28},{28,32},{32,36}... | collective-permute-start | bytes 36872 | tf_op jit(solution)/shard_map/ppermute | solution.py:32
  31.6 14.8 %collective-permute-start.7 = (f32[96,32]{0,1:T(8,128)S(1)}, f32[96,32]{0,1:T(8,128)S(1)}, u32[]{:S(2)}, u32[]{:S(2)}) collective-permute-start(f32[96,32]{0,1:T(8,128)S(1)} %get-tuple-element.30), channel_id=1, source_target_pairs={{4,0},{8,4},{12,8},{16,12},{20,16},{24,20},{28,24},{32,28},{36,32}... | collective-permute-start | bytes 36872 | tf_op jit(solution)/shard_map/ppermute | solution.py:33
  37.7 10.5 %collective-permute-start.5 = (bf16[64,1,258]{2,1,0:T(2,128)(2,1)S(1)}, bf16[64,1,258]{2,1,0:T(2,128)(2,1)S(1)}, u32[]{:S(2)}, u32[]{:S(2)}) collective-permute-start(bf16[64,1,258]{2,1,0:T(2,128)(2,1)S(1)} %pad_maximum_fusion.2), channel_id=1, source_target_pairs={{0,1},{1,2},{2,3},{4,5},{5,6},{6,7},{8,9},{9,10},{10,11},{12,13},{... | collective-permute-start | bytes 99080 | tf_op jit(solution)/shard_map/ppermute | solution.py:22
  45.0 6.5 %collective-permute-start.4 = (bf16[64,1,258]{2,1,0:T(2,128)(2,1)S(1)}, bf16[64,1,258]{2,1,0:T(2,128)(2,1)S(1)}, u32[]{:S(2)}, u32[]{:S(2)}) collective-permute-start(bf16[64,1,258]{2,1,0:T(2,128)(2,1)S(1)} %pad_maximum_fusion.2), channel_id=1, source_target_pairs={{1,0},{2,1},{3,2},{5,4},{6,5},{7,6},{9,8},{10,9},{11,10},{13,12},{... | collective-permute-start | bytes 99080 | tf_op jit(solution)/shard_map/ppermute | solution.py:23
  76.8 16.2 %collective-permute-start.9 = (bf16[64,1,1]{2,0,1:T(8,128)(2,1)S(1)}, bf16[64,1,1]{2,0,1:T(8,128)(2,1)S(1)}, u32[]{:S(2)}, u32[]{:S(2)}) collective-permute-start(bf16[64,1,1]{2,0,1:T(8,128)(2,1)S(1)} %get-tuple-element.67), channel_id=1, source_target_pairs={{4,0},{8,4},{12,8},{16,12},{20,16},{24,20},{28,24},{32,28},{36,32}... | collective-permute-start | bytes 392 | tf_op jit(solution)/shard_map/ppermute | solution.py:23
  78.7 14.3 %collective-permute-start.8 = (bf16[64,1,1]{2,0,1:T(8,128)(2,1)S(1)}, bf16[64,1,1]{2,0,1:T(8,128)(2,1)S(1)}, u32[]{:S(2)}, u32[]{:S(2)}) collective-permute-start(bf16[64,1,1]{2,0,1:T(8,128)(2,1)S(1)} %get-tuple-element.66), channel_id=1, source_target_pairs={{0,4},{4,8},{8,12},{12,16},{16,20},{20,24},{24,28},{28,32},{32,36}... | collective-permute-start | bytes 392 | tf_op jit(solution)/shard_map/ppermute | solution.py:22
  93.0 37.9 %copy-start.1 = (bf16[5,64,64,256]{3,2,1,0:T(8,128)(2,1)S(1)}, bf16[5,64,64,256]{3,2,1,0:T(8,128)(2,1)}, u32[]{:S(2)}) copy-start(bf16[5,64,64,256]{3,2,1,0:T(8,128)(2,1)} %shard_map.152) | copy-start | bytes 31457284
  93.1 5.4 %collective-permute-start.11 = (bf16[64,1,258]{2,0,1:T(8,128)(2,1)S(1)}, bf16[64,1,258]{2,0,1:T(8,128)(2,1)S(1)}, u32[]{:S(2)}, u32[]{:S(2)}) collective-permute-start(bf16[64,1,258]{2,0,1:T(8,128)(2,1)S(1)} %pad_maximum_fusion.5), channel_id=1, source_target_pairs={{0,1},{1,2},{2,3},{4,5},{5,6},{6,7},{8,9},{9,10},{10,11},{12,13},{... | collective-permute-start | bytes 99080 | tf_op jit(solution)/shard_map/ppermute | solution.py:22
  96.8 6.0 %collective-permute-start.10 = (bf16[64,1,258]{2,0,1:T(8,128)(2,1)S(1)}, bf16[64,1,258]{2,0,1:T(8,128)(2,1)S(1)}, u32[]{:S(2)}, u32[]{:S(2)}) collective-permute-start(bf16[64,1,258]{2,0,1:T(8,128)(2,1)S(1)} %pad_maximum_fusion.5), channel_id=1, source_target_pairs={{1,0},{2,1},{3,2},{5,4},{6,5},{7,6},{9,8},{10,9},{11,10},{13,12},{... | collective-permute-start | bytes 99080 | tf_op jit(solution)/shard_map/ppermute | solution.py:23
  110.0 6.1 %collective-permute-start.13 = (bf16[64,1,1]{2,0,1:T(8,128)(2,1)S(1)}, bf16[64,1,1]{2,0,1:T(8,128)(2,1)S(1)}, u32[]{:S(2)}, u32[]{:S(2)}) collective-permute-start(bf16[64,1,1]{2,0,1:T(8,128)(2,1)S(1)} %get-tuple-element.61), channel_id=1, source_target_pairs={{4,0},{8,4},{12,8},{16,12},{20,16},{24,20},{28,24},{32,28},{36,32}... | collective-permute-start | bytes 392 | tf_op jit(solution)/shard_map/ppermute | solution.py:23
  114.0 7.2 %collective-permute-start.12 = (bf16[64,1,1]{2,0,1:T(8,128)(2,1)S(1)}, bf16[64,1,1]{2,0,1:T(8,128)(2,1)S(1)}, u32[]{:S(2)}, u32[]{:S(2)}) collective-permute-start(bf16[64,1,1]{2,0,1:T(8,128)(2,1)S(1)} %get-tuple-element.60), channel_id=1, source_target_pairs={{0,4},{4,8},{8,12},{12,16},{16,20},{20,24},{24,28},{28,32},{32,36}... | collective-permute-start | bytes 392 | tf_op jit(solution)/shard_map/ppermute | solution.py:22
  121.3 5.1 %collective-permute-start.15 = (bf16[64,1,258]{2,0,1:T(8,128)(2,1)S(1)}, bf16[64,1,258]{2,0,1:T(8,128)(2,1)S(1)}, u32[]{:S(2)}, u32[]{:S(2)}) collective-permute-start(bf16[64,1,258]{2,0,1:T(8,128)(2,1)S(1)} %pad_maximum_fusion.6), channel_id=1, source_target_pairs={{0,1},{1,2},{2,3},{4,5},{5,6},{6,7},{8,9},{9,10},{10,11},{12,13},{... | collective-permute-start | bytes 99080 | tf_op jit(solution)/shard_map/ppermute | solution.py:22
  124.7 6.0 %collective-permute-start.14 = (bf16[64,1,258]{2,0,1:T(8,128)(2,1)S(1)}, bf16[64,1,258]{2,0,1:T(8,128)(2,1)S(1)}, u32[]{:S(2)}, u32[]{:S(2)}) collective-permute-start(bf16[64,1,258]{2,0,1:T(8,128)(2,1)S(1)} %pad_maximum_fusion.6), channel_id=1, source_target_pairs={{1,0},{2,1},{3,2},{5,4},{6,5},{7,6},{9,8},{10,9},{11,10},{13,12},{... | collective-permute-start | bytes 99080 | tf_op jit(solution)/shard_map/ppermute | solution.py:23
  134.0 4.5 %collective-permute-start.17 = (bf16[64,1,1]{2,0,1:T(8,128)(2,1)S(1)}, bf16[64,1,1]{2,0,1:T(8,128)(2,1)S(1)}, u32[]{:S(2)}, u32[]{:S(2)}) collective-permute-start(bf16[64,1,1]{2,0,1:T(8,128)(2,1)S(1)} %get-tuple-element.57), channel_id=1, source_target_pairs={{4,0},{8,4},{12,8},{16,12},{20,16},{24,20},{28,24},{32,28},{36,32}... | collective-permute-start | bytes 392 | tf_op jit(solution)/shard_map/ppermute | solution.py:23
  136.0 7.2 %collective-permute-start.16 = (bf16[64,1,1]{2,0,1:T(8,128)(2,1)S(1)}, bf16[64,1,1]{2,0,1:T(8,128)(2,1)S(1)}, u32[]{:S(2)}, u32[]{:S(2)}) collective-permute-start(bf16[64,1,1]{2,0,1:T(8,128)(2,1)S(1)} %get-tuple-element.56), channel_id=1, source_target_pairs={{0,4},{4,8},{8,12},{12,16},{16,20},{20,24},{24,28},{28,32},{32,36}... | collective-permute-start | bytes 392 | tf_op jit(solution)/shard_map/ppermute | solution.py:22
  143.2 4.1 %collective-permute-start.19 = (bf16[64,1,258]{2,0,1:T(8,128)(2,1)S(1)}, bf16[64,1,258]{2,0,1:T(8,128)(2,1)S(1)}, u32[]{:S(2)}, u32[]{:S(2)}) collective-permute-start(bf16[64,1,258]{2,0,1:T(8,128)(2,1)S(1)} %pad_maximum_fusion.7), channel_id=1, source_target_pairs={{0,1},{1,2},{2,3},{4,5},{5,6},{6,7},{8,9},{9,10},{10,11},{12,13},{... | collective-permute-start | bytes 99080 | tf_op jit(solution)/shard_map/ppermute | solution.py:22
  145.6 6.0 %collective-permute-start.18 = (bf16[64,1,258]{2,0,1:T(8,128)(2,1)S(1)}, bf16[64,1,258]{2,0,1:T(8,128)(2,1)S(1)}, u32[]{:S(2)}, u32[]{:S(2)}) collective-permute-start(bf16[64,1,258]{2,0,1:T(8,128)(2,1)S(1)} %pad_maximum_fusion.7), channel_id=1, source_target_pairs={{1,0},{2,1},{3,2},{5,4},{6,5},{7,6},{9,8},{10,9},{11,10},{13,12},{... | collective-permute-start | bytes 99080 | tf_op jit(solution)/shard_map/ppermute | solution.py:23
  (9 other events, 208.1 us)

commit v12 on v10

--- a/solution.py
+++ b/solution.py
@@ -145,7 +145,13 @@
     leave_lo = (send_slot[0, 0][:, None] == lanes[None, :]).astype(jnp.bfloat16)
     leave_hi = (send_slot[0, 1][:, None] == lanes[None, :]).astype(jnp.bfloat16)
     stiff_to_lower, stiff_to_higher = gather_leaving(stiff_flat, leave_lo, leave_hi)
-    stiff_lower, stiff_higher = neighbour_exchange("shaft", stiff_to_lower, stiff_to_higher)
+    cut = (slots + 1) // 2
+    pieces = [
+        neighbour_exchange("shaft", stiff_to_lower[part], stiff_to_higher[part])
+        for part in (slice(0, cut), slice(cut, slots))
+    ]
+    stiff_lower = jnp.concatenate([piece[0] for piece in pieces], 0)
+    stiff_higher = jnp.concatenate([piece[1] for piece in pieces], 0)
 
     count_live = jnp.arange(capacity, dtype=jnp.int32)[None, :] < arrive_count[0][:, None]
     place_lo = (arrive_place[0, 0][:, None] == lanes[None, :]) & count_live[0][:, None]

time: 141 us -> 161 us (1.14)
  waiting for transfers between devices: 31.4 us -> 38 us
  starting transfers between devices: 49.9 us -> 55.4 us
  other arithmetic: 21.3 us -> 25.5 us
  local copies, waits for them, and re-layouts: 14.3 us -> 17.6 us
    slice x0 -> x4, local copies, waits for them, and re-layouts: none -> 6.1 us  [the longest x2 3.06 us: on_device(): stiff_to_higher[part]]
    concatenate x0 -> x2, other arithmetic: none -> 4.86 us  [the longest x1 2.53 us: on_device(): stiff_higher = jnp.concatenate([piece[1] for piece in pieces], 0)]
    ppermute x2 -> x3, waiting for transfers between devices: 0.01 us -> 4.01 us  [neighbour_exchange(): from_lower = lax.ppermute(upper_bound, axis, up)]
    ppermute x2 -> x3, starting transfers between devices: 3.82 us -> 7.42 us  [neighbour_exchange(): from_lower = lax.ppermute(upper_bound, axis, up)]
    unnamed x64 -> x52, local copies, waits for them, and re-layouts: 7.57 us -> 4.78 us
    ppermute x8, starting transfers between devices: 13 us -> 15.7 us  [padded_2(): after = lax.ppermute(first, axis, down)]
    ppermute x2 -> x3, starting transfers between devices: 11.7 us -> 11.7 us  [neighbour_exchange(): from_higher = lax.ppermute(lower_bound, axis, down)]
  transfers between devices with their start and end apart: 20 -> 22, of which waited for: 11 -> 12; matrix products, arithmetic and copies ran while one was open for 10% -> 12% of each run, Pallas kernels for 0% -> 0%
where the time goes in v12:
time: 161 us; the launch traced here: 160 us
  starting transfers between devices  55.4 us (34%)
  waiting for transfers between devices  38 us (24%)
  other arithmetic  25.5 us (16%)
  Pallas kernels  20.1 us (12%)
  local copies, waits for them, and re-layouts  17.6 us (11%)
  matrix products  1.85 us (1%)
    ppermute x8, starting transfers between devices, padded_2(): before = lax.ppermute(last, axis, up)  20.6 us
    ppermute x8, waiting for transfers between devices, padded_2(): after = lax.ppermute(first, axis, down)  17.6 us
    ppermute x8, starting transfers between devices, padded_2(): after = lax.ppermute(first, axis, down)  15.7 us
    reduce_sum x4, other arithmetic, on_device(): jnp.sum(product, axis=(0, 2))  15.3 us
    ppermute x8, waiting for transfers between devices, padded_2(): before = lax.ppermute(last, axis, up)  15 us
    ppermute x3, starting transfers between devices, neighbour_exchange(): from_higher = lax.ppermute(lower_bound, axis, down)  11.7 us
    pallas_call x1, Pallas kernels, merge_arrived(): pl.pallas_call(merge_kernel, grid=(slots,), in_specs=[pl.BlockSpec((1, ro...  11.7 us
    pallas_call x1, Pallas kernels, gather_leaving(): pl.pallas_call(gather_kernel, grid=(slots,), in_specs=[pl.BlockSpec((1, d...  8.42 us
  transfers between devices with their start and end apart: 22, of which 12 were waited for; matrix products, arithmetic and copies ran while one was open for 12% of the time, Pallas kernels for 0%

profile of v12, /device:TPU:96, one launch (start us, length us, event | category | flops | bytes accessed | tf_op | source)
XLA Modules:
  0.0 159.9 jit_solution(12593739674003608227)
XLA Ops:
  2.2 8.4 %shard_map.151 = (bf16[5,32,4096]{2,1,0:T(8,128)(2,1)}, bf16[5,32,4096]{2,1,0:T(8,128)(2,1)}) custom-call(bf16[5,4096,256]{2,1,0:T(8,128)(2,1)} %bitcast.228, bf16[32,256]{1,0:T(8,128)(2,1)} %get-tuple-element.91.lo_ref, bf16[32,256]{1,0:T(8,128)(2,1)} %get-tuple-element.92.hi_ref), custom_call_target="tpu_custom_call" | custom-call | tf_op jit(solution)/shard_map/pallas_call | solution.py:51
  15.6 3.6 %collective-permute-start = (bf16[3,32,4096]{2,1,0:T(8,128)(2,1)S(1)}, bf16[3,32,4096]{2,1,0:T(8,128)(2,1)}, u32[]{:S(2)}, u32[]{:S(2)}) collective-permute-start(bf16[3,32,4096]{2,1,0:T(8,128)(2,1)S(1)} %slice.175), channel_id=1, source_target_pairs={{0,4},{4,8},{8,12},{12,16},{16,20},{20,24},{24,28},{28,32},{32,36}... | collective-permute-start | bytes 2359304 | tf_op jit(solution)/shard_map/ppermute | solution.py:32
  21.0 4.1 %collective-permute-start.3 = (bf16[2,32,4096]{2,1,0:T(8,128)(2,1)}, bf16[2,32,4096]{2,1,0:T(8,128)(2,1)}, u32[]{:S(2)}, u32[]{:S(2)}) collective-permute-start(bf16[2,32,4096]{2,1,0:T(8,128)(2,1)} %slice.178), channel_id=1, source_target_pairs={{4,0},{8,4},{12,8},{16,12},{20,16},{24,20},{28,24},{32,28},{36,32}... | collective-permute-start | bytes 1572872 | tf_op jit(solution)/shard_map/ppermute | solution.py:33
  25.3 2.4 %collective-permute-start.5 = (bf16[64,1,1]{2,1,0:T(2,128)(2,1)S(1)}, bf16[64,1,1]{2,1,0:T(2,128)(2,1)S(1)}, u32[]{:S(2)}, u32[]{:S(2)}) collective-permute-start(bf16[64,1,1]{2,1,0:T(2,128)(2,1)S(1)} %get-tuple-element.33), channel_id=1, source_target_pairs={{4,0},{8,4},{12,8},{16,12},{20,16},{24,20},{28,24},{32,28},{36,32}... | collective-permute-start | bytes 392 | tf_op jit(solution)/shard_map/ppermute | solution.py:23
  37.3 5.7 %collective-permute-start.2 = (bf16[3,32,4096]{2,1,0:T(8,128)(2,1)S(1)}, bf16[3,32,4096]{2,1,0:T(8,128)(2,1)}, u32[]{:S(2)}, u32[]{:S(2)}) collective-permute-start(bf16[3,32,4096]{2,1,0:T(8,128)(2,1)S(1)} %slice.177), channel_id=1, source_target_pairs={{4,0},{8,4},{12,8},{16,12},{20,16},{24,20},{28,24},{32,28},{36,32}... | collective-permute-start | bytes 2359304 | tf_op jit(solution)/shard_map/ppermute | solution.py:33
  46.2 4.0 %collective-permute-done.8 = f32[96,32]{0,1:T(8,128)S(1)} collective-permute-done((f32[96,32]{0,1:T(8,128)S(1)}, f32[96,32]{0,1:T(8,128)S(1)}, u32[]{:S(2)}, u32[]{:S(2)}) %collective-permute-start.8) | collective-permute-done | bytes 12320 | tf_op jit(solution)/shard_map/ppermute | solution.py:32
  53.6 3.4 %collective-permute-start.7 = (bf16[64,1,258]{2,1,0:T(2,128)(2,1)S(1)}, bf16[64,1,258]{2,1,0:T(2,128)(2,1)S(1)}, u32[]{:S(2)}, u32[]{:S(2)}) collective-permute-start(bf16[64,1,258]{2,1,0:T(2,128)(2,1)S(1)} %pad_maximum_fusion.4), channel_id=1, source_target_pairs={{0,1},{1,2},{2,3},{4,5},{5,6},{6,7},{8,9},{9,10},{10,11},{12,13},{... | collective-permute-start | bytes 99080 | tf_op jit(solution)/shard_map/ppermute | solution.py:22
  60.9 5.1 %collective-permute-done.6 = bf16[64,1,258]{2,1,0:T(2,128)(2,1)S(1)} collective-permute-done((bf16[64,1,258]{2,1,0:T(2,128)(2,1)S(1)}, bf16[64,1,258]{2,1,0:T(2,128)(2,1)S(1)}, u32[]{:S(2)}, u32[]{:S(2)}) %collective-permute-start.6) | collective-permute-done | bytes 33056 | tf_op jit(solution)/shard_map/ppermute | solution.py:23
  69.7 2.5 %pad_maximum_fusion.1.hi_ref = bf16[5,32,4096]{2,1,0:T(8,128)(2,1)} fusion(bf16[2,32,4096]{2,1,0:T(8,128)(2,1)} %collective-permute-done.3, bf16[3,32,4096]{2,1,0:T(8,128)(2,1)} %collective-permute-done.2), kind=kLoop, calls=%fused_computation.14 | loop fusion | flops 655360 | bytes 2621440 | tf_op jit(solution)/shard_map/concatenate | solution.py:154
  72.2 11.7 %shard_map.152 = bf16[5,64,64,256]{3,2,1,0:T(8,128)(2,1)} custom-call(bf16[5,64,64,256]{3,2,1,0:T(8,128)(2,1)} %s_ref.1, bf16[5,32,4096]{2,1,0:T(8,128)(2,1)} %pad_maximum_fusion.lo_ref, bf16[5,32,4096]{2,1,0:T(8,128)(2,1)} %pad_maximum_fusion.1.hi_ref, bf16[32,256]{1,0:T(8,128)(2,1)} %get-tuple-element.78.place_lo_ref, ...), custom_call_target="tpu_custom_call" | custom-call | tf_op jit(solution)/shard_map/pallas_call | solution.py:79
  84.0 6.9 %fusion = f32[64,256]{1,0:T(8,128)S(1)} fusion(bf16[5,64,64,256]{3,2,1,0:T(8,128)(2,1)} %shard_map.152, f32[5,64,256]{2,1,0:T(8,128)S(1)} %select_convert_fusion.3), kind=kLoop, calls=%fused_computation.9 | loop fusion | flops 15712256 | bytes 10878976 | tf_op jit(solution)/shard_map/reduce_sum | solution.py:202
  91.3 4.1 %collective-permute-start.11 = (bf16[64,1,1]{2,0,1:T(8,128)(2,1)S(1)}, bf16[64,1,1]{2,0,1:T(8,128)(2,1)S(1)}, u32[]{:S(2)}, u32[]{:S(2)}) collective-permute-start(bf16[64,1,1]{2,0,1:T(8,128)(2,1)S(1)} %get-tuple-element.65), channel_id=1, source_target_pairs={{4,0},{8,4},{12,8},{16,12},{20,16},{24,20},{28,24},{32,28},{36,32}... | collective-permute-start | bytes 392 | tf_op jit(solution)/shard_map/ppermute | solution.py:23
  97.6 5.0 %collective-permute-done.10 = bf16[64,1,1]{2,0,1:T(8,128)(2,1)S(1)} collective-permute-done((bf16[64,1,1]{2,0,1:T(8,128)(2,1)S(1)}, bf16[64,1,1]{2,0,1:T(8,128)(2,1)S(1)}, u32[]{:S(2)}, u32[]{:S(2)}) %collective-permute-start.10) | collective-permute-done | bytes 160 | tf_op jit(solution)/shard_map/ppermute | solution.py:22
  102.7 3.4 %collective-permute-start.13 = (bf16[64,1,258]{2,0,1:T(8,128)(2,1)S(1)}, bf16[64,1,258]{2,0,1:T(8,128)(2,1)S(1)}, u32[]{:S(2)}, u32[]{:S(2)}) collective-permute-start(bf16[64,1,258]{2,0,1:T(8,128)(2,1)S(1)} %pad_maximum_fusion.7), channel_id=1, source_target_pairs={{0,1},{1,2},{2,3},{4,5},{5,6},{6,7},{8,9},{9,10},{10,11},{12,13},{... | collective-permute-start | bytes 99080 | tf_op jit(solution)/shard_map/ppermute | solution.py:22
  107.9 4.2 %collective-permute-done.12 = bf16[64,1,258]{2,0,1:T(8,128)(2,1)S(1)} collective-permute-done((bf16[64,1,258]{2,0,1:T(8,128)(2,1)S(1)}, bf16[64,1,258]{2,0,1:T(8,128)(2,1)S(1)}, u32[]{:S(2)}, u32[]{:S(2)}) %collective-permute-start.12) | collective-permute-done | bytes 33056 | tf_op jit(solution)/shard_map/ppermute | solution.py:23
  112.3 2.8 %fusion.1 = f32[64,256]{1,0:T(8,128)S(1)} fusion(bf16[5,64,64,256]{3,2,1,0:T(8,128)(2,1)S(1)} %copy-done.1, f32[5,64,256]{2,1,0:T(8,128)S(1)} %select_convert_fusion.2), kind=kLoop, calls=%fused_computation.10 | loop fusion | flops 15712256 | bytes 10878976 | tf_op jit(solution)/shard_map/reduce_sum | solution.py:202
  117.4 2.4 %collective-permute-start.14 = (bf16[64,1,1]{2,0,1:T(8,128)(2,1)S(1)}, bf16[64,1,1]{2,0,1:T(8,128)(2,1)S(1)}, u32[]{:S(2)}, u32[]{:S(2)}) collective-permute-start(bf16[64,1,1]{2,0,1:T(8,128)(2,1)S(1)} %get-tuple-element.58), channel_id=1, source_target_pairs={{0,4},{4,8},{8,12},{12,16},{16,20},{20,24},{24,28},{28,32},{32,36}... | collective-permute-start | bytes 392 | tf_op jit(solution)/shard_map/ppermute | solution.py:22
  120.0 4.5 %collective-permute-done.14 = bf16[64,1,1]{2,0,1:T(8,128)(2,1)S(1)} collective-permute-done((bf16[64,1,1]{2,0,1:T(8,128)(2,1)S(1)}, bf16[64,1,1]{2,0,1:T(8,128)(2,1)S(1)}, u32[]{:S(2)}, u32[]{:S(2)}) %collective-permute-start.14) | collective-permute-done | bytes 160 | tf_op jit(solution)/shard_map/ppermute | solution.py:22
  124.7 3.2 %collective-permute-start.17 = (bf16[64,1,258]{2,0,1:T(8,128)(2,1)S(1)}, bf16[64,1,258]{2,0,1:T(8,128)(2,1)S(1)}, u32[]{:S(2)}, u32[]{:S(2)}) collective-permute-start(bf16[64,1,258]{2,0,1:T(8,128)(2,1)S(1)} %pad_maximum_fusion.8), channel_id=1, source_target_pairs={{0,1},{1,2},{2,3},{4,5},{5,6},{6,7},{8,9},{9,10},{10,11},{12,13},{... | collective-permute-start | bytes 99080 | tf_op jit(solution)/shard_map/ppermute | solution.py:22
  129.8 4.2 %collective-permute-done.16 = bf16[64,1,258]{2,0,1:T(8,128)(2,1)S(1)} collective-permute-done((bf16[64,1,258]{2,0,1:T(8,128)(2,1)S(1)}, bf16[64,1,258]{2,0,1:T(8,128)(2,1)S(1)}, u32[]{:S(2)}, u32[]{:S(2)}) %collective-permute-start.16) | collective-permute-done | bytes 33056 | tf_op jit(solution)/shard_map/ppermute | solution.py:23
  134.1 2.8 %fusion.2 = f32[64,256]{1,0:T(8,128)S(1)} fusion(bf16[5,64,64,256]{3,2,1,0:T(8,128)(2,1)S(1)} %copy-done.1, f32[5,64,256]{2,1,0:T(8,128)S(1)} %select_convert_fusion.1), kind=kLoop, calls=%fused_computation.11 | loop fusion | flops 15712256 | bytes 10878976 | tf_op jit(solution)/shard_map/reduce_sum | solution.py:202
  141.8 4.5 %collective-permute-done.18 = bf16[64,1,1]{2,0,1:T(8,128)(2,1)S(1)} collective-permute-done((bf16[64,1,1]{2,0,1:T(8,128)(2,1)S(1)}, bf16[64,1,1]{2,0,1:T(8,128)(2,1)S(1)}, u32[]{:S(2)}, u32[]{:S(2)}) %collective-permute-start.18) | collective-permute-done | bytes 160 | tf_op jit(solution)/shard_map/ppermute | solution.py:22
  150.2 4.2 %collective-permute-done.20 = bf16[64,1,258]{2,0,1:T(8,128)(2,1)S(1)} collective-permute-done((bf16[64,1,258]{2,0,1:T(8,128)(2,1)S(1)}, bf16[64,1,258]{2,0,1:T(8,128)(2,1)S(1)}, u32[]{:S(2)}, u32[]{:S(2)}) %collective-permute-start.20) | collective-permute-done | bytes 33056 | tf_op jit(solution)/shard_map/ppermute | solution.py:23
  154.6 2.8 %fusion.3 = f32[64,256]{1,0:T(8,128)S(1)} fusion(bf16[5,64,64,256]{3,2,1,0:T(8,128)(2,1)S(1)} %copy-done.1, f32[5,64,256]{2,1,0:T(8,128)S(1)} %select_convert_fusion), kind=kLoop, calls=%fused_computation.12 | loop fusion | flops 15712256 | bytes 10878976 | tf_op jit(solution)/shard_map/reduce_sum | solution.py:202
  (150 shorter events, 52.5 us)
Async XLA Ops:
  0.6 90.3 %copy-start = (f32[48,64]{1,0:T(8,128)S(1)}, f32[48,64]{1,0:T(8,128)}, u32[]{:S(2)}) copy-start(f32[48,64]{1,0:T(8,128)} %param.26) | copy-start | bytes 36868
  0.7 35.2 %copy-start.13 = (s32[5,1,256]{2,1,0:T(1,128)S(1)}, s32[5,1,256]{2,1,0:T(1,128)}, u32[]{:S(2)}) copy-start(s32[5,1,256]{2,1,0:T(1,128)} %param.21) | copy-start | bytes 15364
  12.5 54.8 %collective-permute-start.1 = (bf16[2,32,4096]{2,1,0:T(8,128)(2,1)}, bf16[2,32,4096]{2,1,0:T(8,128)(2,1)S(1)}, u32[]{:S(2)}, u32[]{:S(2)}) collective-permute-start(bf16[2,32,4096]{2,1,0:T(8,128)(2,1)} %slice.176), channel_id=1, source_target_pairs={{0,4},{4,8},{8,12},{12,16},{16,20},{20,24},{24,28},{28,32},{32,36}... | collective-permute-start | bytes 1572872 | tf_op jit(solution)/shard_map/ppermute | solution.py:32
  15.6 51.7 %collective-permute-start = (bf16[3,32,4096]{2,1,0:T(8,128)(2,1)S(1)}, bf16[3,32,4096]{2,1,0:T(8,128)(2,1)}, u32[]{:S(2)}, u32[]{:S(2)}) collective-permute-start(bf16[3,32,4096]{2,1,0:T(8,128)(2,1)S(1)} %slice.175), channel_id=1, source_target_pairs={{0,4},{4,8},{8,12},{12,16},{16,20},{20,24},{24,28},{28,32},{32,36}... | collective-permute-start | bytes 2359304 | tf_op jit(solution)/shard_map/ppermute | solution.py:32
  21.0 48.6 %collective-permute-start.3 = (bf16[2,32,4096]{2,1,0:T(8,128)(2,1)}, bf16[2,32,4096]{2,1,0:T(8,128)(2,1)}, u32[]{:S(2)}, u32[]{:S(2)}) collective-permute-start(bf16[2,32,4096]{2,1,0:T(8,128)(2,1)} %slice.178), channel_id=1, source_target_pairs={{4,0},{8,4},{12,8},{16,12},{20,16},{24,20},{28,24},{32,28},{36,32}... | collective-permute-start | bytes 1572872 | tf_op jit(solution)/shard_map/ppermute | solution.py:33
  25.3 12.0 %collective-permute-start.5 = (bf16[64,1,1]{2,1,0:T(2,128)(2,1)S(1)}, bf16[64,1,1]{2,1,0:T(2,128)(2,1)S(1)}, u32[]{:S(2)}, u32[]{:S(2)}) collective-permute-start(bf16[64,1,1]{2,1,0:T(2,128)(2,1)S(1)} %get-tuple-element.33), channel_id=1, source_target_pairs={{4,0},{8,4},{12,8},{16,12},{20,16},{24,20},{28,24},{32,28},{36,32}... | collective-permute-start | bytes 392 | tf_op jit(solution)/shard_map/ppermute | solution.py:23
  27.7 15.3 %collective-permute-start.4 = (bf16[64,1,1]{2,1,0:T(2,128)(2,1)S(1)}, bf16[64,1,1]{2,1,0:T(2,128)(2,1)S(1)}, u32[]{:S(2)}, u32[]{:S(2)}) collective-permute-start(bf16[64,1,1]{2,1,0:T(2,128)(2,1)S(1)} %get-tuple-element.32), channel_id=1, source_target_pairs={{0,4},{4,8},{8,12},{12,16},{16,20},{20,24},{24,28},{28,32},{32,36}... | collective-permute-start | bytes 392 | tf_op jit(solution)/shard_map/ppermute | solution.py:22
  37.3 32.4 %collective-permute-start.2 = (bf16[3,32,4096]{2,1,0:T(8,128)(2,1)S(1)}, bf16[3,32,4096]{2,1,0:T(8,128)(2,1)}, u32[]{:S(2)}, u32[]{:S(2)}) collective-permute-start(bf16[3,32,4096]{2,1,0:T(8,128)(2,1)S(1)} %slice.177), channel_id=1, source_target_pairs={{4,0},{8,4},{12,8},{16,12},{20,16},{24,20},{28,24},{32,28},{36,32}... | collective-permute-start | bytes 2359304 | tf_op jit(solution)/shard_map/ppermute | solution.py:33
  43.1 7.2 %collective-permute-start.8 = (f32[96,32]{0,1:T(8,128)S(1)}, f32[96,32]{0,1:T(8,128)S(1)}, u32[]{:S(2)}, u32[]{:S(2)}) collective-permute-start(f32[96,32]{0,1:T(8,128)S(1)} %get-tuple-element.29), channel_id=1, source_target_pairs={{0,4},{4,8},{8,12},{12,16},{16,20},{20,24},{24,28},{28,32},{32,36}... | collective-permute-start | bytes 36872 | tf_op jit(solution)/shard_map/ppermute | solution.py:32
  50.2 3.3 %collective-permute-start.9 = (f32[96,32]{0,1:T(8,128)S(1)}, f32[96,32]{0,1:T(8,128)S(1)}, u32[]{:S(2)}, u32[]{:S(2)}) collective-permute-start(f32[96,32]{0,1:T(8,128)S(1)} %get-tuple-element.28), channel_id=1, source_target_pairs={{4,0},{8,4},{12,8},{16,12},{20,16},{24,20},{28,24},{32,28},{36,32}... | collective-permute-start | bytes 36872 | tf_op jit(solution)/shard_map/ppermute | solution.py:33
  53.6 5.8 %collective-permute-start.7 = (bf16[64,1,258]{2,1,0:T(2,128)(2,1)S(1)}, bf16[64,1,258]{2,1,0:T(2,128)(2,1)S(1)}, u32[]{:S(2)}, u32[]{:S(2)}) collective-permute-start(bf16[64,1,258]{2,1,0:T(2,128)(2,1)S(1)} %pad_maximum_fusion.4), channel_id=1, source_target_pairs={{0,1},{1,2},{2,3},{4,5},{5,6},{6,7},{8,9},{9,10},{10,11},{12,13},{... | collective-permute-start | bytes 99080 | tf_op jit(solution)/shard_map/ppermute | solution.py:22
  59.3 6.7 %collective-permute-start.6 = (bf16[64,1,258]{2,1,0:T(2,128)(2,1)S(1)}, bf16[64,1,258]{2,1,0:T(2,128)(2,1)S(1)}, u32[]{:S(2)}, u32[]{:S(2)}) collective-permute-start(bf16[64,1,258]{2,1,0:T(2,128)(2,1)S(1)} %pad_maximum_fusion.4), channel_id=1, source_target_pairs={{1,0},{2,1},{3,2},{5,4},{6,5},{7,6},{9,8},{10,9},{11,10},{13,12},{... | collective-permute-start | bytes 99080 | tf_op jit(solution)/shard_map/ppermute | solution.py:23
  91.3 6.2 %collective-permute-start.11 = (bf16[64,1,1]{2,0,1:T(8,128)(2,1)S(1)}, bf16[64,1,1]{2,0,1:T(8,128)(2,1)S(1)}, u32[]{:S(2)}, u32[]{:S(2)}) collective-permute-start(bf16[64,1,1]{2,0,1:T(8,128)(2,1)S(1)} %get-tuple-element.65), channel_id=1, source_target_pairs={{4,0},{8,4},{12,8},{16,12},{20,16},{24,20},{28,24},{32,28},{36,32}... | collective-permute-start | bytes 392 | tf_op jit(solution)/shard_map/ppermute | solution.py:23
  95.4 7.2 %collective-permute-start.10 = (bf16[64,1,1]{2,0,1:T(8,128)(2,1)S(1)}, bf16[64,1,1]{2,0,1:T(8,128)(2,1)S(1)}, u32[]{:S(2)}, u32[]{:S(2)}) collective-permute-start(bf16[64,1,1]{2,0,1:T(8,128)(2,1)S(1)} %get-tuple-element.64), channel_id=1, source_target_pairs={{0,4},{4,8},{8,12},{12,16},{16,20},{20,24},{24,28},{28,32},{32,36}... | collective-permute-start | bytes 392 | tf_op jit(solution)/shard_map/ppermute | solution.py:22
  102.7 5.1 %collective-permute-start.13 = (bf16[64,1,258]{2,0,1:T(8,128)(2,1)S(1)}, bf16[64,1,258]{2,0,1:T(8,128)(2,1)S(1)}, u32[]{:S(2)}, u32[]{:S(2)}) collective-permute-start(bf16[64,1,258]{2,0,1:T(8,128)(2,1)S(1)} %pad_maximum_fusion.7), channel_id=1, source_target_pairs={{0,1},{1,2},{2,3},{4,5},{5,6},{6,7},{8,9},{9,10},{10,11},{12,13},{... | collective-permute-start | bytes 99080 | tf_op jit(solution)/shard_map/ppermute | solution.py:22
  106.1 6.0 %collective-permute-start.12 = (bf16[64,1,258]{2,0,1:T(8,128)(2,1)S(1)}, bf16[64,1,258]{2,0,1:T(8,128)(2,1)S(1)}, u32[]{:S(2)}, u32[]{:S(2)}) collective-permute-start(bf16[64,1,258]{2,0,1:T(8,128)(2,1)S(1)} %pad_maximum_fusion.7), channel_id=1, source_target_pairs={{1,0},{2,1},{3,2},{5,4},{6,5},{7,6},{9,8},{10,9},{11,10},{13,12},{... | collective-permute-start | bytes 99080 | tf_op jit(solution)/shard_map/ppermute | solution.py:23
  115.5 4.5 %collective-permute-start.15 = (bf16[64,1,1]{2,0,1:T(8,128)(2,1)S(1)}, bf16[64,1,1]{2,0,1:T(8,128)(2,1)S(1)}, u32[]{:S(2)}, u32[]{:S(2)}) collective-permute-start(bf16[64,1,1]{2,0,1:T(8,128)(2,1)S(1)} %get-tuple-element.59), channel_id=1, source_target_pairs={{4,0},{8,4},{12,8},{16,12},{20,16},{24,20},{28,24},{32,28},{36,32}... | collective-permute-start | bytes 392 | tf_op jit(solution)/shard_map/ppermute | solution.py:23
  117.4 7.2 %collective-permute-start.14 = (bf16[64,1,1]{2,0,1:T(8,128)(2,1)S(1)}, bf16[64,1,1]{2,0,1:T(8,128)(2,1)S(1)}, u32[]{:S(2)}, u32[]{:S(2)}) collective-permute-start(bf16[64,1,1]{2,0,1:T(8,128)(2,1)S(1)} %get-tuple-element.58), channel_id=1, source_target_pairs={{0,4},{4,8},{8,12},{12,16},{16,20},{20,24},{24,28},{28,32},{32,36}... | collective-permute-start | bytes 392 | tf_op jit(solution)/shard_map/ppermute | solution.py:22
  124.7 5.0 %collective-permute-start.17 = (bf16[64,1,258]{2,0,1:T(8,128)(2,1)S(1)}, bf16[64,1,258]{2,0,1:T(8,128)(2,1)S(1)}, u32[]{:S(2)}, u32[]{:S(2)}) collective-permute-start(bf16[64,1,258]{2,0,1:T(8,128)(2,1)S(1)} %pad_maximum_fusion.8), channel_id=1, source_target_pairs={{0,1},{1,2},{2,3},{4,5},{5,6},{6,7},{8,9},{9,10},{10,11},{12,13},{... | collective-permute-start | bytes 99080 | tf_op jit(solution)/shard_map/ppermute | solution.py:22
  127.9 6.0 %collective-permute-start.16 = (bf16[64,1,258]{2,0,1:T(8,128)(2,1)S(1)}, bf16[64,1,258]{2,0,1:T(8,128)(2,1)S(1)}, u32[]{:S(2)}, u32[]{:S(2)}) collective-permute-start(bf16[64,1,258]{2,0,1:T(8,128)(2,1)S(1)} %pad_maximum_fusion.8), channel_id=1, source_target_pairs={{1,0},{2,1},{3,2},{5,4},{6,5},{7,6},{9,8},{10,9},{11,10},{13,12},{... | collective-permute-start | bytes 99080 | tf_op jit(solution)/shard_map/ppermute | solution.py:23
  137.3 4.5 %collective-permute-start.19 = (bf16[64,1,1]{2,0,1:T(8,128)(2,1)S(1)}, bf16[64,1,1]{2,0,1:T(8,128)(2,1)S(1)}, u32[]{:S(2)}, u32[]{:S(2)}) collective-permute-start(bf16[64,1,1]{2,0,1:T(8,128)(2,1)S(1)} %get-tuple-element.55), channel_id=1, source_target_pairs={{4,0},{8,4},{12,8},{16,12},{20,16},{24,20},{28,24},{32,28},{36,32}... | collective-permute-start | bytes 392 | tf_op jit(solution)/shard_map/ppermute | solution.py:23
  139.2 7.2 %collective-permute-start.18 = (bf16[64,1,1]{2,0,1:T(8,128)(2,1)S(1)}, bf16[64,1,1]{2,0,1:T(8,128)(2,1)S(1)}, u32[]{:S(2)}, u32[]{:S(2)}) collective-permute-start(bf16[64,1,1]{2,0,1:T(8,128)(2,1)S(1)} %get-tuple-element.54), channel_id=1, source_target_pairs={{0,4},{4,8},{8,12},{12,16},{16,20},{20,24},{24,28},{28,32},{32,36}... | collective-permute-start | bytes 392 | tf_op jit(solution)/shard_map/ppermute | solution.py:22
  146.5 3.7 %collective-permute-start.21 = (bf16[64,1,258]{2,0,1:T(8,128)(2,1)S(1)}, bf16[64,1,258]{2,0,1:T(8,128)(2,1)S(1)}, u32[]{:S(2)}, u32[]{:S(2)}) collective-permute-start(bf16[64,1,258]{2,0,1:T(8,128)(2,1)S(1)} %pad_maximum_fusion.9), channel_id=1, source_target_pairs={{0,1},{1,2},{2,3},{4,5},{5,6},{6,7},{8,9},{9,10},{10,11},{12,13},{... | collective-permute-start | bytes 99080 | tf_op jit(solution)/shard_map/ppermute | solution.py:22
  148.4 6.0 %collective-permute-start.20 = (bf16[64,1,258]{2,0,1:T(8,128)(2,1)S(1)}, bf16[64,1,258]{2,0,1:T(8,128)(2,1)S(1)}, u32[]{:S(2)}, u32[]{:S(2)}) collective-permute-start(bf16[64,1,258]{2,0,1:T(8,128)(2,1)S(1)} %pad_maximum_fusion.9), channel_id=1, source_target_pairs={{1,0},{2,1},{3,2},{5,4},{6,5},{7,6},{9,8},{10,9},{11,10},{13,12},{... | collective-permute-start | bytes 99080 | tf_op jit(solution)/shard_map/ppermute | solution.py:23
  (16 other events, 365.9 us)

commit v13 on v10

--- a/solution.py
+++ b/solution.py
@@ -145,6 +145,10 @@
     leave_lo = (send_slot[0, 0][:, None] == lanes[None, :]).astype(jnp.bfloat16)
     leave_hi = (send_slot[0, 1][:, None] == lanes[None, :]).astype(jnp.bfloat16)
     stiff_to_lower, stiff_to_higher = gather_leaving(stiff_flat, leave_lo, leave_hi)
+    shaft_first = padded_2(displacement[:, :1, :].astype(jnp.bfloat16), (("shaft", 2),), 1)
+    stiff_to_lower, stiff_to_higher, shaft_first = lax.optimization_barrier(
+        (stiff_to_lower, stiff_to_higher, shaft_first)
+    )
     stiff_lower, stiff_higher = neighbour_exchange("shaft", stiff_to_lower, stiff_to_higher)
 
     count_live = jnp.arange(capacity, dtype=jnp.int32)[None, :] < arrive_count[0][:, None]
@@ -186,8 +190,11 @@
     live = jnp.arange(slots, dtype=jnp.int32)[:, None] < coupled[0][None, :]
     codes = jnp.where(live, pattern[:, 0, :], 9)[:, None, :]
     for repeat in range(ITERS):
-        rounded = moved.astype(jnp.bfloat16)[:, None, :]
-        padded = padded_2(rounded, (("shaft", 2), ("ply", 1)), 1)
+        if repeat == 0:
+            padded = padded_2(shaft_first, (("ply", 1),), 1)
+        else:
+            rounded = moved.astype(jnp.bfloat16)[:, None, :]
+            padded = padded_2(rounded, (("shaft", 2), ("ply", 1)), 1)
         neighbours = jnp.zeros((slots,) + moved.shape, jnp.bfloat16)
         for code_index in range(9):
             shifted = padded[:, code_index // 3, code_index % 3 : code_index % 3 + blocks]

time: 141 us -> 161 us (1.14)
  waiting for transfers between devices: 31.4 us -> 39.5 us
  starting transfers between devices: 49.9 us -> 57.6 us
  local copies, waits for them, and re-layouts: 14.3 us -> 16.6 us
    ppermute x2, waiting for transfers between devices: 0.01 us -> 8.33 us  [neighbour_exchange(): from_lower = lax.ppermute(upper_bound, axis, up)]
    ppermute x8, starting transfers between devices: 13 us -> 19.2 us  [padded_2(): after = lax.ppermute(first, axis, down)]
    ppermute x8, waiting for transfers between devices: 16.9 us -> 12.5 us  [padded_2(): after = lax.ppermute(first, axis, down)]
    ppermute x2, waiting for transfers between devices: 0.01 us -> 3.72 us  [neighbour_exchange(): from_higher = lax.ppermute(lower_bound, axis, down)]
    ppermute x8, starting transfers between devices: 21.4 us -> 23.1 us  [padded_2(): before = lax.ppermute(last, axis, up)]
    unnamed x64 -> x44, local copies, waits for them, and re-layouts: 7.57 us -> 8.16 us
  transfers between devices with their start and end apart: 20 -> 20, of which waited for: 11 -> 11; matrix products, arithmetic and copies ran while one was open for 10% -> 12% of each run, Pallas kernels for 0% -> 5%
where the time goes in v13:
time: 161 us; the launch traced here: 160 us
  starting transfers between devices  57.6 us (36%)
  waiting for transfers between devices  39.5 us (25%)
  other arithmetic  22.5 us (14%)
  Pallas kernels  20.1 us (12%)
  local copies, waits for them, and re-layouts  16.6 us (10%)
  matrix products  1.84 us (1%)
    ppermute x8, starting transfers between devices, padded_2(): before = lax.ppermute(last, axis, up)  23.1 us
    ppermute x8, starting transfers between devices, padded_2(): after = lax.ppermute(first, axis, down)  19.2 us
    reduce_sum x4, other arithmetic, on_device(): jnp.sum(product, axis=(0, 2))  15.3 us
    ppermute x8, waiting for transfers between devices, padded_2(): before = lax.ppermute(last, axis, up)  15 us
    ppermute x8, waiting for transfers between devices, padded_2(): after = lax.ppermute(first, axis, down)  12.5 us
    pallas_call x1, Pallas kernels, merge_arrived(): pl.pallas_call(merge_kernel, grid=(slots,), in_specs=[pl.BlockSpec((1, ro...  11.7 us
    ppermute x2, starting transfers between devices, neighbour_exchange(): from_higher = lax.ppermute(lower_bound, axis, down)  11.5 us
    pallas_call x1, Pallas kernels, gather_leaving(): pl.pallas_call(gather_kernel, grid=(slots,), in_specs=[pl.BlockSpec((1, d...  8.45 us
  transfers between devices with their start and end apart: 20, of which 11 were waited for; matrix products, arithmetic and copies ran while one was open for 12% of the time, Pallas kernels for 5%

profile of v13, /device:TPU:96, one launch (start us, length us, event | category | flops | bytes accessed | tf_op | source)
XLA Modules:
  0.0 159.6 jit_solution(8640332428322500330)
XLA Ops:
  1.7 4.2 %collective-permute-start.1 = (bf16[64,1,1]{2,1,0:T(2,128)(2,1)S(1)}, bf16[64,1,1]{2,1,0:T(2,128)(2,1)S(1)}, u32[]{:S(2)}, u32[]{:S(2)}) collective-permute-start(bf16[64,1,1]{2,1,0:T(2,128)(2,1)S(1)} %get-tuple-element.40), channel_id=1, source_target_pairs={{4,0},{8,4},{12,8},{16,12},{20,16},{24,20},{28,24},{32,28},{36,32}... | collective-permute-start | bytes 392 | tf_op jit(solution)/shard_map/ppermute | solution.py:23
  16.0 5.8 %collective-permute-start.7 = (f32[96,32]{0,1:T(8,128)S(1)}, f32[96,32]{0,1:T(8,128)S(1)}, u32[]{:S(2)}, u32[]{:S(2)}) collective-permute-start(f32[96,32]{0,1:T(8,128)S(1)} %get-tuple-element.37), channel_id=1, source_target_pairs={{4,0},{8,4},{12,8},{16,12},{20,16},{24,20},{28,24},{32,28},{36,32}... | collective-permute-start | bytes 36872 | tf_op jit(solution)/shard_map/ppermute | solution.py:33
  27.9 8.5 %shard_map.151 = (bf16[5,32,4096]{2,1,0:T(8,128)(2,1)}, bf16[5,32,4096]{2,1,0:T(8,128)(2,1)}) custom-call(bf16[5,4096,256]{2,1,0:T(8,128)(2,1)} %bitcast.237, bf16[32,256]{1,0:T(8,128)(2,1)} %get-tuple-element.98.lo_ref, bf16[32,256]{1,0:T(8,128)(2,1)} %get-tuple-element.99.hi_ref), custom_call_target="tpu_custom_call" | custom-call | tf_op jit(solution)/shard_map/pallas_call | solution.py:51
  36.6 3.4 %collective-permute-start.5 = (bf16[64,1,258]{2,1,0:T(2,128)(2,1)S(1)}, bf16[64,1,258]{2,1,0:T(2,128)(2,1)S(1)}, u32[]{:S(2)}, u32[]{:S(2)}) collective-permute-start(bf16[64,1,258]{2,1,0:T(2,128)(2,1)S(1)} %pad_maximum_fusion.2), channel_id=1, source_target_pairs={{0,1},{1,2},{2,3},{4,5},{5,6},{6,7},{8,9},{9,10},{10,11},{12,13},{... | collective-permute-start | bytes 99080 | tf_op jit(solution)/shard_map/ppermute | solution.py:22
  45.4 5.7 %collective-permute-start.3 = (bf16[5,32,4096]{2,1,0:T(8,128)(2,1)}, bf16[5,32,4096]{2,1,0:T(8,128)(2,1)S(1)}, u32[]{:S(2)}, u32[]{:S(2)}) collective-permute-start(bf16[5,32,4096]{2,1,0:T(8,128)(2,1)} %get-tuple-element.13), channel_id=1, source_target_pairs={{4,0},{8,4},{12,8},{16,12},{20,16},{24,20},{28,24},{32,28},{36,32}... | collective-permute-start | bytes 3932168 | tf_op jit(solution)/shard_map/ppermute | solution.py:33
  54.5 8.3 %collective-permute-done.2.lo_ref = bf16[5,32,4096]{2,1,0:T(8,128)(2,1)S(1)} collective-permute-done((bf16[5,32,4096]{2,1,0:T(8,128)(2,1)}, bf16[5,32,4096]{2,1,0:T(8,128)(2,1)S(1)}, u32[]{:S(2)}, u32[]{:S(2)}) %collective-permute-start.2) | collective-permute-done | bytes 1310752 | tf_op jit(solution)/shard_map/ppermute | solution.py:32
  62.8 3.7 %collective-permute-done.3.hi_ref = bf16[5,32,4096]{2,1,0:T(8,128)(2,1)S(1)} collective-permute-done((bf16[5,32,4096]{2,1,0:T(8,128)(2,1)}, bf16[5,32,4096]{2,1,0:T(8,128)(2,1)S(1)}, u32[]{:S(2)}, u32[]{:S(2)}) %collective-permute-start.3) | collective-permute-done | bytes 1310752 | tf_op jit(solution)/shard_map/ppermute | solution.py:33
  67.7 11.7 %shard_map.152 = bf16[5,64,64,256]{3,2,1,0:T(8,128)(2,1)} custom-call(bf16[5,64,64,256]{3,2,1,0:T(8,128)(2,1)} %s_ref.1, bf16[5,32,4096]{2,1,0:T(8,128)(2,1)} %copy-done.2, bf16[5,32,4096]{2,1,0:T(8,128)(2,1)} %copy-done.3, bf16[32,256]{1,0:T(8,128)(2,1)} %get-tuple-element.85.place_lo_ref, bf16[32,256]{1,0:T(8,128)(2,1)} %get-tuple-element.100.place_hi_ref, ...), custom_call_target="tpu_custom_call" | custom-call | tf_op jit(solution)/shard_map/pallas_call | solution.py:79
  79.4 6.9 %fusion = f32[64,256]{1,0:T(8,128)S(1)} fusion(bf16[5,64,64,256]{3,2,1,0:T(8,128)(2,1)} %shard_map.152, f32[5,64,256]{2,1,0:T(8,128)S(1)} %select_convert_fusion.3), kind=kLoop, calls=%fused_computation.9 | loop fusion | flops 15712256 | bytes 10878976 | tf_op jit(solution)/shard_map/reduce_sum | solution.py:203
  86.8 5.8 %collective-permute-start.9 = (bf16[64,1,1]{2,0,1:T(8,128)(2,1)S(1)}, bf16[64,1,1]{2,0,1:T(8,128)(2,1)S(1)}, u32[]{:S(2)}, u32[]{:S(2)}) collective-permute-start(bf16[64,1,1]{2,0,1:T(8,128)(2,1)S(1)} %get-tuple-element.72), channel_id=1, source_target_pairs={{4,0},{8,4},{12,8},{16,12},{20,16},{24,20},{28,24},{32,28},{36,32}... | collective-permute-start | bytes 392 | tf_op jit(solution)/shard_map/ppermute | solution.py:23
  94.7 5.0 %collective-permute-done.8 = bf16[64,1,1]{2,0,1:T(8,128)(2,1)S(1)} collective-permute-done((bf16[64,1,1]{2,0,1:T(8,128)(2,1)S(1)}, bf16[64,1,1]{2,0,1:T(8,128)(2,1)S(1)}, u32[]{:S(2)}, u32[]{:S(2)}) %collective-permute-start.8) | collective-permute-done | bytes 160 | tf_op jit(solution)/shard_map/ppermute | solution.py:22
  99.8 4.5 %collective-permute-start.11 = (bf16[64,1,258]{2,0,1:T(8,128)(2,1)S(1)}, bf16[64,1,258]{2,0,1:T(8,128)(2,1)S(1)}, u32[]{:S(2)}, u32[]{:S(2)}) collective-permute-start(bf16[64,1,258]{2,0,1:T(8,128)(2,1)S(1)} %pad_maximum_fusion.3), channel_id=1, source_target_pairs={{0,1},{1,2},{2,3},{4,5},{5,6},{6,7},{8,9},{9,10},{10,11},{12,13},{... | collective-permute-start | bytes 99080 | tf_op jit(solution)/shard_map/ppermute | solution.py:22
  106.2 4.2 %collective-permute-done.10 = bf16[64,1,258]{2,0,1:T(8,128)(2,1)S(1)} collective-permute-done((bf16[64,1,258]{2,0,1:T(8,128)(2,1)S(1)}, bf16[64,1,258]{2,0,1:T(8,128)(2,1)S(1)}, u32[]{:S(2)}, u32[]{:S(2)}) %collective-permute-start.10) | collective-permute-done | bytes 33056 | tf_op jit(solution)/shard_map/ppermute | solution.py:23
  110.6 2.8 %fusion.1 = f32[64,256]{1,0:T(8,128)S(1)} fusion(bf16[5,64,64,256]{3,2,1,0:T(8,128)(2,1)S(1)} %copy-done.1, f32[5,64,256]{2,1,0:T(8,128)S(1)} %select_convert_fusion.2), kind=kLoop, calls=%fused_computation.10 | loop fusion | flops 15712256 | bytes 10878976 | tf_op jit(solution)/shard_map/reduce_sum | solution.py:203
  115.7 2.4 %collective-permute-start.12 = (bf16[64,1,1]{2,0,1:T(8,128)(2,1)S(1)}, bf16[64,1,1]{2,0,1:T(8,128)(2,1)S(1)}, u32[]{:S(2)}, u32[]{:S(2)}) collective-permute-start(bf16[64,1,1]{2,0,1:T(8,128)(2,1)S(1)} %get-tuple-element.65), channel_id=1, source_target_pairs={{0,4},{4,8},{8,12},{12,16},{16,20},{20,24},{24,28},{28,32},{32,36}... | collective-permute-start | bytes 392 | tf_op jit(solution)/shard_map/ppermute | solution.py:22
  118.3 4.5 %collective-permute-done.12 = bf16[64,1,1]{2,0,1:T(8,128)(2,1)S(1)} collective-permute-done((bf16[64,1,1]{2,0,1:T(8,128)(2,1)S(1)}, bf16[64,1,1]{2,0,1:T(8,128)(2,1)S(1)}, u32[]{:S(2)}, u32[]{:S(2)}) %collective-permute-start.12) | collective-permute-done | bytes 160 | tf_op jit(solution)/shard_map/ppermute | solution.py:22
  123.0 3.4 %collective-permute-start.15 = (bf16[64,1,258]{2,0,1:T(8,128)(2,1)S(1)}, bf16[64,1,258]{2,0,1:T(8,128)(2,1)S(1)}, u32[]{:S(2)}, u32[]{:S(2)}) collective-permute-start(bf16[64,1,258]{2,0,1:T(8,128)(2,1)S(1)} %pad_maximum_fusion.4), channel_id=1, source_target_pairs={{0,1},{1,2},{2,3},{4,5},{5,6},{6,7},{8,9},{9,10},{10,11},{12,13},{... | collective-permute-start | bytes 99080 | tf_op jit(solution)/shard_map/ppermute | solution.py:22
  128.2 4.2 %collective-permute-done.14 = bf16[64,1,258]{2,0,1:T(8,128)(2,1)S(1)} collective-permute-done((bf16[64,1,258]{2,0,1:T(8,128)(2,1)S(1)}, bf16[64,1,258]{2,0,1:T(8,128)(2,1)S(1)}, u32[]{:S(2)}, u32[]{:S(2)}) %collective-permute-start.14) | collective-permute-done | bytes 33056 | tf_op jit(solution)/shard_map/ppermute | solution.py:23
  132.6 2.8 %fusion.2 = f32[64,256]{1,0:T(8,128)S(1)} fusion(bf16[5,64,64,256]{3,2,1,0:T(8,128)(2,1)S(1)} %copy-done.1, f32[5,64,256]{2,1,0:T(8,128)S(1)} %select_convert_fusion.1), kind=kLoop, calls=%fused_computation.11 | loop fusion | flops 15712256 | bytes 10878976 | tf_op jit(solution)/shard_map/reduce_sum | solution.py:203
  137.6 2.4 %collective-permute-start.16 = (bf16[64,1,1]{2,0,1:T(8,128)(2,1)S(1)}, bf16[64,1,1]{2,0,1:T(8,128)(2,1)S(1)}, u32[]{:S(2)}, u32[]{:S(2)}) collective-permute-start(bf16[64,1,1]{2,0,1:T(8,128)(2,1)S(1)} %get-tuple-element.61), channel_id=1, source_target_pairs={{0,4},{4,8},{8,12},{12,16},{16,20},{20,24},{24,28},{28,32},{32,36}... | collective-permute-start | bytes 392 | tf_op jit(solution)/shard_map/ppermute | solution.py:22
  140.3 4.5 %collective-permute-done.16 = bf16[64,1,1]{2,0,1:T(8,128)(2,1)S(1)} collective-permute-done((bf16[64,1,1]{2,0,1:T(8,128)(2,1)S(1)}, bf16[64,1,1]{2,0,1:T(8,128)(2,1)S(1)}, u32[]{:S(2)}, u32[]{:S(2)}) %collective-permute-start.16) | collective-permute-done | bytes 160 | tf_op jit(solution)/shard_map/ppermute | solution.py:22
  144.9 3.1 %collective-permute-start.19 = (bf16[64,1,258]{2,0,1:T(8,128)(2,1)S(1)}, bf16[64,1,258]{2,0,1:T(8,128)(2,1)S(1)}, u32[]{:S(2)}, u32[]{:S(2)}) collective-permute-start(bf16[64,1,258]{2,0,1:T(8,128)(2,1)S(1)} %pad_maximum_fusion.5), channel_id=1, source_target_pairs={{0,1},{1,2},{2,3},{4,5},{5,6},{6,7},{8,9},{9,10},{10,11},{12,13},{... | collective-permute-start | bytes 99080 | tf_op jit(solution)/shard_map/ppermute | solution.py:22
  149.9 4.2 %collective-permute-done.18 = bf16[64,1,258]{2,0,1:T(8,128)(2,1)S(1)} collective-permute-done((bf16[64,1,258]{2,0,1:T(8,128)(2,1)S(1)}, bf16[64,1,258]{2,0,1:T(8,128)(2,1)S(1)}, u32[]{:S(2)}, u32[]{:S(2)}) %collective-permute-start.18) | collective-permute-done | bytes 33056 | tf_op jit(solution)/shard_map/ppermute | solution.py:23
  154.2 2.8 %fusion.3 = f32[64,256]{1,0:T(8,128)S(1)} fusion(bf16[5,64,64,256]{3,2,1,0:T(8,128)(2,1)S(1)} %copy-done.1, f32[5,64,256]{2,1,0:T(8,128)S(1)} %select_convert_fusion), kind=kLoop, calls=%fused_computation.12 | loop fusion | flops 15712256 | bytes 10878976 | tf_op jit(solution)/shard_map/reduce_sum | solution.py:203
  (132 shorter events, 43.4 us)
Async XLA Ops:
  0.6 85.7 %copy-start = (f32[48,64]{1,0:T(8,128)S(1)}, f32[48,64]{1,0:T(8,128)}, u32[]{:S(2)}) copy-start(f32[48,64]{1,0:T(8,128)} %param.26) | copy-start | bytes 36868
  1.7 34.7 %collective-permute-start.1 = (bf16[64,1,1]{2,1,0:T(2,128)(2,1)S(1)}, bf16[64,1,1]{2,1,0:T(2,128)(2,1)S(1)}, u32[]{:S(2)}, u32[]{:S(2)}) collective-permute-start(bf16[64,1,1]{2,1,0:T(2,128)(2,1)S(1)} %get-tuple-element.40), channel_id=1, source_target_pairs={{4,0},{8,4},{12,8},{16,12},{20,16},{24,20},{28,24},{32,28},{36,32}... | collective-permute-start | bytes 392 | tf_op jit(solution)/shard_map/ppermute | solution.py:23
  5.9 30.4 %collective-permute-start = (bf16[64,1,1]{2,1,0:T(2,128)(2,1)S(1)}, bf16[64,1,1]{2,1,0:T(2,128)(2,1)S(1)}, u32[]{:S(2)}, u32[]{:S(2)}) collective-permute-start(bf16[64,1,1]{2,1,0:T(2,128)(2,1)S(1)} %get-tuple-element.39), channel_id=1, source_target_pairs={{0,4},{4,8},{8,12},{12,16},{16,20},{20,24},{24,28},{28,32},{32,36}... | collective-permute-start | bytes 392 | tf_op jit(solution)/shard_map/ppermute | solution.py:22
  14.1 31.2 %collective-permute-start.6 = (f32[96,32]{0,1:T(8,128)S(1)}, f32[96,32]{0,1:T(8,128)S(1)}, u32[]{:S(2)}, u32[]{:S(2)}) collective-permute-start(f32[96,32]{0,1:T(8,128)S(1)} %get-tuple-element.38), channel_id=1, source_target_pairs={{0,4},{4,8},{8,12},{12,16},{16,20},{20,24},{24,28},{28,32},{32,36}... | collective-permute-start | bytes 36872 | tf_op jit(solution)/shard_map/ppermute | solution.py:32
  16.0 35.1 %collective-permute-start.7 = (f32[96,32]{0,1:T(8,128)S(1)}, f32[96,32]{0,1:T(8,128)S(1)}, u32[]{:S(2)}, u32[]{:S(2)}) collective-permute-start(f32[96,32]{0,1:T(8,128)S(1)} %get-tuple-element.37), channel_id=1, source_target_pairs={{4,0},{8,4},{12,8},{16,12},{20,16},{24,20},{28,24},{32,28},{36,32}... | collective-permute-start | bytes 36872 | tf_op jit(solution)/shard_map/ppermute | solution.py:33
  36.6 16.3 %collective-permute-start.5 = (bf16[64,1,258]{2,1,0:T(2,128)(2,1)S(1)}, bf16[64,1,258]{2,1,0:T(2,128)(2,1)S(1)}, u32[]{:S(2)}, u32[]{:S(2)}) collective-permute-start(bf16[64,1,258]{2,1,0:T(2,128)(2,1)S(1)} %pad_maximum_fusion.2), channel_id=1, source_target_pairs={{0,1},{1,2},{2,3},{4,5},{5,6},{6,7},{8,9},{9,10},{10,11},{12,13},{... | collective-permute-start | bytes 99080 | tf_op jit(solution)/shard_map/ppermute | solution.py:22
  40.3 12.9 %collective-permute-start.4 = (bf16[64,1,258]{2,1,0:T(2,128)(2,1)S(1)}, bf16[64,1,258]{2,1,0:T(2,128)(2,1)S(1)}, u32[]{:S(2)}, u32[]{:S(2)}) collective-permute-start(bf16[64,1,258]{2,1,0:T(2,128)(2,1)S(1)} %pad_maximum_fusion.2), channel_id=1, source_target_pairs={{1,0},{2,1},{3,2},{5,4},{6,5},{7,6},{9,8},{10,9},{11,10},{13,12},{... | collective-permute-start | bytes 99080 | tf_op jit(solution)/shard_map/ppermute | solution.py:23
  41.6 21.2 %collective-permute-start.2 = (bf16[5,32,4096]{2,1,0:T(8,128)(2,1)}, bf16[5,32,4096]{2,1,0:T(8,128)(2,1)S(1)}, u32[]{:S(2)}, u32[]{:S(2)}) collective-permute-start(bf16[5,32,4096]{2,1,0:T(8,128)(2,1)} %get-tuple-element.12), channel_id=1, source_target_pairs={{0,4},{4,8},{8,12},{12,16},{16,20},{20,24},{24,28},{28,32},{32,36}... | collective-permute-start | bytes 3932168 | tf_op jit(solution)/shard_map/ppermute | solution.py:32
  45.4 21.2 %collective-permute-start.3 = (bf16[5,32,4096]{2,1,0:T(8,128)(2,1)}, bf16[5,32,4096]{2,1,0:T(8,128)(2,1)S(1)}, u32[]{:S(2)}, u32[]{:S(2)}) collective-permute-start(bf16[5,32,4096]{2,1,0:T(8,128)(2,1)} %get-tuple-element.13), channel_id=1, source_target_pairs={{4,0},{8,4},{12,8},{16,12},{20,16},{24,20},{28,24},{32,28},{36,32}... | collective-permute-start | bytes 3932168 | tf_op jit(solution)/shard_map/ppermute | solution.py:33
  79.4 31.1 %copy-start.8 = (pred[5,256]{1,0:T(8,128)(4,1)S(1)}, pred[5,256]{1,0:T(8,128)(4,1)}, u32[]{:S(2)}) copy-start(pred[5,256]{1,0:T(8,128)(4,1)} %get-tuple-element.107) | copy-start | bytes 3844
  79.4 31.1 %copy-start.9 = (pred[5,256]{1,0:T(8,128)(4,1)S(1)}, pred[5,256]{1,0:T(8,128)(4,1)}, u32[]{:S(2)}) copy-start(pred[5,256]{1,0:T(8,128)(4,1)} %get-tuple-element.108) | copy-start | bytes 3844
  79.4 31.2 %copy-start.1 = (bf16[5,64,64,256]{3,2,1,0:T(8,128)(2,1)S(1)}, bf16[5,64,64,256]{3,2,1,0:T(8,128)(2,1)}, u32[]{:S(2)}) copy-start(bf16[5,64,64,256]{3,2,1,0:T(8,128)(2,1)} %shard_map.152) | copy-start | bytes 31457284
  86.8 7.9 %collective-permute-start.9 = (bf16[64,1,1]{2,0,1:T(8,128)(2,1)S(1)}, bf16[64,1,1]{2,0,1:T(8,128)(2,1)S(1)}, u32[]{:S(2)}, u32[]{:S(2)}) collective-permute-start(bf16[64,1,1]{2,0,1:T(8,128)(2,1)S(1)} %get-tuple-element.72), channel_id=1, source_target_pairs={{4,0},{8,4},{12,8},{16,12},{20,16},{24,20},{28,24},{32,28},{36,32}... | collective-permute-start | bytes 392 | tf_op jit(solution)/shard_map/ppermute | solution.py:23
  92.6 7.2 %collective-permute-start.8 = (bf16[64,1,1]{2,0,1:T(8,128)(2,1)S(1)}, bf16[64,1,1]{2,0,1:T(8,128)(2,1)S(1)}, u32[]{:S(2)}, u32[]{:S(2)}) collective-permute-start(bf16[64,1,1]{2,0,1:T(8,128)(2,1)S(1)} %get-tuple-element.71), channel_id=1, source_target_pairs={{0,4},{4,8},{8,12},{12,16},{16,20},{20,24},{24,28},{28,32},{32,36}... | collective-permute-start | bytes 392 | tf_op jit(solution)/shard_map/ppermute | solution.py:22
  99.8 6.3 %collective-permute-start.11 = (bf16[64,1,258]{2,0,1:T(8,128)(2,1)S(1)}, bf16[64,1,258]{2,0,1:T(8,128)(2,1)S(1)}, u32[]{:S(2)}, u32[]{:S(2)}) collective-permute-start(bf16[64,1,258]{2,0,1:T(8,128)(2,1)S(1)} %pad_maximum_fusion.3), channel_id=1, source_target_pairs={{0,1},{1,2},{2,3},{4,5},{5,6},{6,7},{8,9},{9,10},{10,11},{12,13},{... | collective-permute-start | bytes 99080 | tf_op jit(solution)/shard_map/ppermute | solution.py:22
  104.4 6.0 %collective-permute-start.10 = (bf16[64,1,258]{2,0,1:T(8,128)(2,1)S(1)}, bf16[64,1,258]{2,0,1:T(8,128)(2,1)S(1)}, u32[]{:S(2)}, u32[]{:S(2)}) collective-permute-start(bf16[64,1,258]{2,0,1:T(8,128)(2,1)S(1)} %pad_maximum_fusion.3), channel_id=1, source_target_pairs={{1,0},{2,1},{3,2},{5,4},{6,5},{7,6},{9,8},{10,9},{11,10},{13,12},{... | collective-permute-start | bytes 99080 | tf_op jit(solution)/shard_map/ppermute | solution.py:23
  113.8 4.5 %collective-permute-start.13 = (bf16[64,1,1]{2,0,1:T(8,128)(2,1)S(1)}, bf16[64,1,1]{2,0,1:T(8,128)(2,1)S(1)}, u32[]{:S(2)}, u32[]{:S(2)}) collective-permute-start(bf16[64,1,1]{2,0,1:T(8,128)(2,1)S(1)} %get-tuple-element.66), channel_id=1, source_target_pairs={{4,0},{8,4},{12,8},{16,12},{20,16},{24,20},{28,24},{32,28},{36,32}... | collective-permute-start | bytes 392 | tf_op jit(solution)/shard_map/ppermute | solution.py:23
  115.7 7.2 %collective-permute-start.12 = (bf16[64,1,1]{2,0,1:T(8,128)(2,1)S(1)}, bf16[64,1,1]{2,0,1:T(8,128)(2,1)S(1)}, u32[]{:S(2)}, u32[]{:S(2)}) collective-permute-start(bf16[64,1,1]{2,0,1:T(8,128)(2,1)S(1)} %get-tuple-element.65), channel_id=1, source_target_pairs={{0,4},{4,8},{8,12},{12,16},{16,20},{20,24},{24,28},{28,32},{32,36}... | collective-permute-start | bytes 392 | tf_op jit(solution)/shard_map/ppermute | solution.py:22
  123.0 5.1 %collective-permute-start.15 = (bf16[64,1,258]{2,0,1:T(8,128)(2,1)S(1)}, bf16[64,1,258]{2,0,1:T(8,128)(2,1)S(1)}, u32[]{:S(2)}, u32[]{:S(2)}) collective-permute-start(bf16[64,1,258]{2,0,1:T(8,128)(2,1)S(1)} %pad_maximum_fusion.4), channel_id=1, source_target_pairs={{0,1},{1,2},{2,3},{4,5},{5,6},{6,7},{8,9},{9,10},{10,11},{12,13},{... | collective-permute-start | bytes 99080 | tf_op jit(solution)/shard_map/ppermute | solution.py:22
  126.4 6.0 %collective-permute-start.14 = (bf16[64,1,258]{2,0,1:T(8,128)(2,1)S(1)}, bf16[64,1,258]{2,0,1:T(8,128)(2,1)S(1)}, u32[]{:S(2)}, u32[]{:S(2)}) collective-permute-start(bf16[64,1,258]{2,0,1:T(8,128)(2,1)S(1)} %pad_maximum_fusion.4), channel_id=1, source_target_pairs={{1,0},{2,1},{3,2},{5,4},{6,5},{7,6},{9,8},{10,9},{11,10},{13,12},{... | collective-permute-start | bytes 99080 | tf_op jit(solution)/shard_map/ppermute | solution.py:23
  135.7 4.5 %collective-permute-start.17 = (bf16[64,1,1]{2,0,1:T(8,128)(2,1)S(1)}, bf16[64,1,1]{2,0,1:T(8,128)(2,1)S(1)}, u32[]{:S(2)}, u32[]{:S(2)}) collective-permute-start(bf16[64,1,1]{2,0,1:T(8,128)(2,1)S(1)} %get-tuple-element.62), channel_id=1, source_target_pairs={{4,0},{8,4},{12,8},{16,12},{20,16},{24,20},{28,24},{32,28},{36,32}... | collective-permute-start | bytes 392 | tf_op jit(solution)/shard_map/ppermute | solution.py:23
  137.6 7.2 %collective-permute-start.16 = (bf16[64,1,1]{2,0,1:T(8,128)(2,1)S(1)}, bf16[64,1,1]{2,0,1:T(8,128)(2,1)S(1)}, u32[]{:S(2)}, u32[]{:S(2)}) collective-permute-start(bf16[64,1,1]{2,0,1:T(8,128)(2,1)S(1)} %get-tuple-element.61), channel_id=1, source_target_pairs={{0,4},{4,8},{8,12},{12,16},{16,20},{20,24},{24,28},{28,32},{32,36}... | collective-permute-start | bytes 392 | tf_op jit(solution)/shard_map/ppermute | solution.py:22
  144.9 4.9 %collective-permute-start.19 = (bf16[64,1,258]{2,0,1:T(8,128)(2,1)S(1)}, bf16[64,1,258]{2,0,1:T(8,128)(2,1)S(1)}, u32[]{:S(2)}, u32[]{:S(2)}) collective-permute-start(bf16[64,1,258]{2,0,1:T(8,128)(2,1)S(1)} %pad_maximum_fusion.5), channel_id=1, source_target_pairs={{0,1},{1,2},{2,3},{4,5},{5,6},{6,7},{8,9},{9,10},{10,11},{12,13},{... | collective-permute-start | bytes 99080 | tf_op jit(solution)/shard_map/ppermute | solution.py:22
  148.0 6.0 %collective-permute-start.18 = (bf16[64,1,258]{2,0,1:T(8,128)(2,1)S(1)}, bf16[64,1,258]{2,0,1:T(8,128)(2,1)S(1)}, u32[]{:S(2)}, u32[]{:S(2)}) collective-permute-start(bf16[64,1,258]{2,0,1:T(8,128)(2,1)S(1)} %pad_maximum_fusion.5), channel_id=1, source_target_pairs={{1,0},{2,1},{3,2},{5,4},{6,5},{7,6},{9,8},{10,9},{11,10},{13,12},{... | collective-permute-start | bytes 99080 | tf_op jit(solution)/shard_map/ppermute | solution.py:23
  (8 other events, 71.1 us)

commit v14 on v10

--- a/solution.py
+++ b/solution.py
@@ -145,7 +145,27 @@
     leave_lo = (send_slot[0, 0][:, None] == lanes[None, :]).astype(jnp.bfloat16)
     leave_hi = (send_slot[0, 1][:, None] == lanes[None, :]).astype(jnp.bfloat16)
     stiff_to_lower, stiff_to_higher = gather_leaving(stiff_flat, leave_lo, leave_hi)
-    stiff_lower, stiff_higher = neighbour_exchange("shaft", stiff_to_lower, stiff_to_higher)
+    outgoing = send_slot[0].reshape(-1)
+    moving_state = jnp.concatenate(
+        [jnp.take(history_old, outgoing, axis=1), jnp.take(decay_old, outgoing, axis=1)], 0
+    )
+    high = lax.reduce_precision(moving_state, exponent_bits=8, mantissa_bits=7)
+    rest = moving_state - high
+    middle = lax.reduce_precision(rest, exponent_bits=8, mantissa_bits=7)
+    low = rest - middle
+    pieces = jnp.concatenate([high, middle, low], 0).astype(jnp.bfloat16).T
+    pieces = jnp.pad(pieces, ((0, 0), (0, rows_i * rows_j - pieces.shape[1])))
+    send_lower = jnp.concatenate([stiff_to_lower, pieces[None, :capacity]], 0)
+    send_higher = jnp.concatenate([stiff_to_higher, pieces[None, capacity:]], 0)
+    recv_lower, recv_higher = neighbour_exchange("shaft", send_lower, send_higher)
+    stiff_lower, stiff_higher = recv_lower[:slots], recv_higher[:slots]
+    state_parts = jnp.concatenate([recv_lower[slots], recv_higher[slots]], 0).T.astype(jnp.float32)
+    state_count = moving_state.shape[0]
+    state_arrived = (
+        state_parts[:state_count]
+        + state_parts[state_count : 2 * state_count]
+        + state_parts[2 * state_count : 3 * state_count]
+    )
 
     count_live = jnp.arange(capacity, dtype=jnp.int32)[None, :] < arrive_count[0][:, None]
     place_lo = (arrive_place[0, 0][:, None] == lanes[None, :]) & count_live[0][:, None]
@@ -160,7 +180,6 @@
         arrival,
     )
 
-    outgoing = send_slot[0].reshape(-1)
     filled = count_live.reshape(-1)
     target = jnp.where(filled, arrive_place[0].reshape(-1), blocks)
     placing = (
@@ -168,13 +187,6 @@
         .at[target]
         .set(blocks + jnp.arange(2 * capacity, dtype=jnp.int32))[:blocks]
     )
-    moving_state = jnp.concatenate(
-        [jnp.take(history_old, outgoing, axis=1), jnp.take(decay_old, outgoing, axis=1)], 0
-    )
-    state_lower, state_higher = neighbour_exchange(
-        "shaft", moving_state[:, :capacity], moving_state[:, capacity:]
-    )
-    state_arrived = jnp.concatenate([state_lower, state_higher], 1)
     depth = history_old.shape[0]
     history = jnp.take(jnp.concatenate([history_old, state_arrived[:depth]], 1), placing, axis=1)
     decay = jnp.take(jnp.concatenate([decay_old, state_arrived[depth:]], 1), placing, axis=1)

time: 141 us -> 150 us (1.064)
  other arithmetic: 21.3 us -> 25.7 us
  starting transfers between devices: 49.9 us -> 53.6 us
    ppermute x8, starting transfers between devices: 13 us -> 28.4 us  [padded_2(): after = lax.ppermute(first, axis, down)]
    ppermute x8, waiting for transfers between devices: 14.5 us -> 1.38 us  [padded_2(): before = lax.ppermute(last, axis, up)]
    ppermute x2 -> x1, starting transfers between devices: 11.7 us -> 1.91 us  [neighbour_exchange(): from_higher = lax.ppermute(lower_bound, axis, down)]
    ppermute x2 -> x1, waiting for transfers between devices: 0.01 us -> 8.52 us  [neighbour_exchange(): from_lower = lax.ppermute(upper_bound, axis, up)]
    concatenate x1 -> x2, other arithmetic: 0.08 us -> 5.24 us  [the longest x1 2.62 us: on_device(): send_lower = jnp.concatenate([stiff_to_lower, pieces[None, :capacity]], 0)]
    slice x0 -> x2, local copies, waits for them, and re-layouts: none -> 3.74 us  [on_device(): stiff_lower, stiff_higher = (recv_lower[:slots], recv_higher[:slots])]
    unnamed x64 -> x35, local copies, waits for them, and re-layouts: 7.57 us -> 3.99 us
    ppermute x8, waiting for transfers between devices: 16.9 us -> 20.1 us  [padded_2(): after = lax.ppermute(first, axis, down)]
  transfers between devices with their start and end apart: 20 -> 18, of which waited for: 11 -> 12; matrix products, arithmetic and copies ran while one was open for 10% -> 11% of each run, Pallas kernels for 0% -> 6%
where the time goes in v14:
time: 150 us; the launch traced here: 148 us
  starting transfers between devices  53.6 us (36%)
  waiting for transfers between devices  30 us (20%)
  other arithmetic  25.7 us (17%)
  Pallas kernels  20.1 us (13%)
  local copies, waits for them, and re-layouts  15.5 us (10%)
  matrix products  1.85 us (1%)
    ppermute x8, starting transfers between devices, padded_2(): after = lax.ppermute(first, axis, down)  28.4 us
    ppermute x8, starting transfers between devices, padded_2(): before = lax.ppermute(last, axis, up)  21 us
    ppermute x8, waiting for transfers between devices, padded_2(): after = lax.ppermute(first, axis, down)  20.1 us
    reduce_sum x4, other arithmetic, on_device(): jnp.sum(product, axis=(0, 2))  15.3 us
    pallas_call x1, Pallas kernels, merge_arrived(): pl.pallas_call(merge_kernel, grid=(slots,), in_specs=[pl.BlockSpec((1, ro...  11.7 us
    ppermute x1, waiting for transfers between devices, neighbour_exchange(): from_lower = lax.ppermute(upper_bound, axis, up)  8.52 us
    pallas_call x1, Pallas kernels, gather_leaving(): pl.pallas_call(gather_kernel, grid=(slots,), in_specs=[pl.BlockSpec((1, d...  8.42 us
    unnamed x35, local copies, waits for them, and re-layouts  3.99 us
  transfers between devices with their start and end apart: 18, of which 12 were waited for; matrix products, arithmetic and copies ran while one was open for 11% of the time, Pallas kernels for 6%

profile of v14, /device:TPU:96, one launch (start us, length us, event | category | flops | bytes accessed | tf_op | source)
XLA Modules:
  0.0 148.1 jit_solution(8470552279467065227)
XLA Ops:
  1.8 1.9 %collective-permute-start.2 = (bf16[64,1,1]{2,1,0:T(2,128)(2,1)S(1)}, bf16[64,1,1]{2,1,0:T(2,128)(2,1)S(1)}, u32[]{:S(2)}, u32[]{:S(2)}) collective-permute-start(bf16[64,1,1]{2,1,0:T(2,128)(2,1)S(1)} %get-tuple-element.30), channel_id=1, source_target_pairs={{0,4},{4,8},{8,12},{12,16},{16,20},{20,24},{24,28},{28,32},{32,36}... | collective-permute-start | bytes 392 | tf_op jit(solution)/shard_map/ppermute | solution.py:22
  3.7 5.8 %collective-permute-start.3 = (bf16[64,1,1]{2,1,0:T(2,128)(2,1)S(1)}, bf16[64,1,1]{2,1,0:T(2,128)(2,1)S(1)}, u32[]{:S(2)}, u32[]{:S(2)}) collective-permute-start(bf16[64,1,1]{2,1,0:T(2,128)(2,1)S(1)} %get-tuple-element.31), channel_id=1, source_target_pairs={{4,0},{8,4},{12,8},{16,12},{20,16},{24,20},{28,24},{32,28},{36,32}... | collective-permute-start | bytes 392 | tf_op jit(solution)/shard_map/ppermute | solution.py:23
  15.0 8.4 %shard_map.151 = (bf16[5,32,4096]{2,1,0:T(8,128)(2,1)}, bf16[5,32,4096]{2,1,0:T(8,128)(2,1)}) custom-call(bf16[5,4096,256]{2,1,0:T(8,128)(2,1)} %bitcast.241, bf16[32,256]{1,0:T(8,128)(2,1)} %get-tuple-element.94.lo_ref, bf16[32,256]{1,0:T(8,128)(2,1)} %get-tuple-element.95.hi_ref), custom_call_target="tpu_custom_call" | custom-call | tf_op jit(solution)/shard_map/pallas_call | solution.py:51
  23.4 2.6 %pad_maximum_fusion.1 = bf16[6,32,4096]{2,1,0:T(8,128)(2,1)} fusion(bf16[1,32,4096]{2,1,0:T(8,128)(2,1)S(1)} %get-tuple-element.53, bf16[5,32,4096]{2,1,0:T(8,128)(2,1)} %get-tuple-element.8), kind=kLoop, calls=%fused_computation.14 | loop fusion | flops 786432 | bytes 3145728 | tf_op jit(solution)/shard_map/concatenate | solution.py:158
  27.9 2.6 %pad_maximum_fusion = bf16[6,32,4096]{2,1,0:T(8,128)(2,1)} fusion(bf16[1,32,4096]{2,1,0:T(8,128)(2,1)S(1)} %get-tuple-element.54, bf16[5,32,4096]{2,1,0:T(8,128)(2,1)} %get-tuple-element.7), kind=kLoop, calls=%fused_computation.13 | loop fusion | flops 786432 | bytes 3145728 | tf_op jit(solution)/shard_map/concatenate | solution.py:159
  30.6 2.4 %collective-permute-start = (bf16[6,32,4096]{2,1,0:T(8,128)(2,1)}, bf16[6,32,4096]{2,1,0:T(8,128)(2,1)}, u32[]{:S(2)}, u32[]{:S(2)}) collective-permute-start(bf16[6,32,4096]{2,1,0:T(8,128)(2,1)} %pad_maximum_fusion), channel_id=1, source_target_pairs={{0,4},{4,8},{8,12},{12,16},{16,20},{20,24},{24,28},{28,32},{32,36}... | collective-permute-start | bytes 4718600 | tf_op jit(solution)/shard_map/ppermute | solution.py:32
  35.8 3.4 %collective-permute-start.5 = (bf16[64,1,258]{2,1,0:T(2,128)(2,1)S(1)}, bf16[64,1,258]{2,1,0:T(2,128)(2,1)S(1)}, u32[]{:S(2)}, u32[]{:S(2)}) collective-permute-start(bf16[64,1,258]{2,1,0:T(2,128)(2,1)S(1)} %pad_maximum_fusion.4), channel_id=1, source_target_pairs={{0,1},{1,2},{2,3},{4,5},{5,6},{6,7},{8,9},{9,10},{10,11},{12,13},{... | collective-permute-start | bytes 99080 | tf_op jit(solution)/shard_map/ppermute | solution.py:22
  41.7 4.0 %collective-permute-done.4 = bf16[64,1,258]{2,1,0:T(2,128)(2,1)S(1)} collective-permute-done((bf16[64,1,258]{2,1,0:T(2,128)(2,1)S(1)}, bf16[64,1,258]{2,1,0:T(2,128)(2,1)S(1)}, u32[]{:S(2)}, u32[]{:S(2)}) %collective-permute-start.4) | collective-permute-done | bytes 33056 | tf_op jit(solution)/shard_map/ppermute | solution.py:23
  46.2 8.5 %collective-permute-done = bf16[6,32,4096]{2,1,0:T(8,128)(2,1)} collective-permute-done((bf16[6,32,4096]{2,1,0:T(8,128)(2,1)}, bf16[6,32,4096]{2,1,0:T(8,128)(2,1)}, u32[]{:S(2)}, u32[]{:S(2)}) %collective-permute-start) | collective-permute-done | bytes 1572896 | tf_op jit(solution)/shard_map/ppermute | solution.py:32
  58.8 2.5 %slice.248.lo_ref = bf16[5,32,4096]{2,1,0:T(8,128)(2,1)} slice(bf16[6,32,4096]{2,1,0:T(8,128)(2,1)} %collective-permute-done), slice={[0:5], [0:32], [0:4096]} | slice | bytes 2621440 | tf_op jit(solution)/shard_map/slice | solution.py:161
  61.3 11.7 %shard_map.152 = bf16[5,64,64,256]{3,2,1,0:T(8,128)(2,1)} custom-call(bf16[5,64,64,256]{3,2,1,0:T(8,128)(2,1)} %s_ref.1, bf16[5,32,4096]{2,1,0:T(8,128)(2,1)} %slice.248.lo_ref, bf16[5,32,4096]{2,1,0:T(8,128)(2,1)} %slice.249.hi_ref, bf16[32,256]{1,0:T(8,128)(2,1)} %get-tuple-element.81.place_lo_ref, bf16[32,256]{1,0:T(8,128)(2,1)} %get-tuple-element.96.place_hi_ref, ...), custom_call_target="tpu_custom_call" | custom-call | tf_op jit(solution)/shard_map/pallas_call | solution.py:79
  73.0 6.9 %fusion = f32[64,256]{1,0:T(8,128)S(1)} fusion(bf16[5,64,64,256]{3,2,1,0:T(8,128)(2,1)} %shard_map.152, f32[5,64,256]{2,1,0:T(8,128)S(1)} %select_convert_fusion.3), kind=kLoop, calls=%fused_computation.9 | loop fusion | flops 15712256 | bytes 10878976 | tf_op jit(solution)/shard_map/reduce_sum | solution.py:208
  82.3 5.8 %collective-permute-start.7 = (bf16[64,1,1]{2,0,1:T(8,128)(2,1)S(1)}, bf16[64,1,1]{2,0,1:T(8,128)(2,1)S(1)}, u32[]{:S(2)}, u32[]{:S(2)}) collective-permute-start(bf16[64,1,1]{2,0,1:T(8,128)(2,1)S(1)} %get-tuple-element.68), channel_id=1, source_target_pairs={{4,0},{8,4},{12,8},{16,12},{20,16},{24,20},{28,24},{32,28},{36,32}... | collective-permute-start | bytes 392 | tf_op jit(solution)/shard_map/ppermute | solution.py:23
  89.5 3.4 %collective-permute-start.9 = (bf16[64,1,258]{2,0,1:T(8,128)(2,1)S(1)}, bf16[64,1,258]{2,0,1:T(8,128)(2,1)S(1)}, u32[]{:S(2)}, u32[]{:S(2)}) collective-permute-start(bf16[64,1,258]{2,0,1:T(8,128)(2,1)S(1)} %pad_maximum_fusion.7), channel_id=1, source_target_pairs={{0,1},{1,2},{2,3},{4,5},{5,6},{6,7},{8,9},{9,10},{10,11},{12,13},{... | collective-permute-start | bytes 99080 | tf_op jit(solution)/shard_map/ppermute | solution.py:22
  94.8 4.2 %collective-permute-done.8 = bf16[64,1,258]{2,0,1:T(8,128)(2,1)S(1)} collective-permute-done((bf16[64,1,258]{2,0,1:T(8,128)(2,1)S(1)}, bf16[64,1,258]{2,0,1:T(8,128)(2,1)S(1)}, u32[]{:S(2)}, u32[]{:S(2)}) %collective-permute-start.8) | collective-permute-done | bytes 33056 | tf_op jit(solution)/shard_map/ppermute | solution.py:23
  99.2 2.8 %fusion.1 = f32[64,256]{1,0:T(8,128)S(1)} fusion(bf16[5,64,64,256]{3,2,1,0:T(8,128)(2,1)S(1)} %copy-done.1, f32[5,64,256]{2,1,0:T(8,128)S(1)} %select_convert_fusion.2), kind=kLoop, calls=%fused_computation.10 | loop fusion | flops 15712256 | bytes 10878976 | tf_op jit(solution)/shard_map/reduce_sum | solution.py:208
  104.2 5.8 %collective-permute-start.11 = (bf16[64,1,1]{2,0,1:T(8,128)(2,1)S(1)}, bf16[64,1,1]{2,0,1:T(8,128)(2,1)S(1)}, u32[]{:S(2)}, u32[]{:S(2)}) collective-permute-start(bf16[64,1,1]{2,0,1:T(8,128)(2,1)S(1)} %get-tuple-element.62), channel_id=1, source_target_pairs={{4,0},{8,4},{12,8},{16,12},{20,16},{24,20},{28,24},{32,28},{36,32}... | collective-permute-start | bytes 392 | tf_op jit(solution)/shard_map/ppermute | solution.py:23
  111.5 3.4 %collective-permute-start.13 = (bf16[64,1,258]{2,0,1:T(8,128)(2,1)S(1)}, bf16[64,1,258]{2,0,1:T(8,128)(2,1)S(1)}, u32[]{:S(2)}, u32[]{:S(2)}) collective-permute-start(bf16[64,1,258]{2,0,1:T(8,128)(2,1)S(1)} %pad_maximum_fusion.8), channel_id=1, source_target_pairs={{0,1},{1,2},{2,3},{4,5},{5,6},{6,7},{8,9},{9,10},{10,11},{12,13},{... | collective-permute-start | bytes 99080 | tf_op jit(solution)/shard_map/ppermute | solution.py:22
  116.7 4.2 %collective-permute-done.12 = bf16[64,1,258]{2,0,1:T(8,128)(2,1)S(1)} collective-permute-done((bf16[64,1,258]{2,0,1:T(8,128)(2,1)S(1)}, bf16[64,1,258]{2,0,1:T(8,128)(2,1)S(1)}, u32[]{:S(2)}, u32[]{:S(2)}) %collective-permute-start.12) | collective-permute-done | bytes 33056 | tf_op jit(solution)/shard_map/ppermute | solution.py:23
  121.1 2.8 %fusion.2 = f32[64,256]{1,0:T(8,128)S(1)} fusion(bf16[5,64,64,256]{3,2,1,0:T(8,128)(2,1)S(1)} %copy-done.1, f32[5,64,256]{2,1,0:T(8,128)S(1)} %select_convert_fusion.1), kind=kLoop, calls=%fused_computation.11 | loop fusion | flops 15712256 | bytes 10878976 | tf_op jit(solution)/shard_map/reduce_sum | solution.py:208
  126.2 5.8 %collective-permute-start.15 = (bf16[64,1,1]{2,0,1:T(8,128)(2,1)S(1)}, bf16[64,1,1]{2,0,1:T(8,128)(2,1)S(1)}, u32[]{:S(2)}, u32[]{:S(2)}) collective-permute-start(bf16[64,1,1]{2,0,1:T(8,128)(2,1)S(1)} %get-tuple-element.58), channel_id=1, source_target_pairs={{4,0},{8,4},{12,8},{16,12},{20,16},{24,20},{28,24},{32,28},{36,32}... | collective-permute-start | bytes 392 | tf_op jit(solution)/shard_map/ppermute | solution.py:23
  133.4 3.1 %collective-permute-start.17 = (bf16[64,1,258]{2,0,1:T(8,128)(2,1)S(1)}, bf16[64,1,258]{2,0,1:T(8,128)(2,1)S(1)}, u32[]{:S(2)}, u32[]{:S(2)}) collective-permute-start(bf16[64,1,258]{2,0,1:T(8,128)(2,1)S(1)} %pad_maximum_fusion.9), channel_id=1, source_target_pairs={{0,1},{1,2},{2,3},{4,5},{5,6},{6,7},{8,9},{9,10},{10,11},{12,13},{... | collective-permute-start | bytes 99080 | tf_op jit(solution)/shard_map/ppermute | solution.py:22
  138.4 4.2 %collective-permute-done.16 = bf16[64,1,258]{2,0,1:T(8,128)(2,1)S(1)} collective-permute-done((bf16[64,1,258]{2,0,1:T(8,128)(2,1)S(1)}, bf16[64,1,258]{2,0,1:T(8,128)(2,1)S(1)}, u32[]{:S(2)}, u32[]{:S(2)}) %collective-permute-start.16) | collective-permute-done | bytes 33056 | tf_op jit(solution)/shard_map/ppermute | solution.py:23
  142.8 2.8 %fusion.3 = f32[64,256]{1,0:T(8,128)S(1)} fusion(bf16[5,64,64,256]{3,2,1,0:T(8,128)(2,1)S(1)} %copy-done.1, f32[5,64,256]{2,1,0:T(8,128)S(1)} %select_convert_fusion), kind=kLoop, calls=%fused_computation.12 | loop fusion | flops 15712256 | bytes 10878976 | tf_op jit(solution)/shard_map/reduce_sum | solution.py:208
  (129 shorter events, 38.0 us)
Async XLA Ops:
  0.6 79.3 %copy-start = (f32[48,64]{1,0:T(8,128)S(1)}, f32[48,64]{1,0:T(8,128)}, u32[]{:S(2)}) copy-start(f32[48,64]{1,0:T(8,128)} %param.26) | copy-start | bytes 36868
  0.6 33.4 %copy-start.4 = (f32[64,1,256]{2,1,0:T(1,128)S(1)}, f32[64,1,256]{2,1,0:T(1,128)}, u32[]{:S(2)}) copy-start(f32[64,1,256]{2,1,0:T(1,128)} %param.17) | copy-start | bytes 196612
  0.7 32.3 %copy-start.9 = (s32[1,2]{1,0:T(1,128)S(1)}, s32[1,2]{1,0:T(1,128)}, u32[]{:S(2)}) copy-start(s32[1,2]{1,0:T(1,128)} %param.29) | copy-start | bytes 28
  0.7 32.5 %copy-start.8 = (s32[1,2,32]{2,1,0:T(2,128)S(1)}, s32[1,2,32]{2,1,0:T(2,128)}, u32[]{:S(2)}) copy-start(s32[1,2,32]{2,1,0:T(2,128)} %param.28) | copy-start | bytes 772
  0.7 34.7 %copy-start.7 = (s32[1,256]{1,0:T(1,128)S(1)}, s32[1,256]{1,0:T(1,128)}, u32[]{:S(2)}) copy-start(s32[1,256]{1,0:T(1,128)} %param.22) | copy-start | bytes 3076
  0.7 34.7 %copy-start.6 = (s32[5,1,256]{2,1,0:T(1,128)S(1)}, s32[5,1,256]{2,1,0:T(1,128)}, u32[]{:S(2)}) copy-start(s32[5,1,256]{2,1,0:T(1,128)} %param.21) | copy-start | bytes 15364
  1.8 33.8 %collective-permute-start.2 = (bf16[64,1,1]{2,1,0:T(2,128)(2,1)S(1)}, bf16[64,1,1]{2,1,0:T(2,128)(2,1)S(1)}, u32[]{:S(2)}, u32[]{:S(2)}) collective-permute-start(bf16[64,1,1]{2,1,0:T(2,128)(2,1)S(1)} %get-tuple-element.30), channel_id=1, source_target_pairs={{0,4},{4,8},{8,12},{12,16},{16,20},{20,24},{24,28},{28,32},{32,36}... | collective-permute-start | bytes 392 | tf_op jit(solution)/shard_map/ppermute | solution.py:22
  3.7 31.8 %collective-permute-start.3 = (bf16[64,1,1]{2,1,0:T(2,128)(2,1)S(1)}, bf16[64,1,1]{2,1,0:T(2,128)(2,1)S(1)}, u32[]{:S(2)}, u32[]{:S(2)}) collective-permute-start(bf16[64,1,1]{2,1,0:T(2,128)(2,1)S(1)} %get-tuple-element.31), channel_id=1, source_target_pairs={{4,0},{8,4},{12,8},{16,12},{20,16},{24,20},{28,24},{32,28},{36,32}... | collective-permute-start | bytes 392 | tf_op jit(solution)/shard_map/ppermute | solution.py:23
  26.0 20.1 %collective-permute-start.1 = (bf16[6,32,4096]{2,1,0:T(8,128)(2,1)}, bf16[6,32,4096]{2,1,0:T(8,128)(2,1)S(1)}, u32[]{:S(2)}, u32[]{:S(2)}) collective-permute-start(bf16[6,32,4096]{2,1,0:T(8,128)(2,1)} %pad_maximum_fusion.1), channel_id=1, source_target_pairs={{4,0},{8,4},{12,8},{16,12},{20,16},{24,20},{28,24},{32,28},{36,32}... | collective-permute-start | bytes 4718600 | tf_op jit(solution)/shard_map/ppermute | solution.py:33
  30.6 24.1 %collective-permute-start = (bf16[6,32,4096]{2,1,0:T(8,128)(2,1)}, bf16[6,32,4096]{2,1,0:T(8,128)(2,1)}, u32[]{:S(2)}, u32[]{:S(2)}) collective-permute-start(bf16[6,32,4096]{2,1,0:T(8,128)(2,1)} %pad_maximum_fusion), channel_id=1, source_target_pairs={{0,4},{4,8},{8,12},{12,16},{16,20},{20,24},{24,28},{28,32},{32,36}... | collective-permute-start | bytes 4718600 | tf_op jit(solution)/shard_map/ppermute | solution.py:32
  35.8 5.6 %collective-permute-start.5 = (bf16[64,1,258]{2,1,0:T(2,128)(2,1)S(1)}, bf16[64,1,258]{2,1,0:T(2,128)(2,1)S(1)}, u32[]{:S(2)}, u32[]{:S(2)}) collective-permute-start(bf16[64,1,258]{2,1,0:T(2,128)(2,1)S(1)} %pad_maximum_fusion.4), channel_id=1, source_target_pairs={{0,1},{1,2},{2,3},{4,5},{5,6},{6,7},{8,9},{9,10},{10,11},{12,13},{... | collective-permute-start | bytes 99080 | tf_op jit(solution)/shard_map/ppermute | solution.py:22
  39.2 6.5 %collective-permute-start.4 = (bf16[64,1,258]{2,1,0:T(2,128)(2,1)S(1)}, bf16[64,1,258]{2,1,0:T(2,128)(2,1)S(1)}, u32[]{:S(2)}, u32[]{:S(2)}) collective-permute-start(bf16[64,1,258]{2,1,0:T(2,128)(2,1)S(1)} %pad_maximum_fusion.4), channel_id=1, source_target_pairs={{1,0},{2,1},{3,2},{5,4},{6,5},{7,6},{9,8},{10,9},{11,10},{13,12},{... | collective-permute-start | bytes 99080 | tf_op jit(solution)/shard_map/ppermute | solution.py:23
  80.3 7.9 %collective-permute-start.6 = (bf16[64,1,1]{2,0,1:T(8,128)(2,1)S(1)}, bf16[64,1,1]{2,0,1:T(8,128)(2,1)S(1)}, u32[]{:S(2)}, u32[]{:S(2)}) collective-permute-start(bf16[64,1,1]{2,0,1:T(8,128)(2,1)S(1)} %get-tuple-element.67), channel_id=1, source_target_pairs={{0,4},{4,8},{8,12},{12,16},{16,20},{20,24},{24,28},{28,32},{32,36}... | collective-permute-start | bytes 392 | tf_op jit(solution)/shard_map/ppermute | solution.py:22
  82.3 7.2 %collective-permute-start.7 = (bf16[64,1,1]{2,0,1:T(8,128)(2,1)S(1)}, bf16[64,1,1]{2,0,1:T(8,128)(2,1)S(1)}, u32[]{:S(2)}, u32[]{:S(2)}) collective-permute-start(bf16[64,1,1]{2,0,1:T(8,128)(2,1)S(1)} %get-tuple-element.68), channel_id=1, source_target_pairs={{4,0},{8,4},{12,8},{16,12},{20,16},{24,20},{28,24},{32,28},{36,32}... | collective-permute-start | bytes 392 | tf_op jit(solution)/shard_map/ppermute | solution.py:23
  89.5 5.1 %collective-permute-start.9 = (bf16[64,1,258]{2,0,1:T(8,128)(2,1)S(1)}, bf16[64,1,258]{2,0,1:T(8,128)(2,1)S(1)}, u32[]{:S(2)}, u32[]{:S(2)}) collective-permute-start(bf16[64,1,258]{2,0,1:T(8,128)(2,1)S(1)} %pad_maximum_fusion.7), channel_id=1, source_target_pairs={{0,1},{1,2},{2,3},{4,5},{5,6},{6,7},{8,9},{9,10},{10,11},{12,13},{... | collective-permute-start | bytes 99080 | tf_op jit(solution)/shard_map/ppermute | solution.py:22
  92.9 6.0 %collective-permute-start.8 = (bf16[64,1,258]{2,0,1:T(8,128)(2,1)S(1)}, bf16[64,1,258]{2,0,1:T(8,128)(2,1)S(1)}, u32[]{:S(2)}, u32[]{:S(2)}) collective-permute-start(bf16[64,1,258]{2,0,1:T(8,128)(2,1)S(1)} %pad_maximum_fusion.7), channel_id=1, source_target_pairs={{1,0},{2,1},{3,2},{5,4},{6,5},{7,6},{9,8},{10,9},{11,10},{13,12},{... | collective-permute-start | bytes 99080 | tf_op jit(solution)/shard_map/ppermute | solution.py:23
  102.3 7.9 %collective-permute-start.10 = (bf16[64,1,1]{2,0,1:T(8,128)(2,1)S(1)}, bf16[64,1,1]{2,0,1:T(8,128)(2,1)S(1)}, u32[]{:S(2)}, u32[]{:S(2)}) collective-permute-start(bf16[64,1,1]{2,0,1:T(8,128)(2,1)S(1)} %get-tuple-element.61), channel_id=1, source_target_pairs={{0,4},{4,8},{8,12},{12,16},{16,20},{20,24},{24,28},{28,32},{32,36}... | collective-permute-start | bytes 392 | tf_op jit(solution)/shard_map/ppermute | solution.py:22
  104.2 7.2 %collective-permute-start.11 = (bf16[64,1,1]{2,0,1:T(8,128)(2,1)S(1)}, bf16[64,1,1]{2,0,1:T(8,128)(2,1)S(1)}, u32[]{:S(2)}, u32[]{:S(2)}) collective-permute-start(bf16[64,1,1]{2,0,1:T(8,128)(2,1)S(1)} %get-tuple-element.62), channel_id=1, source_target_pairs={{4,0},{8,4},{12,8},{16,12},{20,16},{24,20},{28,24},{32,28},{36,32}... | collective-permute-start | bytes 392 | tf_op jit(solution)/shard_map/ppermute | solution.py:23
  111.5 5.1 %collective-permute-start.13 = (bf16[64,1,258]{2,0,1:T(8,128)(2,1)S(1)}, bf16[64,1,258]{2,0,1:T(8,128)(2,1)S(1)}, u32[]{:S(2)}, u32[]{:S(2)}) collective-permute-start(bf16[64,1,258]{2,0,1:T(8,128)(2,1)S(1)} %pad_maximum_fusion.8), channel_id=1, source_target_pairs={{0,1},{1,2},{2,3},{4,5},{5,6},{6,7},{8,9},{9,10},{10,11},{12,13},{... | collective-permute-start | bytes 99080 | tf_op jit(solution)/shard_map/ppermute | solution.py:22
  114.9 6.0 %collective-permute-start.12 = (bf16[64,1,258]{2,0,1:T(8,128)(2,1)S(1)}, bf16[64,1,258]{2,0,1:T(8,128)(2,1)S(1)}, u32[]{:S(2)}, u32[]{:S(2)}) collective-permute-start(bf16[64,1,258]{2,0,1:T(8,128)(2,1)S(1)} %pad_maximum_fusion.8), channel_id=1, source_target_pairs={{1,0},{2,1},{3,2},{5,4},{6,5},{7,6},{9,8},{10,9},{11,10},{13,12},{... | collective-permute-start | bytes 99080 | tf_op jit(solution)/shard_map/ppermute | solution.py:23
  124.2 7.9 %collective-permute-start.14 = (bf16[64,1,1]{2,0,1:T(8,128)(2,1)S(1)}, bf16[64,1,1]{2,0,1:T(8,128)(2,1)S(1)}, u32[]{:S(2)}, u32[]{:S(2)}) collective-permute-start(bf16[64,1,1]{2,0,1:T(8,128)(2,1)S(1)} %get-tuple-element.57), channel_id=1, source_target_pairs={{0,4},{4,8},{8,12},{12,16},{16,20},{20,24},{24,28},{28,32},{32,36}... | collective-permute-start | bytes 392 | tf_op jit(solution)/shard_map/ppermute | solution.py:22
  126.2 7.2 %collective-permute-start.15 = (bf16[64,1,1]{2,0,1:T(8,128)(2,1)S(1)}, bf16[64,1,1]{2,0,1:T(8,128)(2,1)S(1)}, u32[]{:S(2)}, u32[]{:S(2)}) collective-permute-start(bf16[64,1,1]{2,0,1:T(8,128)(2,1)S(1)} %get-tuple-element.58), channel_id=1, source_target_pairs={{4,0},{8,4},{12,8},{16,12},{20,16},{24,20},{28,24},{32,28},{36,32}... | collective-permute-start | bytes 392 | tf_op jit(solution)/shard_map/ppermute | solution.py:23
  133.4 4.8 %collective-permute-start.17 = (bf16[64,1,258]{2,0,1:T(8,128)(2,1)S(1)}, bf16[64,1,258]{2,0,1:T(8,128)(2,1)S(1)}, u32[]{:S(2)}, u32[]{:S(2)}) collective-permute-start(bf16[64,1,258]{2,0,1:T(8,128)(2,1)S(1)} %pad_maximum_fusion.9), channel_id=1, source_target_pairs={{0,1},{1,2},{2,3},{4,5},{5,6},{6,7},{8,9},{9,10},{10,11},{12,13},{... | collective-permute-start | bytes 99080 | tf_op jit(solution)/shard_map/ppermute | solution.py:22
  136.6 6.0 %collective-permute-start.16 = (bf16[64,1,258]{2,0,1:T(8,128)(2,1)S(1)}, bf16[64,1,258]{2,0,1:T(8,128)(2,1)S(1)}, u32[]{:S(2)}, u32[]{:S(2)}) collective-permute-start(bf16[64,1,258]{2,0,1:T(8,128)(2,1)S(1)} %pad_maximum_fusion.9), channel_id=1, source_target_pairs={{1,0},{2,1},{3,2},{5,4},{6,5},{7,6},{9,8},{10,9},{11,10},{13,12},{... | collective-permute-start | bytes 99080 | tf_op jit(solution)/shard_map/ppermute | solution.py:23
  (4 other events, 47.0 us)

commit v15 on v10

--- a/solution.py
+++ b/solution.py
@@ -34,34 +34,32 @@
     return from_lower, from_higher
 
 
-def gather_kernel(s_ref, lo_ref, hi_ref, out_lo_ref, out_hi_ref):
-    width = lo_ref.shape[0]
-    pick = jnp.concatenate([lo_ref[...], hi_ref[...]], 0)
+def gather_kernel(s_ref, pick_ref, out_lo_ref, out_hi_ref):
+    width = out_lo_ref.shape[1]
     picked = lax.dot_general(
-        pick, s_ref[0], (((1,), (1,)), ((), ())), preferred_element_type=jnp.float32
+        pick_ref[...], s_ref[0], (((1,), (1,)), ((), ())), preferred_element_type=jnp.float32
     )
     out_lo_ref[0] = picked[:width].astype(out_lo_ref.dtype)
     out_hi_ref[0] = picked[width:].astype(out_hi_ref.dtype)
 
 
-def gather_leaving(stiffness, pick_lo, pick_hi):
+def gather_leaving(stiffness, pick):
     slots, depth, blocks = stiffness.shape
-    width = pick_lo.shape[0]
+    width = pick.shape[0] // 2
     out = jax.ShapeDtypeStruct((slots, width, depth), stiffness.dtype)
     return pl.pallas_call(
         gather_kernel,
         grid=(slots,),
         in_specs=[
             pl.BlockSpec((1, depth, blocks), lambda k: (k, 0, 0)),
-            pl.BlockSpec((width, blocks), lambda k: (0, 0)),
-            pl.BlockSpec((width, blocks), lambda k: (0, 0)),
+            pl.BlockSpec((2 * width, blocks), lambda k: (0, 0)),
         ],
         out_specs=[
             pl.BlockSpec((1, width, depth), lambda k: (k, 0, 0)),
             pl.BlockSpec((1, width, depth), lambda k: (k, 0, 0)),
         ],
         out_shape=[out, out],
-    )(stiffness, pick_lo, pick_hi)
+    )(stiffness, pick)
 
 
 def merge_kernel(s_ref, lo_ref, hi_ref, place_lo_ref, place_hi_ref, arrival_ref, out_ref):
@@ -142,9 +140,8 @@
 
     slots, rows_i, rows_j, _ = stiffness_old.shape
     stiff_flat = stiffness_old.reshape(slots, rows_i * rows_j, blocks)
-    leave_lo = (send_slot[0, 0][:, None] == lanes[None, :]).astype(jnp.bfloat16)
-    leave_hi = (send_slot[0, 1][:, None] == lanes[None, :]).astype(jnp.bfloat16)
-    stiff_to_lower, stiff_to_higher = gather_leaving(stiff_flat, leave_lo, leave_hi)
+    leaving = (send_slot[0].reshape(-1)[:, None] == lanes[None, :]).astype(jnp.bfloat16)
+    stiff_to_lower, stiff_to_higher = gather_leaving(stiff_flat, leaving)
     stiff_lower, stiff_higher = neighbour_exchange("shaft", stiff_to_lower, stiff_to_higher)
 
     count_live = jnp.arange(capacity, dtype=jnp.int32)[None, :] < arrive_count[0][:, None]

time: 141 us -> 143 us (1.014)
  waiting for transfers between devices: 31.4 us -> 33 us
    unnamed x64 -> x52, local copies, waits for them, and re-layouts: 7.57 us -> 5.78 us
    ppermute x8, waiting for transfers between devices: 16.9 us -> 18.5 us  [padded_2(): after = lax.ppermute(first, axis, down)]
where the time goes in v15:
time: 143 us; the launch traced here: 142 us
  starting transfers between devices  50 us (35%)
  waiting for transfers between devices  33 us (23%)
  other arithmetic  22.6 us (16%)
  Pallas kernels  20.1 us (14%)
  local copies, waits for them, and re-layouts  13.2 us (9%)
  matrix products  1.85 us (1%)
    ppermute x8, starting transfers between devices, padded_2(): before = lax.ppermute(last, axis, up)  21.5 us
    ppermute x8, waiting for transfers between devices, padded_2(): after = lax.ppermute(first, axis, down)  18.5 us
    reduce_sum x4, other arithmetic, on_device(): jnp.sum(product, axis=(0, 2))  15.3 us
    ppermute x8, waiting for transfers between devices, padded_2(): before = lax.ppermute(last, axis, up)  14.5 us
    ppermute x8, starting transfers between devices, padded_2(): after = lax.ppermute(first, axis, down)  13 us
    pallas_call x1, Pallas kernels, merge_arrived(): pl.pallas_call(merge_kernel, grid=(slots,), in_specs=[pl.BlockSpec((1, ro...  11.7 us
    ppermute x2, starting transfers between devices, neighbour_exchange(): from_higher = lax.ppermute(lower_bound, axis, down)  11.7 us
    pallas_call x1, Pallas kernels, gather_leaving(): pl.pallas_call(gather_kernel, grid=(slots,), in_specs=[pl.BlockSpec((1, d...  8.42 us
  transfers between devices with their start and end apart: 20, of which 11 were waited for; matrix products, arithmetic and copies ran while one was open for 10% of the time, Pallas kernels for 0%

profile of v15, /device:TPU:96, one launch (start us, length us, event | category | flops | bytes accessed | tf_op | source)
XLA Modules:
  0.0 142.1 jit_solution(15547699540678609919)
XLA Ops:
  2.2 8.4 %shard_map.151 = (bf16[5,32,4096]{2,1,0:T(8,128)(2,1)}, bf16[5,32,4096]{2,1,0:T(8,128)(2,1)}) custom-call(bf16[5,4096,256]{2,1,0:T(8,128)(2,1)} %bitcast.224, bf16[64,256]{1,0:T(8,128)(2,1)} %fusion.32.pick_ref), custom_call_target="tpu_custom_call" | custom-call | tf_op jit(solution)/shard_map/pallas_call | solution.py:50
  12.6 5.8 %collective-permute-start.1 = (bf16[5,32,4096]{2,1,0:T(8,128)(2,1)}, bf16[5,32,4096]{2,1,0:T(8,128)(2,1)S(1)}, u32[]{:S(2)}, u32[]{:S(2)}) collective-permute-start(bf16[5,32,4096]{2,1,0:T(8,128)(2,1)} %get-tuple-element.8), channel_id=1, source_target_pairs={{4,0},{8,4},{12,8},{16,12},{20,16},{24,20},{28,24},{32,28},{36,32}... | collective-permute-start | bytes 3932168 | tf_op jit(solution)/shard_map/ppermute | solution.py:33
  20.4 2.4 %collective-permute-start.2 = (bf16[64,1,1]{2,1,0:T(2,128)(2,1)S(1)}, bf16[64,1,1]{2,1,0:T(2,128)(2,1)S(1)}, u32[]{:S(2)}, u32[]{:S(2)}) collective-permute-start(bf16[64,1,1]{2,1,0:T(2,128)(2,1)S(1)} %get-tuple-element.32), channel_id=1, source_target_pairs={{0,4},{4,8},{8,12},{12,16},{16,20},{20,24},{24,28},{28,32},{32,36}... | collective-permute-start | bytes 392 | tf_op jit(solution)/shard_map/ppermute | solution.py:22
  31.2 2.9 %collective-permute-done.3 = bf16[64,1,1]{2,1,0:T(2,128)(2,1)S(1)} collective-permute-done((bf16[64,1,1]{2,1,0:T(2,128)(2,1)S(1)}, bf16[64,1,1]{2,1,0:T(2,128)(2,1)S(1)}, u32[]{:S(2)}, u32[]{:S(2)}) %collective-permute-start.3) | collective-permute-done | bytes 160 | tf_op jit(solution)/shard_map/ppermute | solution.py:23
  34.0 5.9 %collective-permute-start.7 = (f32[96,32]{0,1:T(8,128)S(1)}, f32[96,32]{0,1:T(8,128)S(1)}, u32[]{:S(2)}, u32[]{:S(2)}) collective-permute-start(f32[96,32]{0,1:T(8,128)S(1)} %get-tuple-element.28), channel_id=1, source_target_pairs={{4,0},{8,4},{12,8},{16,12},{20,16},{24,20},{28,24},{32,28},{36,32}... | collective-permute-start | bytes 36872 | tf_op jit(solution)/shard_map/ppermute | solution.py:33
  40.8 3.4 %collective-permute-start.5 = (bf16[64,1,258]{2,1,0:T(2,128)(2,1)}, bf16[64,1,258]{2,1,0:T(2,128)(2,1)S(1)}, u32[]{:S(2)}, u32[]{:S(2)}) collective-permute-start(bf16[64,1,258]{2,1,0:T(2,128)(2,1)} %pad_maximum_fusion.2), channel_id=1, source_target_pairs={{0,1},{1,2},{2,3},{4,5},{5,6},{6,7},{8,9},{9,10},{10,11},{12,13},{... | collective-permute-start | bytes 99080 | tf_op jit(solution)/shard_map/ppermute | solution.py:22
  48.8 3.2 %collective-permute-done.4 = bf16[64,1,258]{2,1,0:T(2,128)(2,1)} collective-permute-done((bf16[64,1,258]{2,1,0:T(2,128)(2,1)}, bf16[64,1,258]{2,1,0:T(2,128)(2,1)}, u32[]{:S(2)}, u32[]{:S(2)}) %collective-permute-start.4) | collective-permute-done | bytes 33056 | tf_op jit(solution)/shard_map/ppermute | solution.py:23
  56.7 11.7 %shard_map.152 = bf16[5,64,64,256]{3,2,1,0:T(8,128)(2,1)} custom-call(bf16[5,64,64,256]{3,2,1,0:T(8,128)(2,1)} %s_ref.1, bf16[5,32,4096]{2,1,0:T(8,128)(2,1)} %copy-done.2, bf16[5,32,4096]{2,1,0:T(8,128)(2,1)} %copy-done.3, bf16[32,256]{1,0:T(8,128)(2,1)} %get-tuple-element.78.place_lo_ref, bf16[32,256]{1,0:T(8,128)(2,1)} %get-tuple-element.89.place_hi_ref, ...), custom_call_target="tpu_custom_call" | custom-call | tf_op jit(solution)/shard_map/pallas_call | solution.py:77
  68.4 6.9 %fusion = f32[64,256]{1,0:T(8,128)S(1)} fusion(bf16[5,64,64,256]{3,2,1,0:T(8,128)(2,1)} %shard_map.152, f32[5,64,256]{2,1,0:T(8,128)} %select_convert_fusion.3), kind=kLoop, calls=%fused_computation.9 | loop fusion | flops 15712256 | bytes 10878976 | tf_op jit(solution)/shard_map/reduce_sum | solution.py:193
  77.7 2.4 %collective-permute-start.8 = (bf16[64,1,1]{2,0,1:T(8,128)(2,1)S(1)}, bf16[64,1,1]{2,0,1:T(8,128)(2,1)S(1)}, u32[]{:S(2)}, u32[]{:S(2)}) collective-permute-start(bf16[64,1,1]{2,0,1:T(8,128)(2,1)S(1)} %get-tuple-element.64), channel_id=1, source_target_pairs={{0,4},{4,8},{8,12},{12,16},{16,20},{20,24},{24,28},{28,32},{32,36}... | collective-permute-start | bytes 392 | tf_op jit(solution)/shard_map/ppermute | solution.py:22
  80.3 4.6 %collective-permute-done.8 = bf16[64,1,1]{2,0,1:T(8,128)(2,1)S(1)} collective-permute-done((bf16[64,1,1]{2,0,1:T(8,128)(2,1)S(1)}, bf16[64,1,1]{2,0,1:T(8,128)(2,1)S(1)}, u32[]{:S(2)}, u32[]{:S(2)}) %collective-permute-start.8) | collective-permute-done | bytes 160 | tf_op jit(solution)/shard_map/ppermute | solution.py:22
  84.9 3.4 %collective-permute-start.11 = (bf16[64,1,258]{2,0,1:T(8,128)(2,1)S(1)}, bf16[64,1,258]{2,0,1:T(8,128)(2,1)S(1)}, u32[]{:S(2)}, u32[]{:S(2)}) collective-permute-start(bf16[64,1,258]{2,0,1:T(8,128)(2,1)S(1)} %pad_maximum_fusion.5), channel_id=1, source_target_pairs={{0,1},{1,2},{2,3},{4,5},{5,6},{6,7},{8,9},{9,10},{10,11},{12,13},{... | collective-permute-start | bytes 99080 | tf_op jit(solution)/shard_map/ppermute | solution.py:22
  90.2 4.2 %collective-permute-done.10 = bf16[64,1,258]{2,0,1:T(8,128)(2,1)S(1)} collective-permute-done((bf16[64,1,258]{2,0,1:T(8,128)(2,1)S(1)}, bf16[64,1,258]{2,0,1:T(8,128)(2,1)S(1)}, u32[]{:S(2)}, u32[]{:S(2)}) %collective-permute-start.10) | collective-permute-done | bytes 33056 | tf_op jit(solution)/shard_map/ppermute | solution.py:23
  94.6 2.8 %fusion.1 = f32[64,256]{1,0:T(8,128)S(1)} fusion(bf16[5,64,64,256]{3,2,1,0:T(8,128)(2,1)S(1)} %copy-done.1, f32[5,64,256]{2,1,0:T(8,128)S(1)} %select_convert_fusion.2), kind=kLoop, calls=%fused_computation.10 | loop fusion | flops 15712256 | bytes 10878976 | tf_op jit(solution)/shard_map/reduce_sum | solution.py:193
  99.6 2.4 %collective-permute-start.12 = (bf16[64,1,1]{2,0,1:T(8,128)(2,1)S(1)}, bf16[64,1,1]{2,0,1:T(8,128)(2,1)S(1)}, u32[]{:S(2)}, u32[]{:S(2)}) collective-permute-start(bf16[64,1,1]{2,0,1:T(8,128)(2,1)S(1)} %get-tuple-element.58), channel_id=1, source_target_pairs={{0,4},{4,8},{8,12},{12,16},{16,20},{20,24},{24,28},{28,32},{32,36}... | collective-permute-start | bytes 392 | tf_op jit(solution)/shard_map/ppermute | solution.py:22
  102.3 4.5 %collective-permute-done.12 = bf16[64,1,1]{2,0,1:T(8,128)(2,1)S(1)} collective-permute-done((bf16[64,1,1]{2,0,1:T(8,128)(2,1)S(1)}, bf16[64,1,1]{2,0,1:T(8,128)(2,1)S(1)}, u32[]{:S(2)}, u32[]{:S(2)}) %collective-permute-start.12) | collective-permute-done | bytes 160 | tf_op jit(solution)/shard_map/ppermute | solution.py:22
  106.9 3.1 %collective-permute-start.15 = (bf16[64,1,258]{2,0,1:T(8,128)(2,1)S(1)}, bf16[64,1,258]{2,0,1:T(8,128)(2,1)S(1)}, u32[]{:S(2)}, u32[]{:S(2)}) collective-permute-start(bf16[64,1,258]{2,0,1:T(8,128)(2,1)S(1)} %pad_maximum_fusion.6), channel_id=1, source_target_pairs={{0,1},{1,2},{2,3},{4,5},{5,6},{6,7},{8,9},{9,10},{10,11},{12,13},{... | collective-permute-start | bytes 99080 | tf_op jit(solution)/shard_map/ppermute | solution.py:22
  111.8 4.2 %collective-permute-done.14 = bf16[64,1,258]{2,0,1:T(8,128)(2,1)S(1)} collective-permute-done((bf16[64,1,258]{2,0,1:T(8,128)(2,1)S(1)}, bf16[64,1,258]{2,0,1:T(8,128)(2,1)S(1)}, u32[]{:S(2)}, u32[]{:S(2)}) %collective-permute-start.14) | collective-permute-done | bytes 33056 | tf_op jit(solution)/shard_map/ppermute | solution.py:23
  116.2 2.8 %fusion.2 = f32[64,256]{1,0:T(8,128)S(1)} fusion(bf16[5,64,64,256]{3,2,1,0:T(8,128)(2,1)S(1)} %copy-done.1, f32[5,64,256]{2,1,0:T(8,128)S(1)} %select_convert_fusion.1), kind=kLoop, calls=%fused_computation.11 | loop fusion | flops 15712256 | bytes 10878976 | tf_op jit(solution)/shard_map/reduce_sum | solution.py:193
  121.3 2.4 %collective-permute-start.16 = (bf16[64,1,1]{2,0,1:T(8,128)(2,1)S(1)}, bf16[64,1,1]{2,0,1:T(8,128)(2,1)S(1)}, u32[]{:S(2)}, u32[]{:S(2)}) collective-permute-start(bf16[64,1,1]{2,0,1:T(8,128)(2,1)S(1)} %get-tuple-element.54), channel_id=1, source_target_pairs={{0,4},{4,8},{8,12},{12,16},{16,20},{20,24},{24,28},{28,32},{32,36}... | collective-permute-start | bytes 392 | tf_op jit(solution)/shard_map/ppermute | solution.py:22
  123.9 4.5 %collective-permute-done.16 = bf16[64,1,1]{2,0,1:T(8,128)(2,1)S(1)} collective-permute-done((bf16[64,1,1]{2,0,1:T(8,128)(2,1)S(1)}, bf16[64,1,1]{2,0,1:T(8,128)(2,1)S(1)}, u32[]{:S(2)}, u32[]{:S(2)}) %collective-permute-start.16) | collective-permute-done | bytes 160 | tf_op jit(solution)/shard_map/ppermute | solution.py:22
  128.5 2.0 %collective-permute-start.19 = (bf16[64,1,258]{2,0,1:T(8,128)(2,1)S(1)}, bf16[64,1,258]{2,0,1:T(8,128)(2,1)S(1)}, u32[]{:S(2)}, u32[]{:S(2)}) collective-permute-start(bf16[64,1,258]{2,0,1:T(8,128)(2,1)S(1)} %pad_maximum_fusion.7), channel_id=1, source_target_pairs={{0,1},{1,2},{2,3},{4,5},{5,6},{6,7},{8,9},{9,10},{10,11},{12,13},{... | collective-permute-start | bytes 99080 | tf_op jit(solution)/shard_map/ppermute | solution.py:22
  132.3 4.2 %collective-permute-done.18 = bf16[64,1,258]{2,0,1:T(8,128)(2,1)S(1)} collective-permute-done((bf16[64,1,258]{2,0,1:T(8,128)(2,1)S(1)}, bf16[64,1,258]{2,0,1:T(8,128)(2,1)S(1)}, u32[]{:S(2)}, u32[]{:S(2)}) %collective-permute-start.18) | collective-permute-done | bytes 33056 | tf_op jit(solution)/shard_map/ppermute | solution.py:23
  136.7 2.8 %fusion.3 = f32[64,256]{1,0:T(8,128)S(1)} fusion(bf16[5,64,64,256]{3,2,1,0:T(8,128)(2,1)S(1)} %copy-done.1, f32[5,64,256]{2,1,0:T(8,128)S(1)} %select_convert_fusion), kind=kLoop, calls=%fused_computation.12 | loop fusion | flops 15712256 | bytes 10878976 | tf_op jit(solution)/shard_map/reduce_sum | solution.py:193
  (139 shorter events, 40.0 us)
Async XLA Ops:
  0.6 74.7 %copy-start = (f32[48,64]{1,0:T(8,128)S(1)}, f32[48,64]{1,0:T(8,128)}, u32[]{:S(2)}) copy-start(f32[48,64]{1,0:T(8,128)} %param.26) | copy-start | bytes 36868
  0.7 29.2 %copy-start.14 = (s32[5,1,256]{2,1,0:T(1,128)S(1)}, s32[5,1,256]{2,1,0:T(1,128)}, u32[]{:S(2)}) copy-start(s32[5,1,256]{2,1,0:T(1,128)} %param.21) | copy-start | bytes 15364
  0.7 29.2 %copy-start.15 = (s32[1,256]{1,0:T(1,128)S(1)}, s32[1,256]{1,0:T(1,128)}, u32[]{:S(2)}) copy-start(s32[1,256]{1,0:T(1,128)} %param.22) | copy-start | bytes 3076
  10.7 44.4 %collective-permute-start = (bf16[5,32,4096]{2,1,0:T(8,128)(2,1)}, bf16[5,32,4096]{2,1,0:T(8,128)(2,1)S(1)}, u32[]{:S(2)}, u32[]{:S(2)}) collective-permute-start(bf16[5,32,4096]{2,1,0:T(8,128)(2,1)} %get-tuple-element.7), channel_id=1, source_target_pairs={{0,4},{4,8},{8,12},{12,16},{16,20},{20,24},{24,28},{28,32},{32,36}... | collective-permute-start | bytes 3932168 | tf_op jit(solution)/shard_map/ppermute | solution.py:32
  12.6 42.5 %collective-permute-start.1 = (bf16[5,32,4096]{2,1,0:T(8,128)(2,1)}, bf16[5,32,4096]{2,1,0:T(8,128)(2,1)S(1)}, u32[]{:S(2)}, u32[]{:S(2)}) collective-permute-start(bf16[5,32,4096]{2,1,0:T(8,128)(2,1)} %get-tuple-element.8), channel_id=1, source_target_pairs={{4,0},{8,4},{12,8},{16,12},{20,16},{24,20},{28,24},{32,28},{36,32}... | collective-permute-start | bytes 3932168 | tf_op jit(solution)/shard_map/ppermute | solution.py:33
  18.5 15.5 %collective-permute-start.3 = (bf16[64,1,1]{2,1,0:T(2,128)(2,1)S(1)}, bf16[64,1,1]{2,1,0:T(2,128)(2,1)S(1)}, u32[]{:S(2)}, u32[]{:S(2)}) collective-permute-start(bf16[64,1,1]{2,1,0:T(2,128)(2,1)S(1)} %get-tuple-element.33), channel_id=1, source_target_pairs={{4,0},{8,4},{12,8},{16,12},{20,16},{24,20},{28,24},{32,28},{36,32}... | collective-permute-start | bytes 392 | tf_op jit(solution)/shard_map/ppermute | solution.py:23
  20.4 19.5 %collective-permute-start.2 = (bf16[64,1,1]{2,1,0:T(2,128)(2,1)S(1)}, bf16[64,1,1]{2,1,0:T(2,128)(2,1)S(1)}, u32[]{:S(2)}, u32[]{:S(2)}) collective-permute-start(bf16[64,1,1]{2,1,0:T(2,128)(2,1)S(1)} %get-tuple-element.32), channel_id=1, source_target_pairs={{0,4},{4,8},{8,12},{12,16},{16,20},{20,24},{24,28},{28,32},{32,36}... | collective-permute-start | bytes 392 | tf_op jit(solution)/shard_map/ppermute | solution.py:22
  24.5 20.7 %collective-permute-start.6 = (f32[96,32]{0,1:T(8,128)S(1)}, f32[96,32]{0,1:T(8,128)S(1)}, u32[]{:S(2)}, u32[]{:S(2)}) collective-permute-start(f32[96,32]{0,1:T(8,128)S(1)} %get-tuple-element.29), channel_id=1, source_target_pairs={{0,4},{4,8},{8,12},{12,16},{16,20},{20,24},{24,28},{28,32},{32,36}... | collective-permute-start | bytes 36872 | tf_op jit(solution)/shard_map/ppermute | solution.py:32
  34.0 12.5 %collective-permute-start.7 = (f32[96,32]{0,1:T(8,128)S(1)}, f32[96,32]{0,1:T(8,128)S(1)}, u32[]{:S(2)}, u32[]{:S(2)}) collective-permute-start(f32[96,32]{0,1:T(8,128)S(1)} %get-tuple-element.28), channel_id=1, source_target_pairs={{4,0},{8,4},{12,8},{16,12},{20,16},{24,20},{28,24},{32,28},{36,32}... | collective-permute-start | bytes 36872 | tf_op jit(solution)/shard_map/ppermute | solution.py:33
  40.8 7.7 %collective-permute-start.5 = (bf16[64,1,258]{2,1,0:T(2,128)(2,1)}, bf16[64,1,258]{2,1,0:T(2,128)(2,1)S(1)}, u32[]{:S(2)}, u32[]{:S(2)}) collective-permute-start(bf16[64,1,258]{2,1,0:T(2,128)(2,1)} %pad_maximum_fusion.2), channel_id=1, source_target_pairs={{0,1},{1,2},{2,3},{4,5},{5,6},{6,7},{8,9},{9,10},{10,11},{12,13},{... | collective-permute-start | bytes 99080 | tf_op jit(solution)/shard_map/ppermute | solution.py:22
  45.2 6.8 %collective-permute-start.4 = (bf16[64,1,258]{2,1,0:T(2,128)(2,1)}, bf16[64,1,258]{2,1,0:T(2,128)(2,1)}, u32[]{:S(2)}, u32[]{:S(2)}) collective-permute-start(bf16[64,1,258]{2,1,0:T(2,128)(2,1)} %pad_maximum_fusion.2), channel_id=1, source_target_pairs={{1,0},{2,1},{3,2},{5,4},{6,5},{7,6},{9,8},{10,9},{11,10},{13,12},{... | collective-permute-start | bytes 99080 | tf_op jit(solution)/shard_map/ppermute | solution.py:23
  68.4 26.2 %copy-start.1 = (bf16[5,64,64,256]{3,2,1,0:T(8,128)(2,1)S(1)}, bf16[5,64,64,256]{3,2,1,0:T(8,128)(2,1)}, u32[]{:S(2)}) copy-start(bf16[5,64,64,256]{3,2,1,0:T(8,128)(2,1)} %shard_map.152) | copy-start | bytes 31457284
  75.7 4.5 %collective-permute-start.9 = (bf16[64,1,1]{2,0,1:T(8,128)(2,1)S(1)}, bf16[64,1,1]{2,0,1:T(8,128)(2,1)S(1)}, u32[]{:S(2)}, u32[]{:S(2)}) collective-permute-start(bf16[64,1,1]{2,0,1:T(8,128)(2,1)S(1)} %get-tuple-element.65), channel_id=1, source_target_pairs={{4,0},{8,4},{12,8},{16,12},{20,16},{24,20},{28,24},{32,28},{36,32}... | collective-permute-start | bytes 392 | tf_op jit(solution)/shard_map/ppermute | solution.py:23
  77.7 7.2 %collective-permute-start.8 = (bf16[64,1,1]{2,0,1:T(8,128)(2,1)S(1)}, bf16[64,1,1]{2,0,1:T(8,128)(2,1)S(1)}, u32[]{:S(2)}, u32[]{:S(2)}) collective-permute-start(bf16[64,1,1]{2,0,1:T(8,128)(2,1)S(1)} %get-tuple-element.64), channel_id=1, source_target_pairs={{0,4},{4,8},{8,12},{12,16},{16,20},{20,24},{24,28},{28,32},{32,36}... | collective-permute-start | bytes 392 | tf_op jit(solution)/shard_map/ppermute | solution.py:22
  84.9 5.1 %collective-permute-start.11 = (bf16[64,1,258]{2,0,1:T(8,128)(2,1)S(1)}, bf16[64,1,258]{2,0,1:T(8,128)(2,1)S(1)}, u32[]{:S(2)}, u32[]{:S(2)}) collective-permute-start(bf16[64,1,258]{2,0,1:T(8,128)(2,1)S(1)} %pad_maximum_fusion.5), channel_id=1, source_target_pairs={{0,1},{1,2},{2,3},{4,5},{5,6},{6,7},{8,9},{9,10},{10,11},{12,13},{... | collective-permute-start | bytes 99080 | tf_op jit(solution)/shard_map/ppermute | solution.py:22
  88.3 6.0 %collective-permute-start.10 = (bf16[64,1,258]{2,0,1:T(8,128)(2,1)S(1)}, bf16[64,1,258]{2,0,1:T(8,128)(2,1)S(1)}, u32[]{:S(2)}, u32[]{:S(2)}) collective-permute-start(bf16[64,1,258]{2,0,1:T(8,128)(2,1)S(1)} %pad_maximum_fusion.5), channel_id=1, source_target_pairs={{1,0},{2,1},{3,2},{5,4},{6,5},{7,6},{9,8},{10,9},{11,10},{13,12},{... | collective-permute-start | bytes 99080 | tf_op jit(solution)/shard_map/ppermute | solution.py:23
  97.7 4.5 %collective-permute-start.13 = (bf16[64,1,1]{2,0,1:T(8,128)(2,1)S(1)}, bf16[64,1,1]{2,0,1:T(8,128)(2,1)S(1)}, u32[]{:S(2)}, u32[]{:S(2)}) collective-permute-start(bf16[64,1,1]{2,0,1:T(8,128)(2,1)S(1)} %get-tuple-element.59), channel_id=1, source_target_pairs={{4,0},{8,4},{12,8},{16,12},{20,16},{24,20},{28,24},{32,28},{36,32}... | collective-permute-start | bytes 392 | tf_op jit(solution)/shard_map/ppermute | solution.py:23
  99.6 7.2 %collective-permute-start.12 = (bf16[64,1,1]{2,0,1:T(8,128)(2,1)S(1)}, bf16[64,1,1]{2,0,1:T(8,128)(2,1)S(1)}, u32[]{:S(2)}, u32[]{:S(2)}) collective-permute-start(bf16[64,1,1]{2,0,1:T(8,128)(2,1)S(1)} %get-tuple-element.58), channel_id=1, source_target_pairs={{0,4},{4,8},{8,12},{12,16},{16,20},{20,24},{24,28},{28,32},{32,36}... | collective-permute-start | bytes 392 | tf_op jit(solution)/shard_map/ppermute | solution.py:22
  106.9 4.8 %collective-permute-start.15 = (bf16[64,1,258]{2,0,1:T(8,128)(2,1)S(1)}, bf16[64,1,258]{2,0,1:T(8,128)(2,1)S(1)}, u32[]{:S(2)}, u32[]{:S(2)}) collective-permute-start(bf16[64,1,258]{2,0,1:T(8,128)(2,1)S(1)} %pad_maximum_fusion.6), channel_id=1, source_target_pairs={{0,1},{1,2},{2,3},{4,5},{5,6},{6,7},{8,9},{9,10},{10,11},{12,13},{... | collective-permute-start | bytes 99080 | tf_op jit(solution)/shard_map/ppermute | solution.py:22
  110.0 6.0 %collective-permute-start.14 = (bf16[64,1,258]{2,0,1:T(8,128)(2,1)S(1)}, bf16[64,1,258]{2,0,1:T(8,128)(2,1)S(1)}, u32[]{:S(2)}, u32[]{:S(2)}) collective-permute-start(bf16[64,1,258]{2,0,1:T(8,128)(2,1)S(1)} %pad_maximum_fusion.6), channel_id=1, source_target_pairs={{1,0},{2,1},{3,2},{5,4},{6,5},{7,6},{9,8},{10,9},{11,10},{13,12},{... | collective-permute-start | bytes 99080 | tf_op jit(solution)/shard_map/ppermute | solution.py:23
  119.4 4.5 %collective-permute-start.17 = (bf16[64,1,1]{2,0,1:T(8,128)(2,1)S(1)}, bf16[64,1,1]{2,0,1:T(8,128)(2,1)S(1)}, u32[]{:S(2)}, u32[]{:S(2)}) collective-permute-start(bf16[64,1,1]{2,0,1:T(8,128)(2,1)S(1)} %get-tuple-element.55), channel_id=1, source_target_pairs={{4,0},{8,4},{12,8},{16,12},{20,16},{24,20},{28,24},{32,28},{36,32}... | collective-permute-start | bytes 392 | tf_op jit(solution)/shard_map/ppermute | solution.py:23
  121.3 7.2 %collective-permute-start.16 = (bf16[64,1,1]{2,0,1:T(8,128)(2,1)S(1)}, bf16[64,1,1]{2,0,1:T(8,128)(2,1)S(1)}, u32[]{:S(2)}, u32[]{:S(2)}) collective-permute-start(bf16[64,1,1]{2,0,1:T(8,128)(2,1)S(1)} %get-tuple-element.54), channel_id=1, source_target_pairs={{0,4},{4,8},{8,12},{12,16},{16,20},{20,24},{24,28},{28,32},{32,36}... | collective-permute-start | bytes 392 | tf_op jit(solution)/shard_map/ppermute | solution.py:22
  128.5 3.7 %collective-permute-start.19 = (bf16[64,1,258]{2,0,1:T(8,128)(2,1)S(1)}, bf16[64,1,258]{2,0,1:T(8,128)(2,1)S(1)}, u32[]{:S(2)}, u32[]{:S(2)}) collective-permute-start(bf16[64,1,258]{2,0,1:T(8,128)(2,1)S(1)} %pad_maximum_fusion.7), channel_id=1, source_target_pairs={{0,1},{1,2},{2,3},{4,5},{5,6},{6,7},{8,9},{9,10},{10,11},{12,13},{... | collective-permute-start | bytes 99080 | tf_op jit(solution)/shard_map/ppermute | solution.py:22
  130.5 6.0 %collective-permute-start.18 = (bf16[64,1,258]{2,0,1:T(8,128)(2,1)S(1)}, bf16[64,1,258]{2,0,1:T(8,128)(2,1)S(1)}, u32[]{:S(2)}, u32[]{:S(2)}) collective-permute-start(bf16[64,1,258]{2,0,1:T(8,128)(2,1)S(1)} %pad_maximum_fusion.7), channel_id=1, source_target_pairs={{1,0},{2,1},{3,2},{5,4},{6,5},{7,6},{9,8},{10,9},{11,10},{13,12},{... | collective-permute-start | bytes 99080 | tf_op jit(solution)/shard_map/ppermute | solution.py:23
  (14 other events, 222.8 us)

commit v16 on v10

--- a/solution.py
+++ b/solution.py
@@ -187,7 +187,7 @@
     codes = jnp.where(live, pattern[:, 0, :], 9)[:, None, :]
     for repeat in range(ITERS):
         rounded = moved.astype(jnp.bfloat16)[:, None, :]
-        padded = padded_2(rounded, (("shaft", 2), ("ply", 1)), 1)
+        padded = padded_2(rounded, (("ply", 1), ("shaft", 2)), 1)
         neighbours = jnp.zeros((slots,) + moved.shape, jnp.bfloat16)
         for code_index in range(9):
             shifted = padded[:, code_index // 3, code_index % 3 : code_index % 3 + blocks]

time: 141 us -> 156 us (1.11)
  the two profiles are of different devices: /device:TPU:96 before, /device:TPU:31 now
where the time goes in v16:
time: 156 us; the launch traced here: 155 us
  starting transfers between devices  59.5 us (38%)
  waiting for transfers between devices  31.4 us (20%)
  other arithmetic  26.8 us (17%)
  Pallas kernels  20.1 us (13%)
  local copies, waits for them, and re-layouts  12.7 us (8%)
  matrix products  2.65 us (2%)
    ppermute x8, starting transfers between devices, padded_2(): before = lax.ppermute(last, axis, up)  25.4 us
    ppermute x8, starting transfers between devices, padded_2(): after = lax.ppermute(first, axis, down)  19.2 us
    reduce_sum x4, other arithmetic, on_device(): jnp.sum(product, axis=(0, 2))  19 us
    ppermute x8, waiting for transfers between devices, padded_2(): after = lax.ppermute(first, axis, down)  16.3 us
    pallas_call x1, Pallas kernels, merge_arrived(): pl.pallas_call(merge_kernel, grid=(slots,), in_specs=[pl.BlockSpec((1, ro...  11.7 us
    ppermute x8, waiting for transfers between devices, padded_2(): before = lax.ppermute(last, axis, up)  9.8 us
    ppermute x2, starting transfers between devices, neighbour_exchange(): from_lower = lax.ppermute(upper_bound, axis, up)  9.78 us
    pallas_call x1, Pallas kernels, gather_leaving(): pl.pallas_call(gather_kernel, grid=(slots,), in_specs=[pl.BlockSpec((1, d...  8.41 us
  transfers between devices with their start and end apart: 20, of which 9 were waited for; matrix products, arithmetic and copies ran while one was open for 10% of the time, Pallas kernels for 5%

profile of v16, /device:TPU:31, one launch (start us, length us, event | category | flops | bytes accessed | tf_op | source)
XLA Modules:
  0.0 154.6 jit_solution(9567814489205715671)
XLA Ops:
  1.7 2.5 %collective-permute-start.3 = (bf16[64,1,256]{2,1,0:T(2,128)(2,1)S(1)}, bf16[64,1,256]{2,1,0:T(2,128)(2,1)S(1)}, u32[]{:S(2)}, u32[]{:S(2)}) collective-permute-start(bf16[64,1,256]{2,1,0:T(2,128)(2,1)S(1)} %convert_element_type.85), channel_id=1, source_target_pairs={{1,0},{2,1},{3,2},{5,4},{6,5},{7,6},{9,8},{10,9},{11,10},{13,12},{... | collective-permute-start | bytes 98312 | tf_op jit(solution)/shard_map/ppermute | solution.py:23
  6.9 8.4 %shard_map.151 = (bf16[5,32,4096]{2,1,0:T(8,128)(2,1)}, bf16[5,32,4096]{2,1,0:T(8,128)(2,1)}) custom-call(bf16[5,4096,256]{2,1,0:T(8,128)(2,1)} %bitcast.230, bf16[32,256]{1,0:T(8,128)(2,1)} %get-tuple-element.85.lo_ref, bf16[32,256]{1,0:T(8,128)(2,1)} %get-tuple-element.86.hi_ref), custom_call_target="tpu_custom_call" | custom-call | tf_op jit(solution)/shard_map/pallas_call | solution.py:51
  15.3 4.0 %collective-permute-start = (bf16[5,32,4096]{2,1,0:T(8,128)(2,1)}, bf16[5,32,4096]{2,1,0:T(8,128)(2,1)S(1)}, u32[]{:S(2)}, u32[]{:S(2)}) collective-permute-start(bf16[5,32,4096]{2,1,0:T(8,128)(2,1)} %get-tuple-element.7), channel_id=1, source_target_pairs={{0,4},{4,8},{8,12},{12,16},{16,20},{20,24},{24,28},{28,32},{32,36}... | collective-permute-start | bytes 3932168 | tf_op jit(solution)/shard_map/ppermute | solution.py:32
  24.1 5.8 %collective-permute-start.6 = (f32[96,32]{0,1:T(8,128)S(1)}, f32[96,32]{0,1:T(8,128)S(1)}, u32[]{:S(2)}, u32[]{:S(2)}) collective-permute-start(f32[96,32]{0,1:T(8,128)S(1)} %get-tuple-element.57), channel_id=1, source_target_pairs={{0,4},{4,8},{8,12},{12,16},{16,20},{20,24},{24,28},{28,32},{32,36}... | collective-permute-start | bytes 36872 | tf_op jit(solution)/shard_map/ppermute | solution.py:32
  34.3 3.2 %collective-permute-start.7 = (f32[96,32]{0,1:T(8,128)S(1)}, f32[96,32]{0,1:T(8,128)S(1)}, u32[]{:S(2)}, u32[]{:S(2)}) collective-permute-start(f32[96,32]{0,1:T(8,128)S(1)} %get-tuple-element.56), channel_id=1, source_target_pairs={{4,0},{8,4},{12,8},{16,12},{20,16},{24,20},{28,24},{32,28},{36,32}... | collective-permute-start | bytes 36872 | tf_op jit(solution)/shard_map/ppermute | solution.py:33
  37.5 4.7 %collective-permute-done.7 = f32[96,32]{0,1:T(8,128)S(1)} collective-permute-done((f32[96,32]{0,1:T(8,128)S(1)}, f32[96,32]{0,1:T(8,128)S(1)}, u32[]{:S(2)}, u32[]{:S(2)}) %collective-permute-start.7) | collective-permute-done | bytes 12320 | tf_op jit(solution)/shard_map/ppermute | solution.py:33
  45.8 5.8 %collective-permute-start.5 = (bf16[64,3,1]{2,1,0:T(4,128)(2,1)}, bf16[64,3,1]{2,1,0:T(4,128)(2,1)}, u32[]{:S(2)}, u32[]{:S(2)}) collective-permute-start(bf16[64,3,1]{2,1,0:T(4,128)(2,1)} %get-tuple-element.49), channel_id=1, source_target_pairs={{0,4},{4,8},{8,12},{12,16},{16,20},{20,24},{24,28},{28,32},{32,36}... | collective-permute-start | bytes 1160 | tf_op jit(solution)/shard_map/ppermute | solution.py:22
  58.0 11.7 %shard_map.152 = bf16[5,64,64,256]{3,2,1,0:T(8,128)(2,1)} custom-call(bf16[5,64,64,256]{3,2,1,0:T(8,128)(2,1)} %s_ref.1, bf16[5,32,4096]{2,1,0:T(8,128)(2,1)} %copy-done.2, bf16[5,32,4096]{2,1,0:T(8,128)(2,1)} %copy-done.3, bf16[32,256]{1,0:T(8,128)(2,1)} %get-tuple-element.72.place_lo_ref, bf16[32,256]{1,0:T(8,128)(2,1)} %get-tuple-element.87.place_hi_ref, ...), custom_call_target="tpu_custom_call" | custom-call | tf_op jit(solution)/shard_map/pallas_call | solution.py:79
  69.7 6.8 %fusion = f32[64,256]{1,0:T(8,128)S(1)} fusion(bf16[5,64,64,256]{3,2,1,0:T(8,128)(2,1)} %shard_map.152, f32[5,64,256]{2,1,0:T(8,128)S(1)} %select_convert_fusion.3), kind=kLoop, calls=%fused_computation.9 | loop fusion | flops 15712256 | bytes 10878976 | tf_op jit(solution)/shard_map/reduce_sum | solution.py:196
  76.8 4.3 %collective-permute-start.9 = (bf16[64,1,256]{2,0,1:T(8,128)(2,1)S(1)}, bf16[64,1,256]{2,0,1:T(8,128)(2,1)S(1)}, u32[]{:S(2)}, u32[]{:S(2)}) collective-permute-start(bf16[64,1,256]{2,0,1:T(8,128)(2,1)S(1)} %bitcast.237), channel_id=1, source_target_pairs={{1,0},{2,1},{3,2},{5,4},{6,5},{7,6},{9,8},{10,9},{11,10},{13,12},{... | collective-permute-start | bytes 98312 | tf_op jit(solution)/shard_map/ppermute | solution.py:23
  83.4 2.4 %collective-permute-done.8 = bf16[64,1,256]{2,0,1:T(8,128)(2,1)S(1)} collective-permute-done((bf16[64,1,256]{2,0,1:T(8,128)(2,1)S(1)}, bf16[64,1,256]{2,0,1:T(8,128)(2,1)S(1)}, u32[]{:S(2)}, u32[]{:S(2)}) %collective-permute-start.8) | collective-permute-done | bytes 32800 | tf_op jit(solution)/shard_map/ppermute | solution.py:22
  85.9 7.8 %collective-permute-start.11 = (bf16[64,3,1]{2,0,1:T(8,128)(2,1)S(1)}, bf16[64,3,1]{2,0,1:T(8,128)(2,1)S(1)}, u32[]{:S(2)}, u32[]{:S(2)}) collective-permute-start(bf16[64,3,1]{2,0,1:T(8,128)(2,1)S(1)} %get-tuple-element.55), channel_id=1, source_target_pairs={{0,4},{4,8},{8,12},{12,16},{16,20},{20,24},{24,28},{28,32},{32,36}... | collective-permute-start | bytes 1160 | tf_op jit(solution)/shard_map/ppermute | solution.py:22
  96.9 5.3 %collective-permute-done.10 = bf16[64,3,1]{2,0,1:T(8,128)(2,1)S(1)} collective-permute-done((bf16[64,3,1]{2,0,1:T(8,128)(2,1)S(1)}, bf16[64,3,1]{2,0,1:T(8,128)(2,1)S(1)}, u32[]{:S(2)}, u32[]{:S(2)}) %collective-permute-start.10) | collective-permute-done | bytes 416 | tf_op jit(solution)/shard_map/ppermute | solution.py:23
  102.5 6.7 %fusion.1 = f32[64,256]{1,0:T(8,128)S(1)} fusion(bf16[5,64,64,256]{3,2,1,0:T(8,128)(2,1)} %shard_map.152, f32[5,64,256]{2,1,0:T(8,128)S(1)} %select_convert_fusion.2), kind=kLoop, calls=%fused_computation.10 | loop fusion | flops 15712256 | bytes 10878976 | tf_op jit(solution)/shard_map/reduce_sum | solution.py:196
  109.4 2.4 %collective-permute-start.13 = (bf16[64,1,256]{2,0,1:T(8,128)(2,1)S(1)}, bf16[64,1,256]{2,0,1:T(8,128)(2,1)S(1)}, u32[]{:S(2)}, u32[]{:S(2)}) collective-permute-start(bf16[64,1,256]{2,0,1:T(8,128)(2,1)S(1)} %bitcast.242), channel_id=1, source_target_pairs={{1,0},{2,1},{3,2},{5,4},{6,5},{7,6},{9,8},{10,9},{11,10},{13,12},{... | collective-permute-start | bytes 98312 | tf_op jit(solution)/shard_map/ppermute | solution.py:23
  113.2 3.3 %collective-permute-done.12 = bf16[64,1,256]{2,0,1:T(8,128)(2,1)S(1)} collective-permute-done((bf16[64,1,256]{2,0,1:T(8,128)(2,1)S(1)}, bf16[64,1,256]{2,0,1:T(8,128)(2,1)S(1)}, u32[]{:S(2)}, u32[]{:S(2)}) %collective-permute-start.12) | collective-permute-done | bytes 32800 | tf_op jit(solution)/shard_map/ppermute | solution.py:22
  116.6 3.3 %collective-permute-start.15 = (bf16[64,3,1]{2,0,1:T(8,128)(2,1)S(1)}, bf16[64,3,1]{2,0,1:T(8,128)(2,1)S(1)}, u32[]{:S(2)}, u32[]{:S(2)}) collective-permute-start(bf16[64,3,1]{2,0,1:T(8,128)(2,1)S(1)} %get-tuple-element.53), channel_id=1, source_target_pairs={{0,4},{4,8},{8,12},{12,16},{16,20},{20,24},{24,28},{28,32},{32,36}... | collective-permute-start | bytes 1160 | tf_op jit(solution)/shard_map/ppermute | solution.py:22
  122.2 5.5 %collective-permute-done.14 = bf16[64,3,1]{2,0,1:T(8,128)(2,1)S(1)} collective-permute-done((bf16[64,3,1]{2,0,1:T(8,128)(2,1)S(1)}, bf16[64,3,1]{2,0,1:T(8,128)(2,1)S(1)}, u32[]{:S(2)}, u32[]{:S(2)}) %collective-permute-start.14) | collective-permute-done | bytes 416 | tf_op jit(solution)/shard_map/ppermute | solution.py:23
  127.9 2.8 %fusion.2 = f32[64,256]{1,0:T(8,128)S(1)} fusion(bf16[5,64,64,256]{3,2,1,0:T(8,128)(2,1)S(1)} %copy-done.1, f32[5,64,256]{2,1,0:T(8,128)S(1)} %select_convert_fusion.1), kind=kLoop, calls=%fused_computation.11 | loop fusion | flops 15712256 | bytes 10878976 | tf_op jit(solution)/shard_map/reduce_sum | solution.py:196
  131.0 2.2 %collective-permute-start.17 = (bf16[64,1,256]{2,0,1:T(8,128)(2,1)S(1)}, bf16[64,1,256]{2,0,1:T(8,128)(2,1)S(1)}, u32[]{:S(2)}, u32[]{:S(2)}) collective-permute-start(bf16[64,1,256]{2,0,1:T(8,128)(2,1)S(1)} %bitcast.232), channel_id=1, source_target_pairs={{1,0},{2,1},{3,2},{5,4},{6,5},{7,6},{9,8},{10,9},{11,10},{13,12},{... | collective-permute-start | bytes 98312 | tf_op jit(solution)/shard_map/ppermute | solution.py:23
  134.5 3.3 %collective-permute-done.16 = bf16[64,1,256]{2,0,1:T(8,128)(2,1)S(1)} collective-permute-done((bf16[64,1,256]{2,0,1:T(8,128)(2,1)S(1)}, bf16[64,1,256]{2,0,1:T(8,128)(2,1)S(1)}, u32[]{:S(2)}, u32[]{:S(2)}) %collective-permute-start.16) | collective-permute-done | bytes 32800 | tf_op jit(solution)/shard_map/ppermute | solution.py:22
  137.9 3.3 %collective-permute-start.19 = (bf16[64,3,1]{2,0,1:T(8,128)(2,1)S(1)}, bf16[64,3,1]{2,0,1:T(8,128)(2,1)S(1)}, u32[]{:S(2)}, u32[]{:S(2)}) collective-permute-start(bf16[64,3,1]{2,0,1:T(8,128)(2,1)S(1)} %get-tuple-element.51), channel_id=1, source_target_pairs={{0,4},{4,8},{8,12},{12,16},{16,20},{20,24},{24,28},{28,32},{32,36}... | collective-permute-start | bytes 1160 | tf_op jit(solution)/shard_map/ppermute | solution.py:22
  143.5 5.5 %collective-permute-done.18 = bf16[64,3,1]{2,0,1:T(8,128)(2,1)S(1)} collective-permute-done((bf16[64,3,1]{2,0,1:T(8,128)(2,1)S(1)}, bf16[64,3,1]{2,0,1:T(8,128)(2,1)S(1)}, u32[]{:S(2)}, u32[]{:S(2)}) %collective-permute-start.18) | collective-permute-done | bytes 416 | tf_op jit(solution)/shard_map/ppermute | solution.py:23
  149.2 2.8 %fusion.3 = f32[64,256]{1,0:T(8,128)S(1)} fusion(bf16[5,64,64,256]{3,2,1,0:T(8,128)(2,1)S(1)} %copy-done.1, f32[5,64,256]{2,1,0:T(8,128)S(1)} %select_convert_fusion), kind=kLoop, calls=%fused_computation.12 | loop fusion | flops 15712256 | bytes 10878976 | tf_op jit(solution)/shard_map/reduce_sum | solution.py:196
  (148 shorter events, 39.5 us)
Async XLA Ops:
  0.6 75.9 %copy-start = (f32[48,64]{1,0:T(8,128)S(1)}, f32[48,64]{1,0:T(8,128)}, u32[]{:S(2)}) copy-start(f32[48,64]{1,0:T(8,128)} %param.26) | copy-start | bytes 36868
  1.7 41.2 %collective-permute-start.3 = (bf16[64,1,256]{2,1,0:T(2,128)(2,1)S(1)}, bf16[64,1,256]{2,1,0:T(2,128)(2,1)S(1)}, u32[]{:S(2)}, u32[]{:S(2)}) collective-permute-start(bf16[64,1,256]{2,1,0:T(2,128)(2,1)S(1)} %convert_element_type.85), channel_id=1, source_target_pairs={{1,0},{2,1},{3,2},{5,4},{6,5},{7,6},{9,8},{10,9},{11,10},{13,12},{... | collective-permute-start | bytes 98312 | tf_op jit(solution)/shard_map/ppermute | solution.py:23
  4.2 38.7 %collective-permute-start.2 = (bf16[64,1,256]{2,1,0:T(2,128)(2,1)S(1)}, bf16[64,1,256]{2,1,0:T(2,128)(2,1)S(1)}, u32[]{:S(2)}, u32[]{:S(2)}) collective-permute-start(bf16[64,1,256]{2,1,0:T(2,128)(2,1)S(1)} %convert_element_type.85), channel_id=1, source_target_pairs={{0,1},{1,2},{2,3},{4,5},{5,6},{6,7},{8,9},{9,10},{10,11},{12,13},{... | collective-permute-start | bytes 98312 | tf_op jit(solution)/shard_map/ppermute | solution.py:22
  15.3 41.1 %collective-permute-start = (bf16[5,32,4096]{2,1,0:T(8,128)(2,1)}, bf16[5,32,4096]{2,1,0:T(8,128)(2,1)S(1)}, u32[]{:S(2)}, u32[]{:S(2)}) collective-permute-start(bf16[5,32,4096]{2,1,0:T(8,128)(2,1)} %get-tuple-element.7), channel_id=1, source_target_pairs={{0,4},{4,8},{8,12},{12,16},{16,20},{20,24},{24,28},{28,32},{32,36}... | collective-permute-start | bytes 3932168 | tf_op jit(solution)/shard_map/ppermute | solution.py:32
  19.4 37.0 %collective-permute-start.1 = (bf16[5,32,4096]{2,1,0:T(8,128)(2,1)}, bf16[5,32,4096]{2,1,0:T(8,128)(2,1)S(1)}, u32[]{:S(2)}, u32[]{:S(2)}) collective-permute-start(bf16[5,32,4096]{2,1,0:T(8,128)(2,1)} %get-tuple-element.8), channel_id=1, source_target_pairs={{4,0},{8,4},{12,8},{16,12},{20,16},{24,20},{28,24},{32,28},{36,32}... | collective-permute-start | bytes 3932168 | tf_op jit(solution)/shard_map/ppermute | solution.py:33
  24.1 10.2 %collective-permute-start.6 = (f32[96,32]{0,1:T(8,128)S(1)}, f32[96,32]{0,1:T(8,128)S(1)}, u32[]{:S(2)}, u32[]{:S(2)}) collective-permute-start(f32[96,32]{0,1:T(8,128)S(1)} %get-tuple-element.57), channel_id=1, source_target_pairs={{0,4},{4,8},{8,12},{12,16},{16,20},{20,24},{24,28},{28,32},{32,36}... | collective-permute-start | bytes 36872 | tf_op jit(solution)/shard_map/ppermute | solution.py:32
  34.3 7.9 %collective-permute-start.7 = (f32[96,32]{0,1:T(8,128)S(1)}, f32[96,32]{0,1:T(8,128)S(1)}, u32[]{:S(2)}, u32[]{:S(2)}) collective-permute-start(f32[96,32]{0,1:T(8,128)S(1)} %get-tuple-element.56), channel_id=1, source_target_pairs={{4,0},{8,4},{12,8},{16,12},{20,16},{24,20},{28,24},{32,28},{36,32}... | collective-permute-start | bytes 36872 | tf_op jit(solution)/shard_map/ppermute | solution.py:33
  43.9 8.6 %collective-permute-start.4 = (bf16[64,3,1]{2,1,0:T(4,128)(2,1)}, bf16[64,3,1]{2,1,0:T(4,128)(2,1)}, u32[]{:S(2)}, u32[]{:S(2)}) collective-permute-start(bf16[64,3,1]{2,1,0:T(4,128)(2,1)} %get-tuple-element.48), channel_id=1, source_target_pairs={{4,0},{8,4},{12,8},{16,12},{20,16},{24,20},{28,24},{32,28},{36,32}... | collective-permute-start | bytes 1160 | tf_op jit(solution)/shard_map/ppermute | solution.py:23
  45.8 7.4 %collective-permute-start.5 = (bf16[64,3,1]{2,1,0:T(4,128)(2,1)}, bf16[64,3,1]{2,1,0:T(4,128)(2,1)}, u32[]{:S(2)}, u32[]{:S(2)}) collective-permute-start(bf16[64,3,1]{2,1,0:T(4,128)(2,1)} %get-tuple-element.49), channel_id=1, source_target_pairs={{0,4},{4,8},{8,12},{12,16},{16,20},{20,24},{24,28},{28,32},{32,36}... | collective-permute-start | bytes 1160 | tf_op jit(solution)/shard_map/ppermute | solution.py:22
  69.7 32.6 %copy-start.10 = (pred[5,256]{1,0:T(8,128)(4,1)S(1)}, pred[5,256]{1,0:T(8,128)(4,1)}, u32[]{:S(2)}) copy-start(pred[5,256]{1,0:T(8,128)(4,1)} %get-tuple-element.95) | copy-start | bytes 3844
  69.7 32.6 %copy-start.11 = (pred[5,256]{1,0:T(8,128)(4,1)S(1)}, pred[5,256]{1,0:T(8,128)(4,1)}, u32[]{:S(2)}) copy-start(pred[5,256]{1,0:T(8,128)(4,1)} %get-tuple-element.96) | copy-start | bytes 3844
  76.8 6.6 %collective-permute-start.9 = (bf16[64,1,256]{2,0,1:T(8,128)(2,1)S(1)}, bf16[64,1,256]{2,0,1:T(8,128)(2,1)S(1)}, u32[]{:S(2)}, u32[]{:S(2)}) collective-permute-start(bf16[64,1,256]{2,0,1:T(8,128)(2,1)S(1)} %bitcast.237), channel_id=1, source_target_pairs={{1,0},{2,1},{3,2},{5,4},{6,5},{7,6},{9,8},{10,9},{11,10},{13,12},{... | collective-permute-start | bytes 98312 | tf_op jit(solution)/shard_map/ppermute | solution.py:23
  81.1 4.7 %collective-permute-start.8 = (bf16[64,1,256]{2,0,1:T(8,128)(2,1)S(1)}, bf16[64,1,256]{2,0,1:T(8,128)(2,1)S(1)}, u32[]{:S(2)}, u32[]{:S(2)}) collective-permute-start(bf16[64,1,256]{2,0,1:T(8,128)(2,1)S(1)} %bitcast.238), channel_id=1, source_target_pairs={{0,1},{1,2},{2,3},{4,5},{5,6},{6,7},{8,9},{9,10},{10,11},{12,13},{... | collective-permute-start | bytes 98312 | tf_op jit(solution)/shard_map/ppermute | solution.py:22
  83.4 44.6 %copy-start.1 = (bf16[5,64,64,256]{3,2,1,0:T(8,128)(2,1)S(1)}, bf16[5,64,64,256]{3,2,1,0:T(8,128)(2,1)}, u32[]{:S(2)}) copy-start(bf16[5,64,64,256]{3,2,1,0:T(8,128)(2,1)} %shard_map.152) | copy-start | bytes 31457284
  85.9 10.9 %collective-permute-start.11 = (bf16[64,3,1]{2,0,1:T(8,128)(2,1)S(1)}, bf16[64,3,1]{2,0,1:T(8,128)(2,1)S(1)}, u32[]{:S(2)}, u32[]{:S(2)}) collective-permute-start(bf16[64,3,1]{2,0,1:T(8,128)(2,1)S(1)} %get-tuple-element.55), channel_id=1, source_target_pairs={{0,4},{4,8},{8,12},{12,16},{16,20},{20,24},{24,28},{28,32},{32,36}... | collective-permute-start | bytes 1160 | tf_op jit(solution)/shard_map/ppermute | solution.py:22
  94.7 7.5 %collective-permute-start.10 = (bf16[64,3,1]{2,0,1:T(8,128)(2,1)S(1)}, bf16[64,3,1]{2,0,1:T(8,128)(2,1)S(1)}, u32[]{:S(2)}, u32[]{:S(2)}) collective-permute-start(bf16[64,3,1]{2,0,1:T(8,128)(2,1)S(1)} %get-tuple-element.54), channel_id=1, source_target_pairs={{4,0},{8,4},{12,8},{16,12},{20,16},{24,20},{28,24},{32,28},{36,32}... | collective-permute-start | bytes 1160 | tf_op jit(solution)/shard_map/ppermute | solution.py:23
  109.4 3.7 %collective-permute-start.13 = (bf16[64,1,256]{2,0,1:T(8,128)(2,1)S(1)}, bf16[64,1,256]{2,0,1:T(8,128)(2,1)S(1)}, u32[]{:S(2)}, u32[]{:S(2)}) collective-permute-start(bf16[64,1,256]{2,0,1:T(8,128)(2,1)S(1)} %bitcast.242), channel_id=1, source_target_pairs={{1,0},{2,1},{3,2},{5,4},{6,5},{7,6},{9,8},{10,9},{11,10},{13,12},{... | collective-permute-start | bytes 98312 | tf_op jit(solution)/shard_map/ppermute | solution.py:23
  111.9 4.7 %collective-permute-start.12 = (bf16[64,1,256]{2,0,1:T(8,128)(2,1)S(1)}, bf16[64,1,256]{2,0,1:T(8,128)(2,1)S(1)}, u32[]{:S(2)}, u32[]{:S(2)}) collective-permute-start(bf16[64,1,256]{2,0,1:T(8,128)(2,1)S(1)} %bitcast.243), channel_id=1, source_target_pairs={{0,1},{1,2},{2,3},{4,5},{5,6},{6,7},{8,9},{9,10},{10,11},{12,13},{... | collective-permute-start | bytes 98312 | tf_op jit(solution)/shard_map/ppermute | solution.py:22
  116.6 5.5 %collective-permute-start.15 = (bf16[64,3,1]{2,0,1:T(8,128)(2,1)S(1)}, bf16[64,3,1]{2,0,1:T(8,128)(2,1)S(1)}, u32[]{:S(2)}, u32[]{:S(2)}) collective-permute-start(bf16[64,3,1]{2,0,1:T(8,128)(2,1)S(1)} %get-tuple-element.53), channel_id=1, source_target_pairs={{0,4},{4,8},{8,12},{12,16},{16,20},{20,24},{24,28},{28,32},{32,36}... | collective-permute-start | bytes 1160 | tf_op jit(solution)/shard_map/ppermute | solution.py:22
  120.2 7.5 %collective-permute-start.14 = (bf16[64,3,1]{2,0,1:T(8,128)(2,1)S(1)}, bf16[64,3,1]{2,0,1:T(8,128)(2,1)S(1)}, u32[]{:S(2)}, u32[]{:S(2)}) collective-permute-start(bf16[64,3,1]{2,0,1:T(8,128)(2,1)S(1)} %get-tuple-element.52), channel_id=1, source_target_pairs={{4,0},{8,4},{12,8},{16,12},{20,16},{24,20},{28,24},{32,28},{36,32}... | collective-permute-start | bytes 1160 | tf_op jit(solution)/shard_map/ppermute | solution.py:23
  131.0 3.5 %collective-permute-start.17 = (bf16[64,1,256]{2,0,1:T(8,128)(2,1)S(1)}, bf16[64,1,256]{2,0,1:T(8,128)(2,1)S(1)}, u32[]{:S(2)}, u32[]{:S(2)}) collective-permute-start(bf16[64,1,256]{2,0,1:T(8,128)(2,1)S(1)} %bitcast.232), channel_id=1, source_target_pairs={{1,0},{2,1},{3,2},{5,4},{6,5},{7,6},{9,8},{10,9},{11,10},{13,12},{... | collective-permute-start | bytes 98312 | tf_op jit(solution)/shard_map/ppermute | solution.py:23
  133.2 4.7 %collective-permute-start.16 = (bf16[64,1,256]{2,0,1:T(8,128)(2,1)S(1)}, bf16[64,1,256]{2,0,1:T(8,128)(2,1)S(1)}, u32[]{:S(2)}, u32[]{:S(2)}) collective-permute-start(bf16[64,1,256]{2,0,1:T(8,128)(2,1)S(1)} %bitcast.233), channel_id=1, source_target_pairs={{0,1},{1,2},{2,3},{4,5},{5,6},{6,7},{8,9},{9,10},{10,11},{12,13},{... | collective-permute-start | bytes 98312 | tf_op jit(solution)/shard_map/ppermute | solution.py:22
  137.9 5.5 %collective-permute-start.19 = (bf16[64,3,1]{2,0,1:T(8,128)(2,1)S(1)}, bf16[64,3,1]{2,0,1:T(8,128)(2,1)S(1)}, u32[]{:S(2)}, u32[]{:S(2)}) collective-permute-start(bf16[64,3,1]{2,0,1:T(8,128)(2,1)S(1)} %get-tuple-element.51), channel_id=1, source_target_pairs={{0,4},{4,8},{8,12},{12,16},{16,20},{20,24},{24,28},{28,32},{32,36}... | collective-permute-start | bytes 1160 | tf_op jit(solution)/shard_map/ppermute | solution.py:22
  141.5 7.5 %collective-permute-start.18 = (bf16[64,3,1]{2,0,1:T(8,128)(2,1)S(1)}, bf16[64,3,1]{2,0,1:T(8,128)(2,1)S(1)}, u32[]{:S(2)}, u32[]{:S(2)}) collective-permute-start(bf16[64,3,1]{2,0,1:T(8,128)(2,1)S(1)} %get-tuple-element.50), channel_id=1, source_target_pairs={{4,0},{8,4},{12,8},{16,12},{20,16},{24,20},{28,24},{32,28},{36,32}... | collective-permute-start | bytes 1160 | tf_op jit(solution)/shard_map/ppermute | solution.py:23
  (18 other events, 332.3 us)
